TPU v7x, 32 devices: a whole 2x2x4 slice. The times are simulated.
32 devices in a mesh: dp: 2 (over x), seq: 16 (over z, y, core).
Axes of the slice: x: 2, y: 2, z: 4, core: 2. Of those that a mesh axis runs over, the one named last changes fastest.
Arguments:
- first_query: bfloat16 [2, 16, 128, 1024], P('dp', 'seq'), may hold values from -6 to 6
- first_key: bfloat16 [2, 16, 128, 1024], P('dp', 'seq'), may hold values from -6 to 6
- first_value: bfloat16 [2, 16, 128, 1024], P('dp', 'seq'), may hold values from -6 to 6
- out_weight: bfloat16 [1024, 1024], replicated, may hold values from -1 to 1
- norm_gain: float32 [1024], replicated, may hold values from 0.5 to 2
- joint_weight: bfloat16 [1024, 3072], replicated, may hold values from -1 to 1
- upstream: bfloat16 [2, 16, 128, 1024], P('dp', 'seq'), may hold values from -6 to 6
Outputs:
- grad_query: bfloat16 [2, 16, 128, 1024], P('dp', 'seq')
- grad_key: bfloat16 [2, 16, 128, 1024], P('dp', 'seq')
- grad_value: bfloat16 [2, 16, 128, 1024], P('dp', 'seq')
- column_out: bfloat16 [2, 16, 128, 1024], P('dp', 'seq')
- grad_joint: bfloat16 [1024, 3072], P('seq')
- grad_projection: bfloat16 [1024, 1024], P('seq')
- grad_gain: float32 [1024], P('seq')
All inputs are finite; a program needn't handle non-finite values.
Results may differ from a plain program's by a relative error of at most 0.019.
The roundings to bfloat16 on the way count: a program that leaves them out, or rounds other values in their place, can miss the bound.
Values may be sent and summed in bfloat16 or wider, within the bound.
No kernel may reach another device: no remote copies, remote signals or barrier semaphores. Data moves between devices by JAX's collectives and lax.ppermute only.
A program may use at most 128 MiB of HBM per device.

v0:
```python
import jax
import jax.numpy as jnp
from jax import lax
from jax.sharding import PartitionSpec as P

HEAD_DIM = 128


epsilon = 1e-06


def attend(queries, key_table, values, layout, scores_form):
    keyed = layout.replace("l", "m")
    scaling = HEAD_DIM ** (-0.5)
    scores = (
        jnp.einsum(
            layout + "," + keyed + "->" + scores_form,
            queries,
            key_table,
            preferred_element_type=jnp.float32,
        )
        * scaling
    )
    extent = scores.shape[-1]
    causal = jnp.arange(extent)[:, None] >= jnp.arange(extent)[None, :]
    scores = jnp.where(causal, scores, -1e30)
    peak = jnp.max(scores, axis=-1, keepdims=True)
    weights = jnp.exp(scores - peak)
    prob_table = weights / jnp.sum(weights, axis=-1, keepdims=True)
    rounded = prob_table.astype(jnp.bfloat16)
    output = jnp.einsum(
        scores_form + "," + keyed + "->" + layout,
        rounded,
        values,
        preferred_element_type=jnp.float32,
    )
    return (output.astype(jnp.bfloat16), prob_table)


def attend_back(queries, key_table, values, prob_table, upstream_part, layout, scores_form):
    keyed = layout.replace("l", "m")
    scaling = HEAD_DIM ** (-0.5)
    grad_prob = jnp.einsum(
        layout + "," + keyed + "->" + scores_form,
        upstream_part,
        values,
        preferred_element_type=jnp.float32,
    )
    row_inner = jnp.sum(prob_table * grad_prob, axis=-1, keepdims=True)
    grad_score = (prob_table * (grad_prob - row_inner) * scaling).astype(jnp.bfloat16)
    grad_query = jnp.einsum(
        scores_form + "," + keyed + "->" + layout,
        grad_score,
        key_table,
        preferred_element_type=jnp.float32,
    )
    grad_key = jnp.einsum(
        scores_form + "," + layout + "->" + keyed,
        grad_score,
        queries,
        preferred_element_type=jnp.float32,
    )
    rounded = prob_table.astype(jnp.bfloat16)
    grad_value = jnp.einsum(
        scores_form + "," + layout + "->" + keyed,
        rounded,
        upstream_part,
        preferred_element_type=jnp.float32,
    )
    return (
        grad_query.astype(jnp.bfloat16),
        grad_key.astype(jnp.bfloat16),
        grad_value.astype(jnp.bfloat16),
    )


def on_device(first_query, first_key, first_value, out_weight, norm_gain, joint_weight, upstream):
    batches, local_rows, columns, feature = first_query.shape
    head_count = feature // HEAD_DIM
    model_width = out_weight.shape[1]
    groups = batches * local_rows

    def to_heads(tensor):
        return tensor.reshape(groups, columns, head_count, HEAD_DIM)

    out_first, probs_first = attend(
        to_heads(first_query), to_heads(first_key), to_heads(first_value), "glhe", "ghlm"
    )
    flat_first = out_first.reshape(groups * columns, feature)
    hidden = jnp.dot(flat_first, out_weight, preferred_element_type=jnp.float32)
    inverse = lax.rsqrt(jnp.mean(hidden * hidden, axis=-1, keepdims=True) + epsilon)
    normed = (hidden * inverse * norm_gain).astype(jnp.bfloat16)
    normed_cols = lax.all_to_all(
        normed.reshape(batches, local_rows, columns, model_width),
        "seq",
        split_axis=2,
        concat_axis=1,
        tiled=True,
    )
    joint_flat = jnp.dot(
        normed_cols.reshape(-1, model_width), joint_weight, preferred_element_type=jnp.float32
    )
    joint_cols = joint_flat.astype(jnp.bfloat16).reshape(
        batches, normed_cols.shape[1], normed_cols.shape[2], 3 * feature
    )
    all_rows, col_share = (joint_cols.shape[1], joint_cols.shape[2])
    pieces = joint_cols.reshape(batches, all_rows, col_share, 3, head_count, HEAD_DIM)
    query_cols, key_cols, value_cols = (pieces[:, :, :, 0], pieces[:, :, :, 1], pieces[:, :, :, 2])
    out_cols, probs_cols = attend(query_cols, key_cols, value_cols, "blche", "bchlm")
    column_out = lax.all_to_all(
        out_cols.reshape(batches, all_rows, col_share, feature),
        "seq",
        split_axis=1,
        concat_axis=2,
        tiled=True,
    )
    upstream_cols = lax.all_to_all(upstream, "seq", split_axis=2, concat_axis=1, tiled=True)
    upstream_cols = upstream_cols.reshape(batches, all_rows, col_share, head_count, HEAD_DIM)
    grads_cols = attend_back(
        query_cols, key_cols, value_cols, probs_cols, upstream_cols, "blche", "bchlm"
    )
    stacked = jnp.stack(grads_cols, axis=3).reshape(batches, all_rows, col_share, 3 * feature)
    used_normed = normed_cols.reshape(-1, model_width)
    used_grads = stacked.reshape(-1, 3 * feature)
    grad_local = jnp.dot(used_grads, joint_weight.T, preferred_element_type=jnp.float32).astype(
        jnp.bfloat16
    )
    grad_normed = lax.all_to_all(
        grad_local.reshape(batches, all_rows, col_share, model_width),
        "seq",
        split_axis=1,
        concat_axis=2,
        tiled=True,
    )
    grad_normed = grad_normed.reshape(-1, model_width)
    joint_share = lax.psum_scatter(
        jnp.dot(used_normed.T, used_grads, preferred_element_type=jnp.float32).astype(jnp.bfloat16),
        "seq",
        scatter_dimension=0,
        tiled=True,
    )
    grad_float = grad_normed.astype(jnp.float32)
    gain_term = jnp.sum(grad_float * hidden * inverse, axis=0)
    scaled = norm_gain * grad_float
    grad_hidden = (
        inverse * scaled - hidden * inverse**3 * jnp.mean(scaled * hidden, axis=-1, keepdims=True)
    ).astype(jnp.bfloat16)
    out_term = jnp.dot(flat_first.T, grad_hidden, preferred_element_type=jnp.float32)
    out_share, gain_share = (
        lax.psum_scatter(
            out_term.astype(jnp.bfloat16), "seq", scatter_dimension=0, tiled=True
        ).astype(jnp.float32),
        lax.psum_scatter(
            gain_term.astype(jnp.bfloat16), "seq", scatter_dimension=0, tiled=True
        ).astype(jnp.float32),
    )
    replicas = (
        lax.psum(joint_share, "dp").astype(jnp.float32),
        lax.psum(out_share.astype(jnp.bfloat16), "dp").astype(jnp.float32),
        lax.psum(gain_share.astype(jnp.bfloat16), "dp").astype(jnp.float32),
    )
    grad_first = jnp.dot(grad_hidden, out_weight.T, preferred_element_type=jnp.float32).astype(
        jnp.bfloat16
    )
    grads_rows = attend_back(
        to_heads(first_query),
        to_heads(first_key),
        to_heads(first_value),
        probs_first,
        to_heads(grad_first),
        "glhe",
        "ghlm",
    )
    grad_query = grads_rows[0].reshape(batches, local_rows, columns, feature)
    grad_key = grads_rows[1].reshape(batches, local_rows, columns, feature)
    grad_value = grads_rows[2].reshape(batches, local_rows, columns, feature)
    return (
        grad_query,
        grad_key,
        grad_value,
        column_out,
        replicas[0].astype(jnp.bfloat16),
        replicas[1].astype(jnp.bfloat16),
        replicas[2],
    )


def solution(mesh):
    placed = (
        P("dp", "seq", None, None),
        P("dp", "seq", None, None),
        P("dp", "seq", None, None),
        P(),
        P(),
        P(),
        P("dp", "seq", None, None),
    )
    return jax.shard_map(
        on_device,
        mesh=mesh,
        in_specs=placed,
        out_specs=(
            P("dp", "seq", None, None),
            P("dp", "seq", None, None),
            P("dp", "seq", None, None),
            P("dp", "seq", None, None),
            P("seq", None),
            P("seq", None),
            P("seq"),
        ),
        check_vma=False,
    )
```

profile of v0, /device:TPU:0, one launch (start us, length us, event | category | flops | bytes accessed | tf_op | source)
XLA Modules:
  0.0 294.3 jit_solution(1897687867830645557)
XLA Ops:
  7.2 1.5 copy.162
  9.2 2.1 reduce.14
  12.2 7.4 %all-to-all-start.1 = ((bf16[16,2,4096]{2,1,0:T(2,128)(2,1)}), bf16[16,2,4096]{2,1,0:T(2,128)(2,1)S(1)}, u32[]{:S(2)}, u32[]{:S(2)}) async-start(bf16[16,2,4096]{2,1,0:T(2,128)(2,1)} %reshape.239), calls=%async_computation.1 | async-start | bytes 524288 | tf_op jit(solution)/shard_map/all_to_all | solution.py:117
  22.0 1.8 copy.127
  25.2 1.3 convolution_convert_fusion.5
  27.7 2.9 reduce.15
  30.6 1.8 reshape.241
  32.4 6.1 %all-to-all-start = ((bf16[16,2,4096]{2,1,0:T(2,128)(2,1)}), bf16[16,2,4096]{2,1,0:T(2,128)(2,1)}, u32[]{:S(2)}, u32[]{:S(2)}) async-start(bf16[16,2,4096]{2,1,0:T(2,128)(2,1)} %reshape.241), calls=%async_computation | async-start | bytes 524288 | tf_op jit(solution)/shard_map/all_to_all | solution.py:93
  39.0 1.5 bitcast_reduce_fusion
  40.5 8.0 %all-to-all-done = bf16[16,2,4096]{2,1,0:T(2,128)(2,1)} async-done(((bf16[16,2,4096]{2,1,0:T(2,128)(2,1)}), bf16[16,2,4096]{2,1,0:T(2,128)(2,1)}, u32[]{:S(2)}, u32[]{:S(2)}) %all-to-all-start) | async-done | bytes 262176 | tf_op jit(solution)/shard_map/all_to_all | solution.py:93
  48.6 2.2 reshape.242
  50.7 4.0 %convolution_convert_fusion.1 = bf16[128,3072]{1,0:T(8,128)(2,1)S(1)} fusion(bf16[1024,3072]{1,0:T(8,128)(2,1)} %param.12, bf16[1,1,128,1024]{3,1,0,2:T(2,128)(2,1)S(1)} %bitcast.132), kind=kOutput, calls=%fused_computation.5 | convolution fusion | flops 805699584 | bytes 7340032 | tf_op jit(solution)/shard_map/dot_general | solution.py:100
  56.8 2.6 fusion.66
  59.4 2.1 fusion.19
  61.5 2.5 fusion.22
  64.0 2.4 fusion.18
  68.7 1.4 reshape_reshape.7
  70.1 5.0 %fusion.20 = bf16[1,16,8,1024]{3,2,0,1:T(8,128)(2,1)S(1)} fusion(bf16[128,3072]{1,0:T(8,128)(2,1)S(1)} %reshape_reshape.7, bf16[1024,3072]{1,0:T(8,128)(2,1)} %param.12), kind=kOutput, calls=%fused_computation.36 | convolution fusion | flops 805437440 | bytes 7340032 | tf_op jit(solution)/shard_map/dot_general | solution.py:125
  75.2 12.8 %all_to_all.19 = bf16[1,16,8,1024]{3,2,0,1:T(8,128)(2,1)S(1)} all-to-all(bf16[1,16,8,1024]{3,2,0,1:T(8,128)(2,1)S(1)} %fusion.20), channel_id=1, replica_groups=mesh['dp'=2,'seq'=16] {'seq'}, dimensions={1} | all-to-all | bytes 524288 | tf_op jit(solution)/shard_map/all_to_all | solution.py:128
  88.7 2.2 convolution_convert_fusion.2
  90.9 5.5 %convolution_convert_fusion = bf16[1024,3072]{1,0:T(8,128)(2,1)} fusion(bf16[128,3072]{1,0:T(8,128)(2,1)S(1)} %reshape_reshape.7, bf16[1,1,128,1024]{3,1,0,2:T(2,128)(2,1)} %bitcast.133), kind=kOutput, calls=%fused_computation.4 | convolution fusion | flops 808452096 | bytes 7340032 | tf_op jit(solution)/shard_map/dot_general | solution.py:137
  98.4 1.4 fusion.21
  100.7 3.5 %all-to-all-start.3 = ((bf16[1,16,8,1024]{3,2,0,1:T(8,128)(2,1)}), bf16[1,16,8,1024]{3,2,0,1:T(8,128)(2,1)S(1)}, u32[]{:S(2)}, u32[]{:S(2)}) async-start(bf16[1,16,8,1024]{3,2,0,1:T(8,128)(2,1)} %bitcast.36), calls=%async_computation.3 | async-start | bytes 524288 | tf_op jit(solution)/shard_map/all_to_all | solution.py:110
  106.7 44.2 %reduce-scatter.5.cloned.1.call-done = bf16[64,1024]{1,0:T(8,128)(2,1)} async-done(((bf16[1024,1024]{1,0:T(8,128)(2,1)}), bf16[64,1024]{1,0:T(8,128)(2,1)}) %reduce-scatter.5.cloned.1.call-update) | async-done | bytes 131088 | tf_op jit(solution)/shard_map/reduce_scatter | solution.py:150
  150.9 88.7 %reduce-scatter.3.cloned.1.call-done = bf16[64,3072]{1,0:T(8,128)(2,1)} async-done(((bf16[1024,3072]{1,0:T(8,128)(2,1)}), bf16[64,3072]{1,0:T(8,128)(2,1)}) %reduce-scatter.3.cloned.1.call-update) | async-done | bytes 393232 | tf_op jit(solution)/shard_map/reduce_scatter | solution.py:136
  239.6 1.7 convolution_convert_fusion.8
  241.3 31.1 %all-reduce = bf16[1024]{0:T(1024)(128)(2,1)S(1)} all-reduce(bf16[1024]{0:T(1024)(128)(2,1)S(1)} %get-tuple-element.35), channel_id=4, replica_groups=mesh['dp'=2,'seq'=16] {'seq'}, use_global_device_ids=true, to_apply=%region_13.14.clone | all-reduce | flops 1024 | bytes 4096
  272.5 4.9 %psum.23 = bf16[64]{0:T(256)(128)(2,1)S(1)} all-reduce(bf16[64]{0:T(256)(128)(2,1)S(1)} %dynamic-slice.1), channel_id=1, replica_groups=mesh['dp'=2,'seq'=16] {'dp'}, use_global_device_ids=true, to_apply=%region_14.15 | all-reduce | flops 64 | bytes 256 | tf_op jit(solution)/shard_map/psum | solution.py:160
  278.8 1.6 convolution_convert_fusion.3
  281.3 1.5 convolution_convert_fusion.7
  284.4 1.8 copy.168
  286.2 1.6 copy.169
  (69 shorter events, 20.3 us)
Async XLA Ops:
  7.2 19.3 %copy-start = (bf16[1024,1024]{1,0:T(8,128)(2,1)S(1)}, bf16[1024,1024]{1,0:T(8,128)(2,1)}, u32[]{:S(2)}) copy-start(bf16[1024,1024]{1,0:T(8,128)(2,1)} %param.10) | copy-start | bytes 6291460
  12.2 20.2 %all-to-all-start.1 = ((bf16[16,2,4096]{2,1,0:T(2,128)(2,1)}), bf16[16,2,4096]{2,1,0:T(2,128)(2,1)S(1)}, u32[]{:S(2)}, u32[]{:S(2)}) async-start(bf16[16,2,4096]{2,1,0:T(2,128)(2,1)} %reshape.239), calls=%async_computation.1 | async-start | bytes 524288 | tf_op jit(solution)/shard_map/all_to_all | solution.py:117
  20.8 6.3 %copy-start.8 = (bf16[1,1,128,1024]{2,3,1,0:T(8,128)(2,1)}, bf16[1,1,128,1024]{2,3,1,0:T(8,128)(2,1)S(1)}, u32[]{:S(2)}) copy-start(bf16[1,1,128,1024]{2,3,1,0:T(8,128)(2,1)S(1)} %copy.125) | copy-start | bytes 786436
  20.8 6.4 %copy-start.12 = (f32[1024]{0:T(1024)S(1)}, f32[1024]{0:T(1024)}, u32[]{:S(2)}) copy-start(f32[1024]{0:T(1024)} %param.11) | copy-start | bytes 12292
  22.0 3.2 %copy-start.7 = (bf16[1,1,128,1024]{2,3,1,0:T(8,128)(2,1)}, bf16[1,1,128,1024]{2,3,1,0:T(8,128)(2,1)S(1)}, u32[]{:S(2)}) copy-start(bf16[1,1,128,1024]{2,3,1,0:T(8,128)(2,1)S(1)} %copy.124) | copy-start | bytes 786436
  24.1 2.3 copy-start.4
  26.5 0.7 copy-start.5
  32.4 16.2 %all-to-all-start = ((bf16[16,2,4096]{2,1,0:T(2,128)(2,1)}), bf16[16,2,4096]{2,1,0:T(2,128)(2,1)}, u32[]{:S(2)}, u32[]{:S(2)}) async-start(bf16[16,2,4096]{2,1,0:T(2,128)(2,1)} %reshape.241), calls=%async_computation | async-start | bytes 524288 | tf_op jit(solution)/shard_map/all_to_all | solution.py:93
  38.5 112.4 %reduce-scatter.5.cloned.1.call-start = ((), (), s32[]{:S(2)}) async-start(), calls=%async_computation.7 | async-start | bytes 2228224 | tf_op jit(solution)/shard_map/reduce_scatter | solution.py:150
  50.7 4.0 %copy-start.3 = (bf16[128,1,1,1024]{3,2,1,0:T(2,128)(2,1)}, bf16[128,1,1,1024]{3,2,1,0:T(2,128)(2,1)S(1)}, u32[]{:S(2)}) copy-start(bf16[128,1,1,1024]{3,2,1,0:T(2,128)(2,1)S(1)} %reshape.242) | copy-start | bytes 786436
  55.6 0.7 copy-start.9
  61.5 5.0 %copy-start.11 = (bf16[1,16,8,1,8,128]{5,1,4,2,3,0:T(8,128)(2,1)S(1)}, bf16[1,16,8,1,8,128]{5,1,4,2,3,0:T(8,128)(2,1)}, u32[]{:S(2)}) copy-start(bf16[1,16,8,1,8,128]{5,1,4,2,3,0:T(8,128)(2,1)} %fusion.19) | copy-start | bytes 786436
  70.1 18.6 %copy-start.6 = (bf16[8,128,128]{1,2,0:T(8,128)(2,1)S(1)}, bf16[8,128,128]{1,2,0:T(8,128)(2,1)}, u32[]{:S(2)}) copy-start(bf16[8,128,128]{1,2,0:T(8,128)(2,1)} %copy-done.5) | copy-start | bytes 786436
  88.0 0.7 copy-start.1
  90.9 148.7 %reduce-scatter.3.cloned.1.call-start = ((), (), s32[]{:S(2)}) async-start(), calls=%async_computation.6 | async-start | bytes 6684672 | tf_op jit(solution)/shard_map/reduce_scatter | solution.py:136
  96.5 0.7 copy-start.13
  96.5 1.9 copy-start.10
  96.5 8.0 %copy-start.2 = (bf16[1,16,8,1024]{3,2,0,1:T(8,128)(2,1)S(1)}, bf16[1,16,8,1024]{3,2,0,1:T(8,128)(2,1)}, u32[]{:S(2)}) copy-start(bf16[1,16,8,1024]{3,2,0,1:T(8,128)(2,1)} %copy-done.1) | copy-start | bytes 786436
  100.7 140.6 %all-to-all-start.3 = ((bf16[1,16,8,1024]{3,2,0,1:T(8,128)(2,1)}), bf16[1,16,8,1024]{3,2,0,1:T(8,128)(2,1)S(1)}, u32[]{:S(2)}, u32[]{:S(2)}) async-start(bf16[1,16,8,1024]{3,2,0,1:T(8,128)(2,1)} %bitcast.36), calls=%async_computation.3 | async-start | bytes 524288 | tf_op jit(solution)/shard_map/all_to_all | solution.py:110
  104.2 179.5 %all-reduce.4.cloned.1.call-start = ((), (), s32[]{:S(2)}) async-start(), calls=%async_computation.8 | async-start | bytes 1048576 | tf_op jit(solution)/shard_map/psum | solution.py:158
Sparse Core Ops, SparseCore 0:
  91.0 59.8 reduce-scatter.4
  155.3 84.1 reduce-scatter.2
  241.9 28.0 all-reduce.3
where the time goes:
time: 295 us; the launch traced here: 294 us
  waiting for transfers between devices  141 us (48%)
  blocking collectives  48.9 us (17%)
  matrix products  37.2 us (13%)
  local copies, waits for them, and re-layouts  26.9 us (9%)
  starting transfers between devices  17.5 us (6%)
  between operations  14.7 us (5%)
  other arithmetic  8.05 us (3%)
    reduce_scatter x1, waiting for transfers between devices, on_device(): lax.psum_scatter(jnp.dot(used_normed.T, used_grads, preferred_element_typ...  88.7 us
    reduce_scatter x1, waiting for transfers between devices, on_device(): lax.psum_scatter(out_term.astype(jnp.bfloat16), 'seq', scatter_dimension=...  44.2 us
    unnamed x1, blocking collectives  31.1 us
    unnamed x44, local copies, waits for them, and re-layouts  18.2 us
    all_to_all x1, blocking collectives, on_device(): lax.all_to_all(grad_local.reshape(batches, all_rows, col_share, model_wid...  12.8 us
    all_to_all x1, waiting for transfers between devices, on_device(): lax.all_to_all(normed.reshape(batches, local_rows, columns, model_width),...  8.03 us
    all_to_all x1, starting transfers between devices, on_device(): lax.all_to_all(upstream, 'seq', split_axis=2, concat_axis=1, tiled=True)  7.39 us
    all_to_all x1, starting transfers between devices, on_device(): lax.all_to_all(normed.reshape(batches, local_rows, columns, model_width),...  6.06 us
  transfers between devices with their start and end apart: 6, of which 3 were waited for; matrix products, arithmetic and copies ran while one was open for 11% of the time, Pallas kernels for 0%

commit v1 on v0

--- a/solution.py
+++ b/solution.py
@@ -74,6 +74,64 @@
     )
 
 
+def split_orders(seq_n):
+    bits = seq_n.bit_length() - 1
+    assert 1 << bits == seq_n
+    even = list(range(bits))
+    odd = list(even)
+    if bits >= 3:
+        odd[1], odd[2] = odd[2], odd[1]
+    return even, odd
+
+
+def by_split_order(matrix, orders, core_odd, seq_n):
+    bits = seq_n.bit_length() - 1
+    lead = matrix.shape[0]
+    block = matrix.shape[1] // seq_n
+    grid = matrix.reshape((lead,) + (2,) * bits + (matrix.shape[1] // seq_n,))
+
+    def arrange(order):
+        axes = (0,) + tuple(1 + (bits - 1 - bit) for bit in order) + (bits + 1,)
+        return jnp.transpose(grid, axes).reshape(lead, seq_n * block)
+
+    even, odd = orders
+    if even == odd:
+        return arrange(even)
+    return jnp.where(core_odd, arrange(odd), arrange(even))
+
+
+def reduce_rows(parts, orders, seq_n, dp_n):
+    bits = seq_n.bit_length() - 1
+    index = lax.axis_index("seq")
+    accs = tuple(p.reshape((2,) * bits + (p.shape[0] // seq_n, p.shape[1])) for p in parts)
+    even, odd = orders
+    for step in range(bits):
+        perm = []
+        for member in range(seq_n):
+            bit = (odd if member % 2 else even)[step]
+            perm.append((member, member ^ (1 << bit)))
+        bit_even, bit_odd = even[step], odd[step]
+        keep_even = (index // (1 << bit_even)) % 2
+        keep_odd = (index // (1 << bit_odd)) % 2
+        keep_at = jnp.where(index % 2 == 1, keep_odd, keep_even)
+        kept = tuple(lax.dynamic_index_in_dim(acc, keep_at, 0, keepdims=False) for acc in accs)
+        given = tuple(
+            lax.dynamic_index_in_dim(acc, 1 - keep_at, 0, keepdims=False).astype(jnp.bfloat16)
+            for acc in accs
+        )
+        if step == 0 and even != odd:
+            given = tuple(jnp.swapaxes(g, 0, 1) for g in given)
+        got = lax.ppermute(given, "seq", perm)
+        accs = tuple(k + g.astype(jnp.float32) for k, g in zip(kept, got))
+    dp_bits = dp_n.bit_length() - 1
+    assert 1 << dp_bits == dp_n
+    for step in range(dp_bits):
+        perm = [(member, member ^ (1 << step)) for member in range(dp_n)]
+        mine = tuple(acc.astype(jnp.bfloat16) for acc in accs)
+        got = lax.ppermute(mine, "dp", perm)
+        accs = tuple(m.astype(jnp.float32) + g.astype(jnp.float32) for m, g in zip(mine, got))
+    return accs
+
 def on_device(first_query, first_key, first_value, out_weight, norm_gain, joint_weight, upstream):
     batches, local_rows, columns, feature = first_query.shape
     head_count = feature // HEAD_DIM
@@ -133,11 +191,14 @@
         tiled=True,
     )
     grad_normed = grad_normed.reshape(-1, model_width)
-    joint_share = lax.psum_scatter(
-        jnp.dot(used_normed.T, used_grads, preferred_element_type=jnp.float32).astype(jnp.bfloat16),
-        "seq",
-        scatter_dimension=0,
-        tiled=True,
+    seq_n = lax.axis_size("seq")
+    dp_n = lax.axis_size("dp")
+    orders = split_orders(seq_n)
+    core_odd = lax.axis_index("seq") % 2 == 1
+    joint_term = jnp.dot(
+        by_split_order(used_normed, orders, core_odd, seq_n).T,
+        used_grads,
+        preferred_element_type=jnp.float32,
     )
     grad_float = grad_normed.astype(jnp.float32)
     gain_term = jnp.sum(grad_float * hidden * inverse, axis=0)
@@ -145,20 +206,14 @@
     grad_hidden = (
         inverse * scaled - hidden * inverse**3 * jnp.mean(scaled * hidden, axis=-1, keepdims=True)
     ).astype(jnp.bfloat16)
-    out_term = jnp.dot(flat_first.T, grad_hidden, preferred_element_type=jnp.float32)
-    out_share, gain_share = (
-        lax.psum_scatter(
-            out_term.astype(jnp.bfloat16), "seq", scatter_dimension=0, tiled=True
-        ).astype(jnp.float32),
-        lax.psum_scatter(
-            gain_term.astype(jnp.bfloat16), "seq", scatter_dimension=0, tiled=True
-        ).astype(jnp.float32),
-    )
-    replicas = (
-        lax.psum(joint_share, "dp").astype(jnp.float32),
-        lax.psum(out_share.astype(jnp.bfloat16), "dp").astype(jnp.float32),
-        lax.psum(gain_share.astype(jnp.bfloat16), "dp").astype(jnp.float32),
-    )
+    out_term = jnp.dot(
+        by_split_order(flat_first, orders, core_odd, seq_n).T,
+        grad_hidden,
+        preferred_element_type=jnp.float32,
+    )
+    gain_term = by_split_order(gain_term[None, :], orders, core_odd, seq_n)[0][:, None]
+    joint_sum, out_sum, gain_sum = reduce_rows((joint_term, out_term, gain_term), orders, seq_n, dp_n)
+    replicas = (joint_sum, out_sum, gain_sum[:, 0])
     grad_first = jnp.dot(grad_hidden, out_weight.T, preferred_element_type=jnp.float32).astype(
         jnp.bfloat16
     )

time: 295 us -> 192 us (0.65)
  waiting for transfers between devices: 141 us -> 62.2 us
  blocking collectives: 48.9 us -> 0 us
  starting transfers between devices: 17.5 us -> 39.4 us
  between operations: 14.7 us -> 1.39 us
  other arithmetic: 8.05 us -> 20.3 us
  local copies, waits for them, and re-layouts: 26.9 us -> 34.6 us
  matrix products: 37.2 us -> 33.3 us
    reduce_scatter x2 -> x0, waiting for transfers between devices: 133 us -> none  [the longest x1 88.7 us: on_device(): lax.psum_scatter(jnp.dot(used_normed.T, used_grads, preferred_element_typ...]
    ppermute x0 -> x15, waiting for transfers between devices: none -> 48.8 us  [the longest x12 41.7 us: reduce_rows(): got = lax.ppermute(given, 'seq', perm)]
    unnamed x1 -> x0, blocking collectives: 31.1 us -> none
    ppermute x0 -> x15, starting transfers between devices: none -> 18.2 us  [the longest x12 13.6 us: reduce_rows(): got = lax.ppermute(given, 'seq', perm)]
    all_to_all x1 -> x0, blocking collectives: 12.8 us -> none  [on_device(): lax.all_to_all(grad_local.reshape(batches, all_rows, col_share, model_wid...]
    add x0 -> x9, other arithmetic: none -> 10.5 us  [reduce_rows(): accs = tuple((k + g.astype(jnp.float32) for k, g in zip(kept, got)))]
    all_to_all x0 -> x1, waiting for transfers between devices: none -> 7.6 us  [on_device(): lax.all_to_all(grad_local.reshape(batches, all_rows, col_share, model_wid...]
    psum x1 -> x0, blocking collectives: 4.92 us -> none  [on_device(): lax.psum(gain_share.astype(jnp.bfloat16), 'dp').astype(jnp.float32)]
  transfers between devices with their start and end apart: 6 -> 19, of which waited for: 3 -> 9; matrix products, arithmetic and copies ran while one was open for 11% -> 25% of each run, Pallas kernels for 0% -> 0%
where the time goes in v1:
time: 192 us; the launch traced here: 191 us
  waiting for transfers between devices  62.2 us (32%)
  starting transfers between devices  39.4 us (21%)
  local copies, waits for them, and re-layouts  34.6 us (18%)
  matrix products  33.3 us (17%)
  other arithmetic  20.3 us (11%)
    ppermute x12, waiting for transfers between devices, reduce_rows(): got = lax.ppermute(given, 'seq', perm)  41.7 us
    unnamed x62, local copies, waits for them, and re-layouts  21.4 us
    ppermute x12, starting transfers between devices, reduce_rows(): got = lax.ppermute(given, 'seq', perm)  13.6 us
    add x9, other arithmetic, reduce_rows(): accs = tuple((k + g.astype(jnp.float32) for k, g in zip(kept, got)))  10.5 us
    all_to_all x1, waiting for transfers between devices, on_device(): lax.all_to_all(grad_local.reshape(batches, all_rows, col_share, model_wid...  7.6 us
    all_to_all x1, starting transfers between devices, on_device(): lax.all_to_all(upstream, 'seq', split_axis=2, concat_axis=1, tiled=True)  7.44 us
    ppermute x3, waiting for transfers between devices, reduce_rows(): got = lax.ppermute(mine, 'dp', perm)  7.12 us
    all_to_all x1, starting transfers between devices, on_device(): lax.all_to_all(normed.reshape(batches, local_rows, columns, model_width),...  5.77 us
  transfers between devices with their start and end apart: 19, of which 9 were waited for; matrix products, arithmetic and copies ran while one was open for 25% of the time, Pallas kernels for 0%

profile of v1, /device:TPU:0, one launch (start us, length us, event | category | flops | bytes accessed | tf_op | source)
XLA Modules:
  0.0 191.1 jit_solution(15212695491731509526)
XLA Ops:
  2.7 2.1 %reduce.14 = bf16[128,1024]{1,0:T(8,128)(2,1)S(1)} reduce(bf16[128,1,1,1024]{3,2,1,0:T(2,128)(2,1)S(1)} %bitcast.247, bf16[]{:T(256)} %broadcast.110), dimensions={1,2}, to_apply=%bitcast.237.reduce_sub_computation | reduce | bytes 524290
  5.7 7.4 %all-to-all-start.1 = ((bf16[16,2,4096]{2,1,0:T(2,128)(2,1)}), bf16[16,2,4096]{2,1,0:T(2,128)(2,1)}, u32[]{:S(2)}, u32[]{:S(2)}) async-start(bf16[16,2,4096]{2,1,0:T(2,128)(2,1)} %reshape.351), calls=%async_computation.1 | async-start | bytes 524288 | tf_op jit(solution)/shard_map/all_to_all | solution.py:175
  18.4 2.9 %reduce.15 = bf16[128,1024]{1,0:T(8,128)(2,1)} reduce(bf16[128,1,1,1024]{3,2,1,0:T(2,128)(2,1)S(1)} %bitcast.248, bf16[]{:T(256)} %broadcast.110), dimensions={1,2}, to_apply=%bitcast.238.reduce_sub_computation | reduce | bytes 524290
  21.2 1.8 reshape.353
  23.3 5.8 %all-to-all-start = ((bf16[16,2,4096]{2,1,0:T(2,128)(2,1)}), bf16[16,2,4096]{2,1,0:T(2,128)(2,1)S(1)}, u32[]{:S(2)}, u32[]{:S(2)}) async-start(bf16[16,2,4096]{2,1,0:T(2,128)(2,1)} %reshape.353), calls=%async_computation | async-start | bytes 524288 | tf_op jit(solution)/shard_map/all_to_all | solution.py:151
  29.1 2.2 %reshape.352 = bf16[128,1,1,1024]{3,2,1,0:T(2,128)(2,1)S(1)} reshape(bf16[16,2,4096]{2,1,0:T(2,128)(2,1)} %all-to-all-done.1) | data formatting | bytes 524288
  33.5 5.6 %all-to-all-done = bf16[16,2,4096]{2,1,0:T(2,128)(2,1)S(1)} async-done(((bf16[16,2,4096]{2,1,0:T(2,128)(2,1)}), bf16[16,2,4096]{2,1,0:T(2,128)(2,1)S(1)}, u32[]{:S(2)}, u32[]{:S(2)}) %all-to-all-start) | async-done | bytes 262176 | tf_op jit(solution)/shard_map/all_to_all | solution.py:151
  40.4 3.8 %convolution_convert_fusion = bf16[128,3072]{1,0:T(8,128)(2,1)S(1)} fusion(bf16[1024,3072]{1,0:T(8,128)(2,1)} %param.12, bf16[1,1,128,1024]{3,1,0,2:T(2,128)(2,1)S(1)} %bitcast.243), kind=kOutput, calls=%fused_computation.6 | convolution fusion | flops 805699584 | bytes 7340032 | tf_op jit(solution)/shard_map/dot_general | solution.py:158
  46.3 2.6 %fusion.96 = (f32[8,8,16]{2,1,0:T(8,128)S(1)}, f32[8,8,16,16]{2,3,1,0:T(8,128)}) fusion(pred[16,16]{0,1:T(8,128)(4,1)S(1)} %iota_compare_fusion.1, bf16[1,16,8,1,8,128]{5,2,4,3,1,0:T(8,128)(2,1)} %get-tuple-element.46, bf16[1,16,8,1,8,128]{5,2,4,3,1,0:T(8,128)(2,1)} %get-tuple-element.45), kind=kOutput, calls=%fused_computation.159 | convolution fusion | flops 4259855 | bytes 594176 | tf_op jit(solution)/shard_map/sub | solution.py:28
  49.0 2.1 %fusion.21 = bf16[1,16,8,1,8,128]{5,1,4,2,3,0:T(8,128)(2,1)} fusion(bf16[16,8,8,128]{3,2,1,0:T(8,128)(2,1)S(1)} %copy-done.18, f32[8,8,16,16]{2,3,1,0:T(8,128)} %get-tuple-element.54, f32[8,8,16]{2,1,0:T(8,128)S(1)} %get-tuple-element.53), kind=kOutput, calls=%fused_computation.43 | convolution fusion | flops 4358144 | bytes 593920 | tf_op jit(solution)/shard_map/bchlm,blche->bmche/dot_general | solution.py:64
  51.1 2.5 %fusion.24 = bf16[1,16,8,1,8,128]{5,1,4,2,3,0:T(8,128)(2,1)} fusion(f32[8,8,16,16]{2,3,1,0:T(8,128)S(1)} %convolution_bitcast_fusion, bf16[1,16,8,1,8,128]{5,2,4,3,1,0:T(8,128)(2,1)} %get-tuple-element.45, f32[8,8,16,16]{2,3,1,0:T(8,128)} %get-tuple-element.54, f32[8,8,16]{2,1,0:T(8,128)S(1)} %get-tuple-element.53), kind=kOutput, calls=%fused_computation.46 | convolution fusion | flops 4441103 | bytes 659456 | tf_op jit(solution)/shard_map/bchlm,blche->bmche/dot_general | solution.py:57
  53.6 2.4 %fusion.20 = bf16[1,16,8,1,8,128]{5,1,4,2,3,0:T(8,128)(2,1)} fusion(f32[8,8,16,16]{2,3,1,0:T(8,128)S(1)} %convolution_bitcast_fusion, bf16[1,16,8,1,8,128]{5,2,4,3,1,0:T(8,128)(2,1)S(1)} %copy-done.23, f32[8,8,16,16]{2,3,1,0:T(8,128)} %get-tuple-element.54, f32[8,8,16]{2,1,0:T(8,128)S(1)} %get-tuple-element.53), kind=kOutput, calls=%fused_computation.42 | convolution fusion | flops 4441103 | bytes 659456 | tf_op jit(solution)/shard_map/bchlm,bmche->blche/dot_general | solution.py:51
  59.9 3.1 %fusion.36 = f32[2,2,2,2,64,3072]{5,4,3,2,1,0:T(8,128)S(1)} fusion(bf16[128,3072,1,1,1,1]{1,0,2,3,4,5:T(8,128)(2,1)} %reshape.347, bf16[128,2,2,2,2,64]{0,5,1,2,3,4:T(8,128)(2,1)} %bitcast.245, bf16[128,2,2,2,2,64]{0,5,4,3,2,1:T(8,128)(2,1)} %bitcast.246, pred[]{:T(512)S(6)} %eq.21), kind=kOutput, calls=%fused_computation.60 | convolution fusion | flops 805437440 | bytes 13893633 | tf_op jit(solution)/shard_map/dot_general | solution.py:198
  63.0 4.5 %copy-done.2 = f32[2,2,2,2,64,3072]{5,4,3,2,1,0:T(8,128)} copy-done((f32[2,2,2,2,64,3072]{5,4,3,2,1,0:T(8,128)}, f32[2,2,2,2,64,3072]{5,4,3,2,1,0:T(8,128)S(1)}, u32[]{:S(2)}) %copy-start.2) | copy-done | bytes 12582936
  67.5 2.2 %fusion.4 = bf16[2,2,2,64,3072]{4,3,2,0,1:T(8,128)(2,1)} fusion(f32[2,2,2,2,64,3072]{5,4,3,2,1,0:T(8,128)S(1)} %fusion.36, s32[]{:T(128)S(6)} %select_n.165), kind=kLoop, calls=%fused_computation.7 | loop fusion | bytes 6291460 | tf_op jit(solution)/shard_map/transpose | solution.py:123
  69.7 5.7 %fusion.22 = bf16[1,16,8,1024]{3,2,0,1:T(8,128)(2,1)} fusion(bf16[128,3072]{1,0:T(8,128)(2,1)S(1)} %copy-done.8, bf16[1024,3072]{1,0:T(8,128)(2,1)} %param.12), kind=kOutput, calls=%fused_computation.44 | convolution fusion | flops 805437440 | bytes 7340032 | tf_op jit(solution)/shard_map/dot_general | solution.py:183
  75.4 3.5 %all-to-all-start.2 = ((bf16[1,16,8,1024]{3,2,0,1:T(8,128)(2,1)}), bf16[1,16,8,1024]{3,2,0,1:T(8,128)(2,1)S(1)}, u32[]{:S(2)}, u32[]{:S(2)}) async-start(bf16[1,16,8,1024]{3,2,0,1:T(8,128)(2,1)} %fusion.22), calls=%async_computation.2 | async-start | bytes 524288 | tf_op jit(solution)/shard_map/all_to_all | solution.py:186
  81.4 7.6 %all-to-all-done.2 = bf16[1,16,8,1024]{3,2,0,1:T(8,128)(2,1)S(1)} async-done(((bf16[1,16,8,1024]{3,2,0,1:T(8,128)(2,1)}), bf16[1,16,8,1024]{3,2,0,1:T(8,128)(2,1)S(1)}, u32[]{:S(2)}, u32[]{:S(2)}) %all-to-all-start.2) | async-done | bytes 262176 | tf_op jit(solution)/shard_map/all_to_all | solution.py:186
  89.0 4.4 %all-to-all-start.3 = ((bf16[1,16,8,1024]{3,2,0,1:T(8,128)(2,1)}), bf16[1,16,8,1024]{3,2,0,1:T(8,128)(2,1)}, u32[]{:S(2)}, u32[]{:S(2)}) async-start(bf16[1,16,8,1024]{3,2,0,1:T(8,128)(2,1)} %bitcast.36), calls=%async_computation.3 | async-start | bytes 524288 | tf_op jit(solution)/shard_map/all_to_all | solution.py:168
  95.7 1.9 %copy-done.4 = f32[2,2,2,2,64,1024]{5,4,3,2,1,0:T(8,128)} copy-done((f32[2,2,2,2,64,1024]{5,4,3,2,1,0:T(8,128)}, f32[2,2,2,2,64,1024]{5,4,3,2,1,0:T(8,128)S(1)}, u32[]{:S(2)}) %copy-start.4) | copy-done | bytes 4194328
  100.1 2.3 %convolution_convert_fusion.6 = bf16[8,128,128]{1,2,0:T(8,128)(2,1)} fusion(bf16[128,8,128]{0,2,1:T(8,128)(2,1)S(1)} %bitcast.251, f32[8,128,128]{1,2,0:T(8,128)S(1)} %fusion.63, f32[8,128,128]{1,2,0:T(8,128)} %get-tuple-element.50, f32[8,128]{1,0:T(8,128)S(1)} %get-tuple-element.49), kind=kOutput, calls=%fused_computation.37 | convolution fusion | flops 34604160 | bytes 1576960 | tf_op jit(solution)/shard_map/ghlm,glhe->gmhe/dot_general | solution.py:57
  102.4 4.7 %bitcast_add_fusion = f32[2,2,2,64,3072]{4,3,2,0,1:T(8,128)S(1)} fusion(bf16[2,2,2,64,3072]{4,3,2,0,1:T(8,128)(2,1)} %collective-permute-done, f32[2,2,2,2,64,3072]{5,4,3,2,1,0:T(8,128)} %copy-done.2, s32[]{:T(128)S(6)} %select_n.164), kind=kLoop, calls=%fused_computation.4 | loop fusion | flops 3145728 | bytes 15728644 | tf_op jit(solution)/shard_map/add | solution.py:125
  114.2 2.2 %convolution_convert_fusion.5 = bf16[8,128,128]{2,1,0:T(8,128)(2,1)} fusion(bf16[128,8,128]{0,2,1:T(8,128)(2,1)S(1)} %bitcast.257, f32[8,128]{1,0:T(8,128)S(1)} %get-tuple-element.49, f32[8,128,128]{1,2,0:T(8,128)} %copy-done.9), kind=kOutput, calls=%fused_computation.36 | convolution fusion | flops 34079872 | bytes 1052672 | tf_op jit(solution)/shard_map/ghlm,glhe->gmhe/dot_general | solution.py:64
  119.9 9.6 %collective-permute-done.11 = bf16[2,2,64,1]{2,1,0,3:T(2,128)(2,1)S(1)} collective-permute-done((bf16[2,2,64,1]{2,1,0,3:T(2,128)(2,1)S(1)}, bf16[2,2,64,1]{2,1,0,3:T(2,128)(2,1)S(1)}, u32[]{:S(2)}, u32[]{:S(2)}) %collective-permute-start.11) | collective-permute-done | bytes 544 | tf_op jit(solution)/shard_map/ppermute | solution.py:124
  131.1 4.1 %collective-permute-done.6 = bf16[2,2,64,1024]{3,2,1,0:T(8,128)(2,1)} collective-permute-done((bf16[2,2,64,1024]{3,2,1,0:T(8,128)(2,1)S(1)}, bf16[2,2,64,1024]{3,2,1,0:T(8,128)(2,1)}, u32[]{:S(2)}, u32[]{:S(2)}) %collective-permute-start.6) | collective-permute-done | bytes 524320 | tf_op jit(solution)/shard_map/ppermute | solution.py:124
  136.4 2.8 %bitcast_add_fusion.1 = f32[2,2,64,3072]{3,2,1,0:T(8,128)S(1)} fusion(bf16[2,2,64,3072]{3,2,1,0:T(8,128)(2,1)} %collective-permute-done.1, f32[2,2,2,64,3072]{4,3,2,0,1:T(8,128)} %copy-done.3, s32[]{:T(128)S(6)} %select_n.171), kind=kLoop, calls=%fused_computation.8 | loop fusion | flops 1572864 | bytes 7864324 | tf_op jit(solution)/shard_map/add | solution.py:125
  141.5 2.5 %collective-permute-start.13 = (bf16[64,1]{0,1:T(2,128)(2,1)S(1)}, bf16[64,1]{0,1:T(2,128)(2,1)S(1)}, u32[]{:S(2)}, u32[]{:S(2)}) collective-permute-start(bf16[64,1]{0,1:T(2,128)(2,1)S(1)} %fusion.85), channel_id=1, source_target_pairs={{0,8},{1,9},{2,10},{3,11},{4,12},{5,13},{6,14},{7,15},{8,0},{9,1},... | collective-permute-start | bytes 392 | tf_op jit(solution)/shard_map/ppermute | solution.py:124
  144.1 10.1 %collective-permute-done.7 = bf16[2,64,1024]{2,1,0:T(8,128)(2,1)S(1)} collective-permute-done((bf16[2,64,1024]{2,1,0:T(8,128)(2,1)S(1)}, bf16[2,64,1024]{2,1,0:T(8,128)(2,1)S(1)}, u32[]{:S(2)}, u32[]{:S(2)}) %collective-permute-start.7) | collective-permute-done | bytes 262176 | tf_op jit(solution)/shard_map/ppermute | solution.py:124
  154.3 2.5 %collective-permute-start.8 = (bf16[64,1024]{1,0:T(8,128)(2,1)S(1)}, bf16[64,1024]{1,0:T(8,128)(2,1)S(1)}, u32[]{:S(2)}, u32[]{:S(2)}) collective-permute-start(bf16[64,1024]{1,0:T(8,128)(2,1)S(1)} %fusion.67), channel_id=1, source_target_pairs={{0,8},{1,9},{2,10},{3,11},{4,12},{5,13},{6,14},{7,15},{8,0},{9,1},... | collective-permute-start | bytes 393224 | tf_op jit(solution)/shard_map/ppermute | solution.py:124
  159.2 12.4 %collective-permute-done.8 = bf16[64,1024]{1,0:T(8,128)(2,1)S(1)} collective-permute-done((bf16[64,1024]{1,0:T(8,128)(2,1)S(1)}, bf16[64,1024]{1,0:T(8,128)(2,1)S(1)}, u32[]{:S(2)}, u32[]{:S(2)}) %collective-permute-start.8) | collective-permute-done | bytes 131104 | tf_op jit(solution)/shard_map/ppermute | solution.py:124
  173.1 5.5 %collective-permute-done.3 = bf16[64,3072]{1,0:T(8,128)(2,1)S(1)} collective-permute-done((bf16[64,3072]{1,0:T(8,128)(2,1)S(1)}, bf16[64,3072]{1,0:T(8,128)(2,1)S(1)}, u32[]{:S(2)}, u32[]{:S(2)}) %collective-permute-start.3) | collective-permute-done | bytes 393248 | tf_op jit(solution)/shard_map/ppermute | solution.py:124
  181.5 7.1 %collective-permute-done.4 = bf16[64,3072]{1,0:T(8,128)(2,1)S(1)} collective-permute-done((bf16[64,3072]{1,0:T(8,128)(2,1)S(1)}, bf16[64,3072]{1,0:T(8,128)(2,1)S(1)}, u32[]{:S(2)}, u32[]{:S(2)}) %collective-permute-start.4) | collective-permute-done | bytes 393248 | tf_op jit(solution)/shard_map/ppermute | solution.py:131
  (139 shorter events, 49.5 us)
Async XLA Ops:
  0.6 16.6 %copy-start = (bf16[1024,1024]{1,0:T(8,128)(2,1)S(1)}, bf16[1024,1024]{1,0:T(8,128)(2,1)}, u32[]{:S(2)}) copy-start(bf16[1024,1024]{1,0:T(8,128)(2,1)} %param.10) | copy-start | bytes 6291460
  0.6 13.7 %copy-start.21 = (bf16[1,1,128,1024]{3,2,1,0:T(8,128)(2,1)S(1)}, bf16[1,1,128,1024]{3,2,1,0:T(8,128)(2,1)}, u32[]{:S(2)}) copy-start(bf16[1,1,128,1024]{3,2,1,0:T(8,128)(2,1)} %param.8) | copy-start | bytes 786436
  5.7 17.5 %all-to-all-start.1 = ((bf16[16,2,4096]{2,1,0:T(2,128)(2,1)}), bf16[16,2,4096]{2,1,0:T(2,128)(2,1)}, u32[]{:S(2)}, u32[]{:S(2)}) async-start(bf16[16,2,4096]{2,1,0:T(2,128)(2,1)} %reshape.351), calls=%async_computation.1 | async-start | bytes 524288 | tf_op jit(solution)/shard_map/all_to_all | solution.py:175
  17.2 6.0 %copy-start.6 = (bf16[8,128,128]{1,2,0:T(8,128)(2,1)}, bf16[8,128,128]{1,2,0:T(8,128)(2,1)S(1)}, u32[]{:S(2)}) copy-start(bf16[8,128,128]{1,2,0:T(8,128)(2,1)S(1)} %convolution_convert_fusion.3) | copy-start | bytes 786436
  23.3 15.8 %all-to-all-start = ((bf16[16,2,4096]{2,1,0:T(2,128)(2,1)}), bf16[16,2,4096]{2,1,0:T(2,128)(2,1)S(1)}, u32[]{:S(2)}, u32[]{:S(2)}) async-start(bf16[16,2,4096]{2,1,0:T(2,128)(2,1)} %reshape.353), calls=%async_computation | async-start | bytes 524288 | tf_op jit(solution)/shard_map/all_to_all | solution.py:151
  40.4 5.4 %copy-start.18 = (bf16[16,8,8,128]{3,2,1,0:T(8,128)(2,1)S(1)}, bf16[16,8,8,128]{3,2,1,0:T(8,128)(2,1)}, u32[]{:S(2)}) copy-start(bf16[16,8,8,128]{3,2,1,0:T(8,128)(2,1)} %copy.253) | copy-start | bytes 786436
  63.0 4.5 %copy-start.2 = (f32[2,2,2,2,64,3072]{5,4,3,2,1,0:T(8,128)}, f32[2,2,2,2,64,3072]{5,4,3,2,1,0:T(8,128)S(1)}, u32[]{:S(2)}) copy-start(f32[2,2,2,2,64,3072]{5,4,3,2,1,0:T(8,128)S(1)} %fusion.36) | copy-start | bytes 37748740
  69.7 9.4 %copy-start.20 = (bf16[1,16,8,1,8,128]{5,2,4,3,1,0:T(8,128)(2,1)S(1)}, bf16[1,16,8,1,8,128]{5,2,4,3,1,0:T(8,128)(2,1)}, u32[]{:S(2)}) copy-start(bf16[1,16,8,1,8,128]{5,2,4,3,1,0:T(8,128)(2,1)} %copy-done.19) | copy-start | bytes 786436
  69.7 32.8 %collective-permute-start = (bf16[2,2,2,64,3072]{4,3,2,0,1:T(8,128)(2,1)}, bf16[2,2,2,64,3072]{4,3,2,0,1:T(8,128)(2,1)}, u32[]{:S(2)}, u32[]{:S(2)}) collective-permute-start(bf16[2,2,2,64,3072]{4,3,2,0,1:T(8,128)(2,1)} %fusion.4), channel_id=1, source_target_pairs={{0,1},{1,0},{2,3},{3,2},{4,5},{5,4},{6,7},{7,6},{8,9},{9,8},{10,11... | collective-permute-start | bytes 9437192 | tf_op jit(solution)/shard_map/ppermute | solution.py:124
  75.4 13.5 %all-to-all-start.2 = ((bf16[1,16,8,1024]{3,2,0,1:T(8,128)(2,1)}), bf16[1,16,8,1024]{3,2,0,1:T(8,128)(2,1)S(1)}, u32[]{:S(2)}, u32[]{:S(2)}) async-start(bf16[1,16,8,1024]{3,2,0,1:T(8,128)(2,1)} %fusion.22), calls=%async_computation.2 | async-start | bytes 524288 | tf_op jit(solution)/shard_map/all_to_all | solution.py:186
  80.5 14.3 %copy-start.7 = (bf16[8,128,128]{1,2,0:T(8,128)(2,1)S(1)}, bf16[8,128,128]{1,2,0:T(8,128)(2,1)}, u32[]{:S(2)}) copy-start(bf16[8,128,128]{1,2,0:T(8,128)(2,1)} %copy-done.6) | copy-start | bytes 786436
  89.0 27.4 %all-to-all-start.3 = ((bf16[1,16,8,1024]{3,2,0,1:T(8,128)(2,1)}), bf16[1,16,8,1024]{3,2,0,1:T(8,128)(2,1)}, u32[]{:S(2)}, u32[]{:S(2)}) async-start(bf16[1,16,8,1024]{3,2,0,1:T(8,128)(2,1)} %bitcast.36), calls=%async_computation.3 | async-start | bytes 524288 | tf_op jit(solution)/shard_map/all_to_all | solution.py:168
  93.7 16.6 %collective-permute-start.10 = (bf16[2,2,2,64,1]{3,2,1,0,4:T(2,128)(2,1)S(1)}, bf16[2,2,2,64,1]{3,2,1,0,4:T(2,128)(2,1)S(1)}, u32[]{:S(2)}, u32[]{:S(2)}) collective-permute-start(bf16[2,2,2,64,1]{3,2,1,0,4:T(2,128)(2,1)S(1)} %copy_bitcast_fusion.10), channel_id=1, source_target_pairs={{0,1},{1,0},{2,3},{3,2},{4,5},{5,4},{6,7},{7,6},{8,9},{9,8},{10,11... | collective-permute-start | bytes 3080 | tf_op jit(solution)/shard_map/ppermute | solution.py:124
  94.8 3.7 %copy-start.13 = (bf16[1,1,128,1024]{2,3,1,0:T(8,128)(2,1)S(1)}, bf16[1,1,128,1024]{2,3,1,0:T(8,128)(2,1)}, u32[]{:S(2)}) copy-start(bf16[1,1,128,1024]{2,3,1,0:T(8,128)(2,1)} %copy-done.12) | copy-start | bytes 786436
  97.8 13.2 %collective-permute-start.5 = (bf16[2,2,2,64,1024]{4,3,2,0,1:T(8,128)(2,1)S(1)}, bf16[2,2,2,64,1024]{4,3,2,0,1:T(8,128)(2,1)}, u32[]{:S(2)}, u32[]{:S(2)}) collective-permute-start(bf16[2,2,2,64,1024]{4,3,2,0,1:T(8,128)(2,1)S(1)} %fusion.25), channel_id=1, source_target_pairs={{0,1},{1,0},{2,3},{3,2},{4,5},{5,4},{6,7},{7,6},{8,9},{9,8},{10,11... | collective-permute-start | bytes 3145736 | tf_op jit(solution)/shard_map/ppermute | solution.py:124
  102.4 8.5 %copy-start.5 = (f32[2,2,2,2,64,1024]{5,4,3,2,1,0:T(8,128)S(1)}, f32[2,2,2,2,64,1024]{5,4,3,2,1,0:T(8,128)}, u32[]{:S(2)}) copy-start(f32[2,2,2,2,64,1024]{5,4,3,2,1,0:T(8,128)} %copy-done.4) | copy-start | bytes 12582916
  107.2 5.3 %copy-start.3 = (f32[2,2,2,64,3072]{4,3,2,0,1:T(8,128)}, f32[2,2,2,64,3072]{4,3,2,0,1:T(8,128)S(1)}, u32[]{:S(2)}) copy-start(f32[2,2,2,64,3072]{4,3,2,0,1:T(8,128)S(1)} %bitcast_add_fusion) | copy-start | bytes 18874372
  108.8 27.6 %collective-permute-start.1 = (bf16[2,2,64,3072]{3,2,1,0:T(8,128)(2,1)}, bf16[2,2,64,3072]{3,2,1,0:T(8,128)(2,1)}, u32[]{:S(2)}, u32[]{:S(2)}) collective-permute-start(bf16[2,2,64,3072]{3,2,1,0:T(8,128)(2,1)} %fusion.5), channel_id=1, source_target_pairs={{0,2},{1,5},{2,0},{3,7},{4,6},{5,1},{6,4},{7,3},{8,10},{9,13},{10,... | collective-permute-start | bytes 4718600 | tf_op jit(solution)/shard_map/ppermute | solution.py:124
  110.4 3.8 %copy-start.17 = (bf16[128,1024]{0,1:T(8,128)(2,1)S(1)}, bf16[128,1024]{0,1:T(8,128)(2,1)}, u32[]{:S(2)}) copy-start(bf16[128,1024]{0,1:T(8,128)(2,1)} %copy-done.16) | copy-start | bytes 786436
  110.4 6.0 %copy-start.22 = (bf16[8,128,128]{1,2,0:T(8,128)(2,1)S(1)}, bf16[8,128,128]{1,2,0:T(8,128)(2,1)}, u32[]{:S(2)}) copy-start(bf16[8,128,128]{1,2,0:T(8,128)(2,1)} %convolution_convert_fusion.6) | copy-start | bytes 786436
  110.4 19.1 %collective-permute-start.11 = (bf16[2,2,64,1]{2,1,0,3:T(2,128)(2,1)S(1)}, bf16[2,2,64,1]{2,1,0,3:T(2,128)(2,1)S(1)}, u32[]{:S(2)}, u32[]{:S(2)}) collective-permute-start(bf16[2,2,64,1]{2,1,0,3:T(2,128)(2,1)S(1)} %fusion.76), channel_id=1, source_target_pairs={{0,2},{1,5},{2,0},{3,7},{4,6},{5,1},{6,4},{7,3},{8,10},{9,13},{10,... | collective-permute-start | bytes 1544 | tf_op jit(solution)/shard_map/ppermute | solution.py:124
  112.6 22.6 %collective-permute-start.6 = (bf16[2,2,64,1024]{3,2,1,0:T(8,128)(2,1)S(1)}, bf16[2,2,64,1024]{3,2,1,0:T(8,128)(2,1)}, u32[]{:S(2)}, u32[]{:S(2)}) collective-permute-start(bf16[2,2,64,1024]{3,2,1,0:T(8,128)(2,1)S(1)} %fusion.45), channel_id=1, source_target_pairs={{0,2},{1,5},{2,0},{3,7},{4,6},{5,1},{6,4},{7,3},{8,10},{9,13},{10,... | collective-permute-start | bytes 1572872 | tf_op jit(solution)/shard_map/ppermute | solution.py:124
  129.5 12.0 %collective-permute-start.12 = (bf16[2,64,1]{1,0,2:T(2,128)(2,1)S(1)}, bf16[2,64,1]{1,0,2:T(2,128)(2,1)S(1)}, u32[]{:S(2)}, u32[]{:S(2)}) collective-permute-start(bf16[2,64,1]{1,0,2:T(2,128)(2,1)S(1)} %fusion.80), channel_id=1, source_target_pairs={{0,4},{1,3},{2,6},{3,1},{4,0},{5,7},{6,2},{7,5},{8,12},{9,11},{10,... | collective-permute-start | bytes 776 | tf_op jit(solution)/shard_map/ppermute | solution.py:124
  139.3 17.5 %collective-permute-start.2 = (bf16[2,64,3072]{2,1,0:T(8,128)(2,1)S(1)}, bf16[2,64,3072]{2,1,0:T(8,128)(2,1)S(1)}, u32[]{:S(2)}, u32[]{:S(2)}) collective-permute-start(bf16[2,64,3072]{2,1,0:T(8,128)(2,1)S(1)} %fusion.34), channel_id=1, source_target_pairs={{0,4},{1,3},{2,6},{3,1},{4,0},{5,7},{6,2},{7,5},{8,12},{9,11},{10,... | collective-permute-start | bytes 2359304 | tf_op jit(solution)/shard_map/ppermute | solution.py:124
  141.0 13.2 %collective-permute-start.7 = (bf16[2,64,1024]{2,1,0:T(8,128)(2,1)S(1)}, bf16[2,64,1024]{2,1,0:T(8,128)(2,1)S(1)}, u32[]{:S(2)}, u32[]{:S(2)}) collective-permute-start(bf16[2,64,1024]{2,1,0:T(8,128)(2,1)S(1)} %fusion.48), channel_id=1, source_target_pairs={{0,4},{1,3},{2,6},{3,1},{4,0},{5,7},{6,2},{7,5},{8,12},{9,11},{10,... | collective-permute-start | bytes 786440 | tf_op jit(solution)/shard_map/ppermute | solution.py:124
  141.5 16.1 %collective-permute-start.13 = (bf16[64,1]{0,1:T(2,128)(2,1)S(1)}, bf16[64,1]{0,1:T(2,128)(2,1)S(1)}, u32[]{:S(2)}, u32[]{:S(2)}) collective-permute-start(bf16[64,1]{0,1:T(2,128)(2,1)S(1)} %fusion.85), channel_id=1, source_target_pairs={{0,8},{1,9},{2,10},{3,11},{4,12},{5,13},{6,14},{7,15},{8,0},{9,1},... | collective-permute-start | bytes 392 | tf_op jit(solution)/shard_map/ppermute | solution.py:124
  154.3 17.2 %collective-permute-start.8 = (bf16[64,1024]{1,0:T(8,128)(2,1)S(1)}, bf16[64,1024]{1,0:T(8,128)(2,1)S(1)}, u32[]{:S(2)}, u32[]{:S(2)}) collective-permute-start(bf16[64,1024]{1,0:T(8,128)(2,1)S(1)} %fusion.67), channel_id=1, source_target_pairs={{0,8},{1,9},{2,10},{3,11},{4,12},{5,13},{6,14},{7,15},{8,0},{9,1},... | collective-permute-start | bytes 393224 | tf_op jit(solution)/shard_map/ppermute | solution.py:124
  156.8 34.3 %copy-start.1 = (bf16[1024,1024]{1,0:T(8,128)(2,1)S(1)}, bf16[1024,1024]{1,0:T(8,128)(2,1)}, u32[]{:S(2)}) copy-start(bf16[1024,1024]{1,0:T(8,128)(2,1)} %param.10) | copy-start | bytes 6291460
  157.1 21.5 %collective-permute-start.3 = (bf16[64,3072]{1,0:T(8,128)(2,1)S(1)}, bf16[64,3072]{1,0:T(8,128)(2,1)S(1)}, u32[]{:S(2)}, u32[]{:S(2)}) collective-permute-start(bf16[64,3072]{1,0:T(8,128)(2,1)S(1)} %fusion.46), channel_id=1, source_target_pairs={{0,8},{1,9},{2,10},{3,11},{4,12},{5,13},{6,14},{7,15},{8,0},{9,1},... | collective-permute-start | bytes 1179656 | tf_op jit(solution)/shard_map/ppermute | solution.py:124
  157.6 22.6 %collective-permute-start.14 = (bf16[64,1]{0,1:T(2,128)(2,1)S(1)}, bf16[64,1]{0,1:T(2,128)(2,1)S(1)}, u32[]{:S(2)}, u32[]{:S(2)}) collective-permute-start(bf16[64,1]{0,1:T(2,128)(2,1)S(1)} %fusion.83), channel_id=1, source_target_pairs={{0,16},{16,0},{1,17},{17,1},{2,18},{18,2},{3,19},{19,3},{4,20},{20... | collective-permute-start | bytes 392 | tf_op jit(solution)/shard_map/ppermute | solution.py:131
  171.6 9.2 %collective-permute-start.9 = (bf16[64,1024]{1,0:T(8,128)(2,1)S(1)}, bf16[64,1024]{1,0:T(8,128)(2,1)S(1)}, u32[]{:S(2)}, u32[]{:S(2)}) collective-permute-start(bf16[64,1024]{1,0:T(8,128)(2,1)S(1)} %fusion.55), channel_id=1, source_target_pairs={{0,16},{16,0},{1,17},{17,1},{2,18},{18,2},{3,19},{19,3},{4,20},{20... | collective-permute-start | bytes 393224 | tf_op jit(solution)/shard_map/ppermute | solution.py:131
  178.7 9.9 %collective-permute-start.4 = (bf16[64,3072]{1,0:T(8,128)(2,1)S(1)}, bf16[64,3072]{1,0:T(8,128)(2,1)S(1)}, u32[]{:S(2)}, u32[]{:S(2)}) collective-permute-start(bf16[64,3072]{1,0:T(8,128)(2,1)S(1)} %fusion.35), channel_id=1, source_target_pairs={{0,16},{16,0},{1,17},{17,1},{2,18},{18,2},{3,19},{19,3},{4,20},{20... | collective-permute-start | bytes 1179656 | tf_op jit(solution)/shard_map/ppermute | solution.py:131
  (12 other events, 28.3 us)

commit v2 on v1

--- a/solution.py
+++ b/solution.py
@@ -103,9 +103,9 @@
 def reduce_rows(parts, orders, seq_n, dp_n):
     bits = seq_n.bit_length() - 1
     index = lax.axis_index("seq")
-    accs = tuple(p.reshape((2,) * bits + (p.shape[0] // seq_n, p.shape[1])) for p in parts)
+    accs = tuple(p.reshape((2,) * (bits - 1) + (2 * p.shape[0] // seq_n, p.shape[1])) for p in parts)
     even, odd = orders
-    for step in range(bits):
+    for step in range(1, bits):
         perm = []
         for member in range(seq_n):
             bit = (odd if member % 2 else even)[step]
@@ -119,8 +119,6 @@
             lax.dynamic_index_in_dim(acc, 1 - keep_at, 0, keepdims=False).astype(jnp.bfloat16)
             for acc in accs
         )
-        if step == 0 and even != odd:
-            given = tuple(jnp.swapaxes(g, 0, 1) for g in given)
         got = lax.ppermute(given, "seq", perm)
         accs = tuple(k + g.astype(jnp.float32) for k, g in zip(kept, got))
     dp_bits = dp_n.bit_length() - 1
@@ -195,9 +193,18 @@
     dp_n = lax.axis_size("dp")
     orders = split_orders(seq_n)
     core_odd = lax.axis_index("seq") % 2 == 1
+    pair = [(member, member ^ 1) for member in range(seq_n)]
+    core = lax.axis_index("seq") % 2
+
+    def my_half(factor):
+        arranged = by_split_order(factor, orders, core_odd, seq_n)
+        half = arranged.shape[1] // 2
+        return lax.dynamic_slice_in_dim(arranged, core * half, half, axis=1)
+
+    normed_peer, grads_peer = lax.ppermute((used_normed, used_grads), "seq", pair)
     joint_term = jnp.dot(
-        by_split_order(used_normed, orders, core_odd, seq_n).T,
-        used_grads,
+        my_half(jnp.concatenate([used_normed, normed_peer], axis=0)).T,
+        jnp.concatenate([used_grads, grads_peer], axis=0),
         preferred_element_type=jnp.float32,
     )
     grad_float = grad_normed.astype(jnp.float32)
@@ -206,12 +213,13 @@
     grad_hidden = (
         inverse * scaled - hidden * inverse**3 * jnp.mean(scaled * hidden, axis=-1, keepdims=True)
     ).astype(jnp.bfloat16)
+    first_peer, hidden_peer, gain_peer = lax.ppermute((flat_first, grad_hidden, gain_term), "seq", pair)
     out_term = jnp.dot(
-        by_split_order(flat_first, orders, core_odd, seq_n).T,
-        grad_hidden,
-        preferred_element_type=jnp.float32,
-    )
-    gain_term = by_split_order(gain_term[None, :], orders, core_odd, seq_n)[0][:, None]
+        my_half(jnp.concatenate([flat_first, first_peer], axis=0)).T,
+        jnp.concatenate([grad_hidden, hidden_peer], axis=0),
+        preferred_element_type=jnp.float32,
+    )
+    gain_term = my_half((gain_term + gain_peer)[None, :])[0][:, None]
     joint_sum, out_sum, gain_sum = reduce_rows((joint_term, out_term, gain_term), orders, seq_n, dp_n)
     replicas = (joint_sum, out_sum, gain_sum[:, 0])
     grad_first = jnp.dot(grad_hidden, out_weight.T, preferred_element_type=jnp.float32).astype(

time: 192 us -> 185 us (0.964)
  waiting for transfers between devices: 62.2 us -> 54.8 us
  matrix products: 33.3 us -> 35.9 us
    add x9 -> x6, other arithmetic: 10.5 us -> 4.65 us  [reduce_rows(): accs = tuple((k + g.astype(jnp.float32) for k, g in zip(kept, got)))]
    all_to_all x1, waiting for transfers between devices: 7.6 us -> 4 us  [on_device(): lax.all_to_all(grad_local.reshape(batches, all_rows, col_share, model_wid...]
    ppermute x12 -> x9, waiting for transfers between devices: 41.7 us -> 38.3 us  [reduce_rows(): got = lax.ppermute(given, 'seq', perm)]
    unnamed x62 -> x56, local copies, waits for them, and re-layouts: 21.4 us -> 18.5 us
    transpose x3 -> x0, local copies, waits for them, and re-layouts: 2.3 us -> none  [reduce_rows(): given = tuple((jnp.swapaxes(g, 0, 1) for g in given))]
    all_to_all x1, waiting for transfers between devices: 5.59 us -> 3.44 us  [on_device(): lax.all_to_all(normed.reshape(batches, local_rows, columns, model_width),...]
    ppermute x12 -> x9, starting transfers between devices: 13.6 us -> 13.6 us  [reduce_rows(): got = lax.ppermute(given, 'seq', perm)]
  transfers between devices with their start and end apart: 19 -> 21, of which waited for: 9 -> 9; matrix products, arithmetic and copies ran while one was open for 25% -> 32% of each run, Pallas kernels for 0% -> 0%
where the time goes in v2:
time: 185 us; the launch traced here: 183 us
  waiting for transfers between devices  54.8 us (30%)
  starting transfers between devices  39.5 us (21%)
  matrix products  35.9 us (19%)
  local copies, waits for them, and re-layouts  33.2 us (18%)
  other arithmetic  18.7 us (10%)
    ppermute x9, waiting for transfers between devices, reduce_rows(): got = lax.ppermute(given, 'seq', perm)  38.3 us
    unnamed x56, local copies, waits for them, and re-layouts  18.5 us
    ppermute x9, starting transfers between devices, reduce_rows(): got = lax.ppermute(given, 'seq', perm)  13.6 us
    all_to_all x1, starting transfers between devices, on_device(): lax.all_to_all(upstream, 'seq', split_axis=2, concat_axis=1, tiled=True)  7.44 us
    ppermute x3, waiting for transfers between devices, reduce_rows(): got = lax.ppermute(mine, 'dp', perm)  7.27 us
    dot_general x1, matrix products, on_device(): jnp.dot(used_grads, joint_weight.T, preferred_element_type=jnp.float32)  5.69 us
    dot_general x2, matrix products, attend_back(): jnp.einsum(scores_form + ',' + layout + '->' + keyed, grad_score, queries...  5.1 us
    dot_general x2, matrix products, attend_back(): jnp.einsum(scores_form + ',' + keyed + '->' + layout, grad_score, key_tab...  5.04 us
  transfers between devices with their start and end apart: 21, of which 9 were waited for; matrix products, arithmetic and copies ran while one was open for 32% of the time, Pallas kernels for 0%

profile of v2, /device:TPU:0, one launch (start us, length us, event | category | flops | bytes accessed | tf_op | source)
XLA Modules:
  0.0 183.5 jit_solution(9961489665106279927)
XLA Ops:
  2.7 2.1 %reduce.18 = bf16[128,1024]{1,0:T(8,128)(2,1)S(1)} reduce(bf16[128,1,1,1024]{3,2,1,0:T(2,128)(2,1)S(1)} %bitcast.207, bf16[]{:T(256)} %broadcast.110), dimensions={1,2}, to_apply=%bitcast.196.reduce_sub_computation | reduce | bytes 524290
  5.7 7.4 %all-to-all-start.1 = ((bf16[16,2,4096]{2,1,0:T(2,128)(2,1)}), bf16[16,2,4096]{2,1,0:T(2,128)(2,1)}, u32[]{:S(2)}, u32[]{:S(2)}) async-start(bf16[16,2,4096]{2,1,0:T(2,128)(2,1)} %reshape.344), calls=%async_computation.1 | async-start | bytes 524288 | tf_op jit(solution)/shard_map/all_to_all | solution.py:173
  16.8 2.9 %reduce.19 = bf16[128,1024]{1,0:T(8,128)(2,1)} reduce(bf16[128,1,1,1024]{3,2,1,0:T(2,128)(2,1)S(1)} %bitcast.208, bf16[]{:T(256)} %broadcast.110), dimensions={1,2}, to_apply=%bitcast.197.reduce_sub_computation | reduce | bytes 524290
  19.7 1.8 reshape.346
  23.3 4.0 %all-to-all-start = ((bf16[16,2,4096]{2,1,0:T(2,128)(2,1)}), bf16[16,2,4096]{2,1,0:T(2,128)(2,1)S(1)}, u32[]{:S(2)}, u32[]{:S(2)}) async-start(bf16[16,2,4096]{2,1,0:T(2,128)(2,1)} %reshape.346), calls=%async_computation | async-start | bytes 524288 | tf_op jit(solution)/shard_map/all_to_all | solution.py:149
  29.5 2.2 %reshape.345 = bf16[128,1,1,1024]{3,2,1,0:T(2,128)(2,1)S(1)} reshape(bf16[16,2,4096]{2,1,0:T(2,128)(2,1)} %all-to-all-done.1) | data formatting | bytes 524288
  33.9 3.4 %all-to-all-done = bf16[16,2,4096]{2,1,0:T(2,128)(2,1)S(1)} async-done(((bf16[16,2,4096]{2,1,0:T(2,128)(2,1)}), bf16[16,2,4096]{2,1,0:T(2,128)(2,1)S(1)}, u32[]{:S(2)}, u32[]{:S(2)}) %all-to-all-start) | async-done | bytes 262176 | tf_op jit(solution)/shard_map/all_to_all | solution.py:149
  38.6 3.9 %convolution_convert_fusion = bf16[128,3072]{1,0:T(8,128)(2,1)S(1)} fusion(bf16[1024,3072]{1,0:T(8,128)(2,1)} %param.12, bf16[1,1,128,1024]{2,3,1,0:T(8,128)(2,1)} %copy.107), kind=kOutput, calls=%fused_computation.4 | convolution fusion | flops 805699584 | bytes 7340032 | tf_op jit(solution)/shard_map/dot_general | solution.py:156
  44.6 2.6 %fusion.100 = (f32[8,8,16]{2,1,0:T(8,128)S(1)}, f32[8,8,16,16]{2,3,1,0:T(8,128)}) fusion(pred[16,16]{0,1:T(8,128)(4,1)S(1)} %iota_compare_fusion.1, bf16[1,16,8,1,8,128]{5,2,4,3,1,0:T(8,128)(2,1)} %get-tuple-element.39, bf16[1,16,8,1,8,128]{5,2,4,3,1,0:T(8,128)(2,1)} %get-tuple-element.38), kind=kOutput, calls=%fused_computation.155 | convolution fusion | flops 4259855 | bytes 594176 | tf_op jit(solution)/shard_map/sub | solution.py:28
  47.3 2.1 %fusion.24 = bf16[1,16,8,1,8,128]{5,1,4,2,3,0:T(8,128)(2,1)} fusion(bf16[16,8,8,128]{3,2,1,0:T(8,128)(2,1)S(1)} %copy-done.13, f32[8,8,16,16]{2,3,1,0:T(8,128)} %get-tuple-element.47, f32[8,8,16]{2,1,0:T(8,128)S(1)} %get-tuple-element.46), kind=kOutput, calls=%fused_computation.42 | convolution fusion | flops 4358144 | bytes 593920 | tf_op jit(solution)/shard_map/bchlm,blche->bmche/dot_general | solution.py:64
  49.3 2.5 %fusion.27 = bf16[1,16,8,1,8,128]{5,1,4,2,3,0:T(8,128)(2,1)} fusion(f32[8,8,16,16]{2,3,1,0:T(8,128)S(1)} %convolution_bitcast_fusion, bf16[1,16,8,1,8,128]{5,2,4,3,1,0:T(8,128)(2,1)} %get-tuple-element.38, f32[8,8,16,16]{2,3,1,0:T(8,128)} %get-tuple-element.47, f32[8,8,16]{2,1,0:T(8,128)S(1)} %get-tuple-element.46), kind=kOutput, calls=%fused_computation.45 | convolution fusion | flops 4441103 | bytes 659456 | tf_op jit(solution)/shard_map/bchlm,blche->bmche/dot_general | solution.py:57
  51.9 2.4 %fusion.23 = bf16[1,16,8,1,8,128]{5,1,4,2,3,0:T(8,128)(2,1)} fusion(f32[8,8,16,16]{2,3,1,0:T(8,128)S(1)} %convolution_bitcast_fusion, bf16[1,16,8,1,8,128]{5,2,4,3,1,0:T(8,128)(2,1)S(1)} %copy-done.20, f32[8,8,16,16]{2,3,1,0:T(8,128)} %get-tuple-element.47, f32[8,8,16]{2,1,0:T(8,128)S(1)} %get-tuple-element.46), kind=kOutput, calls=%fused_computation.41 | convolution fusion | flops 4441103 | bytes 659456 | tf_op jit(solution)/shard_map/bchlm,bmche->blche/dot_general | solution.py:51
  58.0 5.7 %fusion.25 = bf16[1,16,8,1024]{3,2,0,1:T(8,128)(2,1)} fusion(bf16[128,3072]{1,0:T(8,128)(2,1)S(1)} %reshape_reshape.7, bf16[1024,3072]{1,0:T(8,128)(2,1)} %param.12), kind=kOutput, calls=%fused_computation.43 | convolution fusion | flops 805437440 | bytes 7340032 | tf_op jit(solution)/shard_map/dot_general | solution.py:181
  64.2 4.2 %all-to-all-start.2 = ((bf16[1,16,8,1024]{3,2,0,1:T(8,128)(2,1)}), bf16[1,16,8,1024]{3,2,0,1:T(8,128)(2,1)}, u32[]{:S(2)}, u32[]{:S(2)}) async-start(bf16[1,16,8,1024]{3,2,0,1:T(8,128)(2,1)} %fusion.25), calls=%async_computation.2 | async-start | bytes 524288 | tf_op jit(solution)/shard_map/all_to_all | solution.py:184
  74.5 4.0 %all-to-all-done.2 = bf16[1,16,8,1024]{3,2,0,1:T(8,128)(2,1)} async-done(((bf16[1,16,8,1024]{3,2,0,1:T(8,128)(2,1)}), bf16[1,16,8,1024]{3,2,0,1:T(8,128)(2,1)}, u32[]{:S(2)}, u32[]{:S(2)}) %all-to-all-start.2) | async-done | bytes 262176 | tf_op jit(solution)/shard_map/all_to_all | solution.py:184
  78.5 4.4 %all-to-all-start.3 = ((bf16[1,16,8,1024]{3,2,0,1:T(8,128)(2,1)}), bf16[1,16,8,1024]{3,2,0,1:T(8,128)(2,1)}, u32[]{:S(2)}, u32[]{:S(2)}) async-start(bf16[1,16,8,1024]{3,2,0,1:T(8,128)(2,1)} %bitcast.212), calls=%async_computation.3 | async-start | bytes 524288 | tf_op jit(solution)/shard_map/all_to_all | solution.py:166
  87.5 1.8 %copy.149 = bf16[128,1024]{0,1:T(8,128)(2,1)} copy(bf16[128,1024]{1,0:T(8,128)(2,1)} %convolution_convert_fusion.7) | data formatting | bytes 524288 | tf_op jit(solution)/shard_map/reshape.73
  89.3 2.0 %fusion.62 = f32[8,128,128]{1,2,0:T(8,128)} fusion(bf16[128,8,128]{0,2,1:T(8,128)(2,1)} %bitcast.219, bf16[128,8,128]{2,1,0:T(8,128)(2,1)} %bitcast.218), kind=kOutput, calls=%fused_computation.103 | convolution fusion | flops 33554432 | bytes 1048576 | tf_op jit(solution)/shard_map/glhe,gmhe->ghlm/dot_general | solution.py:43
  91.3 2.6 %convolution_convert_fusion.1 = bf16[8,128,128]{1,2,0:T(8,128)(2,1)} fusion(bf16[128,8,128]{0,2,1:T(8,128)(2,1)} %bitcast.216, f32[8,128,128]{1,2,0:T(8,128)} %fusion.62, f32[8,128,128]{1,2,0:T(8,128)} %get-tuple-element.43, f32[8,128]{1,0:T(8,128)S(1)} %get-tuple-element.42), kind=kOutput, calls=%fused_computation.31 | convolution fusion | flops 34604160 | bytes 1576960 | tf_op jit(solution)/shard_map/ghlm,gmhe->glhe/dot_general | solution.py:51
  94.0 2.1 %fusion.5 = f32[512,3072]{1,0:T(8,128)S(1)} fusion(bf16[128,3072]{1,0:T(8,128)(2,1)} %collective-permute-done.1, bf16[128,3072]{1,0:T(8,128)(2,1)S(1)} %reshape_reshape.7, bf16[256,1024]{0,1:T(8,128)(2,1)S(1)} %bitcast.210, s32[]{:T(128)S(6)} %select_n.150), kind=kOutput, calls=%fused_computation.8 | convolution fusion | flops 808452096 | bytes 8126468 | tf_op jit(solution)/shard_map/dot_general | solution.py:205
  96.1 2.6 %copy-done.1 = f32[512,3072]{1,0:T(8,128)} copy-done((f32[512,3072]{1,0:T(8,128)}, f32[512,3072]{1,0:T(8,128)S(1)}, u32[]{:S(2)}) %copy-start.1) | copy-done | bytes 6291480
  101.8 2.6 %convolution_convert_fusion.6 = bf16[8,128,128]{1,2,0:T(8,128)(2,1)} fusion(bf16[128,8,128]{0,2,1:T(8,128)(2,1)S(1)} %bitcast.214, f32[8,128,128]{1,2,0:T(8,128)} %fusion.62, f32[8,128,128]{1,2,0:T(8,128)} %get-tuple-element.43, f32[8,128]{1,0:T(8,128)S(1)} %get-tuple-element.42), kind=kOutput, calls=%fused_computation.36 | convolution fusion | flops 34604160 | bytes 1576960 | tf_op jit(solution)/shard_map/ghlm,glhe->gmhe/dot_general | solution.py:57
  109.0 2.2 %convolution_convert_fusion.5 = bf16[8,128,128]{2,1,0:T(8,128)(2,1)} fusion(bf16[128,8,128]{0,2,1:T(8,128)(2,1)S(1)} %bitcast.220, f32[8,128]{1,0:T(8,128)S(1)} %get-tuple-element.42, f32[8,128,128]{1,2,0:T(8,128)} %copy-done.5), kind=kOutput, calls=%fused_computation.35 | convolution fusion | flops 34079872 | bytes 1052672 | tf_op jit(solution)/shard_map/ghlm,glhe->gmhe/dot_general | solution.py:64
  114.8 6.1 %collective-permute-done.13 = bf16[2,2,64,1]{2,1,3,0:T(2,128)(2,1)S(1)} collective-permute-done((bf16[2,2,64,1]{2,1,3,0:T(2,128)(2,1)S(1)}, bf16[2,2,64,1]{2,1,3,0:T(2,128)(2,1)S(1)}, u32[]{:S(2)}, u32[]{:S(2)}) %collective-permute-start.13) | collective-permute-done | bytes 544 | tf_op jit(solution)/shard_map/ppermute | solution.py:122
  122.6 3.9 %collective-permute-done.8 = bf16[2,2,64,1024]{3,2,1,0:T(8,128)(2,1)} collective-permute-done((bf16[2,2,64,1024]{3,2,1,0:T(8,128)(2,1)S(1)}, bf16[2,2,64,1024]{3,2,1,0:T(8,128)(2,1)}, u32[]{:S(2)}, u32[]{:S(2)}) %collective-permute-start.8) | collective-permute-done | bytes 524320 | tf_op jit(solution)/shard_map/ppermute | solution.py:122
  128.1 2.8 %bitcast_add_fusion = f32[2,2,64,3072]{3,2,1,0:T(8,128)S(1)} fusion(bf16[2,2,64,3072]{3,2,1,0:T(8,128)(2,1)} %collective-permute-done.2, f32[2,2,2,64,3072]{4,3,2,1,0:T(8,128)} %bitcast.199, s32[]{:T(128)S(6)} %select_n.156), kind=kLoop, calls=%fused_computation.5 | loop fusion | flops 1572864 | bytes 7864324 | tf_op jit(solution)/shard_map/add | solution.py:123
  133.2 2.7 %collective-permute-start.15 = (bf16[64,1]{0,1:T(2,128)(2,1)S(1)}, bf16[64,1]{0,1:T(2,128)(2,1)S(1)}, u32[]{:S(2)}, u32[]{:S(2)}) collective-permute-start(bf16[64,1]{0,1:T(2,128)(2,1)S(1)} %fusion.86), channel_id=1, source_target_pairs={{0,8},{1,9},{2,10},{3,11},{4,12},{5,13},{6,14},{7,15},{8,0},{9,1},... | collective-permute-start | bytes 392 | tf_op jit(solution)/shard_map/ppermute | solution.py:122
  135.9 10.0 %collective-permute-done.9 = bf16[2,64,1024]{2,1,0:T(8,128)(2,1)S(1)} collective-permute-done((bf16[2,64,1024]{2,1,0:T(8,128)(2,1)S(1)}, bf16[2,64,1024]{2,1,0:T(8,128)(2,1)S(1)}, u32[]{:S(2)}, u32[]{:S(2)}) %collective-permute-start.9) | collective-permute-done | bytes 262176 | tf_op jit(solution)/shard_map/ppermute | solution.py:122
  146.0 2.7 %collective-permute-start.10 = (bf16[64,1024]{1,0:T(8,128)(2,1)S(1)}, bf16[64,1024]{1,0:T(8,128)(2,1)S(1)}, u32[]{:S(2)}, u32[]{:S(2)}) collective-permute-start(bf16[64,1024]{1,0:T(8,128)(2,1)S(1)} %fusion.66), channel_id=1, source_target_pairs={{0,8},{1,9},{2,10},{3,11},{4,12},{5,13},{6,14},{7,15},{8,0},{9,1},... | collective-permute-start | bytes 393224 | tf_op jit(solution)/shard_map/ppermute | solution.py:122
  150.9 12.6 %collective-permute-done.10 = bf16[64,1024]{1,0:T(8,128)(2,1)S(1)} collective-permute-done((bf16[64,1024]{1,0:T(8,128)(2,1)S(1)}, bf16[64,1024]{1,0:T(8,128)(2,1)S(1)}, u32[]{:S(2)}, u32[]{:S(2)}) %collective-permute-start.10) | collective-permute-done | bytes 131104 | tf_op jit(solution)/shard_map/ppermute | solution.py:122
  165.1 5.7 %collective-permute-done.4 = bf16[64,3072]{1,0:T(8,128)(2,1)S(1)} collective-permute-done((bf16[64,3072]{1,0:T(8,128)(2,1)S(1)}, bf16[64,3072]{1,0:T(8,128)(2,1)S(1)}, u32[]{:S(2)}, u32[]{:S(2)}) %collective-permute-start.4) | collective-permute-done | bytes 393248 | tf_op jit(solution)/shard_map/ppermute | solution.py:122
  173.7 7.3 %collective-permute-done.5 = bf16[64,3072]{1,0:T(8,128)(2,1)S(1)} collective-permute-done((bf16[64,3072]{1,0:T(8,128)(2,1)S(1)}, bf16[64,3072]{1,0:T(8,128)(2,1)S(1)}, u32[]{:S(2)}, u32[]{:S(2)}) %collective-permute-start.5) | collective-permute-done | bytes 393248 | tf_op jit(solution)/shard_map/ppermute | solution.py:129
  (139 shorter events, 56.7 us)
Async XLA Ops:
  0.6 15.1 %copy-start = (bf16[1024,1024]{1,0:T(8,128)(2,1)S(1)}, bf16[1024,1024]{1,0:T(8,128)(2,1)}, u32[]{:S(2)}) copy-start(bf16[1024,1024]{1,0:T(8,128)(2,1)} %param.10) | copy-start | bytes 6291460
  0.6 12.6 %copy-start.15 = (bf16[1,1,128,1024]{3,2,1,0:T(8,128)(2,1)S(1)}, bf16[1,1,128,1024]{3,2,1,0:T(8,128)(2,1)}, u32[]{:S(2)}) copy-start(bf16[1,1,128,1024]{3,2,1,0:T(8,128)(2,1)} %param.7) | copy-start | bytes 786436
  0.7 12.7 %copy-start.16 = (bf16[1,1,128,1024]{3,2,1,0:T(8,128)(2,1)S(1)}, bf16[1,1,128,1024]{3,2,1,0:T(8,128)(2,1)}, u32[]{:S(2)}) copy-start(bf16[1,1,128,1024]{3,2,1,0:T(8,128)(2,1)} %param.8) | copy-start | bytes 786436
  4.8 8.7 %copy-start.17 = (bf16[1,1,128,1024]{3,2,1,0:T(8,128)(2,1)S(1)}, bf16[1,1,128,1024]{3,2,1,0:T(8,128)(2,1)}, u32[]{:S(2)}) copy-start(bf16[1,1,128,1024]{3,2,1,0:T(8,128)(2,1)} %param.9) | copy-start | bytes 786436
  5.7 17.5 %all-to-all-start.1 = ((bf16[16,2,4096]{2,1,0:T(2,128)(2,1)}), bf16[16,2,4096]{2,1,0:T(2,128)(2,1)}, u32[]{:S(2)}, u32[]{:S(2)}) async-start(bf16[16,2,4096]{2,1,0:T(2,128)(2,1)} %reshape.344), calls=%async_computation.1 | async-start | bytes 524288 | tf_op jit(solution)/shard_map/all_to_all | solution.py:173
  15.3 12.1 %collective-permute-start.6 = (bf16[128,1024]{0,1:T(8,128)(2,1)S(1)}, bf16[128,1024]{0,1:T(8,128)(2,1)}, u32[]{:S(2)}, u32[]{:S(2)}) collective-permute-start(bf16[128,1024]{0,1:T(8,128)(2,1)S(1)} %bitcast.203), channel_id=1, source_target_pairs={{0,1},{1,0},{2,3},{3,2},{4,5},{5,4},{6,7},{7,6},{8,9},{9,8},{10,11... | collective-permute-start | bytes 786440 | tf_op jit(solution)/shard_map/ppermute | solution.py:216
  23.3 14.0 %all-to-all-start = ((bf16[16,2,4096]{2,1,0:T(2,128)(2,1)}), bf16[16,2,4096]{2,1,0:T(2,128)(2,1)S(1)}, u32[]{:S(2)}, u32[]{:S(2)}) async-start(bf16[16,2,4096]{2,1,0:T(2,128)(2,1)} %reshape.346), calls=%async_computation | async-start | bytes 524288 | tf_op jit(solution)/shard_map/all_to_all | solution.py:149
  38.6 5.5 %copy-start.13 = (bf16[16,8,8,128]{3,2,1,0:T(8,128)(2,1)S(1)}, bf16[16,8,8,128]{3,2,1,0:T(8,128)(2,1)}, u32[]{:S(2)}) copy-start(bf16[16,8,8,128]{3,2,1,0:T(8,128)(2,1)} %copy.179) | copy-start | bytes 786436
  54.3 18.1 %collective-permute-start = (bf16[128,1024]{0,1:T(8,128)(2,1)}, bf16[128,1024]{0,1:T(8,128)(2,1)}, u32[]{:S(2)}, u32[]{:S(2)}) collective-permute-start(bf16[128,1024]{0,1:T(8,128)(2,1)} %bitcast.5), channel_id=1, source_target_pairs={{0,1},{1,0},{2,3},{3,2},{4,5},{5,4},{6,7},{7,6},{8,9},{9,8},{10,11... | collective-permute-start | bytes 786440 | tf_op jit(solution)/shard_map/ppermute | solution.py:204
  63.7 30.3 %collective-permute-start.1 = (bf16[128,3072]{1,0:T(8,128)(2,1)S(1)}, bf16[128,3072]{1,0:T(8,128)(2,1)}, u32[]{:S(2)}, u32[]{:S(2)}) collective-permute-start(bf16[128,3072]{1,0:T(8,128)(2,1)S(1)} %reshape_reshape.7), channel_id=1, source_target_pairs={{0,1},{1,0},{2,3},{3,2},{4,5},{5,4},{6,7},{7,6},{8,9},{9,8},{10,11... | collective-permute-start | bytes 2359304 | tf_op jit(solution)/shard_map/ppermute | solution.py:204
  64.2 14.3 %all-to-all-start.2 = ((bf16[1,16,8,1024]{3,2,0,1:T(8,128)(2,1)}), bf16[1,16,8,1024]{3,2,0,1:T(8,128)(2,1)}, u32[]{:S(2)}, u32[]{:S(2)}) async-start(bf16[1,16,8,1024]{3,2,0,1:T(8,128)(2,1)} %fusion.25), calls=%async_computation.2 | async-start | bytes 524288 | tf_op jit(solution)/shard_map/all_to_all | solution.py:184
  78.5 32.8 %all-to-all-start.3 = ((bf16[1,16,8,1024]{3,2,0,1:T(8,128)(2,1)}), bf16[1,16,8,1024]{3,2,0,1:T(8,128)(2,1)}, u32[]{:S(2)}, u32[]{:S(2)}) async-start(bf16[1,16,8,1024]{3,2,0,1:T(8,128)(2,1)} %bitcast.212), calls=%async_computation.3 | async-start | bytes 524288 | tf_op jit(solution)/shard_map/all_to_all | solution.py:166
  84.0 20.4 %collective-permute-start.12 = (f32[1024]{0:T(1024)S(1)}, f32[1024]{0:T(1024)S(1)}, u32[]{:S(2)}, u32[]{:S(2)}) collective-permute-start(f32[1024]{0:T(1024)S(1)} %get-tuple-element.35), channel_id=1, source_target_pairs={{0,1},{1,0},{2,3},{3,2},{4,5},{5,4},{6,7},{7,6},{8,9},{9,8},{10,11... | collective-permute-start | bytes 12296 | tf_op jit(solution)/shard_map/ppermute | solution.py:216
  87.5 6.5 %copy-start.7 = (bf16[256,2,2,2,2,64]{0,5,4,3,2,1:T(8,128)(2,1)S(1)}, bf16[256,2,2,2,2,64]{0,5,4,3,2,1:T(8,128)(2,1)}, u32[]{:S(2)}) copy-start(bf16[256,2,2,2,2,64]{0,5,4,3,2,1:T(8,128)(2,1)} %copy.130) | copy-start | bytes 1572868
  96.1 5.7 %copy-start.9 = (bf16[1,1,128,1024]{2,3,1,0:T(8,128)(2,1)S(1)}, bf16[1,1,128,1024]{2,3,1,0:T(8,128)(2,1)}, u32[]{:S(2)}) copy-start(bf16[1,1,128,1024]{2,3,1,0:T(8,128)(2,1)} %copy-done.8) | copy-start | bytes 786436
  100.1 6.1 %copy-start.6 = (bf16[256,2,2,2,2,64]{0,5,4,3,2,1:T(8,128)(2,1)S(1)}, bf16[256,2,2,2,2,64]{0,5,4,3,2,1:T(8,128)(2,1)}, u32[]{:S(2)}) copy-start(bf16[256,2,2,2,2,64]{0,5,4,3,2,1:T(8,128)(2,1)} %copy.132) | copy-start | bytes 1572868
  100.1 27.9 %collective-permute-start.2 = (bf16[2,2,64,3072]{3,2,1,0:T(8,128)(2,1)}, bf16[2,2,64,3072]{3,2,1,0:T(8,128)(2,1)}, u32[]{:S(2)}, u32[]{:S(2)}) collective-permute-start(bf16[2,2,64,3072]{3,2,1,0:T(8,128)(2,1)} %fusion.4), channel_id=1, source_target_pairs={{0,2},{1,5},{2,0},{3,7},{4,6},{5,1},{6,4},{7,3},{8,10},{9,13},{10,... | collective-permute-start | bytes 4718600 | tf_op jit(solution)/shard_map/ppermute | solution.py:122
  104.4 4.7 %copy-start.12 = (bf16[128,1024]{0,1:T(8,128)(2,1)S(1)}, bf16[128,1024]{0,1:T(8,128)(2,1)}, u32[]{:S(2)}) copy-start(bf16[128,1024]{0,1:T(8,128)(2,1)} %copy.149) | copy-start | bytes 786436
  104.4 1.9 %collective-permute-start.7 = (bf16[128,1024]{1,0:T(8,128)(2,1)S(1)}, bf16[128,1024]{1,0:T(8,128)(2,1)S(1)}, u32[]{:S(2)}, u32[]{:S(2)}) collective-permute-start(bf16[128,1024]{1,0:T(8,128)(2,1)S(1)} %copy-done.4), channel_id=1, source_target_pairs={{0,1},{1,0},{2,3},{3,2},{4,5},{5,4},{6,7},{7,6},{8,9},{9,8},{10,11... | collective-permute-start | bytes 786440 | tf_op jit(solution)/shard_map/ppermute | solution.py:216
  104.8 16.1 %collective-permute-start.13 = (bf16[2,2,64,1]{2,1,3,0:T(2,128)(2,1)S(1)}, bf16[2,2,64,1]{2,1,3,0:T(2,128)(2,1)S(1)}, u32[]{:S(2)}, u32[]{:S(2)}) collective-permute-start(bf16[2,2,64,1]{2,1,3,0:T(2,128)(2,1)S(1)} %fusion.77), channel_id=1, source_target_pairs={{0,2},{1,5},{2,0},{3,7},{4,6},{5,1},{6,4},{7,3},{8,10},{9,13},{10,... | collective-permute-start | bytes 1544 | tf_op jit(solution)/shard_map/ppermute | solution.py:122
  106.7 4.6 %copy-start.19 = (bf16[8,128,128]{1,2,0:T(8,128)(2,1)S(1)}, bf16[8,128,128]{1,2,0:T(8,128)(2,1)}, u32[]{:S(2)}) copy-start(bf16[8,128,128]{1,2,0:T(8,128)(2,1)} %convolution_convert_fusion.6) | copy-start | bytes 786436
  106.7 5.4 %copy-start.18 = (bf16[8,128,128]{1,2,0:T(8,128)(2,1)S(1)}, bf16[8,128,128]{1,2,0:T(8,128)(2,1)}, u32[]{:S(2)}) copy-start(bf16[8,128,128]{1,2,0:T(8,128)(2,1)} %convolution_convert_fusion.1) | copy-start | bytes 786436
  108.1 18.4 %collective-permute-start.8 = (bf16[2,2,64,1024]{3,2,1,0:T(8,128)(2,1)S(1)}, bf16[2,2,64,1024]{3,2,1,0:T(8,128)(2,1)}, u32[]{:S(2)}, u32[]{:S(2)}) collective-permute-start(bf16[2,2,64,1024]{3,2,1,0:T(8,128)(2,1)S(1)} %fusion.45), channel_id=1, source_target_pairs={{0,2},{1,5},{2,0},{3,7},{4,6},{5,1},{6,4},{7,3},{8,10},{9,13},{10,... | collective-permute-start | bytes 1572872 | tf_op jit(solution)/shard_map/ppermute | solution.py:122
  120.9 12.3 %collective-permute-start.14 = (bf16[2,64,1]{1,0,2:T(2,128)(2,1)S(1)}, bf16[2,64,1]{1,0,2:T(2,128)(2,1)S(1)}, u32[]{:S(2)}, u32[]{:S(2)}) collective-permute-start(bf16[2,64,1]{1,0,2:T(2,128)(2,1)S(1)} %fusion.81), channel_id=1, source_target_pairs={{0,4},{1,3},{2,6},{3,1},{4,0},{5,7},{6,2},{7,5},{8,12},{9,11},{10,... | collective-permute-start | bytes 776 | tf_op jit(solution)/shard_map/ppermute | solution.py:122
  131.0 17.6 %collective-permute-start.3 = (bf16[2,64,3072]{2,1,0:T(8,128)(2,1)S(1)}, bf16[2,64,3072]{2,1,0:T(8,128)(2,1)S(1)}, u32[]{:S(2)}, u32[]{:S(2)}) collective-permute-start(bf16[2,64,3072]{2,1,0:T(8,128)(2,1)S(1)} %fusion.36), channel_id=1, source_target_pairs={{0,4},{1,3},{2,6},{3,1},{4,0},{5,7},{6,2},{7,5},{8,12},{9,11},{10,... | collective-permute-start | bytes 2359304 | tf_op jit(solution)/shard_map/ppermute | solution.py:122
  132.8 13.1 %collective-permute-start.9 = (bf16[2,64,1024]{2,1,0:T(8,128)(2,1)S(1)}, bf16[2,64,1024]{2,1,0:T(8,128)(2,1)S(1)}, u32[]{:S(2)}, u32[]{:S(2)}) collective-permute-start(bf16[2,64,1024]{2,1,0:T(8,128)(2,1)S(1)} %fusion.53), channel_id=1, source_target_pairs={{0,4},{1,3},{2,6},{3,1},{4,0},{5,7},{6,2},{7,5},{8,12},{9,11},{10,... | collective-permute-start | bytes 786440 | tf_op jit(solution)/shard_map/ppermute | solution.py:122
  133.2 16.1 %collective-permute-start.15 = (bf16[64,1]{0,1:T(2,128)(2,1)S(1)}, bf16[64,1]{0,1:T(2,128)(2,1)S(1)}, u32[]{:S(2)}, u32[]{:S(2)}) collective-permute-start(bf16[64,1]{0,1:T(2,128)(2,1)S(1)} %fusion.86), channel_id=1, source_target_pairs={{0,8},{1,9},{2,10},{3,11},{4,12},{5,13},{6,14},{7,15},{8,0},{9,1},... | collective-permute-start | bytes 392 | tf_op jit(solution)/shard_map/ppermute | solution.py:122
  146.0 17.5 %collective-permute-start.10 = (bf16[64,1024]{1,0:T(8,128)(2,1)S(1)}, bf16[64,1024]{1,0:T(8,128)(2,1)S(1)}, u32[]{:S(2)}, u32[]{:S(2)}) collective-permute-start(bf16[64,1024]{1,0:T(8,128)(2,1)S(1)} %fusion.66), channel_id=1, source_target_pairs={{0,8},{1,9},{2,10},{3,11},{4,12},{5,13},{6,14},{7,15},{8,0},{9,1},... | collective-permute-start | bytes 393224 | tf_op jit(solution)/shard_map/ppermute | solution.py:122
  148.9 21.9 %collective-permute-start.4 = (bf16[64,3072]{1,0:T(8,128)(2,1)S(1)}, bf16[64,3072]{1,0:T(8,128)(2,1)S(1)}, u32[]{:S(2)}, u32[]{:S(2)}) collective-permute-start(bf16[64,3072]{1,0:T(8,128)(2,1)S(1)} %fusion.50), channel_id=1, source_target_pairs={{0,8},{1,9},{2,10},{3,11},{4,12},{5,13},{6,14},{7,15},{8,0},{9,1},... | collective-permute-start | bytes 1179656 | tf_op jit(solution)/shard_map/ppermute | solution.py:122
  149.3 23.2 %collective-permute-start.16 = (bf16[64,1]{0,1:T(2,128)(2,1)S(1)}, bf16[64,1]{0,1:T(2,128)(2,1)S(1)}, u32[]{:S(2)}, u32[]{:S(2)}) collective-permute-start(bf16[64,1]{0,1:T(2,128)(2,1)S(1)} %fusion.84), channel_id=1, source_target_pairs={{0,16},{16,0},{1,17},{17,1},{2,18},{18,2},{3,19},{19,3},{4,20},{20... | collective-permute-start | bytes 392 | tf_op jit(solution)/shard_map/ppermute | solution.py:129
  163.5 9.4 %collective-permute-start.11 = (bf16[64,1024]{1,0:T(8,128)(2,1)S(1)}, bf16[64,1024]{1,0:T(8,128)(2,1)S(1)}, u32[]{:S(2)}, u32[]{:S(2)}) collective-permute-start(bf16[64,1024]{1,0:T(8,128)(2,1)S(1)} %fusion.54), channel_id=1, source_target_pairs={{0,16},{16,0},{1,17},{17,1},{2,18},{18,2},{3,19},{19,3},{4,20},{20... | collective-permute-start | bytes 393224 | tf_op jit(solution)/shard_map/ppermute | solution.py:129
  170.9 10.1 %collective-permute-start.5 = (bf16[64,3072]{1,0:T(8,128)(2,1)S(1)}, bf16[64,3072]{1,0:T(8,128)(2,1)S(1)}, u32[]{:S(2)}, u32[]{:S(2)}) collective-permute-start(bf16[64,3072]{1,0:T(8,128)(2,1)S(1)} %fusion.37), channel_id=1, source_target_pairs={{0,16},{16,0},{1,17},{17,1},{2,18},{18,2},{3,19},{19,3},{4,20},{20... | collective-permute-start | bytes 1179656 | tf_op jit(solution)/shard_map/ppermute | solution.py:129
  (11 other events, 19.7 us)

commit v3 on v2

--- a/solution.py
+++ b/solution.py
@@ -181,6 +181,24 @@
     grad_local = jnp.dot(used_grads, joint_weight.T, preferred_element_type=jnp.float32).astype(
         jnp.bfloat16
     )
+    seq_n = lax.axis_size("seq")
+    dp_n = lax.axis_size("dp")
+    orders = split_orders(seq_n)
+    core_odd = lax.axis_index("seq") % 2 == 1
+    pair = [(member, member ^ 1) for member in range(seq_n)]
+    core = lax.axis_index("seq") % 2
+
+    def my_half(factor):
+        arranged = by_split_order(factor, orders, core_odd, seq_n)
+        half = arranged.shape[1] // 2
+        return lax.dynamic_slice_in_dim(arranged, core * half, half, axis=1)
+
+    normed_peer, grads_peer = lax.ppermute((used_normed, used_grads), "seq", pair)
+    joint_term = jnp.dot(
+        my_half(jnp.concatenate([used_normed, normed_peer], axis=0)).T,
+        jnp.concatenate([used_grads, grads_peer], axis=0),
+        preferred_element_type=jnp.float32,
+    )
     grad_normed = lax.all_to_all(
         grad_local.reshape(batches, all_rows, col_share, model_width),
         "seq",
@@ -189,24 +207,7 @@
         tiled=True,
     )
     grad_normed = grad_normed.reshape(-1, model_width)
-    seq_n = lax.axis_size("seq")
-    dp_n = lax.axis_size("dp")
-    orders = split_orders(seq_n)
-    core_odd = lax.axis_index("seq") % 2 == 1
-    pair = [(member, member ^ 1) for member in range(seq_n)]
-    core = lax.axis_index("seq") % 2
-
-    def my_half(factor):
-        arranged = by_split_order(factor, orders, core_odd, seq_n)
-        half = arranged.shape[1] // 2
-        return lax.dynamic_slice_in_dim(arranged, core * half, half, axis=1)
-
-    normed_peer, grads_peer = lax.ppermute((used_normed, used_grads), "seq", pair)
-    joint_term = jnp.dot(
-        my_half(jnp.concatenate([used_normed, normed_peer], axis=0)).T,
-        jnp.concatenate([used_grads, grads_peer], axis=0),
-        preferred_element_type=jnp.float32,
-    )
+    joint_term, grad_normed = lax.optimization_barrier((joint_term, grad_normed))
     grad_float = grad_normed.astype(jnp.float32)
     gain_term = jnp.sum(grad_float * hidden * inverse, axis=0)
     scaled = norm_gain * grad_float
@@ -220,8 +221,11 @@
         preferred_element_type=jnp.float32,
     )
     gain_term = my_half((gain_term + gain_peer)[None, :])[0][:, None]
-    joint_sum, out_sum, gain_sum = reduce_rows((joint_term, out_term, gain_term), orders, seq_n, dp_n)
-    replicas = (joint_sum, out_sum, gain_sum[:, 0])
+    out_width = out_term.shape[1]
+    joint_sum, out_sum = reduce_rows(
+        (joint_term, jnp.concatenate([out_term, gain_term], axis=1)), orders, seq_n, dp_n
+    )
+    replicas = (joint_sum, out_sum[:, :out_width], out_sum[:, out_width])
     grad_first = jnp.dot(grad_hidden, out_weight.T, preferred_element_type=jnp.float32).astype(
         jnp.bfloat16
     )

time: 185 us -> 182 us (0.984)
  starting transfers between devices: 39.5 us -> 30.8 us
  other arithmetic: 18.7 us -> 22.9 us
  matrix products: 35.9 us -> 38.4 us
    ppermute x9 -> x6, starting transfers between devices: 13.6 us -> 6.11 us  [reduce_rows(): got = lax.ppermute(given, 'seq', perm)]
    ppermute x9 -> x6, waiting for transfers between devices: 38.3 us -> 34.5 us  [reduce_rows(): got = lax.ppermute(given, 'seq', perm)]
    convert_element_type x9 -> x5, local copies, waits for them, and re-layouts: 1.65 us -> 5.06 us  [reduce_rows(): lax.dynamic_index_in_dim(acc, 1 - keep_at, 0, keepdims=False)]
    dot_general x1, matrix products: 2.12 us -> 4.8 us  [on_device(): jnp.dot(my_half(jnp.concatenate([used_normed, normed_peer], axis=0)).T, j...]
    add x6 -> x4, other arithmetic: 4.65 us -> 7.18 us  [reduce_rows(): accs = tuple((k + g.astype(jnp.float32) for k, g in zip(kept, got)))]
    all_to_all x1, waiting for transfers between devices: 0.01 us -> 2.01 us  [on_device(): lax.all_to_all(out_cols.reshape(batches, all_rows, col_share, feature), '...]
    ppermute x3 -> x2, starting transfers between devices: 4.74 us -> 3.13 us  [reduce_rows(): got = lax.ppermute(mine, 'dp', perm)]
    ppermute x3 -> x2, waiting for transfers between devices: 7.27 us -> 7.82 us  [reduce_rows(): got = lax.ppermute(mine, 'dp', perm)]
  transfers between devices with their start and end apart: 21 -> 17, of which waited for: 9 -> 9; matrix products, arithmetic and copies ran while one was open for 32% -> 36% of each run, Pallas kernels for 0% -> 0%
where the time goes in v3:
time: 182 us; the launch traced here: 181 us
  waiting for transfers between devices  53.3 us (29%)
  matrix products  38.4 us (21%)
  local copies, waits for them, and re-layouts  33.9 us (19%)
  starting transfers between devices  30.8 us (17%)
  other arithmetic  22.9 us (13%)
    ppermute x6, waiting for transfers between devices, reduce_rows(): got = lax.ppermute(given, 'seq', perm)  34.5 us
    unnamed x52, local copies, waits for them, and re-layouts  18 us
    ppermute x2, waiting for transfers between devices, reduce_rows(): got = lax.ppermute(mine, 'dp', perm)  7.82 us
    all_to_all x1, starting transfers between devices, on_device(): lax.all_to_all(upstream, 'seq', split_axis=2, concat_axis=1, tiled=True)  7.44 us
    add x4, other arithmetic, reduce_rows(): accs = tuple((k + g.astype(jnp.float32) for k, g in zip(kept, got)))  7.18 us
    ppermute x6, starting transfers between devices, reduce_rows(): got = lax.ppermute(given, 'seq', perm)  6.11 us
    dot_general x1, matrix products, on_device(): jnp.dot(used_grads, joint_weight.T, preferred_element_type=jnp.float32)  5.68 us
    dot_general x2, matrix products, attend_back(): jnp.einsum(scores_form + ',' + layout + '->' + keyed, grad_score, queries...  5.46 us
  transfers between devices with their start and end apart: 17, of which 9 were waited for; matrix products, arithmetic and copies ran while one was open for 36% of the time, Pallas kernels for 0%

profile of v3, /device:TPU:0, one launch (start us, length us, event | category | flops | bytes accessed | tf_op | source)
XLA Modules:
  0.0 180.6 jit_solution(9435721938309928108)
XLA Ops:
  2.7 2.1 %reduce.20 = bf16[128,1024]{1,0:T(8,128)(2,1)S(1)} reduce(bf16[128,1,1,1024]{3,2,1,0:T(2,128)(2,1)S(1)} %bitcast.183, bf16[]{:T(256)} %broadcast.111), dimensions={1,2}, to_apply=%bitcast.172.reduce_sub_computation | reduce | bytes 524290
  5.7 7.4 %all-to-all-start.1 = ((bf16[16,2,4096]{2,1,0:T(2,128)(2,1)}), bf16[16,2,4096]{2,1,0:T(2,128)(2,1)}, u32[]{:S(2)}, u32[]{:S(2)}) async-start(bf16[16,2,4096]{2,1,0:T(2,128)(2,1)} %reshape.306), calls=%async_computation.1 | async-start | bytes 524288 | tf_op jit(solution)/shard_map/all_to_all | solution.py:173
  16.8 2.9 %reduce.21 = bf16[128,1024]{1,0:T(8,128)(2,1)} reduce(bf16[128,1,1,1024]{3,2,1,0:T(2,128)(2,1)S(1)} %bitcast.184, bf16[]{:T(256)} %broadcast.111), dimensions={1,2}, to_apply=%bitcast.173.reduce_sub_computation | reduce | bytes 524290
  19.7 1.8 %reshape.308 = bf16[16,2,4096]{2,1,0:T(2,128)(2,1)} reshape(bf16[128,1024]{1,0:T(8,128)(2,1)} %reduce.21) | data formatting | bytes 524288
  23.3 4.0 %all-to-all-start = ((bf16[16,2,4096]{2,1,0:T(2,128)(2,1)}), bf16[16,2,4096]{2,1,0:T(2,128)(2,1)S(1)}, u32[]{:S(2)}, u32[]{:S(2)}) async-start(bf16[16,2,4096]{2,1,0:T(2,128)(2,1)} %reshape.308), calls=%async_computation | async-start | bytes 524288 | tf_op jit(solution)/shard_map/all_to_all | solution.py:149
  29.5 2.2 %reshape.307 = bf16[128,1,1,1024]{3,2,1,0:T(2,128)(2,1)S(1)} reshape(bf16[16,2,4096]{2,1,0:T(2,128)(2,1)} %all-to-all-done.1) | data formatting | bytes 524288
  33.9 3.5 %all-to-all-done = bf16[16,2,4096]{2,1,0:T(2,128)(2,1)S(1)} async-done(((bf16[16,2,4096]{2,1,0:T(2,128)(2,1)}), bf16[16,2,4096]{2,1,0:T(2,128)(2,1)S(1)}, u32[]{:S(2)}, u32[]{:S(2)}) %all-to-all-start) | async-done | bytes 262176 | tf_op jit(solution)/shard_map/all_to_all | solution.py:149
  38.6 3.9 %convolution_convert_fusion = bf16[128,3072]{1,0:T(8,128)(2,1)S(1)} fusion(bf16[1024,3072]{1,0:T(8,128)(2,1)} %param.12, bf16[1,1,128,1024]{2,3,1,0:T(8,128)(2,1)} %copy.109), kind=kOutput, calls=%fused_computation.4 | convolution fusion | flops 805699584 | bytes 7340032 | tf_op jit(solution)/shard_map/dot_general | solution.py:156
  44.7 2.5 %fusion.92 = (f32[8,8,16]{2,1,0:T(8,128)S(1)}, f32[8,8,16,16]{2,3,1,0:T(8,128)}) fusion(pred[16,16]{0,1:T(8,128)(4,1)S(1)} %iota_compare_fusion.1, bf16[1,16,8,1,8,128]{5,2,4,3,1,0:T(8,128)(2,1)S(1)} %get-tuple-element.43, bf16[1,16,8,1,8,128]{5,2,4,3,1,0:T(8,128)(2,1)} %get-tuple-element.42), kind=kOutput, calls=%fused_computation.144 | convolution fusion | flops 4259855 | bytes 594176 | tf_op jit(solution)/shard_map/sub | solution.py:28
  48.6 2.9 %fusion.32 = bf16[1,16,8,1,8,128]{5,1,4,2,3,0:T(8,128)(2,1)} fusion(f32[8,8,16,16]{2,3,1,0:T(8,128)} %convolution_bitcast_fusion, bf16[1,16,8,1,8,128]{5,2,4,3,1,0:T(8,128)(2,1)} %get-tuple-element.42, f32[8,8,16,16]{2,3,1,0:T(8,128)} %get-tuple-element.51, f32[8,8,16]{2,1,0:T(8,128)S(1)} %get-tuple-element.50), kind=kOutput, calls=%fused_computation.54 | convolution fusion | flops 4441103 | bytes 659456 | tf_op jit(solution)/shard_map/bchlm,blche->bmche/dot_general | solution.py:57
  51.4 2.7 %fusion.28 = bf16[1,16,8,1,8,128]{5,1,4,2,3,0:T(8,128)(2,1)} fusion(f32[8,8,16,16]{2,3,1,0:T(8,128)} %convolution_bitcast_fusion, bf16[1,16,8,1,8,128]{5,2,4,3,1,0:T(8,128)(2,1)S(1)} %copy-done.18, f32[8,8,16,16]{2,3,1,0:T(8,128)} %get-tuple-element.51, f32[8,8,16]{2,1,0:T(8,128)S(1)} %get-tuple-element.50), kind=kOutput, calls=%fused_computation.50 | convolution fusion | flops 4441103 | bytes 659456 | tf_op jit(solution)/shard_map/bchlm,bmche->blche/dot_general | solution.py:51
  60.1 4.2 %all-to-all-start.3 = ((bf16[1,16,8,1024]{3,2,0,1:T(8,128)(2,1)}), bf16[1,16,8,1024]{3,2,0,1:T(8,128)(2,1)}, u32[]{:S(2)}, u32[]{:S(2)}) async-start(bf16[1,16,8,1024]{3,2,0,1:T(8,128)(2,1)} %bitcast.188), calls=%async_computation.3 | async-start | bytes 524288 | tf_op jit(solution)/shard_map/all_to_all | solution.py:166
  64.8 5.7 %fusion.30 = bf16[1,16,8,1024]{3,2,0,1:T(8,128)(2,1)} fusion(bf16[128,3072]{1,0:T(8,128)(2,1)S(1)} %reshape_reshape.7, bf16[1024,3072]{1,0:T(8,128)(2,1)} %param.12), kind=kOutput, calls=%fused_computation.52 | convolution fusion | flops 805437440 | bytes 7340032 | tf_op jit(solution)/shard_map/dot_general | solution.py:181
  70.4 1.9 %pad_maximum_fusion.1 = bf16[256,2,2,2,2,64]{0,5,4,3,2,1:T(8,128)(2,1)} fusion(bf16[128,2,2,2,2,64]{0,5,4,3,2,1:T(8,128)(2,1)} %bitcast.7, bf16[128,2,2,2,2,64]{0,5,4,3,2,1:T(8,128)(2,1)} %bitcast.5), kind=kLoop, calls=%fused_computation.79 | loop fusion | flops 1048576 | bytes 1048576 | tf_op jit(solution)/shard_map/concatenate | solution.py:198
  72.4 2.0 %all-to-all-done.3 = bf16[1,16,8,1024]{3,2,0,1:T(8,128)(2,1)} async-done(((bf16[1,16,8,1024]{3,2,0,1:T(8,128)(2,1)}), bf16[1,16,8,1024]{3,2,0,1:T(8,128)(2,1)}, u32[]{:S(2)}, u32[]{:S(2)}) %all-to-all-start.3) | async-done | bytes 262176 | tf_op jit(solution)/shard_map/all_to_all | solution.py:166
  74.4 4.4 %all-to-all-start.2 = ((bf16[1,16,8,1024]{3,2,0,1:T(8,128)(2,1)}), bf16[1,16,8,1024]{3,2,0,1:T(8,128)(2,1)}, u32[]{:S(2)}, u32[]{:S(2)}) async-start(bf16[1,16,8,1024]{3,2,0,1:T(8,128)(2,1)} %fusion.30), calls=%async_computation.2 | async-start | bytes 524288 | tf_op jit(solution)/shard_map/all_to_all | solution.py:202
  80.1 4.8 %fusion.5 = f32[512,3072]{1,0:T(8,128)} fusion(bf16[128,3072]{1,0:T(8,128)(2,1)} %collective-permute-done.1, bf16[128,3072]{1,0:T(8,128)(2,1)S(1)} %reshape_reshape.7, bf16[256,1024]{0,1:T(8,128)(2,1)S(1)} %bitcast.186, s32[]{:T(128)S(6)} %select_n.140), kind=kOutput, calls=%fused_computation.12 | convolution fusion | flops 808452096 | bytes 8126468 | tf_op jit(solution)/shard_map/dot_general | solution.py:197
  84.9 3.7 %all-to-all-done.2 = bf16[1,16,8,1024]{3,2,0,1:T(8,128)(2,1)} async-done(((bf16[1,16,8,1024]{3,2,0,1:T(8,128)(2,1)}), bf16[1,16,8,1024]{3,2,0,1:T(8,128)(2,1)}, u32[]{:S(2)}, u32[]{:S(2)}) %all-to-all-start.2) | async-done | bytes 262176 | tf_op jit(solution)/shard_map/all_to_all | solution.py:202
  91.5 3.2 %fusion.4 = bf16[2,2,64,3072]{3,2,1,0:T(8,128)(2,1)} fusion(f32[2,2,2,64,3072]{4,3,2,1,0:T(8,128)} %bitcast.174, s32[]{:T(128)S(6)} %select_n.148), kind=kLoop, calls=%fused_computation.11 | loop fusion | bytes 3145732 | tf_op jit(solution)/shard_map/convert_element_type | solution.py:119
  100.6 2.0 %collective-permute-start.9 = (bf16[2,2,64,1025]{3,2,1,0:T(8,128)(2,1)}, bf16[2,2,64,1025]{3,2,1,0:T(8,128)(2,1)}, u32[]{:S(2)}, u32[]{:S(2)}) collective-permute-start(bf16[2,2,64,1025]{3,2,1,0:T(8,128)(2,1)} %fusion.45), channel_id=1, source_target_pairs={{0,2},{1,5},{2,0},{3,7},{4,6},{5,1},{6,4},{7,3},{8,10},{9,13},{10,... | collective-permute-start | bytes 1574408 | tf_op jit(solution)/shard_map/ppermute | solution.py:122
  103.6 2.6 %convolution_convert_fusion.1 = bf16[8,128,128]{1,2,0:T(8,128)(2,1)} fusion(bf16[128,8,128]{0,2,1:T(8,128)(2,1)S(1)} %bitcast.192, f32[8,128,128]{1,2,0:T(8,128)} %fusion.67, f32[8,128,128]{1,2,0:T(8,128)} %get-tuple-element.47, f32[8,128]{1,0:T(8,128)S(1)} %get-tuple-element.46), kind=kOutput, calls=%fused_computation.35 | convolution fusion | flops 34604160 | bytes 1576960 | tf_op jit(solution)/shard_map/ghlm,gmhe->glhe/dot_general | solution.py:51
  106.2 2.6 %convolution_convert_fusion.6 = bf16[8,128,128]{1,2,0:T(8,128)(2,1)} fusion(bf16[128,8,128]{0,2,1:T(8,128)(2,1)S(1)} %bitcast.190, f32[8,128,128]{1,2,0:T(8,128)} %fusion.67, f32[8,128,128]{1,2,0:T(8,128)} %get-tuple-element.47, f32[8,128]{1,0:T(8,128)S(1)} %get-tuple-element.46), kind=kOutput, calls=%fused_computation.40 | convolution fusion | flops 34604160 | bytes 1576960 | tf_op jit(solution)/shard_map/ghlm,glhe->gmhe/dot_general | solution.py:57
  108.8 14.7 %collective-permute-done.9 = bf16[2,2,64,1025]{3,2,1,0:T(8,128)(2,1)} collective-permute-done((bf16[2,2,64,1025]{3,2,1,0:T(8,128)(2,1)}, bf16[2,2,64,1025]{3,2,1,0:T(8,128)(2,1)}, u32[]{:S(2)}, u32[]{:S(2)}) %collective-permute-start.9) | collective-permute-done | bytes 524832 | tf_op jit(solution)/shard_map/ppermute | solution.py:122
  126.0 2.8 %bitcast_add_fusion = f32[2,2,64,3072]{3,2,1,0:T(8,128)S(1)} fusion(bf16[2,2,64,3072]{3,2,1,0:T(8,128)(2,1)} %collective-permute-done.2, f32[2,2,2,64,3072]{4,3,2,1,0:T(8,128)} %bitcast.175, s32[]{:T(128)S(6)} %select_n.147), kind=kLoop, calls=%fused_computation.7 | loop fusion | flops 1572864 | bytes 7864324 | tf_op jit(solution)/shard_map/add | solution.py:123
  131.5 1.8 %collective-permute-start.3 = (bf16[2,64,3072]{2,1,0:T(8,128)(2,1)}, bf16[2,64,3072]{2,1,0:T(8,128)(2,1)}, u32[]{:S(2)}, u32[]{:S(2)}) collective-permute-start(bf16[2,64,3072]{2,1,0:T(8,128)(2,1)} %fusion.41), channel_id=1, source_target_pairs={{0,4},{1,3},{2,6},{3,1},{4,0},{5,7},{6,2},{7,5},{8,12},{9,11},{10,... | collective-permute-start | bytes 2359304 | tf_op jit(solution)/shard_map/ppermute | solution.py:122
  133.3 2.2 %convolution_convert_fusion.5 = bf16[8,128,128]{2,1,0:T(8,128)(2,1)} fusion(bf16[128,8,128]{0,2,1:T(8,128)(2,1)S(1)} %bitcast.196, f32[8,128]{1,0:T(8,128)S(1)} %get-tuple-element.46, f32[8,128,128]{1,2,0:T(8,128)} %copy-done.3), kind=kOutput, calls=%fused_computation.39 | convolution fusion | flops 34079872 | bytes 1052672 | tf_op jit(solution)/shard_map/ghlm,glhe->gmhe/dot_general | solution.py:64
  135.5 1.8 copy.139
  137.3 1.8 copy.138
  144.3 1.8 bitcast_add_fusion.1
  147.2 12.2 %collective-permute-done.11 = bf16[64,1025]{1,0:T(8,128)(2,1)S(1)} collective-permute-done((bf16[64,1025]{1,0:T(8,128)(2,1)S(1)}, bf16[64,1025]{1,0:T(8,128)(2,1)S(1)}, u32[]{:S(2)}, u32[]{:S(2)}) %collective-permute-start.11) | collective-permute-done | bytes 131232 | tf_op jit(solution)/shard_map/ppermute | solution.py:122
  161.0 6.4 %collective-permute-done.4 = bf16[64,3072]{1,0:T(8,128)(2,1)S(1)} collective-permute-done((bf16[64,3072]{1,0:T(8,128)(2,1)S(1)}, bf16[64,3072]{1,0:T(8,128)(2,1)S(1)}, u32[]{:S(2)}, u32[]{:S(2)}) %collective-permute-start.4) | collective-permute-done | bytes 393248 | tf_op jit(solution)/shard_map/ppermute | solution.py:122
  170.3 7.8 %collective-permute-done.5 = bf16[64,3072]{1,0:T(8,128)(2,1)S(1)} collective-permute-done((bf16[64,3072]{1,0:T(8,128)(2,1)S(1)}, bf16[64,3072]{1,0:T(8,128)(2,1)S(1)}, u32[]{:S(2)}, u32[]{:S(2)}) %collective-permute-start.5) | collective-permute-done | bytes 393248 | tf_op jit(solution)/shard_map/ppermute | solution.py:129
  (122 shorter events, 52.9 us)
Async XLA Ops:
  0.6 15.1 %copy-start = (bf16[1024,1024]{1,0:T(8,128)(2,1)S(1)}, bf16[1024,1024]{1,0:T(8,128)(2,1)}, u32[]{:S(2)}) copy-start(bf16[1024,1024]{1,0:T(8,128)(2,1)} %param.10) | copy-start | bytes 6291460
  0.6 12.6 %copy-start.14 = (bf16[1,1,128,1024]{3,2,1,0:T(8,128)(2,1)S(1)}, bf16[1,1,128,1024]{3,2,1,0:T(8,128)(2,1)}, u32[]{:S(2)}) copy-start(bf16[1,1,128,1024]{3,2,1,0:T(8,128)(2,1)} %param.7) | copy-start | bytes 786436
  0.7 12.7 %copy-start.15 = (bf16[1,1,128,1024]{3,2,1,0:T(8,128)(2,1)S(1)}, bf16[1,1,128,1024]{3,2,1,0:T(8,128)(2,1)}, u32[]{:S(2)}) copy-start(bf16[1,1,128,1024]{3,2,1,0:T(8,128)(2,1)} %param.8) | copy-start | bytes 786436
  4.8 8.7 %copy-start.16 = (bf16[1,1,128,1024]{3,2,1,0:T(8,128)(2,1)S(1)}, bf16[1,1,128,1024]{3,2,1,0:T(8,128)(2,1)}, u32[]{:S(2)}) copy-start(bf16[1,1,128,1024]{3,2,1,0:T(8,128)(2,1)} %param.9) | copy-start | bytes 786436
  5.7 17.5 %all-to-all-start.1 = ((bf16[16,2,4096]{2,1,0:T(2,128)(2,1)}), bf16[16,2,4096]{2,1,0:T(2,128)(2,1)}, u32[]{:S(2)}, u32[]{:S(2)}) async-start(bf16[16,2,4096]{2,1,0:T(2,128)(2,1)} %reshape.306), calls=%async_computation.1 | async-start | bytes 524288 | tf_op jit(solution)/shard_map/all_to_all | solution.py:173
  13.6 1.7 copy-start.7
  15.3 12.1 %collective-permute-start.6 = (bf16[128,1024]{0,1:T(8,128)(2,1)S(1)}, bf16[128,1024]{0,1:T(8,128)(2,1)}, u32[]{:S(2)}, u32[]{:S(2)}) collective-permute-start(bf16[128,1024]{0,1:T(8,128)(2,1)S(1)} %bitcast.179), channel_id=1, source_target_pairs={{0,1},{1,0},{2,3},{3,2},{4,5},{5,4},{6,7},{7,6},{8,9},{9,8},{10,11... | collective-permute-start | bytes 786440 | tf_op jit(solution)/shard_map/ppermute | solution.py:217
  23.3 14.0 %all-to-all-start = ((bf16[16,2,4096]{2,1,0:T(2,128)(2,1)}), bf16[16,2,4096]{2,1,0:T(2,128)(2,1)S(1)}, u32[]{:S(2)}, u32[]{:S(2)}) async-start(bf16[16,2,4096]{2,1,0:T(2,128)(2,1)} %reshape.308), calls=%async_computation | async-start | bytes 524288 | tf_op jit(solution)/shard_map/all_to_all | solution.py:149
  38.6 4.7 %copy-start.13 = (bf16[16,8,8,128]{3,2,1,0:T(8,128)(2,1)S(1)}, bf16[16,8,8,128]{3,2,1,0:T(8,128)(2,1)}, u32[]{:S(2)}) copy-start(bf16[16,8,8,128]{3,2,1,0:T(8,128)(2,1)} %copy.182) | copy-start | bytes 786436
  43.3 3.9 %copy-start.17 = (bf16[1,16,8,1,8,128]{5,2,4,3,1,0:T(8,128)(2,1)}, bf16[1,16,8,1,8,128]{5,2,4,3,1,0:T(8,128)(2,1)S(1)}, u32[]{:S(2)}) copy-start(bf16[1,16,8,1,8,128]{5,2,4,3,1,0:T(8,128)(2,1)S(1)} %get-tuple-element.43) | copy-start | bytes 786436
  48.6 2.9 %copy-start.18 = (bf16[1,16,8,1,8,128]{5,2,4,3,1,0:T(8,128)(2,1)S(1)}, bf16[1,16,8,1,8,128]{5,2,4,3,1,0:T(8,128)(2,1)}, u32[]{:S(2)}) copy-start(bf16[1,16,8,1,8,128]{5,2,4,3,1,0:T(8,128)(2,1)} %copy-done.17) | copy-start | bytes 786436
  55.5 15.0 %collective-permute-start = (bf16[128,1024]{0,1:T(8,128)(2,1)}, bf16[128,1024]{0,1:T(8,128)(2,1)}, u32[]{:S(2)}, u32[]{:S(2)}) collective-permute-start(bf16[128,1024]{0,1:T(8,128)(2,1)} %bitcast.6), channel_id=1, source_target_pairs={{0,1},{1,0},{2,3},{3,2},{4,5},{5,4},{6,7},{7,6},{8,9},{9,8},{10,11... | collective-permute-start | bytes 786440 | tf_op jit(solution)/shard_map/ppermute | solution.py:196
  60.1 14.3 %all-to-all-start.3 = ((bf16[1,16,8,1024]{3,2,0,1:T(8,128)(2,1)}), bf16[1,16,8,1024]{3,2,0,1:T(8,128)(2,1)}, u32[]{:S(2)}, u32[]{:S(2)}) async-start(bf16[1,16,8,1024]{3,2,0,1:T(8,128)(2,1)} %bitcast.188), calls=%async_computation.3 | async-start | bytes 524288 | tf_op jit(solution)/shard_map/all_to_all | solution.py:166
  64.3 15.8 %collective-permute-start.1 = (bf16[128,3072]{1,0:T(8,128)(2,1)S(1)}, bf16[128,3072]{1,0:T(8,128)(2,1)}, u32[]{:S(2)}, u32[]{:S(2)}) collective-permute-start(bf16[128,3072]{1,0:T(8,128)(2,1)S(1)} %reshape_reshape.7), channel_id=1, source_target_pairs={{0,1},{1,0},{2,3},{3,2},{4,5},{5,4},{6,7},{7,6},{8,9},{9,8},{10,11... | collective-permute-start | bytes 2359304 | tf_op jit(solution)/shard_map/ppermute | solution.py:196
  74.4 14.2 %all-to-all-start.2 = ((bf16[1,16,8,1024]{3,2,0,1:T(8,128)(2,1)}), bf16[1,16,8,1024]{3,2,0,1:T(8,128)(2,1)}, u32[]{:S(2)}, u32[]{:S(2)}) async-start(bf16[1,16,8,1024]{3,2,0,1:T(8,128)(2,1)} %fusion.30), calls=%async_computation.2 | async-start | bytes 524288 | tf_op jit(solution)/shard_map/all_to_all | solution.py:202
  89.8 6.7 %collective-permute-start.8 = (f32[1024]{0:T(1024)S(1)}, f32[1024]{0:T(1024)S(1)}, u32[]{:S(2)}, u32[]{:S(2)}) collective-permute-start(f32[1024]{0:T(1024)S(1)} %get-tuple-element.39), channel_id=1, source_target_pairs={{0,1},{1,0},{2,3},{3,2},{4,5},{5,4},{6,7},{7,6},{8,9},{9,8},{10,11... | collective-permute-start | bytes 12296 | tf_op jit(solution)/shard_map/ppermute | solution.py:217
  91.0 5.9 %collective-permute-start.7 = (bf16[128,1024]{1,0:T(8,128)(2,1)S(1)}, bf16[128,1024]{1,0:T(8,128)(2,1)}, u32[]{:S(2)}, u32[]{:S(2)}) collective-permute-start(bf16[128,1024]{1,0:T(8,128)(2,1)S(1)} %fusion.47), channel_id=1, source_target_pairs={{0,1},{1,0},{2,3},{3,2},{4,5},{5,4},{6,7},{7,6},{8,9},{9,8},{10,11... | collective-permute-start | bytes 786440 | tf_op jit(solution)/shard_map/ppermute | solution.py:217
  94.8 2.1 %copy-start.4 = (bf16[256,2,2,2,2,64]{0,5,4,3,2,1:T(8,128)(2,1)S(1)}, bf16[256,2,2,2,2,64]{0,5,4,3,2,1:T(8,128)(2,1)}, u32[]{:S(2)}) copy-start(bf16[256,2,2,2,2,64]{0,5,4,3,2,1:T(8,128)(2,1)} %copy.134) | copy-start | bytes 1572868
  96.4 29.5 %collective-permute-start.2 = (bf16[2,2,64,3072]{3,2,1,0:T(8,128)(2,1)}, bf16[2,2,64,3072]{3,2,1,0:T(8,128)(2,1)}, u32[]{:S(2)}, u32[]{:S(2)}) collective-permute-start(bf16[2,2,64,3072]{3,2,1,0:T(8,128)(2,1)} %fusion.4), channel_id=1, source_target_pairs={{0,2},{1,5},{2,0},{3,7},{4,6},{5,1},{6,4},{7,3},{8,10},{9,13},{10,... | collective-permute-start | bytes 4718600 | tf_op jit(solution)/shard_map/ppermute | solution.py:122
  98.3 4.2 %copy-start.10 = (bf16[16,8,8,128]{3,2,1,0:T(8,128)(2,1)S(1)}, bf16[16,8,8,128]{3,2,1,0:T(8,128)(2,1)}, u32[]{:S(2)}) copy-start(bf16[16,8,8,128]{3,2,1,0:T(8,128)(2,1)} %copy-done.9) | copy-start | bytes 786436
  98.3 4.2 %copy-start.11 = (bf16[128,1024]{0,1:T(8,128)(2,1)S(1)}, bf16[128,1024]{0,1:T(8,128)(2,1)}, u32[]{:S(2)}) copy-start(bf16[128,1024]{0,1:T(8,128)(2,1)} %copy.152) | copy-start | bytes 786436
  98.3 5.2 %copy-start.8 = (bf16[1,1,128,1024]{2,3,1,0:T(8,128)(2,1)S(1)}, bf16[1,1,128,1024]{2,3,1,0:T(8,128)(2,1)}, u32[]{:S(2)}) copy-start(bf16[1,1,128,1024]{2,3,1,0:T(8,128)(2,1)} %copy-done.7) | copy-start | bytes 786436
  100.6 5.6 %copy-start.6 = (bf16[1,1,128,1024]{2,3,1,0:T(8,128)(2,1)S(1)}, bf16[1,1,128,1024]{2,3,1,0:T(8,128)(2,1)}, u32[]{:S(2)}) copy-start(bf16[1,1,128,1024]{2,3,1,0:T(8,128)(2,1)} %copy-done.5) | copy-start | bytes 786436
  100.6 22.9 %collective-permute-start.9 = (bf16[2,2,64,1025]{3,2,1,0:T(8,128)(2,1)}, bf16[2,2,64,1025]{3,2,1,0:T(8,128)(2,1)}, u32[]{:S(2)}, u32[]{:S(2)}) collective-permute-start(bf16[2,2,64,1025]{3,2,1,0:T(8,128)(2,1)} %fusion.45), channel_id=1, source_target_pairs={{0,2},{1,5},{2,0},{3,7},{4,6},{5,1},{6,4},{7,3},{8,10},{9,13},{10,... | collective-permute-start | bytes 1574408 | tf_op jit(solution)/shard_map/ppermute | solution.py:122
  125.8 7.5 %copy-start.12 = (bf16[128,1024]{0,1:T(8,128)(2,1)S(1)}, bf16[128,1024]{0,1:T(8,128)(2,1)}, u32[]{:S(2)}) copy-start(bf16[128,1024]{0,1:T(8,128)(2,1)} %copy.152) | copy-start | bytes 786436
  125.8 15.1 %collective-permute-start.10 = (bf16[2,64,1025]{2,1,0:T(8,128)(2,1)}, bf16[2,64,1025]{2,1,0:T(8,128)(2,1)}, u32[]{:S(2)}, u32[]{:S(2)}) collective-permute-start(bf16[2,64,1025]{2,1,0:T(8,128)(2,1)} %fusion.57), channel_id=1, source_target_pairs={{0,4},{1,3},{2,6},{3,1},{4,0},{5,7},{6,2},{7,5},{8,12},{9,11},{10,... | collective-permute-start | bytes 787208 | tf_op jit(solution)/shard_map/ppermute | solution.py:122
  128.8 1.7 copy-start.2
  131.5 12.8 %collective-permute-start.3 = (bf16[2,64,3072]{2,1,0:T(8,128)(2,1)}, bf16[2,64,3072]{2,1,0:T(8,128)(2,1)}, u32[]{:S(2)}, u32[]{:S(2)}) collective-permute-start(bf16[2,64,3072]{2,1,0:T(8,128)(2,1)} %fusion.41), channel_id=1, source_target_pairs={{0,4},{1,3},{2,6},{3,1},{4,0},{5,7},{6,2},{7,5},{8,12},{9,11},{10,... | collective-permute-start | bytes 2359304 | tf_op jit(solution)/shard_map/ppermute | solution.py:122
  142.0 17.4 %collective-permute-start.11 = (bf16[64,1025]{1,0:T(8,128)(2,1)S(1)}, bf16[64,1025]{1,0:T(8,128)(2,1)S(1)}, u32[]{:S(2)}, u32[]{:S(2)}) collective-permute-start(bf16[64,1025]{1,0:T(8,128)(2,1)S(1)} %fusion.71), channel_id=1, source_target_pairs={{0,8},{1,9},{2,10},{3,11},{4,12},{5,13},{6,14},{7,15},{8,0},{9,1},... | collective-permute-start | bytes 393608 | tf_op jit(solution)/shard_map/ppermute | solution.py:122
  146.2 21.1 %collective-permute-start.4 = (bf16[64,3072]{1,0:T(8,128)(2,1)S(1)}, bf16[64,3072]{1,0:T(8,128)(2,1)S(1)}, u32[]{:S(2)}, u32[]{:S(2)}) collective-permute-start(bf16[64,3072]{1,0:T(8,128)(2,1)S(1)} %fusion.55), channel_id=1, source_target_pairs={{0,8},{1,9},{2,10},{3,11},{4,12},{5,13},{6,14},{7,15},{8,0},{9,1},... | collective-permute-start | bytes 1179656 | tf_op jit(solution)/shard_map/ppermute | solution.py:122
  159.4 9.6 %collective-permute-start.12 = (bf16[64,1025]{1,0:T(8,128)(2,1)S(1)}, bf16[64,1025]{1,0:T(8,128)(2,1)S(1)}, u32[]{:S(2)}, u32[]{:S(2)}) collective-permute-start(bf16[64,1025]{1,0:T(8,128)(2,1)S(1)} %fusion.58), channel_id=1, source_target_pairs={{0,16},{16,0},{1,17},{17,1},{2,18},{18,2},{3,19},{19,3},{4,20},{20... | collective-permute-start | bytes 393608 | tf_op jit(solution)/shard_map/ppermute | solution.py:129
  167.4 10.7 %collective-permute-start.5 = (bf16[64,3072]{1,0:T(8,128)(2,1)S(1)}, bf16[64,3072]{1,0:T(8,128)(2,1)S(1)}, u32[]{:S(2)}, u32[]{:S(2)}) collective-permute-start(bf16[64,3072]{1,0:T(8,128)(2,1)S(1)} %fusion.42), channel_id=1, source_target_pairs={{0,16},{16,0},{1,17},{17,1},{2,18},{18,2},{3,19},{19,3},{4,20},{20... | collective-permute-start | bytes 1179656 | tf_op jit(solution)/shard_map/ppermute | solution.py:129
  (5 other events, 7.2 us)

commit v4 on v3

--- a/solution.py
+++ b/solution.py
@@ -74,25 +74,34 @@
     )
 
 
-def split_orders(seq_n):
+def split_orders(seq_n, dp_n):
     bits = seq_n.bit_length() - 1
-    assert 1 << bits == seq_n
-    even = list(range(bits))
+    dp_bits = dp_n.bit_length() - 1
+    assert 1 << bits == seq_n and 1 << dp_bits == dp_n and bits >= 1
+    seq_rest = [("s", k) for k in range(1, bits)]
+    dp_all = [("d", k) for k in range(dp_bits)]
+    even = seq_rest[:1] + dp_all[:1] + seq_rest[1:] + dp_all[1:]
     odd = list(even)
-    if bits >= 3:
-        odd[1], odd[2] = odd[2], odd[1]
+    if bits >= 3 and dp_bits >= 1:
+        odd = dp_all[:1] + [seq_rest[1], seq_rest[0]] + seq_rest[2:] + dp_all[1:]
+    assert sorted(even) == sorted(odd)
     return even, odd
 
 
-def by_split_order(matrix, orders, core_odd, seq_n):
+def by_split_order(matrix, orders, core_odd, seq_n, dp_n):
     bits = seq_n.bit_length() - 1
+    dp_bits = dp_n.bit_length() - 1
     lead = matrix.shape[0]
-    block = matrix.shape[1] // seq_n
-    grid = matrix.reshape((lead,) + (2,) * bits + (matrix.shape[1] // seq_n,))
+    sub = matrix.shape[1] // (seq_n * dp_n)
+    grid = matrix.reshape((lead,) + (2,) * (bits + dp_bits) + (sub,))
+
+    def axis_of(item):
+        kind, k = item
+        return 1 + (bits - 1 - k) if kind == "s" else 1 + bits + (dp_bits - 1 - k)
 
     def arrange(order):
-        axes = (0,) + tuple(1 + (bits - 1 - bit) for bit in order) + (bits + 1,)
-        return jnp.transpose(grid, axes).reshape(lead, seq_n * block)
+        axes = (0, axis_of(("s", 0))) + tuple(axis_of(item) for item in order) + (bits + dp_bits + 1,)
+        return jnp.transpose(grid, axes).reshape(matrix.shape)
 
     even, odd = orders
     if even == odd:
@@ -101,34 +110,53 @@
 
 
 def reduce_rows(parts, orders, seq_n, dp_n):
-    bits = seq_n.bit_length() - 1
-    index = lax.axis_index("seq")
-    accs = tuple(p.reshape((2,) * (bits - 1) + (2 * p.shape[0] // seq_n, p.shape[1])) for p in parts)
+    seq_at = lax.axis_index("seq")
+    dp_at = lax.axis_index("dp")
     even, odd = orders
-    for step in range(1, bits):
+    steps = len(even)
+    accs = tuple(p.reshape((2,) * steps + (p.shape[0] >> steps, p.shape[1])) for p in parts)
+
+    def bit_value(item, seq_i, dp_i):
+        kind, k = item
+        return ((seq_i if kind == "s" else dp_i) >> k) & 1
+
+    def flip(item, seq_i, dp_i):
+        kind, k = item
+        if kind == "s":
+            return seq_i ^ (1 << k), dp_i
+        return seq_i, dp_i ^ (1 << k)
+
+    for step in range(steps):
         perm = []
-        for member in range(seq_n):
-            bit = (odd if member % 2 else even)[step]
-            perm.append((member, member ^ (1 << bit)))
-        bit_even, bit_odd = even[step], odd[step]
-        keep_even = (index // (1 << bit_even)) % 2
-        keep_odd = (index // (1 << bit_odd)) % 2
-        keep_at = jnp.where(index % 2 == 1, keep_odd, keep_even)
+        for dp_i in range(dp_n):
+            for seq_i in range(seq_n):
+                item = (odd if seq_i % 2 else even)[step]
+                seq_j, dp_j = flip(item, seq_i, dp_i)
+                perm.append((dp_i * seq_n + seq_i, dp_j * seq_n + seq_j))
+
+        def traced_bit(item):
+            kind, k = item
+            return ((seq_at if kind == "s" else dp_at) // (1 << k)) % 2
+
+        keep_at = jnp.where(seq_at % 2 == 1, traced_bit(odd[step]), traced_bit(even[step]))
         kept = tuple(lax.dynamic_index_in_dim(acc, keep_at, 0, keepdims=False) for acc in accs)
         given = tuple(
             lax.dynamic_index_in_dim(acc, 1 - keep_at, 0, keepdims=False).astype(jnp.bfloat16)
             for acc in accs
         )
-        got = lax.ppermute(given, "seq", perm)
+        got = lax.ppermute(given, ("dp", "seq"), perm)
         accs = tuple(k + g.astype(jnp.float32) for k, g in zip(kept, got))
-    dp_bits = dp_n.bit_length() - 1
-    assert 1 << dp_bits == dp_n
-    for step in range(dp_bits):
+    accs = tuple(acc.astype(jnp.bfloat16) for acc in accs)
+    for step in range(dp_n.bit_length() - 1):
         perm = [(member, member ^ (1 << step)) for member in range(dp_n)]
-        mine = tuple(acc.astype(jnp.bfloat16) for acc in accs)
-        got = lax.ppermute(mine, "dp", perm)
-        accs = tuple(m.astype(jnp.float32) + g.astype(jnp.float32) for m, g in zip(mine, got))
+        got = lax.ppermute(accs, "dp", perm)
+        upper = (dp_at // (1 << step)) % 2 == 1
+        accs = tuple(
+            jnp.where(upper, jnp.concatenate([g, acc], axis=0), jnp.concatenate([acc, g], axis=0))
+            for acc, g in zip(accs, got)
+        )
     return accs
+
 
 def on_device(first_query, first_key, first_value, out_weight, norm_gain, joint_weight, upstream):
     batches, local_rows, columns, feature = first_query.shape
@@ -183,13 +211,13 @@
     )
     seq_n = lax.axis_size("seq")
     dp_n = lax.axis_size("dp")
-    orders = split_orders(seq_n)
+    orders = split_orders(seq_n, dp_n)
     core_odd = lax.axis_index("seq") % 2 == 1
     pair = [(member, member ^ 1) for member in range(seq_n)]
     core = lax.axis_index("seq") % 2
 
     def my_half(factor):
-        arranged = by_split_order(factor, orders, core_odd, seq_n)
+        arranged = by_split_order(factor, orders, core_odd, seq_n, dp_n)
         half = arranged.shape[1] // 2
         return lax.dynamic_slice_in_dim(arranged, core * half, half, axis=1)
 
@@ -225,7 +253,7 @@
     joint_sum, out_sum = reduce_rows(
         (joint_term, jnp.concatenate([out_term, gain_term], axis=1)), orders, seq_n, dp_n
     )
-    replicas = (joint_sum, out_sum[:, :out_width], out_sum[:, out_width])
+    replicas = (joint_sum, out_sum[:, :out_width], out_sum[:, out_width].astype(jnp.float32))
     grad_first = jnp.dot(grad_hidden, out_weight.T, preferred_element_type=jnp.float32).astype(
         jnp.bfloat16
     )

time: 182 us -> 174 us (0.956)
  waiting for transfers between devices: 53.3 us -> 46.7 us
  starting transfers between devices: 30.8 us -> 28.9 us
    ppermute x8 -> x10, waiting for transfers between devices: 42.3 us -> 35.8 us  [the longest x8 32.4 us: reduce_rows(): got = lax.ppermute(given, ('dp', 'seq'), perm)]
    ppermute x8 -> x10, starting transfers between devices: 9.24 us -> 7.31 us  [the longest x8 6.03 us: reduce_rows(): got = lax.ppermute(given, ('dp', 'seq'), perm)]
    add x4 -> x6, other arithmetic: 7.18 us -> 7.28 us  [reduce_rows(): accs = tuple((k + g.astype(jnp.float32) for k, g in zip(kept, got)))]
    convert_element_type x5 -> x7, local copies, waits for them, and re-layouts: 5.06 us -> 5.1 us  [reduce_rows(): lax.dynamic_index_in_dim(acc, 1 - keep_at, 0, keepdims=False)]
  transfers between devices with their start and end apart: 17 -> 19, of which waited for: 9 -> 9; matrix products, arithmetic and copies ran while one was open for 36% -> 38% of each run, Pallas kernels for 0% -> 0%
where the time goes in v4:
time: 174 us; the launch traced here: 172 us
  waiting for transfers between devices  46.7 us (27%)
  matrix products  38.4 us (22%)
  local copies, waits for them, and re-layouts  33.4 us (19%)
  starting transfers between devices  28.9 us (17%)
  other arithmetic  23.6 us (14%)
    ppermute x8, waiting for transfers between devices, reduce_rows(): got = lax.ppermute(given, ('dp', 'seq'), perm)  32.4 us
    unnamed x52, local copies, waits for them, and re-layouts  18 us
    all_to_all x1, starting transfers between devices, on_device(): lax.all_to_all(upstream, 'seq', split_axis=2, concat_axis=1, tiled=True)  7.44 us
    add x6, other arithmetic, reduce_rows(): accs = tuple((k + g.astype(jnp.float32) for k, g in zip(kept, got)))  7.28 us
    ppermute x8, starting transfers between devices, reduce_rows(): got = lax.ppermute(given, ('dp', 'seq'), perm)  6.03 us
    dot_general x1, matrix products, on_device(): jnp.dot(used_grads, joint_weight.T, preferred_element_type=jnp.float32)  5.68 us
    dot_general x2, matrix products, attend_back(): jnp.einsum(scores_form + ',' + layout + '->' + keyed, grad_score, queries...  5.47 us
    dot_general x2, matrix products, attend_back(): jnp.einsum(scores_form + ',' + keyed + '->' + layout, grad_score, key_tab...  5.29 us
  transfers between devices with their start and end apart: 19, of which 9 were waited for; matrix products, arithmetic and copies ran while one was open for 38% of the time, Pallas kernels for 0%

profile of v4, /device:TPU:0, one launch (start us, length us, event | category | flops | bytes accessed | tf_op | source)
XLA Modules:
  0.0 172.3 jit_solution(11365395677182572597)
XLA Ops:
  2.7 2.1 %reduce.20 = bf16[128,1024]{1,0:T(8,128)(2,1)S(1)} reduce(bf16[128,1,1,1024]{3,2,1,0:T(2,128)(2,1)S(1)} %bitcast.191, bf16[]{:T(256)} %broadcast.113), dimensions={1,2}, to_apply=%bitcast.180.reduce_sub_computation | reduce | bytes 524290
  5.7 7.4 %all-to-all-start.1 = ((bf16[16,2,4096]{2,1,0:T(2,128)(2,1)}), bf16[16,2,4096]{2,1,0:T(2,128)(2,1)}, u32[]{:S(2)}, u32[]{:S(2)}) async-start(bf16[16,2,4096]{2,1,0:T(2,128)(2,1)} %reshape.311), calls=%async_computation.1 | async-start | bytes 524288 | tf_op jit(solution)/shard_map/all_to_all | solution.py:201
  16.8 2.9 %reduce.21 = bf16[128,1024]{1,0:T(8,128)(2,1)} reduce(bf16[128,1,1,1024]{3,2,1,0:T(2,128)(2,1)S(1)} %bitcast.192, bf16[]{:T(256)} %broadcast.113), dimensions={1,2}, to_apply=%bitcast.181.reduce_sub_computation | reduce | bytes 524290
  19.7 1.8 %reshape.313 = bf16[16,2,4096]{2,1,0:T(2,128)(2,1)} reshape(bf16[128,1024]{1,0:T(8,128)(2,1)} %reduce.21) | data formatting | bytes 524288
  23.3 4.0 %all-to-all-start = ((bf16[16,2,4096]{2,1,0:T(2,128)(2,1)}), bf16[16,2,4096]{2,1,0:T(2,128)(2,1)S(1)}, u32[]{:S(2)}, u32[]{:S(2)}) async-start(bf16[16,2,4096]{2,1,0:T(2,128)(2,1)} %reshape.313), calls=%async_computation | async-start | bytes 524288 | tf_op jit(solution)/shard_map/all_to_all | solution.py:177
  29.5 2.2 %reshape.312 = bf16[128,1,1,1024]{3,2,1,0:T(2,128)(2,1)S(1)} reshape(bf16[16,2,4096]{2,1,0:T(2,128)(2,1)} %all-to-all-done.1) | data formatting | bytes 524288
  33.9 3.4 %all-to-all-done = bf16[16,2,4096]{2,1,0:T(2,128)(2,1)S(1)} async-done(((bf16[16,2,4096]{2,1,0:T(2,128)(2,1)}), bf16[16,2,4096]{2,1,0:T(2,128)(2,1)S(1)}, u32[]{:S(2)}, u32[]{:S(2)}) %all-to-all-start) | async-done | bytes 262176 | tf_op jit(solution)/shard_map/all_to_all | solution.py:177
  38.6 3.9 %convolution_convert_fusion = bf16[128,3072]{1,0:T(8,128)(2,1)S(1)} fusion(bf16[1024,3072]{1,0:T(8,128)(2,1)} %param.12, bf16[1,1,128,1024]{2,3,1,0:T(8,128)(2,1)} %copy.109), kind=kOutput, calls=%fused_computation.4 | convolution fusion | flops 805699584 | bytes 7340032 | tf_op jit(solution)/shard_map/dot_general | solution.py:184
  44.7 2.5 %fusion.94 = (f32[8,8,16]{2,1,0:T(8,128)S(1)}, f32[8,8,16,16]{2,3,1,0:T(8,128)}) fusion(pred[16,16]{0,1:T(8,128)(4,1)S(1)} %iota_compare_fusion.1, bf16[1,16,8,1,8,128]{5,2,4,3,1,0:T(8,128)(2,1)S(1)} %get-tuple-element.43, bf16[1,16,8,1,8,128]{5,2,4,3,1,0:T(8,128)(2,1)} %get-tuple-element.42), kind=kOutput, calls=%fused_computation.149 | convolution fusion | flops 4259855 | bytes 594176 | tf_op jit(solution)/shard_map/sub | solution.py:28
  48.6 2.9 %fusion.32 = bf16[1,16,8,1,8,128]{5,1,4,2,3,0:T(8,128)(2,1)} fusion(f32[8,8,16,16]{2,3,1,0:T(8,128)} %convolution_bitcast_fusion, bf16[1,16,8,1,8,128]{5,2,4,3,1,0:T(8,128)(2,1)} %get-tuple-element.42, f32[8,8,16,16]{2,3,1,0:T(8,128)} %get-tuple-element.51, f32[8,8,16]{2,1,0:T(8,128)S(1)} %get-tuple-element.50), kind=kOutput, calls=%fused_computation.54 | convolution fusion | flops 4441103 | bytes 659456 | tf_op jit(solution)/shard_map/bchlm,blche->bmche/dot_general | solution.py:57
  51.4 2.7 %fusion.28 = bf16[1,16,8,1,8,128]{5,1,4,2,3,0:T(8,128)(2,1)} fusion(f32[8,8,16,16]{2,3,1,0:T(8,128)} %convolution_bitcast_fusion, bf16[1,16,8,1,8,128]{5,2,4,3,1,0:T(8,128)(2,1)S(1)} %copy-done.18, f32[8,8,16,16]{2,3,1,0:T(8,128)} %get-tuple-element.51, f32[8,8,16]{2,1,0:T(8,128)S(1)} %get-tuple-element.50), kind=kOutput, calls=%fused_computation.50 | convolution fusion | flops 4441103 | bytes 659456 | tf_op jit(solution)/shard_map/bchlm,bmche->blche/dot_general | solution.py:51
  60.1 4.2 %all-to-all-start.3 = ((bf16[1,16,8,1024]{3,2,0,1:T(8,128)(2,1)}), bf16[1,16,8,1024]{3,2,0,1:T(8,128)(2,1)}, u32[]{:S(2)}, u32[]{:S(2)}) async-start(bf16[1,16,8,1024]{3,2,0,1:T(8,128)(2,1)} %bitcast.196), calls=%async_computation.3 | async-start | bytes 524288 | tf_op jit(solution)/shard_map/all_to_all | solution.py:194
  64.8 5.7 %fusion.30 = bf16[1,16,8,1024]{3,2,0,1:T(8,128)(2,1)} fusion(bf16[128,3072]{1,0:T(8,128)(2,1)S(1)} %reshape_reshape.7, bf16[1024,3072]{1,0:T(8,128)(2,1)} %param.12), kind=kOutput, calls=%fused_computation.52 | convolution fusion | flops 805437440 | bytes 7340032 | tf_op jit(solution)/shard_map/dot_general | solution.py:209
  70.4 1.9 %pad_maximum_fusion.1 = bf16[256,2,2,2,2,2,32]{0,6,5,4,3,2,1:T(8,128)(2,1)} fusion(bf16[128,2,2,2,2,2,32]{0,6,5,4,3,2,1:T(8,128)(2,1)} %bitcast.7, bf16[128,2,2,2,2,2,32]{0,6,5,4,3,2,1:T(8,128)(2,1)} %bitcast.5), kind=kLoop, calls=%fused_computation.77 | loop fusion | flops 1048576 | bytes 1048576 | tf_op jit(solution)/shard_map/concatenate | solution.py:226
  72.4 2.0 %all-to-all-done.3 = bf16[1,16,8,1024]{3,2,0,1:T(8,128)(2,1)} async-done(((bf16[1,16,8,1024]{3,2,0,1:T(8,128)(2,1)}), bf16[1,16,8,1024]{3,2,0,1:T(8,128)(2,1)}, u32[]{:S(2)}, u32[]{:S(2)}) %all-to-all-start.3) | async-done | bytes 262176 | tf_op jit(solution)/shard_map/all_to_all | solution.py:194
  74.4 4.4 %all-to-all-start.2 = ((bf16[1,16,8,1024]{3,2,0,1:T(8,128)(2,1)}), bf16[1,16,8,1024]{3,2,0,1:T(8,128)(2,1)}, u32[]{:S(2)}, u32[]{:S(2)}) async-start(bf16[1,16,8,1024]{3,2,0,1:T(8,128)(2,1)} %fusion.30), calls=%async_computation.2 | async-start | bytes 524288 | tf_op jit(solution)/shard_map/all_to_all | solution.py:230
  80.1 4.8 %fusion.5 = f32[512,3072]{1,0:T(8,128)} fusion(bf16[128,3072]{1,0:T(8,128)(2,1)} %collective-permute-done.1, bf16[128,3072]{1,0:T(8,128)(2,1)S(1)} %reshape_reshape.7, bf16[256,1024]{0,1:T(8,128)(2,1)S(1)} %bitcast.194, s32[]{:T(128)S(6)} %select_n.182), kind=kOutput, calls=%fused_computation.12 | convolution fusion | flops 808452096 | bytes 8126468 | tf_op jit(solution)/shard_map/dot_general | solution.py:225
  84.9 3.7 %all-to-all-done.2 = bf16[1,16,8,1024]{3,2,0,1:T(8,128)(2,1)} async-done(((bf16[1,16,8,1024]{3,2,0,1:T(8,128)(2,1)}), bf16[1,16,8,1024]{3,2,0,1:T(8,128)(2,1)}, u32[]{:S(2)}, u32[]{:S(2)}) %all-to-all-start.2) | async-done | bytes 262176 | tf_op jit(solution)/shard_map/all_to_all | solution.py:230
  91.5 3.2 %fusion.4 = bf16[2,2,2,32,3072]{4,3,2,1,0:T(8,128)(2,1)} fusion(f32[2,2,2,2,32,3072]{5,4,3,2,1,0:T(8,128)} %bitcast.182, s32[]{:T(128)S(6)} %select_n.190), kind=kLoop, calls=%fused_computation.11 | loop fusion | bytes 3145732 | tf_op jit(solution)/shard_map/convert_element_type | solution.py:144
  100.6 2.0 %collective-permute-start.10 = (bf16[2,2,2,32,1025]{4,3,2,1,0:T(8,128)(2,1)}, bf16[2,2,2,32,1025]{4,3,2,1,0:T(8,128)(2,1)}, u32[]{:S(2)}, u32[]{:S(2)}) collective-permute-start(bf16[2,2,2,32,1025]{4,3,2,1,0:T(8,128)(2,1)} %fusion.44), channel_id=1, source_target_pairs={{0,2},{1,17},{2,0},{3,19},{4,6},{5,21},{6,4},{7,23},{8,10},{9,25},... | collective-permute-start | bytes 1574408 | tf_op jit(solution)/shard_map/ppermute | solution.py:147
  103.6 2.6 %convolution_convert_fusion.1 = bf16[8,128,128]{1,2,0:T(8,128)(2,1)} fusion(bf16[128,8,128]{0,2,1:T(8,128)(2,1)S(1)} %bitcast.200, f32[8,128,128]{1,2,0:T(8,128)} %fusion.66, f32[8,128,128]{1,2,0:T(8,128)} %get-tuple-element.47, f32[8,128]{1,0:T(8,128)S(1)} %get-tuple-element.46), kind=kOutput, calls=%fused_computation.35 | convolution fusion | flops 34604160 | bytes 1576960 | tf_op jit(solution)/shard_map/ghlm,gmhe->glhe/dot_general | solution.py:51
  106.2 2.6 %convolution_convert_fusion.6 = bf16[8,128,128]{1,2,0:T(8,128)(2,1)} fusion(bf16[128,8,128]{0,2,1:T(8,128)(2,1)S(1)} %bitcast.198, f32[8,128,128]{1,2,0:T(8,128)} %fusion.66, f32[8,128,128]{1,2,0:T(8,128)} %get-tuple-element.47, f32[8,128]{1,0:T(8,128)S(1)} %get-tuple-element.46), kind=kOutput, calls=%fused_computation.40 | convolution fusion | flops 34604160 | bytes 1576960 | tf_op jit(solution)/shard_map/ghlm,glhe->gmhe/dot_general | solution.py:57
  108.9 14.6 %collective-permute-done.10 = bf16[2,2,2,32,1025]{4,3,2,1,0:T(8,128)(2,1)} collective-permute-done((bf16[2,2,2,32,1025]{4,3,2,1,0:T(8,128)(2,1)}, bf16[2,2,2,32,1025]{4,3,2,1,0:T(8,128)(2,1)}, u32[]{:S(2)}, u32[]{:S(2)}) %collective-permute-start.10) | collective-permute-done | bytes 524832 | tf_op jit(solution)/shard_map/ppermute | solution.py:147
  127.3 2.8 %bitcast_add_fusion = f32[2,2,2,32,3072]{4,3,2,1,0:T(8,128)S(1)} fusion(bf16[2,2,2,32,3072]{4,3,2,1,0:T(8,128)(2,1)} %collective-permute-done.2, f32[2,2,2,2,32,3072]{5,4,3,2,1,0:T(8,128)} %bitcast.183, s32[]{:T(128)S(6)} %select_n.189), kind=kLoop, calls=%fused_computation.7 | loop fusion | flops 1572864 | bytes 7864324 | tf_op jit(solution)/shard_map/add | solution.py:148
  133.3 2.2 %convolution_convert_fusion.5 = bf16[8,128,128]{2,1,0:T(8,128)(2,1)} fusion(bf16[128,8,128]{0,2,1:T(8,128)(2,1)S(1)} %bitcast.204, f32[8,128]{1,0:T(8,128)S(1)} %get-tuple-element.46, f32[8,128,128]{1,2,0:T(8,128)} %copy-done.3), kind=kOutput, calls=%fused_computation.39 | convolution fusion | flops 34079872 | bytes 1052672 | tf_op jit(solution)/shard_map/ghlm,glhe->gmhe/dot_general | solution.py:64
  135.5 1.8 %copy.139 = bf16[1,1,128,1024]{3,2,1,0:T(8,128)(2,1)} copy(bf16[1,1,128,1024]{2,3,1,0:T(8,128)(2,1)} %bitcast.207) | data formatting | bytes 524288
  139.1 1.8 %copy.140 = bf16[1,1,128,1024]{3,2,1,0:T(8,128)(2,1)} copy(bf16[1,1,128,1024]{2,3,1,0:T(8,128)(2,1)} %bitcast.208) | data formatting | bytes 524288
  142.2 2.8 %collective-permute-done.3 = bf16[2,2,32,3072]{3,2,1,0:T(8,128)(2,1)} collective-permute-done((bf16[2,2,32,3072]{3,2,1,0:T(8,128)(2,1)}, bf16[2,2,32,3072]{3,2,1,0:T(8,128)(2,1)}, u32[]{:S(2)}, u32[]{:S(2)}) %collective-permute-start.3) | collective-permute-done | bytes 786464 | tf_op jit(solution)/shard_map/ppermute | solution.py:147
  145.1 1.8 %bitcast_add_fusion.1 = f32[2,2,32,3072]{3,2,1,0:T(8,128)S(1)} fusion(bf16[2,2,32,3072]{3,2,1,0:T(8,128)(2,1)} %collective-permute-done.3, f32[2,2,2,32,3072]{4,3,2,1,0:T(8,128)} %copy-done.2, s32[]{:T(128)S(6)} %select_n.194), kind=kLoop, calls=%fused_computation.16 | loop fusion | flops 786432 | bytes 3932164 | tf_op jit(solution)/shard_map/add | solution.py:148
  148.7 7.4 %collective-permute-done.4 = bf16[2,32,3072]{2,1,0:T(8,128)(2,1)S(1)} collective-permute-done((bf16[2,32,3072]{2,1,0:T(8,128)(2,1)S(1)}, bf16[2,32,3072]{2,1,0:T(8,128)(2,1)S(1)}, u32[]{:S(2)}, u32[]{:S(2)}) %collective-permute-start.4) | collective-permute-done | bytes 393248 | tf_op jit(solution)/shard_map/ppermute | solution.py:147
  156.6 7.4 %collective-permute-done.5 = bf16[32,3072]{1,0:T(8,128)(2,1)S(1)} collective-permute-done((bf16[32,3072]{1,0:T(8,128)(2,1)S(1)}, bf16[32,3072]{1,0:T(8,128)(2,1)S(1)}, u32[]{:S(2)}, u32[]{:S(2)}) %collective-permute-start.5) | collective-permute-done | bytes 196640 | tf_op jit(solution)/shard_map/ppermute | solution.py:147
  166.4 3.4 %collective-permute-done.6 = bf16[32,3072]{1,0:T(8,128)(2,1)S(1)} collective-permute-done((bf16[32,3072]{1,0:T(8,128)(2,1)S(1)}, bf16[32,3072]{1,0:T(8,128)(2,1)S(1)}, u32[]{:S(2)}, u32[]{:S(2)}) %collective-permute-start.6) | collective-permute-done | bytes 196640 | tf_op jit(solution)/shard_map/ppermute | solution.py:152
  (130 shorter events, 51.7 us)
Async XLA Ops:
  0.6 15.1 %copy-start = (bf16[1024,1024]{1,0:T(8,128)(2,1)S(1)}, bf16[1024,1024]{1,0:T(8,128)(2,1)}, u32[]{:S(2)}) copy-start(bf16[1024,1024]{1,0:T(8,128)(2,1)} %param.10) | copy-start | bytes 6291460
  0.6 12.6 %copy-start.14 = (bf16[1,1,128,1024]{3,2,1,0:T(8,128)(2,1)S(1)}, bf16[1,1,128,1024]{3,2,1,0:T(8,128)(2,1)}, u32[]{:S(2)}) copy-start(bf16[1,1,128,1024]{3,2,1,0:T(8,128)(2,1)} %param.7) | copy-start | bytes 786436
  0.7 12.7 %copy-start.15 = (bf16[1,1,128,1024]{3,2,1,0:T(8,128)(2,1)S(1)}, bf16[1,1,128,1024]{3,2,1,0:T(8,128)(2,1)}, u32[]{:S(2)}) copy-start(bf16[1,1,128,1024]{3,2,1,0:T(8,128)(2,1)} %param.8) | copy-start | bytes 786436
  4.8 8.7 %copy-start.16 = (bf16[1,1,128,1024]{3,2,1,0:T(8,128)(2,1)S(1)}, bf16[1,1,128,1024]{3,2,1,0:T(8,128)(2,1)}, u32[]{:S(2)}) copy-start(bf16[1,1,128,1024]{3,2,1,0:T(8,128)(2,1)} %param.9) | copy-start | bytes 786436
  5.7 17.5 %all-to-all-start.1 = ((bf16[16,2,4096]{2,1,0:T(2,128)(2,1)}), bf16[16,2,4096]{2,1,0:T(2,128)(2,1)}, u32[]{:S(2)}, u32[]{:S(2)}) async-start(bf16[16,2,4096]{2,1,0:T(2,128)(2,1)} %reshape.311), calls=%async_computation.1 | async-start | bytes 524288 | tf_op jit(solution)/shard_map/all_to_all | solution.py:201
  15.3 12.1 %collective-permute-start.7 = (bf16[128,1024]{0,1:T(8,128)(2,1)S(1)}, bf16[128,1024]{0,1:T(8,128)(2,1)}, u32[]{:S(2)}, u32[]{:S(2)}) collective-permute-start(bf16[128,1024]{0,1:T(8,128)(2,1)S(1)} %bitcast.187), channel_id=1, source_target_pairs={{0,1},{1,0},{2,3},{3,2},{4,5},{5,4},{6,7},{7,6},{8,9},{9,8},{10,11... | collective-permute-start | bytes 786440 | tf_op jit(solution)/shard_map/ppermute | solution.py:245
  23.3 14.0 %all-to-all-start = ((bf16[16,2,4096]{2,1,0:T(2,128)(2,1)}), bf16[16,2,4096]{2,1,0:T(2,128)(2,1)S(1)}, u32[]{:S(2)}, u32[]{:S(2)}) async-start(bf16[16,2,4096]{2,1,0:T(2,128)(2,1)} %reshape.313), calls=%async_computation | async-start | bytes 524288 | tf_op jit(solution)/shard_map/all_to_all | solution.py:177
  38.6 4.7 %copy-start.13 = (bf16[16,8,8,128]{3,2,1,0:T(8,128)(2,1)S(1)}, bf16[16,8,8,128]{3,2,1,0:T(8,128)(2,1)}, u32[]{:S(2)}) copy-start(bf16[16,8,8,128]{3,2,1,0:T(8,128)(2,1)} %copy.182) | copy-start | bytes 786436
  43.3 3.9 %copy-start.17 = (bf16[1,16,8,1,8,128]{5,2,4,3,1,0:T(8,128)(2,1)}, bf16[1,16,8,1,8,128]{5,2,4,3,1,0:T(8,128)(2,1)S(1)}, u32[]{:S(2)}) copy-start(bf16[1,16,8,1,8,128]{5,2,4,3,1,0:T(8,128)(2,1)S(1)} %get-tuple-element.43) | copy-start | bytes 786436
  48.6 2.9 %copy-start.18 = (bf16[1,16,8,1,8,128]{5,2,4,3,1,0:T(8,128)(2,1)S(1)}, bf16[1,16,8,1,8,128]{5,2,4,3,1,0:T(8,128)(2,1)}, u32[]{:S(2)}) copy-start(bf16[1,16,8,1,8,128]{5,2,4,3,1,0:T(8,128)(2,1)} %copy-done.17) | copy-start | bytes 786436
  55.5 15.0 %collective-permute-start = (bf16[128,1024]{0,1:T(8,128)(2,1)}, bf16[128,1024]{0,1:T(8,128)(2,1)}, u32[]{:S(2)}, u32[]{:S(2)}) collective-permute-start(bf16[128,1024]{0,1:T(8,128)(2,1)} %bitcast.6), channel_id=1, source_target_pairs={{0,1},{1,0},{2,3},{3,2},{4,5},{5,4},{6,7},{7,6},{8,9},{9,8},{10,11... | collective-permute-start | bytes 786440 | tf_op jit(solution)/shard_map/ppermute | solution.py:224
  60.1 14.3 %all-to-all-start.3 = ((bf16[1,16,8,1024]{3,2,0,1:T(8,128)(2,1)}), bf16[1,16,8,1024]{3,2,0,1:T(8,128)(2,1)}, u32[]{:S(2)}, u32[]{:S(2)}) async-start(bf16[1,16,8,1024]{3,2,0,1:T(8,128)(2,1)} %bitcast.196), calls=%async_computation.3 | async-start | bytes 524288 | tf_op jit(solution)/shard_map/all_to_all | solution.py:194
  64.3 15.8 %collective-permute-start.1 = (bf16[128,3072]{1,0:T(8,128)(2,1)S(1)}, bf16[128,3072]{1,0:T(8,128)(2,1)}, u32[]{:S(2)}, u32[]{:S(2)}) collective-permute-start(bf16[128,3072]{1,0:T(8,128)(2,1)S(1)} %reshape_reshape.7), channel_id=1, source_target_pairs={{0,1},{1,0},{2,3},{3,2},{4,5},{5,4},{6,7},{7,6},{8,9},{9,8},{10,11... | collective-permute-start | bytes 2359304 | tf_op jit(solution)/shard_map/ppermute | solution.py:224
  74.4 14.2 %all-to-all-start.2 = ((bf16[1,16,8,1024]{3,2,0,1:T(8,128)(2,1)}), bf16[1,16,8,1024]{3,2,0,1:T(8,128)(2,1)}, u32[]{:S(2)}, u32[]{:S(2)}) async-start(bf16[1,16,8,1024]{3,2,0,1:T(8,128)(2,1)} %fusion.30), calls=%async_computation.2 | async-start | bytes 524288 | tf_op jit(solution)/shard_map/all_to_all | solution.py:230
  89.8 6.7 %collective-permute-start.9 = (f32[1024]{0:T(1024)S(1)}, f32[1024]{0:T(1024)S(1)}, u32[]{:S(2)}, u32[]{:S(2)}) collective-permute-start(f32[1024]{0:T(1024)S(1)} %get-tuple-element.39), channel_id=1, source_target_pairs={{0,1},{1,0},{2,3},{3,2},{4,5},{5,4},{6,7},{7,6},{8,9},{9,8},{10,11... | collective-permute-start | bytes 12296 | tf_op jit(solution)/shard_map/ppermute | solution.py:245
  91.0 6.0 %collective-permute-start.8 = (bf16[128,1024]{1,0:T(8,128)(2,1)S(1)}, bf16[128,1024]{1,0:T(8,128)(2,1)}, u32[]{:S(2)}, u32[]{:S(2)}) collective-permute-start(bf16[128,1024]{1,0:T(8,128)(2,1)S(1)} %fusion.46), channel_id=1, source_target_pairs={{0,1},{1,0},{2,3},{3,2},{4,5},{5,4},{6,7},{7,6},{8,9},{9,8},{10,11... | collective-permute-start | bytes 786440 | tf_op jit(solution)/shard_map/ppermute | solution.py:245
  94.8 2.2 %copy-start.4 = (bf16[256,2,2,2,2,2,32]{0,6,5,4,3,2,1:T(8,128)(2,1)S(1)}, bf16[256,2,2,2,2,2,32]{0,6,5,4,3,2,1:T(8,128)(2,1)}, u32[]{:S(2)}) copy-start(bf16[256,2,2,2,2,2,32]{0,6,5,4,3,2,1:T(8,128)(2,1)} %copy.134) | copy-start | bytes 1572868
  96.4 30.8 %collective-permute-start.2 = (bf16[2,2,2,32,3072]{4,3,2,1,0:T(8,128)(2,1)}, bf16[2,2,2,32,3072]{4,3,2,1,0:T(8,128)(2,1)}, u32[]{:S(2)}, u32[]{:S(2)}) collective-permute-start(bf16[2,2,2,32,3072]{4,3,2,1,0:T(8,128)(2,1)} %fusion.4), channel_id=1, source_target_pairs={{0,2},{1,17},{2,0},{3,19},{4,6},{5,21},{6,4},{7,23},{8,10},{9,25},... | collective-permute-start | bytes 4718600 | tf_op jit(solution)/shard_map/ppermute | solution.py:147
  98.4 4.2 %copy-start.10 = (bf16[16,8,8,128]{3,2,1,0:T(8,128)(2,1)S(1)}, bf16[16,8,8,128]{3,2,1,0:T(8,128)(2,1)}, u32[]{:S(2)}) copy-start(bf16[16,8,8,128]{3,2,1,0:T(8,128)(2,1)} %copy-done.9) | copy-start | bytes 786436
  98.4 4.2 %copy-start.11 = (bf16[128,1024]{0,1:T(8,128)(2,1)S(1)}, bf16[128,1024]{0,1:T(8,128)(2,1)}, u32[]{:S(2)}) copy-start(bf16[128,1024]{0,1:T(8,128)(2,1)} %copy.152) | copy-start | bytes 786436
  98.4 5.2 %copy-start.8 = (bf16[1,1,128,1024]{2,3,1,0:T(8,128)(2,1)S(1)}, bf16[1,1,128,1024]{2,3,1,0:T(8,128)(2,1)}, u32[]{:S(2)}) copy-start(bf16[1,1,128,1024]{2,3,1,0:T(8,128)(2,1)} %copy-done.7) | copy-start | bytes 786436
  100.6 5.6 %copy-start.6 = (bf16[1,1,128,1024]{2,3,1,0:T(8,128)(2,1)S(1)}, bf16[1,1,128,1024]{2,3,1,0:T(8,128)(2,1)}, u32[]{:S(2)}) copy-start(bf16[1,1,128,1024]{2,3,1,0:T(8,128)(2,1)} %copy-done.5) | copy-start | bytes 786436
  100.6 22.9 %collective-permute-start.10 = (bf16[2,2,2,32,1025]{4,3,2,1,0:T(8,128)(2,1)}, bf16[2,2,2,32,1025]{4,3,2,1,0:T(8,128)(2,1)}, u32[]{:S(2)}, u32[]{:S(2)}) collective-permute-start(bf16[2,2,2,32,1025]{4,3,2,1,0:T(8,128)(2,1)} %fusion.44), channel_id=1, source_target_pairs={{0,2},{1,17},{2,0},{3,19},{4,6},{5,21},{6,4},{7,23},{8,10},{9,25},... | collective-permute-start | bytes 1574408 | tf_op jit(solution)/shard_map/ppermute | solution.py:147
  125.8 7.5 %copy-start.12 = (bf16[128,1024]{0,1:T(8,128)(2,1)S(1)}, bf16[128,1024]{0,1:T(8,128)(2,1)}, u32[]{:S(2)}) copy-start(bf16[128,1024]{0,1:T(8,128)(2,1)} %copy.152) | copy-start | bytes 786436
  125.8 15.1 %collective-permute-start.11 = (bf16[2,2,32,1025]{3,2,1,0:T(8,128)(2,1)}, bf16[2,2,32,1025]{3,2,1,0:T(8,128)(2,1)}, u32[]{:S(2)}, u32[]{:S(2)}) collective-permute-start(bf16[2,2,32,1025]{3,2,1,0:T(8,128)(2,1)} %fusion.57), channel_id=1, source_target_pairs={{0,16},{1,5},{2,18},{3,7},{4,20},{5,1},{6,22},{7,3},{8,24},{9,13},... | collective-permute-start | bytes 787208 | tf_op jit(solution)/shard_map/ppermute | solution.py:147
  132.8 12.3 %collective-permute-start.3 = (bf16[2,2,32,3072]{3,2,1,0:T(8,128)(2,1)}, bf16[2,2,32,3072]{3,2,1,0:T(8,128)(2,1)}, u32[]{:S(2)}, u32[]{:S(2)}) collective-permute-start(bf16[2,2,32,3072]{3,2,1,0:T(8,128)(2,1)} %fusion.41), channel_id=1, source_target_pairs={{0,16},{1,5},{2,18},{3,7},{4,20},{5,1},{6,22},{7,3},{8,24},{9,13},... | collective-permute-start | bytes 2359304 | tf_op jit(solution)/shard_map/ppermute | solution.py:147
  142.0 5.2 %collective-permute-start.12 = (bf16[2,32,1025]{2,1,0:T(8,128)(2,1)S(1)}, bf16[2,32,1025]{2,1,0:T(8,128)(2,1)S(1)}, u32[]{:S(2)}, u32[]{:S(2)}) collective-permute-start(bf16[2,32,1025]{2,1,0:T(8,128)(2,1)S(1)} %fusion.71), channel_id=1, source_target_pairs={{0,4},{1,3},{2,6},{3,1},{4,0},{5,7},{6,2},{7,5},{8,12},{9,11},{10,... | collective-permute-start | bytes 393608 | tf_op jit(solution)/shard_map/ppermute | solution.py:147
  146.9 9.2 %collective-permute-start.4 = (bf16[2,32,3072]{2,1,0:T(8,128)(2,1)S(1)}, bf16[2,32,3072]{2,1,0:T(8,128)(2,1)S(1)}, u32[]{:S(2)}, u32[]{:S(2)}) collective-permute-start(bf16[2,32,3072]{2,1,0:T(8,128)(2,1)S(1)} %fusion.54), channel_id=1, source_target_pairs={{0,4},{1,3},{2,6},{3,1},{4,0},{5,7},{6,2},{7,5},{8,12},{9,11},{10,... | collective-permute-start | bytes 1179656 | tf_op jit(solution)/shard_map/ppermute | solution.py:147
  147.3 9.0 %collective-permute-start.13 = (bf16[32,1025]{1,0:T(8,128)(2,1)S(1)}, bf16[32,1025]{1,0:T(8,128)(2,1)S(1)}, u32[]{:S(2)}, u32[]{:S(2)}) collective-permute-start(bf16[32,1025]{1,0:T(8,128)(2,1)S(1)} %fusion.77), channel_id=1, source_target_pairs={{0,8},{1,9},{2,10},{3,11},{4,12},{5,13},{6,14},{7,15},{8,0},{9,1},... | collective-permute-start | bytes 196808 | tf_op jit(solution)/shard_map/ppermute | solution.py:147
  156.2 7.8 %collective-permute-start.5 = (bf16[32,3072]{1,0:T(8,128)(2,1)S(1)}, bf16[32,3072]{1,0:T(8,128)(2,1)S(1)}, u32[]{:S(2)}, u32[]{:S(2)}) collective-permute-start(bf16[32,3072]{1,0:T(8,128)(2,1)S(1)} %fusion.70), channel_id=1, source_target_pairs={{0,8},{1,9},{2,10},{3,11},{4,12},{5,13},{6,14},{7,15},{8,0},{9,1},... | collective-permute-start | bytes 589832 | tf_op jit(solution)/shard_map/ppermute | solution.py:147
  156.3 8.7 %collective-permute-start.14 = (bf16[32,1025]{1,0:T(8,128)(2,1)S(1)}, bf16[32,1025]{1,0:T(8,128)(2,1)S(1)}, u32[]{:S(2)}, u32[]{:S(2)}) collective-permute-start(bf16[32,1025]{1,0:T(8,128)(2,1)S(1)} %fusion.72), channel_id=1, source_target_pairs={{0,16},{16,0},{1,17},{17,1},{2,18},{18,2},{3,19},{19,3},{4,20},{20... | collective-permute-start | bytes 196808 | tf_op jit(solution)/shard_map/ppermute | solution.py:152
  164.1 5.7 %collective-permute-start.6 = (bf16[32,3072]{1,0:T(8,128)(2,1)S(1)}, bf16[32,3072]{1,0:T(8,128)(2,1)S(1)}, u32[]{:S(2)}, u32[]{:S(2)}) collective-permute-start(bf16[32,3072]{1,0:T(8,128)(2,1)S(1)} %fusion.55), channel_id=1, source_target_pairs={{0,16},{16,0},{1,17},{17,1},{2,18},{18,2},{3,19},{19,3},{4,20},{20... | collective-permute-start | bytes 589832 | tf_op jit(solution)/shard_map/ppermute | solution.py:152
  (7 other events, 10.6 us)

commit v5 on v4

--- a/solution.py
+++ b/solution.py
@@ -174,13 +174,14 @@
     hidden = jnp.dot(flat_first, out_weight, preferred_element_type=jnp.float32)
     inverse = lax.rsqrt(jnp.mean(hidden * hidden, axis=-1, keepdims=True) + epsilon)
     normed = (hidden * inverse * norm_gain).astype(jnp.bfloat16)
-    normed_cols = lax.all_to_all(
-        normed.reshape(batches, local_rows, columns, model_width),
+    both_cols = lax.all_to_all(
+        jnp.concatenate([normed.reshape(batches, local_rows, columns, model_width), upstream], axis=3),
         "seq",
         split_axis=2,
         concat_axis=1,
         tiled=True,
     )
+    normed_cols = both_cols[..., :model_width]
     joint_flat = jnp.dot(
         normed_cols.reshape(-1, model_width), joint_weight, preferred_element_type=jnp.float32
     )
@@ -191,14 +192,7 @@
     pieces = joint_cols.reshape(batches, all_rows, col_share, 3, head_count, HEAD_DIM)
     query_cols, key_cols, value_cols = (pieces[:, :, :, 0], pieces[:, :, :, 1], pieces[:, :, :, 2])
     out_cols, probs_cols = attend(query_cols, key_cols, value_cols, "blche", "bchlm")
-    column_out = lax.all_to_all(
-        out_cols.reshape(batches, all_rows, col_share, feature),
-        "seq",
-        split_axis=1,
-        concat_axis=2,
-        tiled=True,
-    )
-    upstream_cols = lax.all_to_all(upstream, "seq", split_axis=2, concat_axis=1, tiled=True)
+    upstream_cols = both_cols[..., model_width:]
     upstream_cols = upstream_cols.reshape(batches, all_rows, col_share, head_count, HEAD_DIM)
     grads_cols = attend_back(
         query_cols, key_cols, value_cols, probs_cols, upstream_cols, "blche", "bchlm"
@@ -227,14 +221,21 @@
         jnp.concatenate([used_grads, grads_peer], axis=0),
         preferred_element_type=jnp.float32,
     )
-    grad_normed = lax.all_to_all(
-        grad_local.reshape(batches, all_rows, col_share, model_width),
+    both_rows = lax.all_to_all(
+        jnp.concatenate(
+            [
+                out_cols.reshape(batches, all_rows, col_share, feature),
+                grad_local.reshape(batches, all_rows, col_share, model_width),
+            ],
+            axis=3,
+        ),
         "seq",
         split_axis=1,
         concat_axis=2,
         tiled=True,
     )
-    grad_normed = grad_normed.reshape(-1, model_width)
+    column_out = both_rows[..., :feature]
+    grad_normed = both_rows[..., feature:].reshape(-1, model_width)
     joint_term, grad_normed = lax.optimization_barrier((joint_term, grad_normed))
     grad_float = grad_normed.astype(jnp.float32)
     gain_term = jnp.sum(grad_float * hidden * inverse, axis=0)

time: 174 us -> 200 us (1.15)
  local copies, waits for them, and re-layouts: 33.4 us -> 65.6 us
  waiting for transfers between devices: 46.7 us -> 30.6 us
  other arithmetic: 23.6 us -> 34.4 us
    concatenate x0 -> x5, local copies, waits for them, and re-layouts: none -> 16.7 us  [the longest x2 7.78 us: on_device(): jnp.concatenate([flat_first, first_peer], axis=0)]
    all_to_all x4 -> x2, waiting for transfers between devices: 10.9 us -> 0.01 us  [the longest x1 0.01 us: on_device(): lax.all_to_all(jnp.concatenate([normed.reshape(batches, local_rows, colum...]
    select_n x4, local copies, waits for them, and re-layouts: 0.98 us -> 11.4 us  [by_split_order(): return jnp.where(core_odd, arrange(odd), arrange(even))]
    all_to_all x4 -> x2, starting transfers between devices: 20 us -> 13 us  [the longest x1 7.16 us: on_device(): lax.all_to_all(jnp.concatenate([normed.reshape(batches, local_rows, colum...]
    select_n x3, other arithmetic: 2.49 us -> 9.47 us  [by_split_order(): return jnp.where(core_odd, arrange(odd), arrange(even))]
    ppermute x8, starting transfers between devices: 6.03 us -> 12.4 us  [reduce_rows(): got = lax.ppermute(given, ('dp', 'seq'), perm)]
    ppermute x8, waiting for transfers between devices: 32.4 us -> 27.6 us  [reduce_rows(): got = lax.ppermute(given, ('dp', 'seq'), perm)]
    concatenate x0 -> x3, other arithmetic: none -> 2.93 us  [the longest x1 1.88 us: on_device(): jnp.concatenate([out_cols.reshape(batches, all_rows, col_share, feature),...]
  transfers between devices with their start and end apart: 19 -> 17, of which waited for: 9 -> 5; matrix products, arithmetic and copies ran while one was open for 38% -> 52% of each run, Pallas kernels for 0% -> 0%
where the time goes in v5:
time: 200 us; the launch traced here: 198 us
  local copies, waits for them, and re-layouts  65.6 us (33%)
  matrix products  37.6 us (19%)
  other arithmetic  34.4 us (17%)
  waiting for transfers between devices  30.6 us (15%)
  starting transfers between devices  28.6 us (14%)
    ppermute x8, waiting for transfers between devices, reduce_rows(): got = lax.ppermute(given, ('dp', 'seq'), perm)  27.6 us
    unnamed x45, local copies, waits for them, and re-layouts  17.7 us
    ppermute x8, starting transfers between devices, reduce_rows(): got = lax.ppermute(given, ('dp', 'seq'), perm)  12.4 us
    select_n x4, local copies, waits for them, and re-layouts, by_split_order(): return jnp.where(core_odd, arrange(odd), arrange(even))  11.4 us
    select_n x3, other arithmetic, by_split_order(): return jnp.where(core_odd, arrange(odd), arrange(even))  9.47 us
    concatenate x2, local copies, waits for them, and re-layouts, on_device(): jnp.concatenate([flat_first, first_peer], axis=0)  7.78 us
    add x6, other arithmetic, reduce_rows(): accs = tuple((k + g.astype(jnp.float32) for k, g in zip(kept, got)))  7.28 us
    all_to_all x1, starting transfers between devices, on_device(): lax.all_to_all(jnp.concatenate([normed.reshape(batches, local_rows, colum...  7.16 us
  transfers between devices with their start and end apart: 17, of which 5 were waited for; matrix products, arithmetic and copies ran while one was open for 52% of the time, Pallas kernels for 0%

profile of v5, /device:TPU:0, one launch (start us, length us, event | category | flops | bytes accessed | tf_op | source)
XLA Modules:
  0.0 198.1 jit_solution(16974452908018079554)
XLA Ops:
  11.2 4.8 %reduce.18 = bf16[128,2048]{1,0:T(8,128)(2,1)S(1)} reduce(bf16[128,1,1,2048]{3,2,1,0:T(2,128)(2,1)} %bitcast.187, bf16[]{:T(256)} %broadcast.112), dimensions={1,2}, to_apply=%bitcast.179.reduce_sub_computation | reduce | bytes 1048578
  17.3 7.2 %all-to-all-start = ((bf16[16,2,8192]{2,1,0:T(2,128)(2,1)}), bf16[16,2,8192]{2,1,0:T(2,128)(2,1)}, u32[]{:S(2)}, u32[]{:S(2)}) async-start(bf16[16,2,8192]{2,1,0:T(2,128)(2,1)} %reshape.301), calls=%async_computation | async-start | bytes 1048576 | tf_op jit(solution)/shard_map/all_to_all | solution.py:177
  25.7 3.9 %copy.239 = bf16[256,2,2,2,2,2,32]{6,5,4,3,2,1,0:T(2,128)(2,1)} copy(bf16[256,2,2,2,2,2,32]{0,6,5,4,3,2,1:T(8,128)(2,1)S(1)} %pad_maximum_fusion.3) | data formatting | bytes 1048576 | tf_op jit(solution)/shard_map/concatenate | solution.py:248
  29.6 3.9 %copy.238 = bf16[256,2,2,2,2,2,32]{6,2,4,5,3,1,0:T(2,128)(2,1)} copy(bf16[256,2,2,2,2,2,32]{0,6,5,4,3,2,1:T(8,128)(2,1)S(1)} %pad_maximum_fusion.3) | data formatting | bytes 1048576 | tf_op jit(solution)/shard_map/concatenate | solution.py:248
  33.5 5.7 %broadcast_select_fusion = bf16[256,2,2,2,2,2,32]{6,3,1,2,4,5,0:T(2,128)(2,1)} fusion(pred[]{:T(512)S(6)} %eq.26, bf16[256,2,2,2,2,2,32]{6,5,4,3,2,1,0:T(2,128)(2,1)} %copy.239, bf16[256,2,2,2,2,2,32]{6,2,4,5,3,1,0:T(2,128)(2,1)} %copy.238), kind=kLoop, calls=%fused_computation.4 | loop fusion | flops 262144 | bytes 1572865 | tf_op jit(solution)/shard_map/jit(_where)/select_n | solution.py:109
  39.1 5.7 %copy.240 = bf16[256,2,2,2,2,2,32]{0,6,5,4,3,2,1:T(8,128)(2,1)} copy(bf16[256,2,2,2,2,2,32]{6,3,1,2,4,5,0:T(2,128)(2,1)} %broadcast_select_fusion) | data formatting | bytes 1048576 | tf_op jit(solution)/shard_map/jit(_where)/select_n | solution.py:109
  44.8 3.5 %reshape.302 = bf16[128,1,1,2048]{3,2,1,0:T(2,128)(2,1)} reshape(bf16[16,2,8192]{2,1,0:T(2,128)(2,1)} %all-to-all-done) | data formatting | bytes 1048576
  50.7 3.8 %convolution_convert_fusion = bf16[128,3072]{1,0:T(8,128)(2,1)S(1)} fusion(bf16[1024,3072]{1,0:T(8,128)(2,1)} %param.12, bf16[1,16,8,2048]{3,2,1,0:T(8,128)(2,1)S(1)} %bitcast.185), kind=kOutput, calls=%fused_computation.6 | convolution fusion | flops 805699584 | bytes 7340032 | tf_op jit(solution)/shard_map/dot_general | solution.py:185
  56.5 2.6 %fusion.97 = (f32[8,8,16]{2,1,0:T(8,128)S(1)}, f32[8,8,16,16]{2,3,1,0:T(8,128)}) fusion(pred[16,16]{0,1:T(8,128)(4,1)S(1)} %iota_compare_fusion.1, bf16[1,16,8,1,8,128]{5,2,4,3,1,0:T(8,128)(2,1)} %get-tuple-element.64, bf16[1,16,8,1,8,128]{5,2,4,3,1,0:T(8,128)(2,1)} %get-tuple-element.63), kind=kOutput, calls=%fused_computation.157 | convolution fusion | flops 4259855 | bytes 594176 | tf_op jit(solution)/shard_map/sub | solution.py:28
  59.2 2.1 %fusion.32 = bf16[1,16,8,1,8,128]{5,1,4,2,3,0:T(8,128)(2,1)} fusion(bf16[16,8,8,128]{3,2,1,0:T(8,128)(2,1)S(1)} %copy.289, f32[8,8,16,16]{2,3,1,0:T(8,128)} %get-tuple-element.77, f32[8,8,16]{2,1,0:T(8,128)S(1)} %get-tuple-element.76), kind=kOutput, calls=%fused_computation.56 | convolution fusion | flops 4358144 | bytes 593920 | tf_op jit(solution)/shard_map/bchlm,blche->bmche/dot_general | solution.py:64
  61.2 2.5 %fusion.31 = bf16[1,16,8,1,8,128]{5,1,4,2,3,0:T(8,128)(2,1)} fusion(f32[8,8,16,16]{2,3,1,0:T(8,128)S(1)} %fusion.64, bf16[1,16,8,1,8,128]{5,2,4,3,1,0:T(8,128)(2,1)} %get-tuple-element.63, f32[8,8,16,16]{2,3,1,0:T(8,128)} %get-tuple-element.77, f32[8,8,16]{2,1,0:T(8,128)S(1)} %get-tuple-element.76), kind=kOutput, calls=%fused_computation.55 | convolution fusion | flops 4441103 | bytes 659456 | tf_op jit(solution)/shard_map/bchlm,blche->bmche/dot_general | solution.py:57
  63.8 2.4 %fusion.28 = bf16[1,16,8,1,8,128]{5,1,4,2,3,0:T(8,128)(2,1)} fusion(f32[8,8,16,16]{2,3,1,0:T(8,128)S(1)} %fusion.64, bf16[1,16,8,1,8,128]{5,2,4,3,1,0:T(8,128)(2,1)S(1)} %copy-done.15, f32[8,8,16,16]{2,3,1,0:T(8,128)} %get-tuple-element.77, f32[8,8,16]{2,1,0:T(8,128)S(1)} %get-tuple-element.76), kind=kOutput, calls=%fused_computation.52 | convolution fusion | flops 4441103 | bytes 659456 | tf_op jit(solution)/shard_map/bchlm,bmche->blche/dot_general | solution.py:51
  70.1 5.8 %fusion.30 = bf16[1,16,8,1024]{3,2,1,0:T(8,128)(2,1)} fusion(bf16[128,3072]{1,0:T(8,128)(2,1)S(1)} %reshape_reshape.7, bf16[1024,3072]{1,0:T(8,128)(2,1)} %param.12), kind=kOutput, calls=%fused_computation.54 | convolution fusion | flops 805437440 | bytes 7340032 | tf_op jit(solution)/shard_map/dot_general | solution.py:203
  81.0 5.9 %all-to-all-start.1 = ((bf16[1,16,8,2048]{3,2,0,1:T(8,128)(2,1)}), bf16[1,16,8,2048]{3,2,0,1:T(8,128)(2,1)}, u32[]{:S(2)}, u32[]{:S(2)}) async-start(bf16[1,16,8,2048]{3,2,0,1:T(8,128)(2,1)} %maximum_bitcast_fusion), calls=%async_computation.1 | async-start | bytes 1048576 | tf_op jit(solution)/shard_map/all_to_all | solution.py:224
  86.8 3.7 %concatenate.49 = bf16[128,2,2,2,2,2,32]{6,5,4,3,2,1,0:T(2,128)(2,1)} reshape(bf16[1,16,8,1024]{3,2,1,0:T(8,128)(2,1)} %get-tuple-element.67) | data formatting | bytes 524288 | tf_op jit(solution)/shard_map/concatenate | solution.py:220
  92.3 3.5 %copy.217 = bf16[128,2,2,2,2,2,32]{6,5,4,3,2,1,0:T(2,128)(2,1)} copy(bf16[128,2,2,2,2,2,32]{0,6,5,4,3,2,1:T(8,128)(2,1)} %bitcast.191) | data formatting | bytes 524288 | tf_op jit(solution)/shard_map/concatenate | solution.py:220
  95.7 4.8 %pad_maximum_fusion = bf16[256,2,2,2,2,2,32]{6,5,4,3,2,1,0:T(2,128)(2,1)S(1)} fusion(bf16[128,2,2,2,2,2,32]{6,5,4,3,2,1,0:T(2,128)(2,1)} %copy.217, bf16[128,2,2,2,2,2,32]{6,5,4,3,2,1,0:T(2,128)(2,1)} %concatenate.49), kind=kLoop, calls=%fused_computation.13 | loop fusion | flops 262144 | bytes 1048576 | tf_op jit(solution)/shard_map/concatenate | solution.py:220
  100.5 3.8 %broadcast_select_fusion.1 = bf16[256,2,2,2,2,2,32]{6,3,1,2,4,5,0:T(2,128)(2,1)} fusion(pred[]{:T(512)S(6)} %eq.26, bf16[256,2,2,2,2,2,32]{6,5,4,3,2,1,0:T(2,128)(2,1)S(1)} %pad_maximum_fusion), kind=kLoop, calls=%fused_computation.5 | loop fusion | flops 262144 | bytes 1048577 | tf_op jit(solution)/shard_map/jit(_where)/select_n | solution.py:109
  104.3 5.7 %copy.219 = bf16[256,2,2,2,2,2,32]{0,6,5,4,3,2,1:T(8,128)(2,1)} copy(bf16[256,2,2,2,2,2,32]{6,3,1,2,4,5,0:T(2,128)(2,1)} %broadcast_select_fusion.1) | data formatting | bytes 1048576 | tf_op jit(solution)/shard_map/jit(_where)/select_n | solution.py:109
  110.0 4.9 %fusion.5 = f32[512,3072]{1,0:T(8,128)} fusion(bf16[128,3072]{1,0:T(8,128)(2,1)} %collective-permute-done.1, bf16[128,3072]{1,0:T(8,128)(2,1)S(1)} %reshape_reshape.7, bf16[256,1024]{0,1:T(8,128)(2,1)} %bitcast.190, s32[]{:T(128)S(6)} %select_n.182), kind=kOutput, calls=%fused_computation.15 | convolution fusion | flops 808452096 | bytes 8126468 | tf_op jit(solution)/shard_map/dot_general | solution.py:219
  117.6 3.2 %fusion.4 = bf16[2,2,2,32,3072]{4,3,2,1,0:T(8,128)(2,1)} fusion(f32[2,2,2,2,32,3072]{5,4,3,2,1,0:T(8,128)} %bitcast.180, s32[]{:T(128)S(6)} %select_n.190), kind=kLoop, calls=%fused_computation.14 | loop fusion | bytes 3145732 | tf_op jit(solution)/shard_map/convert_element_type | solution.py:144
  129.7 2.6 %convolution_convert_fusion.1 = bf16[8,128,128]{1,2,0:T(8,128)(2,1)} fusion(bf16[128,8,128]{0,2,1:T(8,128)(2,1)S(1)} %bitcast.198, f32[8,128,128]{1,2,0:T(8,128)} %fusion.66, f32[8,128,128]{1,2,0:T(8,128)} %get-tuple-element.73, f32[8,128]{1,0:T(8,128)S(1)} %get-tuple-element.72), kind=kOutput, calls=%fused_computation.37 | convolution fusion | flops 34604160 | bytes 1576960 | tf_op jit(solution)/shard_map/ghlm,gmhe->glhe/dot_general | solution.py:51
  132.3 2.6 %convolution_convert_fusion.6 = bf16[8,128,128]{1,2,0:T(8,128)(2,1)} fusion(bf16[128,8,128]{0,2,1:T(8,128)(2,1)S(1)} %bitcast.196, f32[8,128,128]{1,2,0:T(8,128)} %fusion.66, f32[8,128,128]{1,2,0:T(8,128)} %get-tuple-element.73, f32[8,128]{1,0:T(8,128)S(1)} %get-tuple-element.72), kind=kOutput, calls=%fused_computation.42 | convolution fusion | flops 34604160 | bytes 1576960 | tf_op jit(solution)/shard_map/ghlm,glhe->gmhe/dot_general | solution.py:57
  134.9 14.7 %collective-permute-done.10 = bf16[2,2,2,32,1025]{4,3,2,1,0:T(8,128)(2,1)} collective-permute-done((bf16[2,2,2,32,1025]{4,3,2,1,0:T(8,128)(2,1)}, bf16[2,2,2,32,1025]{4,3,2,1,0:T(8,128)(2,1)}, u32[]{:S(2)}, u32[]{:S(2)}) %collective-permute-start.10) | collective-permute-done | bytes 524832 | tf_op jit(solution)/shard_map/ppermute | solution.py:147
  153.4 2.8 %bitcast_add_fusion = f32[2,2,2,32,3072]{4,3,2,1,0:T(8,128)S(1)} fusion(bf16[2,2,2,32,3072]{4,3,2,1,0:T(8,128)(2,1)} %collective-permute-done.2, f32[2,2,2,2,32,3072]{5,4,3,2,1,0:T(8,128)} %bitcast.181, s32[]{:T(128)S(6)} %select_n.189), kind=kLoop, calls=%fused_computation.9 | loop fusion | flops 1572864 | bytes 7864324 | tf_op jit(solution)/shard_map/add | solution.py:148
  159.4 2.2 %convolution_convert_fusion.5 = bf16[8,128,128]{2,1,0:T(8,128)(2,1)} fusion(bf16[128,8,128]{0,2,1:T(8,128)(2,1)S(1)} %bitcast.202, f32[8,128]{1,0:T(8,128)S(1)} %get-tuple-element.72, f32[8,128,128]{1,2,0:T(8,128)} %copy-done.3), kind=kOutput, calls=%fused_computation.41 | convolution fusion | flops 34079872 | bytes 1052672 | tf_op jit(solution)/shard_map/ghlm,glhe->gmhe/dot_general | solution.py:64
  168.1 1.9 collective-permute-start.12
  175.0 2.4 %collective-permute-start.13 = (bf16[32,1025]{1,0:T(8,128)(2,1)S(1)}, bf16[32,1025]{1,0:T(8,128)(2,1)S(1)}, u32[]{:S(2)}, u32[]{:S(2)}) collective-permute-start(bf16[32,1025]{1,0:T(8,128)(2,1)S(1)} %fusion.77), channel_id=1, source_target_pairs={{0,8},{1,9},{2,10},{3,11},{4,12},{5,13},{6,14},{7,15},{8,0},{9,1},... | collective-permute-start | bytes 196808 | tf_op jit(solution)/shard_map/ppermute | solution.py:147
  177.5 5.2 %collective-permute-done.4 = bf16[2,32,3072]{2,1,0:T(8,128)(2,1)S(1)} collective-permute-done((bf16[2,32,3072]{2,1,0:T(8,128)(2,1)S(1)}, bf16[2,32,3072]{2,1,0:T(8,128)(2,1)S(1)}, u32[]{:S(2)}, u32[]{:S(2)}) %collective-permute-start.4) | collective-permute-done | bytes 393248 | tf_op jit(solution)/shard_map/ppermute | solution.py:147
  182.8 2.0 %collective-permute-start.5 = (bf16[32,3072]{1,0:T(8,128)(2,1)S(1)}, bf16[32,3072]{1,0:T(8,128)(2,1)S(1)}, u32[]{:S(2)}, u32[]{:S(2)}) collective-permute-start(bf16[32,3072]{1,0:T(8,128)(2,1)S(1)} %fusion.70), channel_id=1, source_target_pairs={{0,8},{1,9},{2,10},{3,11},{4,12},{5,13},{6,14},{7,15},{8,0},{9,1},... | collective-permute-start | bytes 589832 | tf_op jit(solution)/shard_map/ppermute | solution.py:147
  184.9 6.6 %collective-permute-done.5 = bf16[32,3072]{1,0:T(8,128)(2,1)S(1)} collective-permute-done((bf16[32,3072]{1,0:T(8,128)(2,1)S(1)}, bf16[32,3072]{1,0:T(8,128)(2,1)S(1)}, u32[]{:S(2)}, u32[]{:S(2)}) %collective-permute-start.5) | collective-permute-done | bytes 196640 | tf_op jit(solution)/shard_map/ppermute | solution.py:147
  194.3 3.0 %collective-permute-done.6 = bf16[32,3072]{1,0:T(8,128)(2,1)S(1)} collective-permute-done((bf16[32,3072]{1,0:T(8,128)(2,1)S(1)}, bf16[32,3072]{1,0:T(8,128)(2,1)S(1)}, u32[]{:S(2)}, u32[]{:S(2)}) %collective-permute-start.6) | collective-permute-done | bytes 196640 | tf_op jit(solution)/shard_map/ppermute | solution.py:152
  (126 shorter events, 61.8 us)
Async XLA Ops:
  0.6 7.5 %copy-start = (bf16[1024,1024]{1,0:T(8,128)(2,1)S(1)}, bf16[1024,1024]{1,0:T(8,128)(2,1)}, u32[]{:S(2)}) copy-start(bf16[1024,1024]{1,0:T(8,128)(2,1)} %param.10) | copy-start | bytes 6291460
  1.9 5.6 %copy-start.5 = (bf16[1,1,128,1024]{2,3,1,0:T(8,128)(2,1)}, bf16[1,1,128,1024]{2,3,1,0:T(8,128)(2,1)S(1)}, u32[]{:S(2)}) copy-start(bf16[1,1,128,1024]{2,3,1,0:T(8,128)(2,1)S(1)} %copy.258) | copy-start | bytes 786436
  3.2 4.4 %copy-start.7 = (bf16[1,1,128,1024]{2,3,1,0:T(8,128)(2,1)}, bf16[1,1,128,1024]{2,3,1,0:T(8,128)(2,1)S(1)}, u32[]{:S(2)}) copy-start(bf16[1,1,128,1024]{2,3,1,0:T(8,128)(2,1)S(1)} %copy.257) | copy-start | bytes 786436
  5.3 2.4 %copy-start.3 = (f32[8,128,128]{1,2,0:T(8,128)}, f32[8,128,128]{1,2,0:T(8,128)S(1)}, u32[]{:S(2)}) copy-start(f32[8,128,128]{1,2,0:T(8,128)S(1)} %fusion.20) | copy-start | bytes 1572868
  6.3 2.4 %copy-start.16 = (f32[1024]{0:T(1024)S(1)}, f32[1024]{0:T(1024)}, u32[]{:S(2)}) copy-start(f32[1024]{0:T(1024)} %param.11) | copy-start | bytes 12292
  7.6 17.0 %collective-permute-start.7 = (bf16[128,1024]{0,1:T(8,128)(2,1)S(1)}, bf16[128,1024]{0,1:T(8,128)(2,1)}, u32[]{:S(2)}, u32[]{:S(2)}) collective-permute-start(bf16[128,1024]{0,1:T(8,128)(2,1)S(1)} %bitcast.192), channel_id=1, source_target_pairs={{0,1},{1,0},{2,3},{3,2},{4,5},{5,4},{6,7},{7,6},{8,9},{9,8},{10,11... | collective-permute-start | bytes 786440 | tf_op jit(solution)/shard_map/ppermute | solution.py:246
  17.3 27.5 %all-to-all-start = ((bf16[16,2,8192]{2,1,0:T(2,128)(2,1)}), bf16[16,2,8192]{2,1,0:T(2,128)(2,1)}, u32[]{:S(2)}, u32[]{:S(2)}) async-start(bf16[16,2,8192]{2,1,0:T(2,128)(2,1)} %reshape.301), calls=%async_computation | async-start | bytes 1048576 | tf_op jit(solution)/shard_map/all_to_all | solution.py:177
  61.2 2.5 %copy-start.15 = (bf16[1,16,8,1,8,128]{5,2,4,3,1,0:T(8,128)(2,1)S(1)}, bf16[1,16,8,1,8,128]{5,2,4,3,1,0:T(8,128)(2,1)}, u32[]{:S(2)}) copy-start(bf16[1,16,8,1,8,128]{5,2,4,3,1,0:T(8,128)(2,1)} %get-tuple-element.64) | copy-start | bytes 786436
  66.1 24.4 %collective-permute-start = (bf16[128,1024]{1,0:T(8,128)(2,1)}, bf16[128,1024]{1,0:T(8,128)(2,1)}, u32[]{:S(2)}, u32[]{:S(2)}) collective-permute-start(bf16[128,1024]{1,0:T(8,128)(2,1)} %get-tuple-element.68), channel_id=1, source_target_pairs={{0,1},{1,0},{2,3},{3,2},{4,5},{5,4},{6,7},{7,6},{8,9},{9,8},{10,11... | collective-permute-start | bytes 786440 | tf_op jit(solution)/shard_map/ppermute | solution.py:218
  70.0 5.8 %copy-start.13 = (bf16[1,16,8,1,8,128]{5,2,4,3,1,0:T(8,128)(2,1)S(1)}, bf16[1,16,8,1,8,128]{5,2,4,3,1,0:T(8,128)(2,1)}, u32[]{:S(2)}) copy-start(bf16[1,16,8,1,8,128]{5,2,4,3,1,0:T(8,128)(2,1)} %copy-done.12) | copy-start | bytes 786436
  70.0 5.8 %copy-start.17 = (f32[8,8,16,16]{2,3,1,0:T(8,128)S(1)}, f32[8,8,16,16]{2,3,1,0:T(8,128)}, u32[]{:S(2)}) copy-start(f32[8,8,16,16]{2,3,1,0:T(8,128)} %get-tuple-element.77) | copy-start | bytes 196612
  76.2 33.8 %collective-permute-start.1 = (bf16[128,3072]{1,0:T(8,128)(2,1)S(1)}, bf16[128,3072]{1,0:T(8,128)(2,1)}, u32[]{:S(2)}, u32[]{:S(2)}) collective-permute-start(bf16[128,3072]{1,0:T(8,128)(2,1)S(1)} %reshape_reshape.7), channel_id=1, source_target_pairs={{0,1},{1,0},{2,3},{3,2},{4,5},{5,4},{6,7},{7,6},{8,9},{9,8},{10,11... | collective-permute-start | bytes 2359304 | tf_op jit(solution)/shard_map/ppermute | solution.py:218
  81.0 33.9 %all-to-all-start.1 = ((bf16[1,16,8,2048]{3,2,0,1:T(8,128)(2,1)}), bf16[1,16,8,2048]{3,2,0,1:T(8,128)(2,1)}, u32[]{:S(2)}, u32[]{:S(2)}) async-start(bf16[1,16,8,2048]{3,2,0,1:T(8,128)(2,1)} %maximum_bitcast_fusion), calls=%async_computation.1 | async-start | bytes 1048576 | tf_op jit(solution)/shard_map/all_to_all | solution.py:224
  116.8 7.6 %collective-permute-start.9 = (f32[1024]{0:T(1024)S(1)}, f32[1024]{0:T(1024)S(1)}, u32[]{:S(2)}, u32[]{:S(2)}) collective-permute-start(f32[1024]{0:T(1024)S(1)} %get-tuple-element.60), channel_id=1, source_target_pairs={{0,1},{1,0},{2,3},{3,2},{4,5},{5,4},{6,7},{7,6},{8,9},{9,8},{10,11... | collective-permute-start | bytes 12296 | tf_op jit(solution)/shard_map/ppermute | solution.py:246
  117.4 7.5 %collective-permute-start.8 = (bf16[128,1024]{1,0:T(8,128)(2,1)S(1)}, bf16[128,1024]{1,0:T(8,128)(2,1)}, u32[]{:S(2)}, u32[]{:S(2)}) collective-permute-start(bf16[128,1024]{1,0:T(8,128)(2,1)S(1)} %fusion.46), channel_id=1, source_target_pairs={{0,1},{1,0},{2,3},{3,2},{4,5},{5,4},{6,7},{7,6},{8,9},{9,8},{10,11... | collective-permute-start | bytes 786440 | tf_op jit(solution)/shard_map/ppermute | solution.py:246
  120.9 4.0 %copy-start.4 = (bf16[256,2,2,2,2,2,32]{0,6,5,4,3,2,1:T(8,128)(2,1)S(1)}, bf16[256,2,2,2,2,2,32]{0,6,5,4,3,2,1:T(8,128)(2,1)}, u32[]{:S(2)}) copy-start(bf16[256,2,2,2,2,2,32]{0,6,5,4,3,2,1:T(8,128)(2,1)} %copy.240) | copy-start | bytes 1572868
  122.6 30.8 %collective-permute-start.2 = (bf16[2,2,2,32,3072]{4,3,2,1,0:T(8,128)(2,1)}, bf16[2,2,2,32,3072]{4,3,2,1,0:T(8,128)(2,1)}, u32[]{:S(2)}, u32[]{:S(2)}) collective-permute-start(bf16[2,2,2,32,3072]{4,3,2,1,0:T(8,128)(2,1)} %fusion.4), channel_id=1, source_target_pairs={{0,2},{1,17},{2,0},{3,19},{4,6},{5,21},{6,4},{7,23},{8,10},{9,25},... | collective-permute-start | bytes 4718600 | tf_op jit(solution)/shard_map/ppermute | solution.py:147
  126.3 2.4 %copy-start.9 = (bf16[16,8,8,128]{3,2,1,0:T(8,128)(2,1)S(1)}, bf16[16,8,8,128]{3,2,1,0:T(8,128)(2,1)}, u32[]{:S(2)}) copy-start(bf16[16,8,8,128]{3,2,1,0:T(8,128)(2,1)} %copy.260) | copy-start | bytes 786436
  126.3 2.4 %copy-start.10 = (bf16[128,1024]{0,1:T(8,128)(2,1)S(1)}, bf16[128,1024]{0,1:T(8,128)(2,1)}, u32[]{:S(2)}) copy-start(bf16[128,1024]{0,1:T(8,128)(2,1)} %copy.259) | copy-start | bytes 786436
  126.3 3.4 %copy-start.8 = (bf16[1,1,128,1024]{2,3,1,0:T(8,128)(2,1)S(1)}, bf16[1,1,128,1024]{2,3,1,0:T(8,128)(2,1)}, u32[]{:S(2)}) copy-start(bf16[1,1,128,1024]{2,3,1,0:T(8,128)(2,1)} %copy-done.7) | copy-start | bytes 786436
  128.5 3.8 %copy-start.6 = (bf16[1,1,128,1024]{2,3,1,0:T(8,128)(2,1)S(1)}, bf16[1,1,128,1024]{2,3,1,0:T(8,128)(2,1)}, u32[]{:S(2)}) copy-start(bf16[1,1,128,1024]{2,3,1,0:T(8,128)(2,1)} %copy-done.5) | copy-start | bytes 786436
  128.5 21.1 %collective-permute-start.10 = (bf16[2,2,2,32,1025]{4,3,2,1,0:T(8,128)(2,1)}, bf16[2,2,2,32,1025]{4,3,2,1,0:T(8,128)(2,1)}, u32[]{:S(2)}, u32[]{:S(2)}) collective-permute-start(bf16[2,2,2,32,1025]{4,3,2,1,0:T(8,128)(2,1)} %fusion.44), channel_id=1, source_target_pairs={{0,2},{1,17},{2,0},{3,19},{4,6},{5,21},{6,4},{7,23},{8,10},{9,25},... | collective-permute-start | bytes 1574408 | tf_op jit(solution)/shard_map/ppermute | solution.py:147
  151.9 7.5 %copy-start.11 = (bf16[128,1024]{0,1:T(8,128)(2,1)S(1)}, bf16[128,1024]{0,1:T(8,128)(2,1)}, u32[]{:S(2)}) copy-start(bf16[128,1024]{0,1:T(8,128)(2,1)} %copy.259) | copy-start | bytes 786436
  151.9 15.1 %collective-permute-start.11 = (bf16[2,2,32,1025]{3,2,1,0:T(8,128)(2,1)}, bf16[2,2,32,1025]{3,2,1,0:T(8,128)(2,1)}, u32[]{:S(2)}, u32[]{:S(2)}) collective-permute-start(bf16[2,2,32,1025]{3,2,1,0:T(8,128)(2,1)} %fusion.56), channel_id=1, source_target_pairs={{0,16},{1,5},{2,18},{3,7},{4,20},{5,1},{6,22},{7,3},{8,24},{9,13},... | collective-permute-start | bytes 787208 | tf_op jit(solution)/shard_map/ppermute | solution.py:147
  156.2 1.7 copy-start.2
  158.9 12.3 %collective-permute-start.3 = (bf16[2,2,32,3072]{3,2,1,0:T(8,128)(2,1)}, bf16[2,2,32,3072]{3,2,1,0:T(8,128)(2,1)}, u32[]{:S(2)}, u32[]{:S(2)}) collective-permute-start(bf16[2,2,32,3072]{3,2,1,0:T(8,128)(2,1)} %fusion.41), channel_id=1, source_target_pairs={{0,16},{1,5},{2,18},{3,7},{4,20},{5,1},{6,22},{7,3},{8,24},{9,13},... | collective-permute-start | bytes 2359304 | tf_op jit(solution)/shard_map/ppermute | solution.py:147
  168.1 6.9 %collective-permute-start.12 = (bf16[2,32,1025]{2,1,0:T(8,128)(2,1)S(1)}, bf16[2,32,1025]{2,1,0:T(8,128)(2,1)S(1)}, u32[]{:S(2)}, u32[]{:S(2)}) collective-permute-start(bf16[2,32,1025]{2,1,0:T(8,128)(2,1)S(1)} %fusion.71), channel_id=1, source_target_pairs={{0,4},{1,3},{2,6},{3,1},{4,0},{5,7},{6,2},{7,5},{8,12},{9,11},{10,... | collective-permute-start | bytes 393608 | tf_op jit(solution)/shard_map/ppermute | solution.py:147
  173.0 9.6 %collective-permute-start.4 = (bf16[2,32,3072]{2,1,0:T(8,128)(2,1)S(1)}, bf16[2,32,3072]{2,1,0:T(8,128)(2,1)S(1)}, u32[]{:S(2)}, u32[]{:S(2)}) collective-permute-start(bf16[2,32,3072]{2,1,0:T(8,128)(2,1)S(1)} %fusion.54), channel_id=1, source_target_pairs={{0,4},{1,3},{2,6},{3,1},{4,0},{5,7},{6,2},{7,5},{8,12},{9,11},{10,... | collective-permute-start | bytes 1179656 | tf_op jit(solution)/shard_map/ppermute | solution.py:147
  175.0 9.8 %collective-permute-start.13 = (bf16[32,1025]{1,0:T(8,128)(2,1)S(1)}, bf16[32,1025]{1,0:T(8,128)(2,1)S(1)}, u32[]{:S(2)}, u32[]{:S(2)}) collective-permute-start(bf16[32,1025]{1,0:T(8,128)(2,1)S(1)} %fusion.77), channel_id=1, source_target_pairs={{0,8},{1,9},{2,10},{3,11},{4,12},{5,13},{6,14},{7,15},{8,0},{9,1},... | collective-permute-start | bytes 196808 | tf_op jit(solution)/shard_map/ppermute | solution.py:147
  182.8 8.7 %collective-permute-start.5 = (bf16[32,3072]{1,0:T(8,128)(2,1)S(1)}, bf16[32,3072]{1,0:T(8,128)(2,1)S(1)}, u32[]{:S(2)}, u32[]{:S(2)}) collective-permute-start(bf16[32,3072]{1,0:T(8,128)(2,1)S(1)} %fusion.70), channel_id=1, source_target_pairs={{0,8},{1,9},{2,10},{3,11},{4,12},{5,13},{6,14},{7,15},{8,0},{9,1},... | collective-permute-start | bytes 589832 | tf_op jit(solution)/shard_map/ppermute | solution.py:147
  184.8 8.1 %collective-permute-start.14 = (bf16[32,1025]{1,0:T(8,128)(2,1)S(1)}, bf16[32,1025]{1,0:T(8,128)(2,1)S(1)}, u32[]{:S(2)}, u32[]{:S(2)}) collective-permute-start(bf16[32,1025]{1,0:T(8,128)(2,1)S(1)} %fusion.72), channel_id=1, source_target_pairs={{0,16},{16,0},{1,17},{17,1},{2,18},{18,2},{3,19},{19,3},{4,20},{20... | collective-permute-start | bytes 196808 | tf_op jit(solution)/shard_map/ppermute | solution.py:152
  191.5 5.7 %collective-permute-start.6 = (bf16[32,3072]{1,0:T(8,128)(2,1)S(1)}, bf16[32,3072]{1,0:T(8,128)(2,1)S(1)}, u32[]{:S(2)}, u32[]{:S(2)}) collective-permute-start(bf16[32,3072]{1,0:T(8,128)(2,1)S(1)} %fusion.55), channel_id=1, source_target_pairs={{0,16},{16,0},{1,17},{17,1},{2,18},{18,2},{3,19},{19,3},{4,20},{20... | collective-permute-start | bytes 589832 | tf_op jit(solution)/shard_map/ppermute | solution.py:152
  (3 other events, 3.3 us)

commit v6 on v4

--- a/solution.py
+++ b/solution.py
@@ -74,7 +74,7 @@
     )
 
 
-def split_orders(seq_n, dp_n):
+def split_orders(seq_n, dp_n, z_first=False):
     bits = seq_n.bit_length() - 1
     dp_bits = dp_n.bit_length() - 1
     assert 1 << bits == seq_n and 1 << dp_bits == dp_n and bits >= 1
@@ -84,6 +84,9 @@
     odd = list(even)
     if bits >= 3 and dp_bits >= 1:
         odd = dp_all[:1] + [seq_rest[1], seq_rest[0]] + seq_rest[2:] + dp_all[1:]
+        if z_first:
+            even = [seq_rest[1], seq_rest[0]] + dp_all[:1] + seq_rest[2:] + dp_all[1:]
+            odd = [seq_rest[1]] + dp_all[:1] + [seq_rest[0]] + seq_rest[2:] + dp_all[1:]
     assert sorted(even) == sorted(odd)
     return even, odd
 
@@ -109,11 +112,10 @@
     return jnp.where(core_odd, arrange(odd), arrange(even))
 
 
-def reduce_rows(parts, orders, seq_n, dp_n):
+def reduce_rows(parts, part_orders, seq_n, dp_n):
     seq_at = lax.axis_index("seq")
     dp_at = lax.axis_index("dp")
-    even, odd = orders
-    steps = len(even)
+    steps = len(part_orders[0][0])
     accs = tuple(p.reshape((2,) * steps + (p.shape[0] >> steps, p.shape[1])) for p in parts)
 
     def bit_value(item, seq_i, dp_i):
@@ -126,26 +128,25 @@
             return seq_i ^ (1 << k), dp_i
         return seq_i, dp_i ^ (1 << k)
 
+    def traced_bit(item):
+        kind, k = item
+        return ((seq_at if kind == "s" else dp_at) // (1 << k)) % 2
+
     for step in range(steps):
-        perm = []
-        for dp_i in range(dp_n):
-            for seq_i in range(seq_n):
-                item = (odd if seq_i % 2 else even)[step]
-                seq_j, dp_j = flip(item, seq_i, dp_i)
-                perm.append((dp_i * seq_n + seq_i, dp_j * seq_n + seq_j))
-
-        def traced_bit(item):
-            kind, k = item
-            return ((seq_at if kind == "s" else dp_at) // (1 << k)) % 2
-
-        keep_at = jnp.where(seq_at % 2 == 1, traced_bit(odd[step]), traced_bit(even[step]))
-        kept = tuple(lax.dynamic_index_in_dim(acc, keep_at, 0, keepdims=False) for acc in accs)
-        given = tuple(
-            lax.dynamic_index_in_dim(acc, 1 - keep_at, 0, keepdims=False).astype(jnp.bfloat16)
-            for acc in accs
-        )
-        got = lax.ppermute(given, ("dp", "seq"), perm)
-        accs = tuple(k + g.astype(jnp.float32) for k, g in zip(kept, got))
+        next_accs = []
+        for acc, (even, odd) in zip(accs, part_orders):
+            perm = []
+            for dp_i in range(dp_n):
+                for seq_i in range(seq_n):
+                    item = (odd if seq_i % 2 else even)[step]
+                    seq_j, dp_j = flip(item, seq_i, dp_i)
+                    perm.append((dp_i * seq_n + seq_i, dp_j * seq_n + seq_j))
+            keep_at = jnp.where(seq_at % 2 == 1, traced_bit(odd[step]), traced_bit(even[step]))
+            kept = lax.dynamic_index_in_dim(acc, keep_at, 0, keepdims=False)
+            given = lax.dynamic_index_in_dim(acc, 1 - keep_at, 0, keepdims=False).astype(jnp.bfloat16)
+            got = lax.ppermute(given, ("dp", "seq"), perm)
+            next_accs.append(kept + got.astype(jnp.float32))
+        accs = tuple(next_accs)
     accs = tuple(acc.astype(jnp.bfloat16) for acc in accs)
     for step in range(dp_n.bit_length() - 1):
         perm = [(member, member ^ (1 << step)) for member in range(dp_n)]
@@ -191,13 +192,6 @@
     pieces = joint_cols.reshape(batches, all_rows, col_share, 3, head_count, HEAD_DIM)
     query_cols, key_cols, value_cols = (pieces[:, :, :, 0], pieces[:, :, :, 1], pieces[:, :, :, 2])
     out_cols, probs_cols = attend(query_cols, key_cols, value_cols, "blche", "bchlm")
-    column_out = lax.all_to_all(
-        out_cols.reshape(batches, all_rows, col_share, feature),
-        "seq",
-        split_axis=1,
-        concat_axis=2,
-        tiled=True,
-    )
     upstream_cols = lax.all_to_all(upstream, "seq", split_axis=2, concat_axis=1, tiled=True)
     upstream_cols = upstream_cols.reshape(batches, all_rows, col_share, head_count, HEAD_DIM)
     grads_cols = attend_back(
@@ -212,11 +206,12 @@
     seq_n = lax.axis_size("seq")
     dp_n = lax.axis_size("dp")
     orders = split_orders(seq_n, dp_n)
+    out_orders = split_orders(seq_n, dp_n, z_first=True)
     core_odd = lax.axis_index("seq") % 2 == 1
     pair = [(member, member ^ 1) for member in range(seq_n)]
     core = lax.axis_index("seq") % 2
 
-    def my_half(factor):
+    def my_half(factor, orders=orders):
         arranged = by_split_order(factor, orders, core_odd, seq_n, dp_n)
         half = arranged.shape[1] // 2
         return lax.dynamic_slice_in_dim(arranged, core * half, half, axis=1)
@@ -242,16 +237,24 @@
     grad_hidden = (
         inverse * scaled - hidden * inverse**3 * jnp.mean(scaled * hidden, axis=-1, keepdims=True)
     ).astype(jnp.bfloat16)
+    out_cols, grad_hidden = lax.optimization_barrier((out_cols, grad_hidden))
+    column_out = lax.all_to_all(
+        out_cols.reshape(batches, all_rows, col_share, feature),
+        "seq",
+        split_axis=1,
+        concat_axis=2,
+        tiled=True,
+    )
     first_peer, hidden_peer, gain_peer = lax.ppermute((flat_first, grad_hidden, gain_term), "seq", pair)
     out_term = jnp.dot(
-        my_half(jnp.concatenate([flat_first, first_peer], axis=0)).T,
+        my_half(jnp.concatenate([flat_first, first_peer], axis=0), out_orders).T,
         jnp.concatenate([grad_hidden, hidden_peer], axis=0),
         preferred_element_type=jnp.float32,
     )
-    gain_term = my_half((gain_term + gain_peer)[None, :])[0][:, None]
+    gain_term = my_half((gain_term + gain_peer)[None, :], out_orders)[0][:, None]
     out_width = out_term.shape[1]
     joint_sum, out_sum = reduce_rows(
-        (joint_term, jnp.concatenate([out_term, gain_term], axis=1)), orders, seq_n, dp_n
+        (joint_term, jnp.concatenate([out_term, gain_term], axis=1)), (orders, out_orders), seq_n, dp_n
     )
     replicas = (joint_sum, out_sum[:, :out_width], out_sum[:, out_width].astype(jnp.float32))
     grad_first = jnp.dot(grad_hidden, out_weight.T, preferred_element_type=jnp.float32).astype(

time: 174 us -> 171 us (0.983)
  waiting for transfers between devices: 46.7 us -> 33.4 us
  starting transfers between devices: 28.9 us -> 36.7 us
  matrix products: 38.4 us -> 41.8 us
  other arithmetic: 23.6 us -> 20.6 us
  local copies, waits for them, and re-layouts: 33.4 us -> 35.4 us
    ppermute x8, waiting for transfers between devices: 32.4 us -> 21.8 us  [reduce_rows(): got = lax.ppermute(given, ('dp', 'seq'), perm)]
    ppermute x8, starting transfers between devices: 6.03 us -> 11.6 us  [reduce_rows(): got = lax.ppermute(given, ('dp', 'seq'), perm)]
    all_to_all x1, waiting for transfers between devices: 3.39 us -> 6.19 us  [on_device(): lax.all_to_all(normed.reshape(batches, local_rows, columns, model_width),...]
    dot_general x2, matrix products: 1.68 us -> 4.13 us  [attend(): jnp.einsum(scores_form + ',' + keyed + '->' + layout, rounded, values, pr...]
    select_n x3, other arithmetic: 2.49 us -> 0.11 us  [by_split_order(): return jnp.where(core_odd, arrange(odd), arrange(even))]
    all_to_all x1, waiting for transfers between devices: 2 us -> 0.01 us  [on_device(): lax.all_to_all(out_cols.reshape(batches, all_rows, col_share, feature), '...]
    all_to_all x1, starting transfers between devices: 3.99 us -> 5.86 us  [on_device(): lax.all_to_all(normed.reshape(batches, local_rows, columns, model_width),...]
    all_to_all x1, waiting for transfers between devices: 3.71 us -> 1.87 us  [on_device(): lax.all_to_all(grad_local.reshape(batches, all_rows, col_share, model_wid...]
  transfers between devices with their start and end apart: 19 -> 19, of which waited for: 9 -> 7; matrix products, arithmetic and copies ran while one was open for 38% -> 38% of each run, Pallas kernels for 0% -> 0%
where the time goes in v6:
time: 171 us; the launch traced here: 169 us
  matrix products  41.8 us (24%)
  starting transfers between devices  36.7 us (21%)
  local copies, waits for them, and re-layouts  35.4 us (21%)
  waiting for transfers between devices  33.4 us (20%)
  other arithmetic  20.6 us (12%)
    ppermute x8, waiting for transfers between devices, reduce_rows(): got = lax.ppermute(given, ('dp', 'seq'), perm)  21.8 us
    unnamed x48, local copies, waits for them, and re-layouts  18 us
    ppermute x8, starting transfers between devices, reduce_rows(): got = lax.ppermute(given, ('dp', 'seq'), perm)  11.6 us
    all_to_all x1, starting transfers between devices, on_device(): lax.all_to_all(upstream, 'seq', split_axis=2, concat_axis=1, tiled=True)  7.39 us
    add x6, other arithmetic, reduce_rows(): next_accs.append(kept + got.astype(jnp.float32))  7.28 us
    all_to_all x1, waiting for transfers between devices, on_device(): lax.all_to_all(normed.reshape(batches, local_rows, columns, model_width),...  6.19 us
    all_to_all x1, starting transfers between devices, on_device(): lax.all_to_all(normed.reshape(batches, local_rows, columns, model_width),...  5.86 us
    dot_general x1, matrix products, on_device(): jnp.dot(used_grads, joint_weight.T, preferred_element_type=jnp.float32)  5.69 us
  transfers between devices with their start and end apart: 19, of which 7 were waited for; matrix products, arithmetic and copies ran while one was open for 38% of the time, Pallas kernels for 0%

profile of v6, /device:TPU:0, one launch (start us, length us, event | category | flops | bytes accessed | tf_op | source)
XLA Modules:
  0.0 169.0 jit_solution(6089413252115985080)
XLA Ops:
  2.7 2.1 %reduce.21 = bf16[128,1024]{1,0:T(8,128)(2,1)S(1)} reduce(bf16[128,1,1,1024]{3,2,1,0:T(2,128)(2,1)S(1)} %bitcast.188, bf16[]{:T(256)} %broadcast.113), dimensions={1,2}, to_apply=%bitcast.180.reduce_sub_computation | reduce | bytes 524290
  5.7 7.4 %all-to-all-start.1 = ((bf16[16,2,4096]{2,1,0:T(2,128)(2,1)}), bf16[16,2,4096]{2,1,0:T(2,128)(2,1)S(1)}, u32[]{:S(2)}, u32[]{:S(2)}) async-start(bf16[16,2,4096]{2,1,0:T(2,128)(2,1)} %reshape.313), calls=%async_computation.1 | async-start | bytes 524288 | tf_op jit(solution)/shard_map/all_to_all | solution.py:195
  16.7 2.0 %convolution_convert_fusion.3 = bf16[8,128,128]{1,2,0:T(8,128)(2,1)} fusion(bf16[128,8,128]{2,1,0:T(8,128)(2,1)} %bitcast.197, f32[8,128]{1,0:T(8,128)S(1)} %get-tuple-element.52, f32[8,128,128]{1,2,0:T(8,128)S(1)} %fusion.20), kind=kOutput, calls=%fused_computation.37 | convolution fusion | flops 34079872 | bytes 1052672 | tf_op jit(solution)/shard_map/ghlm,gmhe->glhe/dot_general | solution.py:31
  21.2 2.9 %reduce.20 = bf16[128,1024]{1,0:T(8,128)(2,1)} reduce(bf16[128,1,1,1024]{3,2,1,0:T(2,128)(2,1)S(1)} %bitcast.189, bf16[]{:T(256)} %broadcast.113), dimensions={1,2}, to_apply=%bitcast.181.reduce_sub_computation | reduce | bytes 524290
  24.0 1.8 %reshape.311 = bf16[16,2,4096]{2,1,0:T(2,128)(2,1)} reshape(bf16[128,1024]{1,0:T(8,128)(2,1)} %reduce.20) | data formatting | bytes 524288
  25.9 5.9 %all-to-all-start = ((bf16[16,2,4096]{2,1,0:T(2,128)(2,1)}), bf16[16,2,4096]{2,1,0:T(2,128)(2,1)}, u32[]{:S(2)}, u32[]{:S(2)}) async-start(bf16[16,2,4096]{2,1,0:T(2,128)(2,1)} %reshape.311), calls=%async_computation | async-start | bytes 524288 | tf_op jit(solution)/shard_map/all_to_all | solution.py:178
  35.6 6.2 %all-to-all-done = bf16[16,2,4096]{2,1,0:T(2,128)(2,1)} async-done(((bf16[16,2,4096]{2,1,0:T(2,128)(2,1)}), bf16[16,2,4096]{2,1,0:T(2,128)(2,1)}, u32[]{:S(2)}, u32[]{:S(2)}) %all-to-all-start) | async-done | bytes 262176 | tf_op jit(solution)/shard_map/all_to_all | solution.py:178
  41.8 2.2 %reshape.312 = bf16[128,1,1,1024]{3,2,1,0:T(2,128)(2,1)S(1)} reshape(bf16[16,2,4096]{2,1,0:T(2,128)(2,1)} %all-to-all-done) | data formatting | bytes 524288
  45.1 3.9 %convolution_convert_fusion = bf16[128,3072]{1,0:T(8,128)(2,1)S(1)} fusion(bf16[1024,3072]{1,0:T(8,128)(2,1)} %param.12, bf16[1,1,128,1024]{2,3,1,0:T(8,128)(2,1)} %copy.112), kind=kOutput, calls=%fused_computation.4 | convolution fusion | flops 805699584 | bytes 7340032 | tf_op jit(solution)/shard_map/dot_general | solution.py:185
  51.0 2.5 %fusion.94 = (f32[8,8,16]{2,1,0:T(8,128)S(1)}, f32[8,8,16,16]{2,3,1,0:T(8,128)}) fusion(pred[16,16]{0,1:T(8,128)(4,1)S(1)} %iota_compare_fusion.1, bf16[1,16,8,1,8,128]{5,2,4,3,1,0:T(8,128)(2,1)S(1)} %get-tuple-element.46, bf16[1,16,8,1,8,128]{5,2,4,3,1,0:T(8,128)(2,1)} %get-tuple-element.45), kind=kOutput, calls=%fused_computation.149 | convolution fusion | flops 4259855 | bytes 594176 | tf_op jit(solution)/shard_map/sub | solution.py:28
  53.6 2.8 %fusion.29 = bf16[1,16,8,1,8,128]{5,1,4,2,3,0:T(8,128)(2,1)} fusion(f32[8,8,16,16]{2,3,1,0:T(8,128)} %convolution_bitcast_fusion, bf16[1,16,8,1,8,128]{5,2,4,3,1,0:T(8,128)(2,1)} %get-tuple-element.45, f32[8,8,16,16]{2,3,1,0:T(8,128)} %get-tuple-element.57, f32[8,8,16]{2,1,0:T(8,128)S(1)} %get-tuple-element.56), kind=kOutput, calls=%fused_computation.51 | convolution fusion | flops 4441103 | bytes 659456 | tf_op jit(solution)/shard_map/bchlm,bmche->blche/dot_general | solution.py:51
  56.4 2.7 %fusion.32 = bf16[1,16,8,1,8,128]{5,1,4,2,3,0:T(8,128)(2,1)} fusion(f32[8,8,16,16]{2,3,1,0:T(8,128)} %convolution_bitcast_fusion, bf16[1,16,8,1,8,128]{5,2,4,3,1,0:T(8,128)(2,1)S(1)} %get-tuple-element.46, f32[8,8,16,16]{2,3,1,0:T(8,128)} %get-tuple-element.57, f32[8,8,16]{2,1,0:T(8,128)S(1)} %get-tuple-element.56), kind=kOutput, calls=%fused_computation.54 | convolution fusion | flops 4441103 | bytes 659456 | tf_op jit(solution)/shard_map/bchlm,blche->bmche/dot_general | solution.py:57
  63.8 5.7 %fusion.31 = bf16[1,16,8,1024]{3,2,0,1:T(8,128)(2,1)} fusion(bf16[128,3072]{1,0:T(8,128)(2,1)S(1)} %reshape_reshape.7, bf16[1024,3072]{1,0:T(8,128)(2,1)} %param.12), kind=kOutput, calls=%fused_computation.53 | convolution fusion | flops 805437440 | bytes 7340032 | tf_op jit(solution)/shard_map/dot_general | solution.py:203
  69.5 4.2 %all-to-all-start.2 = ((bf16[1,16,8,1024]{3,2,0,1:T(8,128)(2,1)}), bf16[1,16,8,1024]{3,2,0,1:T(8,128)(2,1)}, u32[]{:S(2)}, u32[]{:S(2)}) async-start(bf16[1,16,8,1024]{3,2,0,1:T(8,128)(2,1)} %fusion.31), calls=%async_computation.2 | async-start | bytes 524288 | tf_op jit(solution)/shard_map/all_to_all | solution.py:225
  73.7 2.2 %fusion.28 = bf16[1,16,8,8,128]{4,1,3,2,0:T(8,128)(2,1)} fusion(bf16[1,16,8,1,8,128]{5,2,4,3,1,0:T(8,128)(2,1)} %copy-done.12, f32[8,8,16,16]{2,3,1,0:T(8,128)} %get-tuple-element.57, f32[8,8,16]{2,1,0:T(8,128)S(1)} %get-tuple-element.56), kind=kOutput, calls=%fused_computation.50 | convolution fusion | flops 4358144 | bytes 593920 | tf_op jit(solution)/shard_map/bchlm,bmche->blche/dot_general | solution.py:31
  77.0 4.8 %fusion.5 = f32[512,3072]{1,0:T(8,128)} fusion(bf16[128,3072]{1,0:T(8,128)(2,1)} %collective-permute-done.1, bf16[128,3072]{1,0:T(8,128)(2,1)S(1)} %reshape_reshape.7, bf16[256,1024]{0,1:T(8,128)(2,1)S(1)} %bitcast.191, s32[]{:T(128)S(6)} %select_n.229), kind=kOutput, calls=%fused_computation.12 | convolution fusion | flops 808452096 | bytes 8126468 | tf_op jit(solution)/shard_map/dot_general | solution.py:220
  81.8 1.9 %all-to-all-done.2 = bf16[1,16,8,1024]{3,2,0,1:T(8,128)(2,1)} async-done(((bf16[1,16,8,1024]{3,2,0,1:T(8,128)(2,1)}), bf16[1,16,8,1024]{3,2,0,1:T(8,128)(2,1)}, u32[]{:S(2)}, u32[]{:S(2)}) %all-to-all-start.2) | async-done | bytes 262176 | tf_op jit(solution)/shard_map/all_to_all | solution.py:225
  87.8 4.4 %all-to-all-start.3 = ((bf16[1,16,8,1024]{3,2,0,1:T(8,128)(2,1)}), bf16[1,16,8,1024]{3,2,0,1:T(8,128)(2,1)}, u32[]{:S(2)}, u32[]{:S(2)}) async-start(bf16[1,16,8,1024]{3,2,0,1:T(8,128)(2,1)} %bitcast.42), calls=%async_computation.3 | async-start | bytes 524288 | tf_op jit(solution)/shard_map/all_to_all | solution.py:241
  92.8 3.2 %fusion.4 = bf16[2,2,2,32,3072]{4,3,2,1,0:T(8,128)(2,1)} fusion(f32[2,2,2,2,32,3072]{5,4,3,2,1,0:T(8,128)} %bitcast.182, s32[]{:T(128)S(6)} %select_n.236), kind=kLoop, calls=%fused_computation.11 | loop fusion | bytes 3145732 | tf_op jit(solution)/shard_map/convert_element_type | solution.py:146
  105.9 2.6 %convolution_convert_fusion.1 = bf16[8,128,128]{1,2,0:T(8,128)(2,1)} fusion(bf16[128,8,128]{0,2,1:T(8,128)(2,1)S(1)} %bitcast.196, f32[8,128,128]{1,2,0:T(8,128)} %fusion.65, f32[8,128,128]{1,2,0:T(8,128)} %get-tuple-element.53, f32[8,128]{1,0:T(8,128)S(1)} %get-tuple-element.52), kind=kOutput, calls=%fused_computation.35 | convolution fusion | flops 34604160 | bytes 1576960 | tf_op jit(solution)/shard_map/ghlm,gmhe->glhe/dot_general | solution.py:51
  108.5 2.6 %convolution_convert_fusion.5 = bf16[8,128,128]{1,2,0:T(8,128)(2,1)} fusion(bf16[128,8,128]{0,2,1:T(8,128)(2,1)S(1)} %bitcast.194, f32[8,128,128]{1,2,0:T(8,128)} %fusion.65, f32[8,128,128]{1,2,0:T(8,128)} %get-tuple-element.53, f32[8,128]{1,0:T(8,128)S(1)} %get-tuple-element.52), kind=kOutput, calls=%fused_computation.39 | convolution fusion | flops 34604160 | bytes 1576960 | tf_op jit(solution)/shard_map/ghlm,glhe->gmhe/dot_general | solution.py:57
  111.2 7.6 %collective-permute-done.10 = bf16[2,2,2,32,1025]{4,3,2,1,0:T(8,128)(2,1)} collective-permute-done((bf16[2,2,2,32,1025]{4,3,2,1,0:T(8,128)(2,1)}, bf16[2,2,2,32,1025]{4,3,2,1,0:T(8,128)(2,1)}, u32[]{:S(2)}, u32[]{:S(2)}) %collective-permute-start.10) | collective-permute-done | bytes 524832 | tf_op jit(solution)/shard_map/ppermute | solution.py:147
  122.6 2.8 %bitcast_add_fusion = f32[2,2,2,32,3072]{4,3,2,1,0:T(8,128)S(1)} fusion(bf16[2,2,2,32,3072]{4,3,2,1,0:T(8,128)(2,1)} %collective-permute-done.2, f32[2,2,2,2,32,3072]{5,4,3,2,1,0:T(8,128)} %bitcast.183, s32[]{:T(128)S(6)} %select_n.235), kind=kLoop, calls=%fused_computation.7 | loop fusion | flops 1572864 | bytes 7864324 | tf_op jit(solution)/shard_map/add | solution.py:148
  128.7 2.2 %convolution_convert_fusion.4 = bf16[8,128,128]{2,1,0:T(8,128)(2,1)} fusion(bf16[128,8,128]{0,2,1:T(8,128)(2,1)S(1)} %bitcast.200, f32[8,128]{1,0:T(8,128)S(1)} %get-tuple-element.52, f32[8,128,128]{1,2,0:T(8,128)} %copy-done.3), kind=kOutput, calls=%fused_computation.38 | convolution fusion | flops 34079872 | bytes 1052672 | tf_op jit(solution)/shard_map/ghlm,glhe->gmhe/dot_general | solution.py:64
  130.9 1.8 %copy.144 = bf16[1,1,128,1024]{3,2,1,0:T(8,128)(2,1)} copy(bf16[1,1,128,1024]{2,3,1,0:T(8,128)(2,1)} %bitcast.203) | data formatting | bytes 524288
  132.7 1.8 %copy.143 = bf16[1,1,128,1024]{3,2,1,0:T(8,128)(2,1)} copy(bf16[1,1,128,1024]{2,3,1,0:T(8,128)(2,1)} %bitcast.202) | data formatting | bytes 524288
  134.5 1.8 %copy.145 = bf16[1,1,128,1024]{3,2,1,0:T(8,128)(2,1)} copy(bf16[1,1,128,1024]{2,3,1,0:T(8,128)(2,1)} %bitcast.204) | data formatting | bytes 524288
  140.4 1.8 %bitcast_add_fusion.1 = f32[2,2,32,3072]{3,2,1,0:T(8,128)S(1)} fusion(bf16[2,2,32,3072]{3,2,1,0:T(8,128)(2,1)} %collective-permute-done.3, f32[2,2,2,32,3072]{4,3,2,1,0:T(8,128)} %copy-done.2, s32[]{:T(128)S(6)} %select_n.240), kind=kLoop, calls=%fused_computation.16 | loop fusion | flops 786432 | bytes 3932164 | tf_op jit(solution)/shard_map/add | solution.py:148
  143.9 2.5 %collective-permute-start.13 = (bf16[32,1025]{1,0:T(8,128)(2,1)S(1)}, bf16[32,1025]{1,0:T(8,128)(2,1)S(1)}, u32[]{:S(2)}, u32[]{:S(2)}) collective-permute-start(bf16[32,1025]{1,0:T(8,128)(2,1)S(1)} %fusion.76), channel_id=1, source_target_pairs={{0,8},{1,9},{2,10},{3,11},{4,12},{5,13},{6,14},{7,15},{8,0},{9,1},... | collective-permute-start | bytes 196808 | tf_op jit(solution)/shard_map/ppermute | solution.py:147
  146.4 5.9 %collective-permute-done.4 = bf16[2,32,3072]{2,1,0:T(8,128)(2,1)S(1)} collective-permute-done((bf16[2,32,3072]{2,1,0:T(8,128)(2,1)S(1)}, bf16[2,32,3072]{2,1,0:T(8,128)(2,1)S(1)}, u32[]{:S(2)}, u32[]{:S(2)}) %collective-permute-start.4) | collective-permute-done | bytes 393248 | tf_op jit(solution)/shard_map/ppermute | solution.py:147
  154.0 6.7 %collective-permute-done.5 = bf16[32,3072]{1,0:T(8,128)(2,1)S(1)} collective-permute-done((bf16[32,3072]{1,0:T(8,128)(2,1)S(1)}, bf16[32,3072]{1,0:T(8,128)(2,1)S(1)}, u32[]{:S(2)}, u32[]{:S(2)}) %collective-permute-start.5) | collective-permute-done | bytes 196640 | tf_op jit(solution)/shard_map/ppermute | solution.py:147
  163.0 3.6 %collective-permute-done.6 = bf16[32,3072]{1,0:T(8,128)(2,1)S(1)} collective-permute-done((bf16[32,3072]{1,0:T(8,128)(2,1)S(1)}, bf16[32,3072]{1,0:T(8,128)(2,1)S(1)}, u32[]{:S(2)}, u32[]{:S(2)}) %collective-permute-start.6) | collective-permute-done | bytes 196640 | tf_op jit(solution)/shard_map/ppermute | solution.py:153
  (127 shorter events, 55.4 us)
Async XLA Ops:
  0.6 18.5 %copy-start = (bf16[1024,1024]{1,0:T(8,128)(2,1)S(1)}, bf16[1024,1024]{1,0:T(8,128)(2,1)}, u32[]{:S(2)}) copy-start(bf16[1024,1024]{1,0:T(8,128)(2,1)} %param.10) | copy-start | bytes 6291460
  0.6 12.5 %copy-start.13 = (bf16[1,1,128,1024]{3,2,1,0:T(8,128)(2,1)S(1)}, bf16[1,1,128,1024]{3,2,1,0:T(8,128)(2,1)}, u32[]{:S(2)}) copy-start(bf16[1,1,128,1024]{3,2,1,0:T(8,128)(2,1)} %param.7) | copy-start | bytes 786436
  4.8 9.7 %copy-start.14 = (bf16[1,1,128,1024]{3,2,1,0:T(8,128)(2,1)S(1)}, bf16[1,1,128,1024]{3,2,1,0:T(8,128)(2,1)}, u32[]{:S(2)}) copy-start(bf16[1,1,128,1024]{3,2,1,0:T(8,128)(2,1)} %param.9) | copy-start | bytes 786436
  5.7 20.1 %all-to-all-start.1 = ((bf16[16,2,4096]{2,1,0:T(2,128)(2,1)}), bf16[16,2,4096]{2,1,0:T(2,128)(2,1)S(1)}, u32[]{:S(2)}, u32[]{:S(2)}) async-start(bf16[16,2,4096]{2,1,0:T(2,128)(2,1)} %reshape.313), calls=%async_computation.1 | async-start | bytes 524288 | tf_op jit(solution)/shard_map/all_to_all | solution.py:195
  13.3 5.3 %copy-start.5 = (bf16[1,1,128,1024]{2,3,1,0:T(8,128)(2,1)}, bf16[1,1,128,1024]{2,3,1,0:T(8,128)(2,1)S(1)}, u32[]{:S(2)}) copy-start(bf16[1,1,128,1024]{2,3,1,0:T(8,128)(2,1)S(1)} %copy.158) | copy-start | bytes 786436
  14.6 4.1 %copy-start.7 = (bf16[1,1,128,1024]{2,3,1,0:T(8,128)(2,1)}, bf16[1,1,128,1024]{2,3,1,0:T(8,128)(2,1)S(1)}, u32[]{:S(2)}) copy-start(bf16[1,1,128,1024]{2,3,1,0:T(8,128)(2,1)S(1)} %copy.157) | copy-start | bytes 786436
  15.6 3.5 %copy-start.3 = (f32[8,128,128]{1,2,0:T(8,128)}, f32[8,128,128]{1,2,0:T(8,128)S(1)}, u32[]{:S(2)}) copy-start(f32[8,128,128]{1,2,0:T(8,128)S(1)} %fusion.20) | copy-start | bytes 1572868
  18.7 13.1 %collective-permute-start.7 = (bf16[128,1024]{0,1:T(8,128)(2,1)}, bf16[128,1024]{0,1:T(8,128)(2,1)}, u32[]{:S(2)}, u32[]{:S(2)}) collective-permute-start(bf16[128,1024]{0,1:T(8,128)(2,1)} %bitcast.3), channel_id=1, source_target_pairs={{0,1},{1,0},{2,3},{3,2},{4,5},{5,4},{6,7},{7,6},{8,9},{9,8},{10,11... | collective-permute-start | bytes 786440 | tf_op jit(solution)/shard_map/ppermute | solution.py:248
  25.9 16.0 %all-to-all-start = ((bf16[16,2,4096]{2,1,0:T(2,128)(2,1)}), bf16[16,2,4096]{2,1,0:T(2,128)(2,1)}, u32[]{:S(2)}, u32[]{:S(2)}) async-start(bf16[16,2,4096]{2,1,0:T(2,128)(2,1)} %reshape.311), calls=%async_computation | async-start | bytes 524288 | tf_op jit(solution)/shard_map/all_to_all | solution.py:178
  49.7 6.6 %copy-start.12 = (bf16[1,16,8,1,8,128]{5,2,4,3,1,0:T(8,128)(2,1)}, bf16[1,16,8,1,8,128]{5,2,4,3,1,0:T(8,128)(2,1)S(1)}, u32[]{:S(2)}) copy-start(bf16[1,16,8,1,8,128]{5,2,4,3,1,0:T(8,128)(2,1)S(1)} %get-tuple-element.47) | copy-start | bytes 786436
  60.5 15.3 %collective-permute-start = (bf16[128,1024]{0,1:T(8,128)(2,1)}, bf16[128,1024]{0,1:T(8,128)(2,1)}, u32[]{:S(2)}, u32[]{:S(2)}) collective-permute-start(bf16[128,1024]{0,1:T(8,128)(2,1)} %bitcast.5), channel_id=1, source_target_pairs={{0,1},{1,0},{2,3},{3,2},{4,5},{5,4},{6,7},{7,6},{8,9},{9,8},{10,11... | collective-permute-start | bytes 786440 | tf_op jit(solution)/shard_map/ppermute | solution.py:219
  63.2 13.8 %collective-permute-start.1 = (bf16[128,3072]{1,0:T(8,128)(2,1)S(1)}, bf16[128,3072]{1,0:T(8,128)(2,1)}, u32[]{:S(2)}, u32[]{:S(2)}) collective-permute-start(bf16[128,3072]{1,0:T(8,128)(2,1)S(1)} %reshape_reshape.7), channel_id=1, source_target_pairs={{0,1},{1,0},{2,3},{3,2},{4,5},{5,4},{6,7},{7,6},{8,9},{9,8},{10,11... | collective-permute-start | bytes 2359304 | tf_op jit(solution)/shard_map/ppermute | solution.py:219
  69.5 14.2 %all-to-all-start.2 = ((bf16[1,16,8,1024]{3,2,0,1:T(8,128)(2,1)}), bf16[1,16,8,1024]{3,2,0,1:T(8,128)(2,1)}, u32[]{:S(2)}, u32[]{:S(2)}) async-start(bf16[1,16,8,1024]{3,2,0,1:T(8,128)(2,1)} %fusion.31), calls=%async_computation.2 | async-start | bytes 524288 | tf_op jit(solution)/shard_map/all_to_all | solution.py:225
  87.8 48.4 %all-to-all-start.3 = ((bf16[1,16,8,1024]{3,2,0,1:T(8,128)(2,1)}), bf16[1,16,8,1024]{3,2,0,1:T(8,128)(2,1)}, u32[]{:S(2)}, u32[]{:S(2)}) async-start(bf16[1,16,8,1024]{3,2,0,1:T(8,128)(2,1)} %bitcast.42), calls=%async_computation.3 | async-start | bytes 524288 | tf_op jit(solution)/shard_map/all_to_all | solution.py:241
  92.3 7.1 %collective-permute-start.9 = (f32[1024]{0:T(1024)S(1)}, f32[1024]{0:T(1024)S(1)}, u32[]{:S(2)}, u32[]{:S(2)}) collective-permute-start(f32[1024]{0:T(1024)S(1)} %get-tuple-element.43), channel_id=1, source_target_pairs={{0,1},{1,0},{2,3},{3,2},{4,5},{5,4},{6,7},{7,6},{8,9},{9,8},{10,11... | collective-permute-start | bytes 12296 | tf_op jit(solution)/shard_map/ppermute | solution.py:248
  92.4 7.4 %collective-permute-start.8 = (bf16[128,1024]{1,0:T(8,128)(2,1)S(1)}, bf16[128,1024]{1,0:T(8,128)(2,1)}, u32[]{:S(2)}, u32[]{:S(2)}) collective-permute-start(bf16[128,1024]{1,0:T(8,128)(2,1)S(1)} %fusion.46), channel_id=1, source_target_pairs={{0,1},{1,0},{2,3},{3,2},{4,5},{5,4},{6,7},{7,6},{8,9},{9,8},{10,11... | collective-permute-start | bytes 786440 | tf_op jit(solution)/shard_map/ppermute | solution.py:248
  96.1 3.7 %copy-start.4 = (bf16[256,2,2,2,2,2,32]{0,6,5,4,3,2,1:T(8,128)(2,1)S(1)}, bf16[256,2,2,2,2,2,32]{0,6,5,4,3,2,1:T(8,128)(2,1)}, u32[]{:S(2)}) copy-start(bf16[256,2,2,2,2,2,32]{0,6,5,4,3,2,1:T(8,128)(2,1)} %copy.139) | copy-start | bytes 1572868
  97.8 24.9 %collective-permute-start.2 = (bf16[2,2,2,32,3072]{4,3,2,1,0:T(8,128)(2,1)}, bf16[2,2,2,32,3072]{4,3,2,1,0:T(8,128)(2,1)}, u32[]{:S(2)}, u32[]{:S(2)}) collective-permute-start(bf16[2,2,2,32,3072]{4,3,2,1,0:T(8,128)(2,1)} %fusion.4), channel_id=1, source_target_pairs={{0,2},{1,17},{2,0},{3,19},{4,6},{5,21},{6,4},{7,23},{8,10},{9,25},... | collective-permute-start | bytes 4718600 | tf_op jit(solution)/shard_map/ppermute | solution.py:147
  101.2 3.7 %copy-start.9 = (bf16[16,8,8,128]{3,2,1,0:T(8,128)(2,1)S(1)}, bf16[16,8,8,128]{3,2,1,0:T(8,128)(2,1)}, u32[]{:S(2)}) copy-start(bf16[16,8,8,128]{3,2,1,0:T(8,128)(2,1)} %copy.160) | copy-start | bytes 786436
  101.2 3.7 %copy-start.10 = (bf16[128,1024]{0,1:T(8,128)(2,1)S(1)}, bf16[128,1024]{0,1:T(8,128)(2,1)}, u32[]{:S(2)}) copy-start(bf16[128,1024]{0,1:T(8,128)(2,1)} %copy.159) | copy-start | bytes 786436
  101.2 4.7 %copy-start.8 = (bf16[1,1,128,1024]{2,3,1,0:T(8,128)(2,1)S(1)}, bf16[1,1,128,1024]{2,3,1,0:T(8,128)(2,1)}, u32[]{:S(2)}) copy-start(bf16[1,1,128,1024]{2,3,1,0:T(8,128)(2,1)} %copy-done.7) | copy-start | bytes 786436
  103.4 5.1 %copy-start.6 = (bf16[1,1,128,1024]{2,3,1,0:T(8,128)(2,1)S(1)}, bf16[1,1,128,1024]{2,3,1,0:T(8,128)(2,1)}, u32[]{:S(2)}) copy-start(bf16[1,1,128,1024]{2,3,1,0:T(8,128)(2,1)} %copy-done.5) | copy-start | bytes 786436
  103.4 15.3 %collective-permute-start.10 = (bf16[2,2,2,32,1025]{4,3,2,1,0:T(8,128)(2,1)}, bf16[2,2,2,32,1025]{4,3,2,1,0:T(8,128)(2,1)}, u32[]{:S(2)}, u32[]{:S(2)}) collective-permute-start(bf16[2,2,2,32,1025]{4,3,2,1,0:T(8,128)(2,1)} %fusion.44), channel_id=1, source_target_pairs={{0,4},{1,5},{2,6},{3,7},{4,0},{5,1},{6,2},{7,3},{8,12},{9,13},{10,... | collective-permute-start | bytes 1574408 | tf_op jit(solution)/shard_map/ppermute | solution.py:147
  121.0 7.7 %copy-start.11 = (bf16[128,1024]{0,1:T(8,128)(2,1)S(1)}, bf16[128,1024]{0,1:T(8,128)(2,1)}, u32[]{:S(2)}) copy-start(bf16[128,1024]{0,1:T(8,128)(2,1)} %copy.159) | copy-start | bytes 786436
  121.0 15.3 %collective-permute-start.11 = (bf16[2,2,32,1025]{3,2,1,0:T(8,128)(2,1)}, bf16[2,2,32,1025]{3,2,1,0:T(8,128)(2,1)}, u32[]{:S(2)}, u32[]{:S(2)}) collective-permute-start(bf16[2,2,32,1025]{3,2,1,0:T(8,128)(2,1)} %fusion.56), channel_id=1, source_target_pairs={{0,2},{1,17},{2,0},{3,19},{4,6},{5,21},{6,4},{7,23},{8,10},{9,25},... | collective-permute-start | bytes 787208 | tf_op jit(solution)/shard_map/ppermute | solution.py:147
  128.1 12.3 %collective-permute-start.3 = (bf16[2,2,32,3072]{3,2,1,0:T(8,128)(2,1)}, bf16[2,2,32,3072]{3,2,1,0:T(8,128)(2,1)}, u32[]{:S(2)}, u32[]{:S(2)}) collective-permute-start(bf16[2,2,32,3072]{3,2,1,0:T(8,128)(2,1)} %fusion.41), channel_id=1, source_target_pairs={{0,16},{1,5},{2,18},{3,7},{4,20},{5,1},{6,22},{7,3},{8,24},{9,13},... | collective-permute-start | bytes 2359304 | tf_op jit(solution)/shard_map/ppermute | solution.py:147
  137.3 6.5 %collective-permute-start.12 = (bf16[2,32,1025]{2,1,0:T(8,128)(2,1)S(1)}, bf16[2,32,1025]{2,1,0:T(8,128)(2,1)S(1)}, u32[]{:S(2)}, u32[]{:S(2)}) collective-permute-start(bf16[2,32,1025]{2,1,0:T(8,128)(2,1)S(1)} %fusion.70), channel_id=1, source_target_pairs={{0,16},{1,3},{2,18},{3,1},{4,20},{5,7},{6,22},{7,5},{8,24},{9,11},... | collective-permute-start | bytes 393608 | tf_op jit(solution)/shard_map/ppermute | solution.py:147
  142.3 10.0 %collective-permute-start.4 = (bf16[2,32,3072]{2,1,0:T(8,128)(2,1)S(1)}, bf16[2,32,3072]{2,1,0:T(8,128)(2,1)S(1)}, u32[]{:S(2)}, u32[]{:S(2)}) collective-permute-start(bf16[2,32,3072]{2,1,0:T(8,128)(2,1)S(1)} %fusion.54), channel_id=1, source_target_pairs={{0,4},{1,3},{2,6},{3,1},{4,0},{5,7},{6,2},{7,5},{8,12},{9,11},{10,... | collective-permute-start | bytes 1179656 | tf_op jit(solution)/shard_map/ppermute | solution.py:147
  143.9 9.5 %collective-permute-start.13 = (bf16[32,1025]{1,0:T(8,128)(2,1)S(1)}, bf16[32,1025]{1,0:T(8,128)(2,1)S(1)}, u32[]{:S(2)}, u32[]{:S(2)}) collective-permute-start(bf16[32,1025]{1,0:T(8,128)(2,1)S(1)} %fusion.76), channel_id=1, source_target_pairs={{0,8},{1,9},{2,10},{3,11},{4,12},{5,13},{6,14},{7,15},{8,0},{9,1},... | collective-permute-start | bytes 196808 | tf_op jit(solution)/shard_map/ppermute | solution.py:147
  152.4 8.3 %collective-permute-start.5 = (bf16[32,3072]{1,0:T(8,128)(2,1)S(1)}, bf16[32,3072]{1,0:T(8,128)(2,1)S(1)}, u32[]{:S(2)}, u32[]{:S(2)}) collective-permute-start(bf16[32,3072]{1,0:T(8,128)(2,1)S(1)} %fusion.69), channel_id=1, source_target_pairs={{0,8},{1,9},{2,10},{3,11},{4,12},{5,13},{6,14},{7,15},{8,0},{9,1},... | collective-permute-start | bytes 589832 | tf_op jit(solution)/shard_map/ppermute | solution.py:147
  153.4 8.3 %collective-permute-start.14 = (bf16[32,1025]{1,0:T(8,128)(2,1)S(1)}, bf16[32,1025]{1,0:T(8,128)(2,1)S(1)}, u32[]{:S(2)}, u32[]{:S(2)}) collective-permute-start(bf16[32,1025]{1,0:T(8,128)(2,1)S(1)} %fusion.71), channel_id=1, source_target_pairs={{0,16},{16,0},{1,17},{17,1},{2,18},{18,2},{3,19},{19,3},{4,20},{20... | collective-permute-start | bytes 196808 | tf_op jit(solution)/shard_map/ppermute | solution.py:153
  160.8 5.7 %collective-permute-start.6 = (bf16[32,3072]{1,0:T(8,128)(2,1)S(1)}, bf16[32,3072]{1,0:T(8,128)(2,1)S(1)}, u32[]{:S(2)}, u32[]{:S(2)}) collective-permute-start(bf16[32,3072]{1,0:T(8,128)(2,1)S(1)} %fusion.55), channel_id=1, source_target_pairs={{0,16},{16,0},{1,17},{17,1},{2,18},{18,2},{3,19},{19,3},{4,20},{20... | collective-permute-start | bytes 589832 | tf_op jit(solution)/shard_map/ppermute | solution.py:153
  (5 other events, 8.0 us)

commit v7 on v6

--- a/solution.py
+++ b/solution.py
@@ -112,7 +112,7 @@
     return jnp.where(core_odd, arrange(odd), arrange(even))
 
 
-def reduce_rows(parts, part_orders, seq_n, dp_n):
+def reduce_rows(parts, part_orders, seq_n, dp_n, tie):
     seq_at = lax.axis_index("seq")
     dp_at = lax.axis_index("dp")
     steps = len(part_orders[0][0])
@@ -133,7 +133,7 @@
         return ((seq_at if kind == "s" else dp_at) // (1 << k)) % 2
 
     for step in range(steps):
-        next_accs = []
+        perms, kepts, givens = [], [], []
         for acc, (even, odd) in zip(accs, part_orders):
             perm = []
             for dp_i in range(dp_n):
@@ -142,11 +142,17 @@
                     seq_j, dp_j = flip(item, seq_i, dp_i)
                     perm.append((dp_i * seq_n + seq_i, dp_j * seq_n + seq_j))
             keep_at = jnp.where(seq_at % 2 == 1, traced_bit(odd[step]), traced_bit(even[step]))
-            kept = lax.dynamic_index_in_dim(acc, keep_at, 0, keepdims=False)
-            given = lax.dynamic_index_in_dim(acc, 1 - keep_at, 0, keepdims=False).astype(jnp.bfloat16)
-            got = lax.ppermute(given, ("dp", "seq"), perm)
-            next_accs.append(kept + got.astype(jnp.float32))
-        accs = tuple(next_accs)
+            perms.append(perm)
+            kepts.append(lax.dynamic_index_in_dim(acc, keep_at, 0, keepdims=False))
+            givens.append(
+                lax.dynamic_index_in_dim(acc, 1 - keep_at, 0, keepdims=False).astype(jnp.bfloat16)
+            )
+        if step == 0:
+            givens, tie = lax.optimization_barrier((givens, tie))
+        accs = tuple(
+            kept + lax.ppermute(given, ("dp", "seq"), perm).astype(jnp.float32)
+            for kept, given, perm in zip(kepts, givens, perms)
+        )
     accs = tuple(acc.astype(jnp.bfloat16) for acc in accs)
     for step in range(dp_n.bit_length() - 1):
         perm = [(member, member ^ (1 << step)) for member in range(dp_n)]
@@ -156,7 +162,7 @@
             jnp.where(upper, jnp.concatenate([g, acc], axis=0), jnp.concatenate([acc, g], axis=0))
             for acc, g in zip(accs, got)
         )
-    return accs
+    return accs, tie
 
 
 def on_device(first_query, first_key, first_value, out_weight, norm_gain, joint_weight, upstream):
@@ -230,31 +236,30 @@
         tiled=True,
     )
     grad_normed = grad_normed.reshape(-1, model_width)
-    joint_term, grad_normed = lax.optimization_barrier((joint_term, grad_normed))
+    (joint_sum,), grad_normed = reduce_rows((joint_term,), (orders,), seq_n, dp_n, grad_normed)
     grad_float = grad_normed.astype(jnp.float32)
     gain_term = jnp.sum(grad_float * hidden * inverse, axis=0)
     scaled = norm_gain * grad_float
     grad_hidden = (
         inverse * scaled - hidden * inverse**3 * jnp.mean(scaled * hidden, axis=-1, keepdims=True)
     ).astype(jnp.bfloat16)
-    out_cols, grad_hidden = lax.optimization_barrier((out_cols, grad_hidden))
+    first_peer, hidden_peer, gain_peer = lax.ppermute((flat_first, grad_hidden, gain_term), "seq", pair)
+    out_term = jnp.dot(
+        my_half(jnp.concatenate([flat_first, first_peer], axis=0), out_orders).T,
+        jnp.concatenate([grad_hidden, hidden_peer], axis=0),
+        preferred_element_type=jnp.float32,
+    )
+    gain_term = my_half((gain_term + gain_peer)[None, :], out_orders)[0][:, None]
+    out_width = out_term.shape[1]
+    (out_sum,), out_cols = reduce_rows(
+        (jnp.concatenate([out_term, gain_term], axis=1),), (out_orders,), seq_n, dp_n, out_cols
+    )
     column_out = lax.all_to_all(
         out_cols.reshape(batches, all_rows, col_share, feature),
         "seq",
         split_axis=1,
         concat_axis=2,
         tiled=True,
-    )
-    first_peer, hidden_peer, gain_peer = lax.ppermute((flat_first, grad_hidden, gain_term), "seq", pair)
-    out_term = jnp.dot(
-        my_half(jnp.concatenate([flat_first, first_peer], axis=0), out_orders).T,
-        jnp.concatenate([grad_hidden, hidden_peer], axis=0),
-        preferred_element_type=jnp.float32,
-    )
-    gain_term = my_half((gain_term + gain_peer)[None, :], out_orders)[0][:, None]
-    out_width = out_term.shape[1]
-    joint_sum, out_sum = reduce_rows(
-        (joint_term, jnp.concatenate([out_term, gain_term], axis=1)), (orders, out_orders), seq_n, dp_n
     )
     replicas = (joint_sum, out_sum[:, :out_width], out_sum[:, out_width].astype(jnp.float32))
     grad_first = jnp.dot(grad_hidden, out_weight.T, preferred_element_type=jnp.float32).astype(

time: 171 us -> 162 us (0.947)
  waiting for transfers between devices: 33.4 us -> 26.8 us
  matrix products: 41.8 us -> 39.6 us
    ppermute x8, waiting for transfers between devices: 21.8 us -> 16.5 us  [reduce_rows(): lax.ppermute(given, ('dp', 'seq'), perm).astype(jnp.float32)]
    dot_general x1, matrix products: 4.8 us -> 2.14 us  [on_device(): jnp.dot(my_half(jnp.concatenate([used_normed, normed_peer], axis=0)).T, j...]
    unnamed x48 -> x54, local copies, waits for them, and re-layouts: 18 us -> 20.7 us
    convert_element_type x7, local copies, waits for them, and re-layouts: 5.1 us -> 3.29 us  [reduce_rows(): lax.dynamic_index_in_dim(acc, 1 - keep_at, 0, keepdims=False)]
  transfers between devices with their start and end apart: 19 -> 19, of which waited for: 7 -> 7; matrix products, arithmetic and copies ran while one was open for 38% -> 39% of each run, Pallas kernels for 0% -> 0%
where the time goes in v7:
time: 162 us; the launch traced here: 161 us
  matrix products  39.6 us (24%)
  starting transfers between devices  36.5 us (23%)
  local copies, waits for them, and re-layouts  35.3 us (22%)
  waiting for transfers between devices  26.8 us (17%)
  other arithmetic  21.7 us (13%)
    unnamed x54, local copies, waits for them, and re-layouts  20.7 us
    ppermute x8, waiting for transfers between devices, reduce_rows(): lax.ppermute(given, ('dp', 'seq'), perm).astype(jnp.float32)  16.5 us
    ppermute x8, starting transfers between devices, reduce_rows(): lax.ppermute(given, ('dp', 'seq'), perm).astype(jnp.float32)  11.7 us
    all_to_all x1, starting transfers between devices, on_device(): lax.all_to_all(upstream, 'seq', split_axis=2, concat_axis=1, tiled=True)  7.39 us
    add x6, other arithmetic, reduce_rows(): kept + lax.ppermute(given, ('dp', 'seq'), perm).astype(jnp.float32)  7.28 us
    all_to_all x1, waiting for transfers between devices, on_device(): lax.all_to_all(normed.reshape(batches, local_rows, columns, model_width),...  6.19 us
    all_to_all x1, starting transfers between devices, on_device(): lax.all_to_all(normed.reshape(batches, local_rows, columns, model_width),...  5.86 us
    dot_general x1, matrix products, on_device(): jnp.dot(used_grads, joint_weight.T, preferred_element_type=jnp.float32)  5.68 us
  transfers between devices with their start and end apart: 19, of which 7 were waited for; matrix products, arithmetic and copies ran while one was open for 39% of the time, Pallas kernels for 0%

profile of v7, /device:TPU:0, one launch (start us, length us, event | category | flops | bytes accessed | tf_op | source)
XLA Modules:
  0.0 160.9 jit_solution(4468088092045372894)
XLA Ops:
  2.7 2.1 %reduce.20 = bf16[128,1024]{1,0:T(8,128)(2,1)S(1)} reduce(bf16[128,1,1,1024]{3,2,1,0:T(2,128)(2,1)S(1)} %bitcast.188, bf16[]{:T(256)} %broadcast.113), dimensions={1,2}, to_apply=%bitcast.180.reduce_sub_computation | reduce | bytes 524290
  5.7 7.4 %all-to-all-start.1 = ((bf16[16,2,4096]{2,1,0:T(2,128)(2,1)}), bf16[16,2,4096]{2,1,0:T(2,128)(2,1)S(1)}, u32[]{:S(2)}, u32[]{:S(2)}) async-start(bf16[16,2,4096]{2,1,0:T(2,128)(2,1)} %reshape.311), calls=%async_computation.1 | async-start | bytes 524288 | tf_op jit(solution)/shard_map/all_to_all | solution.py:201
  16.7 2.0 %convolution_convert_fusion.3 = bf16[8,128,128]{1,2,0:T(8,128)(2,1)} fusion(bf16[128,8,128]{2,1,0:T(8,128)(2,1)} %bitcast.197, f32[8,128]{1,0:T(8,128)S(1)} %get-tuple-element.52, f32[8,128,128]{1,2,0:T(8,128)S(1)} %fusion.20), kind=kOutput, calls=%fused_computation.37 | convolution fusion | flops 34079872 | bytes 1052672 | tf_op jit(solution)/shard_map/ghlm,gmhe->glhe/dot_general | solution.py:31
  21.2 2.9 %reduce.21 = bf16[128,1024]{1,0:T(8,128)(2,1)} reduce(bf16[128,1,1,1024]{3,2,1,0:T(2,128)(2,1)S(1)} %bitcast.189, bf16[]{:T(256)} %broadcast.113), dimensions={1,2}, to_apply=%bitcast.181.reduce_sub_computation | reduce | bytes 524290
  24.0 1.8 %reshape.313 = bf16[16,2,4096]{2,1,0:T(2,128)(2,1)} reshape(bf16[128,1024]{1,0:T(8,128)(2,1)} %reduce.21) | data formatting | bytes 524288
  25.9 5.9 %all-to-all-start = ((bf16[16,2,4096]{2,1,0:T(2,128)(2,1)}), bf16[16,2,4096]{2,1,0:T(2,128)(2,1)}, u32[]{:S(2)}, u32[]{:S(2)}) async-start(bf16[16,2,4096]{2,1,0:T(2,128)(2,1)} %reshape.313), calls=%async_computation | async-start | bytes 524288 | tf_op jit(solution)/shard_map/all_to_all | solution.py:184
  35.6 6.2 %all-to-all-done = bf16[16,2,4096]{2,1,0:T(2,128)(2,1)} async-done(((bf16[16,2,4096]{2,1,0:T(2,128)(2,1)}), bf16[16,2,4096]{2,1,0:T(2,128)(2,1)}, u32[]{:S(2)}, u32[]{:S(2)}) %all-to-all-start) | async-done | bytes 262176 | tf_op jit(solution)/shard_map/all_to_all | solution.py:184
  41.8 2.2 %reshape.314 = bf16[128,1,1,1024]{3,2,1,0:T(2,128)(2,1)S(1)} reshape(bf16[16,2,4096]{2,1,0:T(2,128)(2,1)} %all-to-all-done) | data formatting | bytes 524288
  45.1 3.9 %convolution_convert_fusion = bf16[128,3072]{1,0:T(8,128)(2,1)S(1)} fusion(bf16[1024,3072]{1,0:T(8,128)(2,1)} %param.12, bf16[1,1,128,1024]{2,3,1,0:T(8,128)(2,1)} %copy.112), kind=kOutput, calls=%fused_computation.4 | convolution fusion | flops 805699584 | bytes 7340032 | tf_op jit(solution)/shard_map/dot_general | solution.py:191
  51.0 2.5 %fusion.94 = (f32[8,8,16]{2,1,0:T(8,128)S(1)}, f32[8,8,16,16]{2,3,1,0:T(8,128)}) fusion(pred[16,16]{0,1:T(8,128)(4,1)S(1)} %iota_compare_fusion.1, bf16[1,16,8,1,8,128]{5,2,4,3,1,0:T(8,128)(2,1)S(1)} %get-tuple-element.47, bf16[1,16,8,1,8,128]{5,2,4,3,1,0:T(8,128)(2,1)} %get-tuple-element.46), kind=kOutput, calls=%fused_computation.149 | convolution fusion | flops 4259855 | bytes 594176 | tf_op jit(solution)/shard_map/sub | solution.py:28
  53.6 2.1 %fusion.29 = bf16[1,16,8,1,8,128]{5,1,4,2,3,0:T(8,128)(2,1)} fusion(bf16[16,8,8,128]{3,2,1,0:T(8,128)(2,1)S(1)} %copy.190, f32[8,8,16,16]{2,3,1,0:T(8,128)} %get-tuple-element.57, f32[8,8,16]{2,1,0:T(8,128)S(1)} %get-tuple-element.56), kind=kOutput, calls=%fused_computation.51 | convolution fusion | flops 4358144 | bytes 593920 | tf_op jit(solution)/shard_map/bchlm,blche->bmche/dot_general | solution.py:64
  55.7 2.9 %fusion.32 = bf16[1,16,8,1,8,128]{5,1,4,2,3,0:T(8,128)(2,1)} fusion(f32[8,8,16,16]{2,3,1,0:T(8,128)} %convolution_bitcast_fusion, bf16[1,16,8,1,8,128]{5,2,4,3,1,0:T(8,128)(2,1)} %get-tuple-element.46, f32[8,8,16,16]{2,3,1,0:T(8,128)} %get-tuple-element.57, f32[8,8,16]{2,1,0:T(8,128)S(1)} %get-tuple-element.56), kind=kOutput, calls=%fused_computation.54 | convolution fusion | flops 4441103 | bytes 659456 | tf_op jit(solution)/shard_map/bchlm,blche->bmche/dot_general | solution.py:57
  58.5 2.5 %fusion.28 = bf16[1,16,8,1,8,128]{5,1,4,2,3,0:T(8,128)(2,1)} fusion(f32[8,8,16,16]{2,3,1,0:T(8,128)S(1)} %copy-done.14, bf16[1,16,8,1,8,128]{5,2,4,3,1,0:T(8,128)(2,1)} %copy-done.18, f32[8,8,16,16]{2,3,1,0:T(8,128)} %get-tuple-element.57, f32[8,8,16]{2,1,0:T(8,128)S(1)} %get-tuple-element.56), kind=kOutput, calls=%fused_computation.50 | convolution fusion | flops 4441103 | bytes 659456 | tf_op jit(solution)/shard_map/bchlm,bmche->blche/dot_general | solution.py:51
  65.2 5.7 %fusion.30 = bf16[1,16,8,1024]{3,2,0,1:T(8,128)(2,1)} fusion(bf16[128,3072]{1,0:T(8,128)(2,1)S(1)} %reshape_reshape.7, bf16[1024,3072]{1,0:T(8,128)(2,1)} %param.12), kind=kOutput, calls=%fused_computation.52 | convolution fusion | flops 805437440 | bytes 7340032 | tf_op jit(solution)/shard_map/dot_general | solution.py:209
  70.9 4.4 %all-to-all-start.2 = ((bf16[1,16,8,1024]{3,2,0,1:T(8,128)(2,1)}), bf16[1,16,8,1024]{3,2,0,1:T(8,128)(2,1)}, u32[]{:S(2)}, u32[]{:S(2)}) async-start(bf16[1,16,8,1024]{3,2,0,1:T(8,128)(2,1)} %fusion.30), calls=%async_computation.2 | async-start | bytes 524288 | tf_op jit(solution)/shard_map/all_to_all | solution.py:231
  75.3 2.2 %fusion.31 = bf16[1,16,8,8,128]{4,1,3,2,0:T(8,128)(2,1)} fusion(bf16[1,16,8,1,8,128]{5,2,4,3,1,0:T(8,128)(2,1)} %copy-done.13, f32[8,8,16,16]{2,3,1,0:T(8,128)} %get-tuple-element.57, f32[8,8,16]{2,1,0:T(8,128)S(1)} %get-tuple-element.56), kind=kOutput, calls=%fused_computation.53 | convolution fusion | flops 4358144 | bytes 593920 | tf_op jit(solution)/shard_map/bchlm,bmche->blche/dot_general | solution.py:31
  78.7 2.1 %fusion.5 = f32[512,3072]{1,0:T(8,128)S(1)} fusion(bf16[128,3072]{1,0:T(8,128)(2,1)} %collective-permute-done.1, bf16[128,3072]{1,0:T(8,128)(2,1)S(1)} %reshape_reshape.7, bf16[256,1024]{0,1:T(8,128)(2,1)S(1)} %bitcast.191, s32[]{:T(128)S(6)} %select_n.231), kind=kOutput, calls=%fused_computation.12 | convolution fusion | flops 808452096 | bytes 8126468 | tf_op jit(solution)/shard_map/dot_general | solution.py:226
  80.9 2.7 %copy-done.1 = f32[512,3072]{1,0:T(8,128)} copy-done((f32[512,3072]{1,0:T(8,128)}, f32[512,3072]{1,0:T(8,128)S(1)}, u32[]{:S(2)}) %copy-start.1) | copy-done | bytes 6291480
  97.7 2.6 %convolution_convert_fusion.1 = bf16[8,128,128]{1,2,0:T(8,128)(2,1)} fusion(bf16[128,8,128]{0,2,1:T(8,128)(2,1)S(1)} %bitcast.196, f32[8,128,128]{1,2,0:T(8,128)} %fusion.65, f32[8,128,128]{1,2,0:T(8,128)} %get-tuple-element.53, f32[8,128]{1,0:T(8,128)S(1)} %get-tuple-element.52), kind=kOutput, calls=%fused_computation.35 | convolution fusion | flops 34604160 | bytes 1576960 | tf_op jit(solution)/shard_map/ghlm,gmhe->glhe/dot_general | solution.py:51
  100.3 2.6 %convolution_convert_fusion.6 = bf16[8,128,128]{1,2,0:T(8,128)(2,1)} fusion(bf16[128,8,128]{0,2,1:T(8,128)(2,1)S(1)} %bitcast.194, f32[8,128,128]{1,2,0:T(8,128)} %fusion.65, f32[8,128,128]{1,2,0:T(8,128)} %get-tuple-element.53, f32[8,128]{1,0:T(8,128)S(1)} %get-tuple-element.52), kind=kOutput, calls=%fused_computation.40 | convolution fusion | flops 34604160 | bytes 1576960 | tf_op jit(solution)/shard_map/ghlm,glhe->gmhe/dot_general | solution.py:57
  103.8 4.2 %all-to-all-start.3 = ((bf16[1,16,8,1024]{3,2,0,1:T(8,128)(2,1)}), bf16[1,16,8,1024]{3,2,0,1:T(8,128)(2,1)}, u32[]{:S(2)}, u32[]{:S(2)}) async-start(bf16[1,16,8,1024]{3,2,0,1:T(8,128)(2,1)} %bitcast.58), calls=%async_computation.3 | async-start | bytes 524288 | tf_op jit(solution)/shard_map/all_to_all | solution.py:257
  108.0 2.6 %collective-permute-done.10 = bf16[2,2,2,32,1025]{4,3,2,1,0:T(8,128)(2,1)} collective-permute-done((bf16[2,2,2,32,1025]{4,3,2,1,0:T(8,128)(2,1)}, bf16[2,2,2,32,1025]{4,3,2,1,0:T(8,128)(2,1)}, u32[]{:S(2)}, u32[]{:S(2)}) %collective-permute-start.10) | collective-permute-done | bytes 524832 | tf_op jit(solution)/shard_map/ppermute | solution.py:153
  114.4 2.8 %bitcast_add_fusion = f32[2,2,2,32,3072]{4,3,2,1,0:T(8,128)S(1)} fusion(bf16[2,2,2,32,3072]{4,3,2,1,0:T(8,128)(2,1)} %collective-permute-done.5, f32[2,2,2,2,32,3072]{5,4,3,2,1,0:T(8,128)} %bitcast.183, s32[]{:T(128)S(6)} %select_n.247), kind=kLoop, calls=%fused_computation.7 | loop fusion | flops 1572864 | bytes 7864324 | tf_op jit(solution)/shard_map/add | solution.py:153
  120.4 2.2 %convolution_convert_fusion.5 = bf16[8,128,128]{2,1,0:T(8,128)(2,1)} fusion(bf16[128,8,128]{0,2,1:T(8,128)(2,1)S(1)} %bitcast.200, f32[8,128]{1,0:T(8,128)S(1)} %get-tuple-element.52, f32[8,128,128]{1,2,0:T(8,128)} %copy-done.4), kind=kOutput, calls=%fused_computation.39 | convolution fusion | flops 34079872 | bytes 1052672 | tf_op jit(solution)/shard_map/ghlm,glhe->gmhe/dot_general | solution.py:64
  122.7 1.8 %copy.144 = bf16[1,1,128,1024]{3,2,1,0:T(8,128)(2,1)} copy(bf16[1,1,128,1024]{2,3,1,0:T(8,128)(2,1)} %bitcast.203) | data formatting | bytes 524288
  124.4 1.8 %copy.143 = bf16[1,1,128,1024]{3,2,1,0:T(8,128)(2,1)} copy(bf16[1,1,128,1024]{2,3,1,0:T(8,128)(2,1)} %bitcast.202) | data formatting | bytes 524288
  126.2 1.8 %copy.145 = bf16[1,1,128,1024]{3,2,1,0:T(8,128)(2,1)} copy(bf16[1,1,128,1024]{2,3,1,0:T(8,128)(2,1)} %bitcast.204) | data formatting | bytes 524288
  132.2 1.8 %bitcast_add_fusion.1 = f32[2,2,32,3072]{3,2,1,0:T(8,128)S(1)} fusion(bf16[2,2,32,3072]{3,2,1,0:T(8,128)(2,1)} %collective-permute-done.6, f32[2,2,2,32,3072]{4,3,2,1,0:T(8,128)} %copy-done.3, s32[]{:T(128)S(6)} %select_n.249), kind=kLoop, calls=%fused_computation.16 | loop fusion | flops 786432 | bytes 3932164 | tf_op jit(solution)/shard_map/add | solution.py:153
  135.8 2.8 %collective-permute-start.13 = (bf16[32,1025]{1,0:T(8,128)(2,1)S(1)}, bf16[32,1025]{1,0:T(8,128)(2,1)S(1)}, u32[]{:S(2)}, u32[]{:S(2)}) collective-permute-start(bf16[32,1025]{1,0:T(8,128)(2,1)S(1)} %fusion.76), channel_id=1, source_target_pairs={{0,8},{1,9},{2,10},{3,11},{4,12},{5,13},{6,14},{7,15},{8,0},{9,1},... | collective-permute-start | bytes 196808 | tf_op jit(solution)/shard_map/ppermute | solution.py:153
  138.7 5.4 %collective-permute-done.7 = bf16[2,32,3072]{2,1,0:T(8,128)(2,1)S(1)} collective-permute-done((bf16[2,32,3072]{2,1,0:T(8,128)(2,1)S(1)}, bf16[2,32,3072]{2,1,0:T(8,128)(2,1)S(1)}, u32[]{:S(2)}, u32[]{:S(2)}) %collective-permute-start.7) | collective-permute-done | bytes 393248 | tf_op jit(solution)/shard_map/ppermute | solution.py:153
  145.7 6.9 %collective-permute-done.8 = bf16[32,3072]{1,0:T(8,128)(2,1)S(1)} collective-permute-done((bf16[32,3072]{1,0:T(8,128)(2,1)S(1)}, bf16[32,3072]{1,0:T(8,128)(2,1)S(1)}, u32[]{:S(2)}, u32[]{:S(2)}) %collective-permute-start.8) | collective-permute-done | bytes 196640 | tf_op jit(solution)/shard_map/ppermute | solution.py:153
  154.6 3.8 %collective-permute-done.9 = bf16[32,3072]{1,0:T(8,128)(2,1)S(1)} collective-permute-done((bf16[32,3072]{1,0:T(8,128)(2,1)S(1)}, bf16[32,3072]{1,0:T(8,128)(2,1)S(1)}, u32[]{:S(2)}, u32[]{:S(2)}) %collective-permute-start.9) | collective-permute-done | bytes 196640 | tf_op jit(solution)/shard_map/ppermute | solution.py:159
  (133 shorter events, 55.2 us)
Async XLA Ops:
  0.6 18.5 %copy-start = (bf16[1024,1024]{1,0:T(8,128)(2,1)S(1)}, bf16[1024,1024]{1,0:T(8,128)(2,1)}, u32[]{:S(2)}) copy-start(bf16[1024,1024]{1,0:T(8,128)(2,1)} %param.10) | copy-start | bytes 6291460
  0.6 12.5 %copy-start.15 = (bf16[1,1,128,1024]{3,2,1,0:T(8,128)(2,1)S(1)}, bf16[1,1,128,1024]{3,2,1,0:T(8,128)(2,1)}, u32[]{:S(2)}) copy-start(bf16[1,1,128,1024]{3,2,1,0:T(8,128)(2,1)} %param.7) | copy-start | bytes 786436
  4.8 9.7 %copy-start.16 = (bf16[1,1,128,1024]{3,2,1,0:T(8,128)(2,1)S(1)}, bf16[1,1,128,1024]{3,2,1,0:T(8,128)(2,1)}, u32[]{:S(2)}) copy-start(bf16[1,1,128,1024]{3,2,1,0:T(8,128)(2,1)} %param.9) | copy-start | bytes 786436
  5.7 20.1 %all-to-all-start.1 = ((bf16[16,2,4096]{2,1,0:T(2,128)(2,1)}), bf16[16,2,4096]{2,1,0:T(2,128)(2,1)S(1)}, u32[]{:S(2)}, u32[]{:S(2)}) async-start(bf16[16,2,4096]{2,1,0:T(2,128)(2,1)} %reshape.311), calls=%async_computation.1 | async-start | bytes 524288 | tf_op jit(solution)/shard_map/all_to_all | solution.py:201
  13.3 5.3 %copy-start.6 = (bf16[1,1,128,1024]{2,3,1,0:T(8,128)(2,1)}, bf16[1,1,128,1024]{2,3,1,0:T(8,128)(2,1)S(1)}, u32[]{:S(2)}) copy-start(bf16[1,1,128,1024]{2,3,1,0:T(8,128)(2,1)S(1)} %copy.158) | copy-start | bytes 786436
  14.6 4.1 %copy-start.8 = (bf16[1,1,128,1024]{2,3,1,0:T(8,128)(2,1)}, bf16[1,1,128,1024]{2,3,1,0:T(8,128)(2,1)S(1)}, u32[]{:S(2)}) copy-start(bf16[1,1,128,1024]{2,3,1,0:T(8,128)(2,1)S(1)} %copy.157) | copy-start | bytes 786436
  18.7 13.1 %collective-permute-start.2 = (bf16[128,1024]{0,1:T(8,128)(2,1)}, bf16[128,1024]{0,1:T(8,128)(2,1)}, u32[]{:S(2)}, u32[]{:S(2)}) collective-permute-start(bf16[128,1024]{0,1:T(8,128)(2,1)} %bitcast.3), channel_id=1, source_target_pairs={{0,1},{1,0},{2,3},{3,2},{4,5},{5,4},{6,7},{7,6},{8,9},{9,8},{10,11... | collective-permute-start | bytes 786440 | tf_op jit(solution)/shard_map/ppermute | solution.py:246
  25.9 16.0 %all-to-all-start = ((bf16[16,2,4096]{2,1,0:T(2,128)(2,1)}), bf16[16,2,4096]{2,1,0:T(2,128)(2,1)}, u32[]{:S(2)}, u32[]{:S(2)}) async-start(bf16[16,2,4096]{2,1,0:T(2,128)(2,1)} %reshape.313), calls=%async_computation | async-start | bytes 524288 | tf_op jit(solution)/shard_map/all_to_all | solution.py:184
  49.7 3.9 %copy-start.18 = (bf16[1,16,8,1,8,128]{5,2,4,3,1,0:T(8,128)(2,1)}, bf16[1,16,8,1,8,128]{5,2,4,3,1,0:T(8,128)(2,1)S(1)}, u32[]{:S(2)}) copy-start(bf16[1,16,8,1,8,128]{5,2,4,3,1,0:T(8,128)(2,1)S(1)} %get-tuple-element.47) | copy-start | bytes 786436
  49.7 5.9 %copy-start.13 = (bf16[1,16,8,1,8,128]{5,2,4,3,1,0:T(8,128)(2,1)}, bf16[1,16,8,1,8,128]{5,2,4,3,1,0:T(8,128)(2,1)S(1)}, u32[]{:S(2)}) copy-start(bf16[1,16,8,1,8,128]{5,2,4,3,1,0:T(8,128)(2,1)S(1)} %get-tuple-element.45) | copy-start | bytes 786436
  61.0 16.5 %collective-permute-start = (bf16[128,1024]{0,1:T(8,128)(2,1)}, bf16[128,1024]{0,1:T(8,128)(2,1)}, u32[]{:S(2)}, u32[]{:S(2)}) collective-permute-start(bf16[128,1024]{0,1:T(8,128)(2,1)} %bitcast.6), channel_id=1, source_target_pairs={{0,1},{1,0},{2,3},{3,2},{4,5},{5,4},{6,7},{7,6},{8,9},{9,8},{10,11... | collective-permute-start | bytes 786440 | tf_op jit(solution)/shard_map/ppermute | solution.py:225
  64.7 14.0 %collective-permute-start.1 = (bf16[128,3072]{1,0:T(8,128)(2,1)S(1)}, bf16[128,3072]{1,0:T(8,128)(2,1)}, u32[]{:S(2)}, u32[]{:S(2)}) collective-permute-start(bf16[128,3072]{1,0:T(8,128)(2,1)S(1)} %reshape_reshape.7), channel_id=1, source_target_pairs={{0,1},{1,0},{2,3},{3,2},{4,5},{5,4},{6,7},{7,6},{8,9},{9,8},{10,11... | collective-permute-start | bytes 2359304 | tf_op jit(solution)/shard_map/ppermute | solution.py:225
  70.9 14.3 %all-to-all-start.2 = ((bf16[1,16,8,1024]{3,2,0,1:T(8,128)(2,1)}), bf16[1,16,8,1024]{3,2,0,1:T(8,128)(2,1)}, u32[]{:S(2)}, u32[]{:S(2)}) async-start(bf16[1,16,8,1024]{3,2,0,1:T(8,128)(2,1)} %fusion.30), calls=%async_computation.2 | async-start | bytes 524288 | tf_op jit(solution)/shard_map/all_to_all | solution.py:231
  86.3 4.8 %collective-permute-start.4 = (f32[1024]{0:T(1024)S(1)}, f32[1024]{0:T(1024)S(1)}, u32[]{:S(2)}, u32[]{:S(2)}) collective-permute-start(f32[1024]{0:T(1024)S(1)} %get-tuple-element.43), channel_id=1, source_target_pairs={{0,1},{1,0},{2,3},{3,2},{4,5},{5,4},{6,7},{7,6},{8,9},{9,8},{10,11... | collective-permute-start | bytes 12296 | tf_op jit(solution)/shard_map/ppermute | solution.py:246
  87.5 4.0 %copy-start.5 = (bf16[256,2,2,2,2,2,32]{0,6,5,4,3,2,1:T(8,128)(2,1)S(1)}, bf16[256,2,2,2,2,2,32]{0,6,5,4,3,2,1:T(8,128)(2,1)}, u32[]{:S(2)}) copy-start(bf16[256,2,2,2,2,2,32]{0,6,5,4,3,2,1:T(8,128)(2,1)} %copy.136) | copy-start | bytes 1572868
  87.5 4.0 %collective-permute-start.3 = (bf16[128,1024]{1,0:T(8,128)(2,1)S(1)}, bf16[128,1024]{1,0:T(8,128)(2,1)}, u32[]{:S(2)}, u32[]{:S(2)}) collective-permute-start(bf16[128,1024]{1,0:T(8,128)(2,1)S(1)} %fusion.46), channel_id=1, source_target_pairs={{0,1},{1,0},{2,3},{3,2},{4,5},{5,4},{6,7},{7,6},{8,9},{9,8},{10,11... | collective-permute-start | bytes 786440 | tf_op jit(solution)/shard_map/ppermute | solution.py:246
  89.7 24.6 %collective-permute-start.5 = (bf16[2,2,2,32,3072]{4,3,2,1,0:T(8,128)(2,1)}, bf16[2,2,2,32,3072]{4,3,2,1,0:T(8,128)(2,1)}, u32[]{:S(2)}, u32[]{:S(2)}) collective-permute-start(bf16[2,2,2,32,3072]{4,3,2,1,0:T(8,128)(2,1)} %fusion.4), channel_id=1, source_target_pairs={{0,2},{1,17},{2,0},{3,19},{4,6},{5,21},{6,4},{7,23},{8,10},{9,25},... | collective-permute-start | bytes 4718600 | tf_op jit(solution)/shard_map/ppermute | solution.py:153
  93.0 3.7 %copy-start.10 = (bf16[16,8,8,128]{3,2,1,0:T(8,128)(2,1)S(1)}, bf16[16,8,8,128]{3,2,1,0:T(8,128)(2,1)}, u32[]{:S(2)}) copy-start(bf16[16,8,8,128]{3,2,1,0:T(8,128)(2,1)} %copy.160) | copy-start | bytes 786436
  93.0 4.7 %copy-start.9 = (bf16[1,1,128,1024]{2,3,1,0:T(8,128)(2,1)S(1)}, bf16[1,1,128,1024]{2,3,1,0:T(8,128)(2,1)}, u32[]{:S(2)}) copy-start(bf16[1,1,128,1024]{2,3,1,0:T(8,128)(2,1)} %copy-done.8) | copy-start | bytes 786436
  95.2 5.1 %copy-start.7 = (bf16[1,1,128,1024]{2,3,1,0:T(8,128)(2,1)S(1)}, bf16[1,1,128,1024]{2,3,1,0:T(8,128)(2,1)}, u32[]{:S(2)}) copy-start(bf16[1,1,128,1024]{2,3,1,0:T(8,128)(2,1)} %copy-done.6) | copy-start | bytes 786436
  95.2 15.5 %collective-permute-start.10 = (bf16[2,2,2,32,1025]{4,3,2,1,0:T(8,128)(2,1)}, bf16[2,2,2,32,1025]{4,3,2,1,0:T(8,128)(2,1)}, u32[]{:S(2)}, u32[]{:S(2)}) collective-permute-start(bf16[2,2,2,32,1025]{4,3,2,1,0:T(8,128)(2,1)} %fusion.44), channel_id=1, source_target_pairs={{0,4},{1,5},{2,6},{3,7},{4,0},{5,1},{6,2},{7,3},{8,12},{9,13},{10,... | collective-permute-start | bytes 1574408 | tf_op jit(solution)/shard_map/ppermute | solution.py:153
  97.7 5.2 %copy-start.17 = (bf16[1,16,8,8,128]{4,1,3,2,0:T(8,128)(2,1)S(1)}, bf16[1,16,8,8,128]{4,1,3,2,0:T(8,128)(2,1)}, u32[]{:S(2)}) copy-start(bf16[1,16,8,8,128]{4,1,3,2,0:T(8,128)(2,1)} %fusion.31) | copy-start | bytes 786436
  103.8 24.2 %all-to-all-start.3 = ((bf16[1,16,8,1024]{3,2,0,1:T(8,128)(2,1)}), bf16[1,16,8,1024]{3,2,0,1:T(8,128)(2,1)}, u32[]{:S(2)}, u32[]{:S(2)}) async-start(bf16[1,16,8,1024]{3,2,0,1:T(8,128)(2,1)} %bitcast.58), calls=%async_computation.3 | async-start | bytes 524288 | tf_op jit(solution)/shard_map/all_to_all | solution.py:257
  112.9 7.5 %copy-start.12 = (bf16[128,1024]{0,1:T(8,128)(2,1)S(1)}, bf16[128,1024]{0,1:T(8,128)(2,1)}, u32[]{:S(2)}) copy-start(bf16[128,1024]{0,1:T(8,128)(2,1)} %copy.159) | copy-start | bytes 786436
  112.9 15.1 %collective-permute-start.11 = (bf16[2,2,32,1025]{3,2,1,0:T(8,128)(2,1)}, bf16[2,2,32,1025]{3,2,1,0:T(8,128)(2,1)}, u32[]{:S(2)}, u32[]{:S(2)}) collective-permute-start(bf16[2,2,32,1025]{3,2,1,0:T(8,128)(2,1)} %fusion.56), channel_id=1, source_target_pairs={{0,2},{1,17},{2,0},{3,19},{4,6},{5,21},{6,4},{7,23},{8,10},{9,25},... | collective-permute-start | bytes 787208 | tf_op jit(solution)/shard_map/ppermute | solution.py:153
  119.9 12.3 %collective-permute-start.6 = (bf16[2,2,32,3072]{3,2,1,0:T(8,128)(2,1)}, bf16[2,2,32,3072]{3,2,1,0:T(8,128)(2,1)}, u32[]{:S(2)}, u32[]{:S(2)}) collective-permute-start(bf16[2,2,32,3072]{3,2,1,0:T(8,128)(2,1)} %fusion.41), channel_id=1, source_target_pairs={{0,16},{1,5},{2,18},{3,7},{4,20},{5,1},{6,22},{7,3},{8,24},{9,13},... | collective-permute-start | bytes 2359304 | tf_op jit(solution)/shard_map/ppermute | solution.py:153
  129.1 6.7 %collective-permute-start.12 = (bf16[2,32,1025]{2,1,0:T(8,128)(2,1)S(1)}, bf16[2,32,1025]{2,1,0:T(8,128)(2,1)S(1)}, u32[]{:S(2)}, u32[]{:S(2)}) collective-permute-start(bf16[2,32,1025]{2,1,0:T(8,128)(2,1)S(1)} %fusion.70), channel_id=1, source_target_pairs={{0,16},{1,3},{2,18},{3,1},{4,20},{5,7},{6,22},{7,5},{8,24},{9,11},... | collective-permute-start | bytes 393608 | tf_op jit(solution)/shard_map/ppermute | solution.py:153
  134.1 10.0 %collective-permute-start.7 = (bf16[2,32,3072]{2,1,0:T(8,128)(2,1)S(1)}, bf16[2,32,3072]{2,1,0:T(8,128)(2,1)S(1)}, u32[]{:S(2)}, u32[]{:S(2)}) collective-permute-start(bf16[2,32,3072]{2,1,0:T(8,128)(2,1)S(1)} %fusion.54), channel_id=1, source_target_pairs={{0,4},{1,3},{2,6},{3,1},{4,0},{5,7},{6,2},{7,5},{8,12},{9,11},{10,... | collective-permute-start | bytes 1179656 | tf_op jit(solution)/shard_map/ppermute | solution.py:153
  135.8 9.2 %collective-permute-start.13 = (bf16[32,1025]{1,0:T(8,128)(2,1)S(1)}, bf16[32,1025]{1,0:T(8,128)(2,1)S(1)}, u32[]{:S(2)}, u32[]{:S(2)}) collective-permute-start(bf16[32,1025]{1,0:T(8,128)(2,1)S(1)} %fusion.76), channel_id=1, source_target_pairs={{0,8},{1,9},{2,10},{3,11},{4,12},{5,13},{6,14},{7,15},{8,0},{9,1},... | collective-permute-start | bytes 196808 | tf_op jit(solution)/shard_map/ppermute | solution.py:153
  144.2 8.4 %collective-permute-start.8 = (bf16[32,3072]{1,0:T(8,128)(2,1)S(1)}, bf16[32,3072]{1,0:T(8,128)(2,1)S(1)}, u32[]{:S(2)}, u32[]{:S(2)}) collective-permute-start(bf16[32,3072]{1,0:T(8,128)(2,1)S(1)} %fusion.69), channel_id=1, source_target_pairs={{0,8},{1,9},{2,10},{3,11},{4,12},{5,13},{6,14},{7,15},{8,0},{9,1},... | collective-permute-start | bytes 589832 | tf_op jit(solution)/shard_map/ppermute | solution.py:153
  145.0 8.2 %collective-permute-start.14 = (bf16[32,1025]{1,0:T(8,128)(2,1)S(1)}, bf16[32,1025]{1,0:T(8,128)(2,1)S(1)}, u32[]{:S(2)}, u32[]{:S(2)}) collective-permute-start(bf16[32,1025]{1,0:T(8,128)(2,1)S(1)} %fusion.71), channel_id=1, source_target_pairs={{0,16},{16,0},{1,17},{17,1},{2,18},{18,2},{3,19},{19,3},{4,20},{20... | collective-permute-start | bytes 196808 | tf_op jit(solution)/shard_map/ppermute | solution.py:159
  152.7 5.7 %collective-permute-start.9 = (bf16[32,3072]{1,0:T(8,128)(2,1)S(1)}, bf16[32,3072]{1,0:T(8,128)(2,1)S(1)}, u32[]{:S(2)}, u32[]{:S(2)}) collective-permute-start(bf16[32,3072]{1,0:T(8,128)(2,1)S(1)} %fusion.55), channel_id=1, source_target_pairs={{0,16},{16,0},{1,17},{17,1},{2,18},{18,2},{3,19},{19,3},{4,20},{20... | collective-permute-start | bytes 589832 | tf_op jit(solution)/shard_map/ppermute | solution.py:159
  (8 other events, 20.2 us)

commit v8 on v7

--- a/solution.py
+++ b/solution.py
@@ -132,9 +132,17 @@
         kind, k = item
         return ((seq_at if kind == "s" else dp_at) // (1 << k)) % 2
 
+    def half(pending, at):
+        own, received = pending
+        part = lax.dynamic_index_in_dim(own, at, 0, keepdims=False)
+        if received is None:
+            return part
+        return part + lax.dynamic_index_in_dim(received, at, 0, keepdims=False).astype(jnp.float32)
+
+    pendings = [(acc, None) for acc in accs]
     for step in range(steps):
         perms, kepts, givens = [], [], []
-        for acc, (even, odd) in zip(accs, part_orders):
+        for pending, (even, odd) in zip(pendings, part_orders):
             perm = []
             for dp_i in range(dp_n):
                 for seq_i in range(seq_n):
@@ -143,16 +151,15 @@
                     perm.append((dp_i * seq_n + seq_i, dp_j * seq_n + seq_j))
             keep_at = jnp.where(seq_at % 2 == 1, traced_bit(odd[step]), traced_bit(even[step]))
             perms.append(perm)
-            kepts.append(lax.dynamic_index_in_dim(acc, keep_at, 0, keepdims=False))
-            givens.append(
-                lax.dynamic_index_in_dim(acc, 1 - keep_at, 0, keepdims=False).astype(jnp.bfloat16)
-            )
+            kepts.append(half(pending, keep_at))
+            givens.append(half(pending, 1 - keep_at).astype(jnp.bfloat16))
         if step == 0:
             givens, tie = lax.optimization_barrier((givens, tie))
-        accs = tuple(
-            kept + lax.ppermute(given, ("dp", "seq"), perm).astype(jnp.float32)
+        pendings = [
+            (kept, lax.ppermute(given, ("dp", "seq"), perm))
             for kept, given, perm in zip(kepts, givens, perms)
-        )
+        ]
+    accs = tuple(own + received.astype(jnp.float32) for own, received in pendings)
     accs = tuple(acc.astype(jnp.bfloat16) for acc in accs)
     for step in range(dp_n.bit_length() - 1):
         perm = [(member, member ^ (1 << step)) for member in range(dp_n)]

time: 162 us -> 164 us (1.012)
  local copies, waits for them, and re-layouts: 35.3 us -> 29.5 us
  other arithmetic: 21.7 us -> 25.4 us
  waiting for transfers between devices: 26.8 us -> 29.3 us
    convert_element_type x1 -> x7, other arithmetic: 0.9 us -> 10.2 us  [reduce_rows(): givens.append(half(pending, 1 - keep_at).astype(jnp.bfloat16))]
    add x6 -> x0, other arithmetic: 7.28 us -> none  [reduce_rows(): kept + lax.ppermute(given, ('dp', 'seq'), perm).astype(jnp.float32)]
    unnamed x54 -> x46, local copies, waits for them, and re-layouts: 20.7 us -> 15.9 us
    ppermute x8, waiting for transfers between devices: 16.5 us -> 18.9 us  [reduce_rows(): lax.ppermute(given, ('dp', 'seq'), perm)]
    convert_element_type x7 -> x1, local copies, waits for them, and re-layouts: 3.29 us -> 1.44 us  [reduce_rows(): givens.append(half(pending, 1 - keep_at).astype(jnp.bfloat16))]
    convert_element_type x2, other arithmetic: 0.06 us -> 1.91 us  [reduce_rows(): accs = tuple((acc.astype(jnp.bfloat16) for acc in accs))]
  transfers between devices with their start and end apart: 19 -> 19, of which waited for: 7 -> 6; matrix products, arithmetic and copies ran while one was open for 39% -> 40% of each run, Pallas kernels for 0% -> 0%
where the time goes in v8:
time: 164 us; the launch traced here: 163 us
  matrix products  40 us (24%)
  starting transfers between devices  37.5 us (23%)
  local copies, waits for them, and re-layouts  29.5 us (18%)
  waiting for transfers between devices  29.3 us (18%)
  other arithmetic  25.4 us (15%)
    ppermute x8, waiting for transfers between devices, reduce_rows(): lax.ppermute(given, ('dp', 'seq'), perm)  18.9 us
    unnamed x46, local copies, waits for them, and re-layouts  15.9 us
    ppermute x8, starting transfers between devices, reduce_rows(): lax.ppermute(given, ('dp', 'seq'), perm)  12.2 us
    convert_element_type x7, other arithmetic, reduce_rows(): givens.append(half(pending, 1 - keep_at).astype(jnp.bfloat16))  10.2 us
    all_to_all x1, starting transfers between devices, on_device(): lax.all_to_all(upstream, 'seq', split_axis=2, concat_axis=1, tiled=True)  7.39 us
    all_to_all x1, waiting for transfers between devices, on_device(): lax.all_to_all(normed.reshape(batches, local_rows, columns, model_width),...  6.16 us
    all_to_all x1, starting transfers between devices, on_device(): lax.all_to_all(normed.reshape(batches, local_rows, columns, model_width),...  5.88 us
    dot_general x1, matrix products, on_device(): jnp.dot(used_grads, joint_weight.T, preferred_element_type=jnp.float32)  5.68 us
  transfers between devices with their start and end apart: 19, of which 6 were waited for; matrix products, arithmetic and copies ran while one was open for 40% of the time, Pallas kernels for 0%

profile of v8, /device:TPU:0, one launch (start us, length us, event | category | flops | bytes accessed | tf_op | source)
XLA Modules:
  0.0 162.9 jit_solution(16128740495842630655)
XLA Ops:
  2.7 2.1 %reduce.20 = bf16[128,1024]{1,0:T(8,128)(2,1)S(1)} reduce(bf16[128,1,1,1024]{3,2,1,0:T(2,128)(2,1)S(1)} %bitcast.216, bf16[]{:T(256)} %broadcast.113), dimensions={1,2}, to_apply=%bitcast.208.reduce_sub_computation | reduce | bytes 524290
  5.7 7.4 %all-to-all-start.1 = ((bf16[16,2,4096]{2,1,0:T(2,128)(2,1)}), bf16[16,2,4096]{2,1,0:T(2,128)(2,1)S(1)}, u32[]{:S(2)}, u32[]{:S(2)}) async-start(bf16[16,2,4096]{2,1,0:T(2,128)(2,1)} %reshape.349), calls=%async_computation.1 | async-start | bytes 524288 | tf_op jit(solution)/shard_map/all_to_all | solution.py:208
  17.5 2.0 %convolution_convert_fusion.3 = bf16[8,128,128]{1,2,0:T(8,128)(2,1)} fusion(bf16[128,8,128]{2,1,0:T(8,128)(2,1)} %bitcast.226, f32[8,128]{1,0:T(8,128)S(1)} %get-tuple-element.60, f32[8,128,128]{1,2,0:T(8,128)S(1)} %fusion.21), kind=kOutput, calls=%fused_computation.39 | convolution fusion | flops 34079872 | bytes 1052672 | tf_op jit(solution)/shard_map/ghlm,gmhe->glhe/dot_general | solution.py:31
  22.0 2.9 %reduce.21 = bf16[128,1024]{1,0:T(8,128)(2,1)} reduce(bf16[128,1,1,1024]{3,2,1,0:T(2,128)(2,1)S(1)} %bitcast.217, bf16[]{:T(256)} %broadcast.113), dimensions={1,2}, to_apply=%bitcast.209.reduce_sub_computation | reduce | bytes 524290
  24.9 1.8 %reshape.351 = bf16[16,2,4096]{2,1,0:T(2,128)(2,1)} reshape(bf16[128,1024]{1,0:T(8,128)(2,1)} %reduce.21) | data formatting | bytes 524288
  26.7 5.9 %all-to-all-start = ((bf16[16,2,4096]{2,1,0:T(2,128)(2,1)}), bf16[16,2,4096]{2,1,0:T(2,128)(2,1)}, u32[]{:S(2)}, u32[]{:S(2)}) async-start(bf16[16,2,4096]{2,1,0:T(2,128)(2,1)} %reshape.351), calls=%async_computation | async-start | bytes 524288 | tf_op jit(solution)/shard_map/all_to_all | solution.py:191
  36.5 6.2 %all-to-all-done = bf16[16,2,4096]{2,1,0:T(2,128)(2,1)} async-done(((bf16[16,2,4096]{2,1,0:T(2,128)(2,1)}), bf16[16,2,4096]{2,1,0:T(2,128)(2,1)}, u32[]{:S(2)}, u32[]{:S(2)}) %all-to-all-start) | async-done | bytes 262176 | tf_op jit(solution)/shard_map/all_to_all | solution.py:191
  42.7 2.2 %reshape.352 = bf16[128,1,1,1024]{3,2,1,0:T(2,128)(2,1)S(1)} reshape(bf16[16,2,4096]{2,1,0:T(2,128)(2,1)} %all-to-all-done) | data formatting | bytes 524288
  45.9 3.9 %convolution_convert_fusion = bf16[128,3072]{1,0:T(8,128)(2,1)S(1)} fusion(bf16[1024,3072]{1,0:T(8,128)(2,1)} %param.12, bf16[1,1,128,1024]{2,3,1,0:T(8,128)(2,1)} %copy.112), kind=kOutput, calls=%fused_computation.7 | convolution fusion | flops 805699584 | bytes 7340032 | tf_op jit(solution)/shard_map/dot_general | solution.py:198
  51.9 2.5 %fusion.99 = (f32[8,8,16]{2,1,0:T(8,128)S(1)}, f32[8,8,16,16]{2,3,1,0:T(8,128)}) fusion(pred[16,16]{0,1:T(8,128)(4,1)S(1)} %iota_compare_fusion.1, bf16[1,16,8,1,8,128]{5,2,4,3,1,0:T(8,128)(2,1)S(1)} %get-tuple-element.55, bf16[1,16,8,1,8,128]{5,2,4,3,1,0:T(8,128)(2,1)} %get-tuple-element.54), kind=kOutput, calls=%fused_computation.155 | convolution fusion | flops 4259855 | bytes 594176 | tf_op jit(solution)/shard_map/sub | solution.py:28
  54.5 2.1 %fusion.27 = bf16[1,16,8,1,8,128]{5,1,4,2,3,0:T(8,128)(2,1)} fusion(bf16[16,8,8,128]{3,2,1,0:T(8,128)(2,1)S(1)} %copy.190, f32[8,8,16,16]{2,3,1,0:T(8,128)} %get-tuple-element.65, f32[8,8,16]{2,1,0:T(8,128)S(1)} %get-tuple-element.64), kind=kOutput, calls=%fused_computation.50 | convolution fusion | flops 4358144 | bytes 593920 | tf_op jit(solution)/shard_map/bchlm,blche->bmche/dot_general | solution.py:64
  56.5 2.9 %fusion.30 = bf16[1,16,8,1,8,128]{5,1,4,2,3,0:T(8,128)(2,1)} fusion(f32[8,8,16,16]{2,3,1,0:T(8,128)} %convolution_bitcast_fusion, bf16[1,16,8,1,8,128]{5,2,4,3,1,0:T(8,128)(2,1)} %get-tuple-element.54, f32[8,8,16,16]{2,3,1,0:T(8,128)} %get-tuple-element.65, f32[8,8,16]{2,1,0:T(8,128)S(1)} %get-tuple-element.64), kind=kOutput, calls=%fused_computation.53 | convolution fusion | flops 4441103 | bytes 659456 | tf_op jit(solution)/shard_map/bchlm,blche->bmche/dot_general | solution.py:57
  59.4 2.5 %fusion.26 = bf16[1,16,8,1,8,128]{5,1,4,2,3,0:T(8,128)(2,1)} fusion(f32[8,8,16,16]{2,3,1,0:T(8,128)S(1)} %copy-done.11, bf16[1,16,8,1,8,128]{5,2,4,3,1,0:T(8,128)(2,1)} %copy-done.14, f32[8,8,16,16]{2,3,1,0:T(8,128)} %get-tuple-element.65, f32[8,8,16]{2,1,0:T(8,128)S(1)} %get-tuple-element.64), kind=kOutput, calls=%fused_computation.49 | convolution fusion | flops 4441103 | bytes 659456 | tf_op jit(solution)/shard_map/bchlm,bmche->blche/dot_general | solution.py:51
  66.1 5.7 %fusion.28 = bf16[1,16,8,1024]{3,2,0,1:T(8,128)(2,1)} fusion(bf16[128,3072]{1,0:T(8,128)(2,1)S(1)} %reshape_reshape.7, bf16[1024,3072]{1,0:T(8,128)(2,1)} %param.12), kind=kOutput, calls=%fused_computation.51 | convolution fusion | flops 805437440 | bytes 7340032 | tf_op jit(solution)/shard_map/dot_general | solution.py:216
  71.8 4.4 %all-to-all-start.2 = ((bf16[1,16,8,1024]{3,2,0,1:T(8,128)(2,1)}), bf16[1,16,8,1024]{3,2,0,1:T(8,128)(2,1)}, u32[]{:S(2)}, u32[]{:S(2)}) async-start(bf16[1,16,8,1024]{3,2,0,1:T(8,128)(2,1)} %fusion.28), calls=%async_computation.2 | async-start | bytes 524288 | tf_op jit(solution)/shard_map/all_to_all | solution.py:238
  76.2 2.1 %fusion.29 = bf16[1,16,8,8,128]{4,1,3,2,0:T(8,128)(2,1)} fusion(bf16[1,16,8,1,8,128]{5,2,4,3,1,0:T(8,128)(2,1)} %copy-done.10, f32[8,8,16,16]{2,3,1,0:T(8,128)} %get-tuple-element.65, f32[8,8,16]{2,1,0:T(8,128)S(1)} %get-tuple-element.64), kind=kOutput, calls=%fused_computation.52 | convolution fusion | flops 4358144 | bytes 593920 | tf_op jit(solution)/shard_map/bchlm,bmche->blche/dot_general | solution.py:31
  79.6 2.1 %fusion.5 = f32[512,3072]{1,0:T(8,128)S(1)} fusion(bf16[128,3072]{1,0:T(8,128)(2,1)} %collective-permute-done.1, bf16[128,3072]{1,0:T(8,128)(2,1)S(1)} %reshape_reshape.7, bf16[256,1024]{0,1:T(8,128)(2,1)S(1)} %bitcast.219, s32[]{:T(128)S(6)} %select_n.259), kind=kOutput, calls=%fused_computation.13 | convolution fusion | flops 808452096 | bytes 8126468 | tf_op jit(solution)/shard_map/dot_general | solution.py:233
  81.7 2.7 %copy-done.1 = f32[512,3072]{1,0:T(8,128)} copy-done((f32[512,3072]{1,0:T(8,128)}, f32[512,3072]{1,0:T(8,128)S(1)}, u32[]{:S(2)}) %copy-start.1) | copy-done | bytes 6291480
  95.4 2.0 %fusion.69 = f32[8,128,128]{1,2,0:T(8,128)} fusion(bf16[128,8,128]{0,2,1:T(8,128)(2,1)} %bitcast.228, bf16[128,8,128]{2,1,0:T(8,128)(2,1)S(1)} %bitcast.227), kind=kOutput, calls=%fused_computation.113 | convolution fusion | flops 33554432 | bytes 1048576 | tf_op jit(solution)/shard_map/glhe,gmhe->ghlm/dot_general | solution.py:43
  97.4 10.7 %collective-permute-done.5 = bf16[2,2,2,32,3072]{4,3,2,1,0:T(8,128)(2,1)} collective-permute-done((bf16[2,2,2,32,3072]{4,3,2,1,0:T(8,128)(2,1)}, bf16[2,2,2,32,3072]{4,3,2,1,0:T(8,128)(2,1)}, u32[]{:S(2)}, u32[]{:S(2)}) %collective-permute-start.5) | collective-permute-done | bytes 1572896 | tf_op jit(solution)/shard_map/ppermute | solution.py:159
  108.1 3.2 %fusion.9 = (bf16[2,2,32,3072]{3,2,1,0:T(8,128)(2,1)}, f32[2,2,32,3072]{3,2,1,0:T(8,128)}) fusion(f32[2,2,2,2,32,3072]{5,4,3,2,1,0:T(8,128)S(1)} %bitcast.211, s32[]{:T(128)S(6)} %select_n.276, s32[]{:T(128)S(6)} %select_n.283, bf16[2,2,2,32,3072]{4,3,2,1,0:T(8,128)(2,1)} %collective-permute-done.5, s32[]{:T(128)S(6)} %select_n.282, s32[]{:T(128)S(6)} %select_n.278, ...), kind=kLoop, calls=%fused_computation.18 | loop fusion | flops 1966080 | bytes 7077908 | tf_op jit(solution)/shard_map/convert_element_type | solution.py:155
  115.0 2.6 %convolution_convert_fusion.6 = bf16[8,128,128]{1,2,0:T(8,128)(2,1)} fusion(bf16[128,8,128]{0,2,1:T(8,128)(2,1)S(1)} %bitcast.225, f32[8,128,128]{1,2,0:T(8,128)} %fusion.69, f32[8,128,128]{1,2,0:T(8,128)} %get-tuple-element.61, f32[8,128]{1,0:T(8,128)S(1)} %get-tuple-element.60), kind=kOutput, calls=%fused_computation.42 | convolution fusion | flops 34604160 | bytes 1576960 | tf_op jit(solution)/shard_map/ghlm,glhe->gmhe/dot_general | solution.py:57
  117.6 1.8 %copy.144 = bf16[1,1,128,1024]{3,2,1,0:T(8,128)(2,1)} copy(bf16[1,1,128,1024]{2,3,1,0:T(8,128)(2,1)} %bitcast.233) | data formatting | bytes 524288
  119.4 1.9 %convolution_convert_fusion.1 = bf16[8,128,128]{1,2,0:T(8,128)(2,1)S(1)} fusion(bf16[128,8,128]{0,2,1:T(8,128)(2,1)S(1)} %bitcast.223, f32[8,128,128]{1,2,0:T(8,128)} %fusion.69, f32[8,128,128]{1,2,0:T(8,128)} %get-tuple-element.61, f32[8,128]{1,0:T(8,128)S(1)} %get-tuple-element.60), kind=kOutput, calls=%fused_computation.37 | convolution fusion | flops 34604160 | bytes 1576960 | tf_op jit(solution)/shard_map/ghlm,gmhe->glhe/dot_general | solution.py:51
  123.0 4.7 %all-to-all-start.3 = ((bf16[1,16,8,1024]{3,2,0,1:T(8,128)(2,1)}), bf16[1,16,8,1024]{3,2,0,1:T(8,128)(2,1)S(1)}, u32[]{:S(2)}, u32[]{:S(2)}) async-start(bf16[1,16,8,1024]{3,2,0,1:T(8,128)(2,1)} %bitcast.58), calls=%async_computation.3 | async-start | bytes 524288 | tf_op jit(solution)/shard_map/all_to_all | solution.py:264
  130.0 2.5 %fusion.58 = (bf16[2,32,3072]{2,1,0:T(8,128)(2,1)}, f32[1,2,32,3072]{3,2,1,0:T(8,128)S(1)}) fusion(f32[2,2,32,3072]{3,2,1,0:T(8,128)} %get-tuple-element.46, s32[]{:T(128)S(6)} %select_n.287, bf16[2,2,32,3072]{3,2,1,0:T(8,128)(2,1)} %collective-permute-done.6, s32[]{:T(128)S(6)} %select_n.281), kind=kLoop, calls=%fused_computation.90 | loop fusion | flops 983040 | bytes 3538952 | tf_op jit(solution)/shard_map/convert_element_type | solution.py:155
  132.5 1.9 %collective-permute-start.7 = (bf16[2,32,3072]{2,1,0:T(8,128)(2,1)}, bf16[2,32,3072]{2,1,0:T(8,128)(2,1)}, u32[]{:S(2)}, u32[]{:S(2)}) collective-permute-start(bf16[2,32,3072]{2,1,0:T(8,128)(2,1)} %get-tuple-element.49), channel_id=1, source_target_pairs={{0,4},{1,3},{2,6},{3,1},{4,0},{5,7},{6,2},{7,5},{8,12},{9,11},{10,... | collective-permute-start | bytes 1179656 | tf_op jit(solution)/shard_map/ppermute | solution.py:159
  134.4 2.3 %convolution_convert_fusion.5 = bf16[8,128,128]{2,1,0:T(8,128)(2,1)} fusion(bf16[128,8,128]{0,2,1:T(8,128)(2,1)} %bitcast.229, f32[8,128]{1,0:T(8,128)S(1)} %get-tuple-element.60, f32[8,128,128]{1,2,0:T(8,128)} %copy-done.3), kind=kOutput, calls=%fused_computation.41 | convolution fusion | flops 34079872 | bytes 1052672 | tf_op jit(solution)/shard_map/ghlm,glhe->gmhe/dot_general | solution.py:64
  136.7 1.8 %copy.145 = bf16[1,1,128,1024]{3,2,1,0:T(8,128)(2,1)} copy(bf16[1,1,128,1024]{2,3,1,0:T(8,128)(2,1)} %bitcast.232) | data formatting | bytes 524288
  139.4 2.4 %collective-permute-start.13 = (bf16[32,1025]{1,0:T(8,128)(2,1)S(1)}, bf16[32,1025]{1,0:T(8,128)(2,1)S(1)}, u32[]{:S(2)}, u32[]{:S(2)}) collective-permute-start(bf16[32,1025]{1,0:T(8,128)(2,1)S(1)} %fusion.81), channel_id=1, source_target_pairs={{0,8},{1,9},{2,10},{3,11},{4,12},{5,13},{6,14},{7,15},{8,0},{9,1},... | collective-permute-start | bytes 196808 | tf_op jit(solution)/shard_map/ppermute | solution.py:159
  147.6 6.7 %collective-permute-done.8 = bf16[32,3072]{1,0:T(8,128)(2,1)S(1)} collective-permute-done((bf16[32,3072]{1,0:T(8,128)(2,1)S(1)}, bf16[32,3072]{1,0:T(8,128)(2,1)S(1)}, u32[]{:S(2)}, u32[]{:S(2)}) %collective-permute-start.8) | collective-permute-done | bytes 196640 | tf_op jit(solution)/shard_map/ppermute | solution.py:159
  157.4 4.0 %collective-permute-done.9 = bf16[32,3072]{1,0:T(8,128)(2,1)S(1)} collective-permute-done((bf16[32,3072]{1,0:T(8,128)(2,1)S(1)}, bf16[32,3072]{1,0:T(8,128)(2,1)S(1)}, u32[]{:S(2)}, u32[]{:S(2)}) %collective-permute-start.9) | collective-permute-done | bytes 196640 | tf_op jit(solution)/shard_map/ppermute | solution.py:166
  (119 shorter events, 52.0 us)
Async XLA Ops:
  0.6 19.4 %copy-start = (bf16[1024,1024]{1,0:T(8,128)(2,1)S(1)}, bf16[1024,1024]{1,0:T(8,128)(2,1)}, u32[]{:S(2)}) copy-start(bf16[1024,1024]{1,0:T(8,128)(2,1)} %param.10) | copy-start | bytes 6291460
  4.8 10.7 %copy-start.12 = (bf16[1,1,128,1024]{3,2,1,0:T(8,128)(2,1)S(1)}, bf16[1,1,128,1024]{3,2,1,0:T(8,128)(2,1)}, u32[]{:S(2)}) copy-start(bf16[1,1,128,1024]{3,2,1,0:T(8,128)(2,1)} %param.9) | copy-start | bytes 786436
  5.7 21.0 %all-to-all-start.1 = ((bf16[16,2,4096]{2,1,0:T(2,128)(2,1)}), bf16[16,2,4096]{2,1,0:T(2,128)(2,1)S(1)}, u32[]{:S(2)}, u32[]{:S(2)}) async-start(bf16[16,2,4096]{2,1,0:T(2,128)(2,1)} %reshape.349), calls=%async_computation.1 | async-start | bytes 524288 | tf_op jit(solution)/shard_map/all_to_all | solution.py:208
  14.2 5.3 %copy-start.7 = (bf16[1,1,128,1024]{2,3,1,0:T(8,128)(2,1)}, bf16[1,1,128,1024]{2,3,1,0:T(8,128)(2,1)S(1)}, u32[]{:S(2)}) copy-start(bf16[1,1,128,1024]{2,3,1,0:T(8,128)(2,1)S(1)} %copy.158) | copy-start | bytes 786436
  15.5 4.0 %copy-start.5 = (bf16[1,1,128,1024]{2,3,1,0:T(8,128)(2,1)}, bf16[1,1,128,1024]{2,3,1,0:T(8,128)(2,1)S(1)}, u32[]{:S(2)}) copy-start(bf16[1,1,128,1024]{2,3,1,0:T(8,128)(2,1)S(1)} %copy.157) | copy-start | bytes 786436
  16.6 3.4 %copy-start.3 = (f32[8,128,128]{1,2,0:T(8,128)}, f32[8,128,128]{1,2,0:T(8,128)S(1)}, u32[]{:S(2)}) copy-start(f32[8,128,128]{1,2,0:T(8,128)S(1)} %fusion.21) | copy-start | bytes 1572868
  19.5 13.1 %collective-permute-start.2 = (bf16[128,1024]{0,1:T(8,128)(2,1)}, bf16[128,1024]{0,1:T(8,128)(2,1)}, u32[]{:S(2)}, u32[]{:S(2)}) collective-permute-start(bf16[128,1024]{0,1:T(8,128)(2,1)} %bitcast.3), channel_id=1, source_target_pairs={{0,1},{1,0},{2,3},{3,2},{4,5},{5,4},{6,7},{7,6},{8,9},{9,8},{10,11... | collective-permute-start | bytes 786440 | tf_op jit(solution)/shard_map/ppermute | solution.py:253
  26.7 16.0 %all-to-all-start = ((bf16[16,2,4096]{2,1,0:T(2,128)(2,1)}), bf16[16,2,4096]{2,1,0:T(2,128)(2,1)}, u32[]{:S(2)}, u32[]{:S(2)}) async-start(bf16[16,2,4096]{2,1,0:T(2,128)(2,1)} %reshape.351), calls=%async_computation | async-start | bytes 524288 | tf_op jit(solution)/shard_map/all_to_all | solution.py:191
  50.6 3.9 %copy-start.14 = (bf16[1,16,8,1,8,128]{5,2,4,3,1,0:T(8,128)(2,1)}, bf16[1,16,8,1,8,128]{5,2,4,3,1,0:T(8,128)(2,1)S(1)}, u32[]{:S(2)}) copy-start(bf16[1,16,8,1,8,128]{5,2,4,3,1,0:T(8,128)(2,1)S(1)} %get-tuple-element.55) | copy-start | bytes 786436
  50.6 5.9 %copy-start.10 = (bf16[1,16,8,1,8,128]{5,2,4,3,1,0:T(8,128)(2,1)}, bf16[1,16,8,1,8,128]{5,2,4,3,1,0:T(8,128)(2,1)S(1)}, u32[]{:S(2)}) copy-start(bf16[1,16,8,1,8,128]{5,2,4,3,1,0:T(8,128)(2,1)S(1)} %get-tuple-element.53) | copy-start | bytes 786436
  56.5 2.9 %copy-start.11 = (f32[8,8,16,16]{2,3,1,0:T(8,128)S(1)}, f32[8,8,16,16]{2,3,1,0:T(8,128)}, u32[]{:S(2)}) copy-start(f32[8,8,16,16]{2,3,1,0:T(8,128)} %convolution_bitcast_fusion) | copy-start | bytes 196612
  61.9 16.5 %collective-permute-start = (bf16[128,1024]{0,1:T(8,128)(2,1)}, bf16[128,1024]{0,1:T(8,128)(2,1)}, u32[]{:S(2)}, u32[]{:S(2)}) collective-permute-start(bf16[128,1024]{0,1:T(8,128)(2,1)} %bitcast.6), channel_id=1, source_target_pairs={{0,1},{1,0},{2,3},{3,2},{4,5},{5,4},{6,7},{7,6},{8,9},{9,8},{10,11... | collective-permute-start | bytes 786440 | tf_op jit(solution)/shard_map/ppermute | solution.py:232
  65.5 14.0 %collective-permute-start.1 = (bf16[128,3072]{1,0:T(8,128)(2,1)S(1)}, bf16[128,3072]{1,0:T(8,128)(2,1)}, u32[]{:S(2)}, u32[]{:S(2)}) collective-permute-start(bf16[128,3072]{1,0:T(8,128)(2,1)S(1)} %reshape_reshape.7), channel_id=1, source_target_pairs={{0,1},{1,0},{2,3},{3,2},{4,5},{5,4},{6,7},{7,6},{8,9},{9,8},{10,11... | collective-permute-start | bytes 2359304 | tf_op jit(solution)/shard_map/ppermute | solution.py:232
  71.8 14.3 %all-to-all-start.2 = ((bf16[1,16,8,1024]{3,2,0,1:T(8,128)(2,1)}), bf16[1,16,8,1024]{3,2,0,1:T(8,128)(2,1)}, u32[]{:S(2)}, u32[]{:S(2)}) async-start(bf16[1,16,8,1024]{3,2,0,1:T(8,128)(2,1)} %fusion.28), calls=%async_computation.2 | async-start | bytes 524288 | tf_op jit(solution)/shard_map/all_to_all | solution.py:238
  87.2 4.6 %collective-permute-start.4 = (f32[1024]{0:T(1024)S(1)}, f32[1024]{0:T(1024)S(1)}, u32[]{:S(2)}, u32[]{:S(2)}) collective-permute-start(f32[1024]{0:T(1024)S(1)} %get-tuple-element.43), channel_id=1, source_target_pairs={{0,1},{1,0},{2,3},{3,2},{4,5},{5,4},{6,7},{7,6},{8,9},{9,8},{10,11... | collective-permute-start | bytes 12296 | tf_op jit(solution)/shard_map/ppermute | solution.py:253
  87.3 20.8 %collective-permute-start.5 = (bf16[2,2,2,32,3072]{4,3,2,1,0:T(8,128)(2,1)}, bf16[2,2,2,32,3072]{4,3,2,1,0:T(8,128)(2,1)}, u32[]{:S(2)}, u32[]{:S(2)}) collective-permute-start(bf16[2,2,2,32,3072]{4,3,2,1,0:T(8,128)(2,1)} %fusion.4), channel_id=1, source_target_pairs={{0,2},{1,17},{2,0},{3,19},{4,6},{5,21},{6,4},{7,23},{8,10},{9,25},... | collective-permute-start | bytes 4718600 | tf_op jit(solution)/shard_map/ppermute | solution.py:159
  89.8 2.5 %collective-permute-start.3 = (bf16[128,1024]{1,0:T(8,128)(2,1)S(1)}, bf16[128,1024]{1,0:T(8,128)(2,1)}, u32[]{:S(2)}, u32[]{:S(2)}) collective-permute-start(bf16[128,1024]{1,0:T(8,128)(2,1)S(1)} %fusion.50), channel_id=1, source_target_pairs={{0,1},{1,0},{2,3},{3,2},{4,5},{5,4},{6,7},{7,6},{8,9},{9,8},{10,11... | collective-permute-start | bytes 786440 | tf_op jit(solution)/shard_map/ppermute | solution.py:253
  92.0 3.4 %copy-start.9 = (bf16[16,8,8,128]{3,2,1,0:T(8,128)(2,1)S(1)}, bf16[16,8,8,128]{3,2,1,0:T(8,128)(2,1)}, u32[]{:S(2)}) copy-start(bf16[16,8,8,128]{3,2,1,0:T(8,128)(2,1)} %copy.160) | copy-start | bytes 786436
  92.3 15.7 %copy-start.2 = (f32[512,3072]{1,0:T(8,128)S(1)}, f32[512,3072]{1,0:T(8,128)}, u32[]{:S(2)}) copy-start(f32[512,3072]{1,0:T(8,128)} %copy-done.1) | copy-start | bytes 18874372
  94.0 18.8 %collective-permute-start.10 = (bf16[2,2,2,32,1025]{4,3,2,1,0:T(8,128)(2,1)S(1)}, bf16[2,2,2,32,1025]{4,3,2,1,0:T(8,128)(2,1)S(1)}, u32[]{:S(2)}, u32[]{:S(2)}) collective-permute-start(bf16[2,2,2,32,1025]{4,3,2,1,0:T(8,128)(2,1)S(1)} %fusion.41), channel_id=1, source_target_pairs={{0,4},{1,5},{2,6},{3,7},{4,0},{5,1},{6,2},{7,3},{8,12},{9,13},{10,... | collective-permute-start | bytes 1574408 | tf_op jit(solution)/shard_map/ppermute | solution.py:159
  111.3 3.7 %copy-start.8 = (bf16[1,1,128,1024]{2,3,1,0:T(8,128)(2,1)S(1)}, bf16[1,1,128,1024]{2,3,1,0:T(8,128)(2,1)}, u32[]{:S(2)}) copy-start(bf16[1,1,128,1024]{2,3,1,0:T(8,128)(2,1)} %copy-done.7) | copy-start | bytes 786436
  111.3 18.7 %collective-permute-start.6 = (bf16[2,2,32,3072]{3,2,1,0:T(8,128)(2,1)}, bf16[2,2,32,3072]{3,2,1,0:T(8,128)(2,1)}, u32[]{:S(2)}, u32[]{:S(2)}) collective-permute-start(bf16[2,2,32,3072]{3,2,1,0:T(8,128)(2,1)} %get-tuple-element.45), channel_id=1, source_target_pairs={{0,16},{1,5},{2,18},{3,7},{4,20},{5,1},{6,22},{7,3},{8,24},{9,13},... | collective-permute-start | bytes 2359304 | tf_op jit(solution)/shard_map/ppermute | solution.py:159
  113.6 5.8 %copy-start.6 = (bf16[1,1,128,1024]{2,3,1,0:T(8,128)(2,1)S(1)}, bf16[1,1,128,1024]{2,3,1,0:T(8,128)(2,1)}, u32[]{:S(2)}) copy-start(bf16[1,1,128,1024]{2,3,1,0:T(8,128)(2,1)} %copy-done.5) | copy-start | bytes 786436
  113.6 14.1 %collective-permute-start.11 = (bf16[2,2,32,1025]{3,2,1,0:T(8,128)(2,1)}, bf16[2,2,32,1025]{3,2,1,0:T(8,128)(2,1)}, u32[]{:S(2)}, u32[]{:S(2)}) collective-permute-start(bf16[2,2,32,1025]{3,2,1,0:T(8,128)(2,1)} %get-tuple-element.47), channel_id=1, source_target_pairs={{0,2},{1,17},{2,0},{3,19},{4,6},{5,21},{6,4},{7,23},{8,10},{9,25},... | collective-permute-start | bytes 787208 | tf_op jit(solution)/shard_map/ppermute | solution.py:159
  117.6 4.6 %copy-start.13 = (bf16[1,16,8,8,128]{4,1,3,2,0:T(8,128)(2,1)S(1)}, bf16[1,16,8,8,128]{4,1,3,2,0:T(8,128)(2,1)}, u32[]{:S(2)}) copy-start(bf16[1,16,8,8,128]{4,1,3,2,0:T(8,128)(2,1)} %fusion.29) | copy-start | bytes 786436
  123.0 15.5 %all-to-all-start.3 = ((bf16[1,16,8,1024]{3,2,0,1:T(8,128)(2,1)}), bf16[1,16,8,1024]{3,2,0,1:T(8,128)(2,1)S(1)}, u32[]{:S(2)}, u32[]{:S(2)}) async-start(bf16[1,16,8,1024]{3,2,0,1:T(8,128)(2,1)} %bitcast.58), calls=%async_computation.3 | async-start | bytes 524288 | tf_op jit(solution)/shard_map/all_to_all | solution.py:264
  129.5 9.1 %collective-permute-start.12 = (bf16[2,32,1025]{2,1,0:T(8,128)(2,1)}, bf16[2,32,1025]{2,1,0:T(8,128)(2,1)}, u32[]{:S(2)}, u32[]{:S(2)}) collective-permute-start(bf16[2,32,1025]{2,1,0:T(8,128)(2,1)} %get-tuple-element.51), channel_id=1, source_target_pairs={{0,16},{1,3},{2,18},{3,1},{4,20},{5,7},{6,22},{7,5},{8,24},{9,11},... | collective-permute-start | bytes 393608 | tf_op jit(solution)/shard_map/ppermute | solution.py:159
  132.5 9.4 %collective-permute-start.7 = (bf16[2,32,3072]{2,1,0:T(8,128)(2,1)}, bf16[2,32,3072]{2,1,0:T(8,128)(2,1)}, u32[]{:S(2)}, u32[]{:S(2)}) collective-permute-start(bf16[2,32,3072]{2,1,0:T(8,128)(2,1)} %get-tuple-element.49), channel_id=1, source_target_pairs={{0,4},{1,3},{2,6},{3,1},{4,0},{5,7},{6,2},{7,5},{8,12},{9,11},{10,... | collective-permute-start | bytes 1179656 | tf_op jit(solution)/shard_map/ppermute | solution.py:159
  139.4 6.5 %collective-permute-start.13 = (bf16[32,1025]{1,0:T(8,128)(2,1)S(1)}, bf16[32,1025]{1,0:T(8,128)(2,1)S(1)}, u32[]{:S(2)}, u32[]{:S(2)}) collective-permute-start(bf16[32,1025]{1,0:T(8,128)(2,1)S(1)} %fusion.81), channel_id=1, source_target_pairs={{0,8},{1,9},{2,10},{3,11},{4,12},{5,13},{6,14},{7,15},{8,0},{9,1},... | collective-permute-start | bytes 196808 | tf_op jit(solution)/shard_map/ppermute | solution.py:159
  142.8 11.5 %collective-permute-start.8 = (bf16[32,3072]{1,0:T(8,128)(2,1)S(1)}, bf16[32,3072]{1,0:T(8,128)(2,1)S(1)}, u32[]{:S(2)}, u32[]{:S(2)}) collective-permute-start(bf16[32,3072]{1,0:T(8,128)(2,1)S(1)} %fusion.73), channel_id=1, source_target_pairs={{0,8},{1,9},{2,10},{3,11},{4,12},{5,13},{6,14},{7,15},{8,0},{9,1},... | collective-permute-start | bytes 589832 | tf_op jit(solution)/shard_map/ppermute | solution.py:159
  146.8 9.2 %collective-permute-start.14 = (bf16[32,1025]{1,0:T(8,128)(2,1)S(1)}, bf16[32,1025]{1,0:T(8,128)(2,1)S(1)}, u32[]{:S(2)}, u32[]{:S(2)}) collective-permute-start(bf16[32,1025]{1,0:T(8,128)(2,1)S(1)} %fusion.76), channel_id=1, source_target_pairs={{0,16},{16,0},{1,17},{17,1},{2,18},{18,2},{3,19},{19,3},{4,20},{20... | collective-permute-start | bytes 196808 | tf_op jit(solution)/shard_map/ppermute | solution.py:166
  155.3 6.1 %collective-permute-start.9 = (bf16[32,3072]{1,0:T(8,128)(2,1)S(1)}, bf16[32,3072]{1,0:T(8,128)(2,1)S(1)}, u32[]{:S(2)}, u32[]{:S(2)}) collective-permute-start(bf16[32,3072]{1,0:T(8,128)(2,1)S(1)} %fusion.60), channel_id=1, source_target_pairs={{0,16},{16,0},{1,17},{17,1},{2,18},{18,2},{3,19},{19,3},{4,20},{20... | collective-permute-start | bytes 589832 | tf_op jit(solution)/shard_map/ppermute | solution.py:166
  (4 other events, 9.6 us)

commit v9 on v8

--- a/solution.py
+++ b/solution.py
@@ -112,15 +112,9 @@
     return jnp.where(core_odd, arrange(odd), arrange(even))
 
 
-def reduce_rows(parts, part_orders, seq_n, dp_n, tie):
+def halving_steps(pendings, part_orders, seq_n, dp_n, steps, ties):
     seq_at = lax.axis_index("seq")
     dp_at = lax.axis_index("dp")
-    steps = len(part_orders[0][0])
-    accs = tuple(p.reshape((2,) * steps + (p.shape[0] >> steps, p.shape[1])) for p in parts)
-
-    def bit_value(item, seq_i, dp_i):
-        kind, k = item
-        return ((seq_i if kind == "s" else dp_i) >> k) & 1
 
     def flip(item, seq_i, dp_i):
         kind, k = item
@@ -139,8 +133,8 @@
             return part
         return part + lax.dynamic_index_in_dim(received, at, 0, keepdims=False).astype(jnp.float32)
 
-    pendings = [(acc, None) for acc in accs]
-    for step in range(steps):
+    ties = dict(ties)
+    for step in steps:
         perms, kepts, givens = [], [], []
         for pending, (even, odd) in zip(pendings, part_orders):
             perm = []
@@ -153,14 +147,23 @@
             perms.append(perm)
             kepts.append(half(pending, keep_at))
             givens.append(half(pending, 1 - keep_at).astype(jnp.bfloat16))
-        if step == 0:
-            givens, tie = lax.optimization_barrier((givens, tie))
+        if step in ties:
+            givens, ties[step] = lax.optimization_barrier((givens, ties[step]))
         pendings = [
             (kept, lax.ppermute(given, ("dp", "seq"), perm))
             for kept, given, perm in zip(kepts, givens, perms)
         ]
-    accs = tuple(own + received.astype(jnp.float32) for own, received in pendings)
-    accs = tuple(acc.astype(jnp.bfloat16) for acc in accs)
+    return pendings, ties
+
+
+def start_rows(parts, seq_n, dp_n):
+    steps = (seq_n.bit_length() - 1) + (dp_n.bit_length() - 1) - 1
+    return [(p.reshape((2,) * steps + (p.shape[0] >> steps, p.shape[1])), None) for p in parts]
+
+
+def finish_rows(pendings, dp_n):
+    dp_at = lax.axis_index("dp")
+    accs = tuple((own + received.astype(jnp.float32)).astype(jnp.bfloat16) for own, received in pendings)
     for step in range(dp_n.bit_length() - 1):
         perm = [(member, member ^ (1 << step)) for member in range(dp_n)]
         got = lax.ppermute(accs, "dp", perm)
@@ -169,7 +172,7 @@
             jnp.where(upper, jnp.concatenate([g, acc], axis=0), jnp.concatenate([acc, g], axis=0))
             for acc, g in zip(accs, got)
         )
-    return accs, tie
+    return accs
 
 
 def on_device(first_query, first_key, first_value, out_weight, norm_gain, joint_weight, upstream):
@@ -243,7 +246,11 @@
         tiled=True,
     )
     grad_normed = grad_normed.reshape(-1, model_width)
-    (joint_sum,), grad_normed = reduce_rows((joint_term,), (orders,), seq_n, dp_n, grad_normed)
+    steps = len(orders[0])
+    joint_rows, ties = halving_steps(
+        start_rows((joint_term,), seq_n, dp_n), (orders,), seq_n, dp_n, [0], {0: grad_normed}
+    )
+    grad_normed = ties[0]
     grad_float = grad_normed.astype(jnp.float32)
     gain_term = jnp.sum(grad_float * hidden * inverse, axis=0)
     scaled = norm_gain * grad_float
@@ -258,9 +265,15 @@
     )
     gain_term = my_half((gain_term + gain_peer)[None, :], out_orders)[0][:, None]
     out_width = out_term.shape[1]
-    (out_sum,), out_cols = reduce_rows(
-        (jnp.concatenate([out_term, gain_term], axis=1),), (out_orders,), seq_n, dp_n, out_cols
-    )
+    out_rows, ties = halving_steps(
+        start_rows((jnp.concatenate([out_term, gain_term], axis=1),), seq_n, dp_n),
+        (out_orders,),
+        seq_n,
+        dp_n,
+        range(steps),
+        {0: out_cols},
+    )
+    out_cols = ties[0]
     column_out = lax.all_to_all(
         out_cols.reshape(batches, all_rows, col_share, feature),
         "seq",
@@ -268,7 +281,6 @@
         concat_axis=2,
         tiled=True,
     )
-    replicas = (joint_sum, out_sum[:, :out_width], out_sum[:, out_width].astype(jnp.float32))
     grad_first = jnp.dot(grad_hidden, out_weight.T, preferred_element_type=jnp.float32).astype(
         jnp.bfloat16
     )
@@ -281,6 +293,13 @@
         "glhe",
         "ghlm",
     )
+    joint_rows, ties = halving_steps(
+        joint_rows, (orders,), seq_n, dp_n, range(1, steps), {1: column_out, 2: grads_rows}
+    )
+    column_out, grads_rows = ties[1], ties[2]
+    (joint_sum,) = finish_rows(joint_rows, dp_n)
+    (out_sum,) = finish_rows(out_rows, dp_n)
+    replicas = (joint_sum, out_sum[:, :out_width], out_sum[:, out_width].astype(jnp.float32))
     grad_query = grads_rows[0].reshape(batches, local_rows, columns, feature)
     grad_key = grads_rows[1].reshape(batches, local_rows, columns, feature)
     grad_value = grads_rows[2].reshape(batches, local_rows, columns, feature)

time: 164 us -> 165 us (level)
  other arithmetic: 25.4 us -> 28.9 us
  matrix products: 40 us -> 37.8 us
  waiting for transfers between devices: 29.3 us -> 27.4 us
    ppermute x10, waiting for transfers between devices: 22.9 us -> 20.2 us  [the longest x8 19.8 us: halving_steps(): lax.ppermute(given, ('dp', 'seq'), perm)]
    convert_element_type x9 -> x8, other arithmetic: 12.1 us -> 9.4 us  [the longest x6 7.7 us: halving_steps(): givens.append(half(pending, 1 - keep_at).astype(jnp.bfloat16))]
    optimization_barrier x1 -> x3, local copies, waits for them, and re-layouts: 0.07 us -> 2.3 us  [halving_steps(): givens, ties[step] = lax.optimization_barrier((givens, ties[step]))]
    add x0 -> x1, other arithmetic: none -> 2.03 us  [half(): part + lax.dynamic_index_in_dim(received, at, 0, keepdims=False).astype(j...]
    select_n x3 -> x2, other arithmetic: 0.11 us -> 2.1 us  [by_split_order(): return jnp.where(core_odd, arrange(odd), arrange(even))]
    another operation x2 -> x1, local copies, waits for them, and re-layouts: 2.05 us -> 0.17 us
    unnamed x46 -> x52, local copies, waits for them, and re-layouts: 15.9 us -> 17.6 us
    dot_general x2, matrix products: 3.32 us -> 1.53 us  [attend_back(): jnp.einsum(layout + ',' + keyed + '->' + scores_form, upstream_part, valu...]
  transfers between devices with their start and end apart: 19 -> 19, of which waited for: 6 -> 10; matrix products, arithmetic and copies ran while one was open for 40% -> 40% of each run, Pallas kernels for 0% -> 0%
where the time goes in v9:
time: 165 us; the launch traced here: 164 us
  starting transfers between devices  38.1 us (23%)
  matrix products  37.8 us (23%)
  local copies, waits for them, and re-layouts  30.6 us (19%)
  other arithmetic  28.9 us (18%)
  waiting for transfers between devices  27.4 us (17%)
    ppermute x8, waiting for transfers between devices, halving_steps(): lax.ppermute(given, ('dp', 'seq'), perm)  19.8 us
    unnamed x52, local copies, waits for them, and re-layouts  17.6 us
    ppermute x8, starting transfers between devices, halving_steps(): lax.ppermute(given, ('dp', 'seq'), perm)  11.4 us
    convert_element_type x6, other arithmetic, halving_steps(): givens.append(half(pending, 1 - keep_at).astype(jnp.bfloat16))  7.7 us
    all_to_all x1, starting transfers between devices, on_device(): lax.all_to_all(upstream, 'seq', split_axis=2, concat_axis=1, tiled=True)  7.39 us
    all_to_all x1, waiting for transfers between devices, on_device(): lax.all_to_all(normed.reshape(batches, local_rows, columns, model_width),...  5.92 us
    all_to_all x1, starting transfers between devices, on_device(): lax.all_to_all(normed.reshape(batches, local_rows, columns, model_width),...  5.83 us
    dot_general x1, matrix products, on_device(): jnp.dot(used_grads, joint_weight.T, preferred_element_type=jnp.float32)  5.69 us
  transfers between devices with their start and end apart: 19, of which 10 were waited for; matrix products, arithmetic and copies ran while one was open for 40% of the time, Pallas kernels for 0%

profile of v9, /device:TPU:0, one launch (start us, length us, event | category | flops | bytes accessed | tf_op | source)
XLA Modules:
  0.0 164.0 jit_solution(5344330282383672552)
XLA Ops:
  2.7 2.1 %reduce.20 = bf16[128,1024]{1,0:T(8,128)(2,1)S(1)} reduce(bf16[128,1,1,1024]{3,2,1,0:T(2,128)(2,1)S(1)} %bitcast.218, bf16[]{:T(256)} %broadcast.113), dimensions={1,2}, to_apply=%bitcast.210.reduce_sub_computation | reduce | bytes 524290
  5.7 7.4 %all-to-all-start.1 = ((bf16[16,2,4096]{2,1,0:T(2,128)(2,1)}), bf16[16,2,4096]{2,1,0:T(2,128)(2,1)S(1)}, u32[]{:S(2)}, u32[]{:S(2)}) async-start(bf16[16,2,4096]{2,1,0:T(2,128)(2,1)} %reshape.349), calls=%async_computation.1 | async-start | bytes 524288 | tf_op jit(solution)/shard_map/all_to_all | solution.py:211
  19.5 2.9 %reduce.21 = bf16[128,1024]{1,0:T(8,128)(2,1)} reduce(bf16[128,1,1,1024]{3,2,1,0:T(2,128)(2,1)S(1)} %bitcast.219, bf16[]{:T(256)} %broadcast.113), dimensions={1,2}, to_apply=%bitcast.211.reduce_sub_computation | reduce | bytes 524290
  22.4 1.8 %reshape.351 = bf16[16,2,4096]{2,1,0:T(2,128)(2,1)} reshape(bf16[128,1024]{1,0:T(8,128)(2,1)} %reduce.21) | data formatting | bytes 524288
  24.2 5.8 %all-to-all-start = ((bf16[16,2,4096]{2,1,0:T(2,128)(2,1)}), bf16[16,2,4096]{2,1,0:T(2,128)(2,1)}, u32[]{:S(2)}, u32[]{:S(2)}) async-start(bf16[16,2,4096]{2,1,0:T(2,128)(2,1)} %reshape.351), calls=%async_computation | async-start | bytes 524288 | tf_op jit(solution)/shard_map/all_to_all | solution.py:194
  30.2 2.2 %pad_maximum_fusion.2 = (bf16[256,2,2,2,2,2,32]{0,6,5,4,3,2,1:T(8,128)(2,1)}, bf16[256,2,2,2,2,2,32]{0,6,3,1,4,2,5:T(8,128)(2,1)}) fusion(bf16[128,2,2,2,2,2,32]{0,6,5,4,3,2,1:T(8,128)(2,1)} %bitcast.39, bf16[128,2,2,2,2,2,32]{0,6,5,4,3,2,1:T(8,128)(2,1)} %bitcast.37), kind=kLoop, calls=%fused_computation.84 | loop fusion | flops 1048576 | bytes 1572864 | tf_op jit(solution)/shard_map/concatenate | solution.py:262
  34.2 5.9 %all-to-all-done = bf16[16,2,4096]{2,1,0:T(2,128)(2,1)} async-done(((bf16[16,2,4096]{2,1,0:T(2,128)(2,1)}), bf16[16,2,4096]{2,1,0:T(2,128)(2,1)}, u32[]{:S(2)}, u32[]{:S(2)}) %all-to-all-start) | async-done | bytes 262176 | tf_op jit(solution)/shard_map/all_to_all | solution.py:194
  40.1 2.2 %reshape.352 = bf16[128,1,1,1024]{3,2,1,0:T(2,128)(2,1)S(1)} reshape(bf16[16,2,4096]{2,1,0:T(2,128)(2,1)} %all-to-all-done) | data formatting | bytes 524288
  43.3 3.9 %convolution_convert_fusion = bf16[128,3072]{1,0:T(8,128)(2,1)S(1)} fusion(bf16[1024,3072]{1,0:T(8,128)(2,1)} %param.12, bf16[1,1,128,1024]{2,3,1,0:T(8,128)(2,1)} %copy.111), kind=kOutput, calls=%fused_computation.7 | convolution fusion | flops 805699584 | bytes 7340032 | tf_op jit(solution)/shard_map/dot_general | solution.py:201
  49.3 2.6 %fusion.106 = (f32[8,8,16]{2,1,0:T(8,128)S(1)}, f32[8,8,16,16]{2,3,1,0:T(8,128)}) fusion(pred[16,16]{0,1:T(8,128)(4,1)S(1)} %iota_compare_fusion.1, bf16[1,16,8,1,8,128]{5,2,4,3,1,0:T(8,128)(2,1)} %get-tuple-element.67, bf16[1,16,8,1,8,128]{5,2,4,3,1,0:T(8,128)(2,1)} %get-tuple-element.66), kind=kOutput, calls=%fused_computation.162 | convolution fusion | flops 4259855 | bytes 594176 | tf_op jit(solution)/shard_map/sub | solution.py:28
  51.9 2.1 %fusion.27 = bf16[1,16,8,1,8,128]{5,1,4,2,3,0:T(8,128)(2,1)} fusion(bf16[16,8,8,128]{3,2,1,0:T(8,128)(2,1)S(1)} %copy.197, f32[8,8,16,16]{2,3,1,0:T(8,128)} %get-tuple-element.77, f32[8,8,16]{2,1,0:T(8,128)S(1)} %get-tuple-element.76), kind=kOutput, calls=%fused_computation.50 | convolution fusion | flops 4358144 | bytes 593920 | tf_op jit(solution)/shard_map/bchlm,blche->bmche/dot_general | solution.py:64
  54.0 2.5 %fusion.33 = bf16[1,16,8,1,8,128]{5,1,4,2,3,0:T(8,128)(2,1)} fusion(f32[8,8,16,16]{2,3,1,0:T(8,128)S(1)} %convolution_bitcast_fusion, bf16[1,16,8,1,8,128]{5,2,4,3,1,0:T(8,128)(2,1)} %get-tuple-element.66, f32[8,8,16,16]{2,3,1,0:T(8,128)} %get-tuple-element.77, f32[8,8,16]{2,1,0:T(8,128)S(1)} %get-tuple-element.76), kind=kOutput, calls=%fused_computation.56 | convolution fusion | flops 4441103 | bytes 659456 | tf_op jit(solution)/shard_map/bchlm,blche->bmche/dot_general | solution.py:57
  56.5 2.4 %fusion.26 = bf16[1,16,8,1,8,128]{5,1,4,2,3,0:T(8,128)(2,1)} fusion(f32[8,8,16,16]{2,3,1,0:T(8,128)S(1)} %convolution_bitcast_fusion, bf16[1,16,8,1,8,128]{5,2,4,3,1,0:T(8,128)(2,1)S(1)} %copy-done.17, f32[8,8,16,16]{2,3,1,0:T(8,128)} %get-tuple-element.77, f32[8,8,16]{2,1,0:T(8,128)S(1)} %get-tuple-element.76), kind=kOutput, calls=%fused_computation.49 | convolution fusion | flops 4441103 | bytes 659456 | tf_op jit(solution)/shard_map/bchlm,bmche->blche/dot_general | solution.py:51
  63.2 5.7 %fusion.28 = bf16[1,16,8,1024]{3,2,0,1:T(8,128)(2,1)} fusion(bf16[128,3072]{1,0:T(8,128)(2,1)S(1)} %reshape_reshape.7, bf16[1024,3072]{1,0:T(8,128)(2,1)} %param.12), kind=kOutput, calls=%fused_computation.51 | convolution fusion | flops 805437440 | bytes 7340032 | tf_op jit(solution)/shard_map/dot_general | solution.py:219
  68.9 4.4 %all-to-all-start.2 = ((bf16[1,16,8,1024]{3,2,0,1:T(8,128)(2,1)}), bf16[1,16,8,1024]{3,2,0,1:T(8,128)(2,1)}, u32[]{:S(2)}, u32[]{:S(2)}) async-start(bf16[1,16,8,1024]{3,2,0,1:T(8,128)(2,1)} %fusion.28), calls=%async_computation.2 | async-start | bytes 524288 | tf_op jit(solution)/shard_map/all_to_all | solution.py:241
  74.4 2.1 %bitcast_select_fusion = (bf16[256,2,2,2,2,2,32]{0,6,3,1,2,4,5:T(8,128)(2,1)}, bf16[256,2,2,2,2,2,32]{0,6,3,1,2,4,5:T(8,128)(2,1)S(1)}) fusion(bf16[256,2,2,2,2,2,32]{0,6,3,1,4,2,5:T(8,128)(2,1)} %get-tuple-element.69, bf16[256,2,2,2,2,2,32]{0,6,5,4,3,2,1:T(8,128)(2,1)} %get-tuple-element.68, pred[]{:T(512)S(6)} %eq.44, ...), kind=kLoop, calls=%fused_computation.89 | loop fusion | flops 524288 | bytes 2621441 | tf_op jit(solution)/shard_map/jit(_where)/select_n | solution.py:112
  76.6 2.1 %fusion.5 = f32[512,3072]{1,0:T(8,128)S(1)} fusion(bf16[128,3072]{1,0:T(8,128)(2,1)} %collective-permute-done.1, bf16[128,3072]{1,0:T(8,128)(2,1)S(1)} %reshape_reshape.7, bf16[256,1024]{0,1:T(8,128)(2,1)S(1)} %bitcast.221, s32[]{:T(128)S(6)} %select_n.259), kind=kOutput, calls=%fused_computation.13 | convolution fusion | flops 808452096 | bytes 8126468 | tf_op jit(solution)/shard_map/dot_general | solution.py:236
  78.7 2.6 %copy-done.1 = f32[512,3072]{1,0:T(8,128)} copy-done((f32[512,3072]{1,0:T(8,128)}, f32[512,3072]{1,0:T(8,128)S(1)}, u32[]{:S(2)}) %copy-start.1) | copy-done | bytes 6291480
  87.3 2.2 %fusion.29 = bf16[1,16,8,8,128]{4,1,3,2,0:T(8,128)(2,1)} fusion(bf16[1,16,8,1,8,128]{5,2,4,3,1,0:T(8,128)(2,1)} %copy-done.9, f32[8,8,16,16]{2,3,1,0:T(8,128)} %get-tuple-element.77, f32[8,8,16]{2,1,0:T(8,128)S(1)} %get-tuple-element.76), kind=kOutput, calls=%fused_computation.52 | convolution fusion | flops 4358144 | bytes 593920 | tf_op jit(solution)/shard_map/bchlm,bmche->blche/dot_general | solution.py:31
  95.3 5.4 %all-to-all-start.3 = ((bf16[1,16,8,1024]{3,2,0,1:T(8,128)(2,1)}), bf16[1,16,8,1024]{3,2,0,1:T(8,128)(2,1)S(1)}, u32[]{:S(2)}, u32[]{:S(2)}) async-start(bf16[1,16,8,1024]{3,2,0,1:T(8,128)(2,1)} %bitcast.51), calls=%async_computation.3 | async-start | bytes 524288 | tf_op jit(solution)/shard_map/all_to_all | solution.py:277
  101.7 2.0 %collective-permute-start.10 = (bf16[2,2,2,32,1025]{4,3,2,1,0:T(8,128)(2,1)}, bf16[2,2,2,32,1025]{4,3,2,1,0:T(8,128)(2,1)}, u32[]{:S(2)}, u32[]{:S(2)}) collective-permute-start(bf16[2,2,2,32,1025]{4,3,2,1,0:T(8,128)(2,1)} %fusion.44), channel_id=1, source_target_pairs={{0,4},{1,5},{2,6},{3,7},{4,0},{5,1},{6,2},{7,3},{8,12},{9,13},{10,... | collective-permute-start | bytes 1574408 | tf_op jit(solution)/shard_map/ppermute | solution.py:153
  103.7 2.5 %collective-permute-done.2 = bf16[2,2,2,32,3072]{4,3,2,1,0:T(8,128)(2,1)} collective-permute-done((bf16[2,2,2,32,3072]{4,3,2,1,0:T(8,128)(2,1)}, bf16[2,2,2,32,3072]{4,3,2,1,0:T(8,128)(2,1)}, u32[]{:S(2)}, u32[]{:S(2)}) %collective-permute-start.2) | collective-permute-done | bytes 1572896 | tf_op jit(solution)/shard_map/ppermute | solution.py:153
  106.2 4.1 %fusion.9 = (bf16[2,2,32,3072]{3,2,1,0:T(8,128)(2,1)}, f32[2,2,32,3072]{3,2,1,0:T(8,128)}) fusion(f32[2,2,2,2,32,3072]{5,4,3,2,1,0:T(8,128)} %bitcast.213, s32[]{:T(128)S(6)} %select_n.266, s32[]{:T(128)S(6)} %select_n.276, bf16[2,2,2,32,3072]{4,3,2,1,0:T(8,128)(2,1)} %collective-permute-done.2, s32[]{:T(128)S(6)} %select_n.275, s32[]{:T(128)S(6)} %select_n.270, ...), kind=kLoop, calls=%fused_computation.18 | loop fusion | flops 1966080 | bytes 7077908 | tf_op jit(solution)/shard_map/convert_element_type | solution.py:149
  112.3 2.3 %fusion.32 = bf16[1,128,8,128]{1,3,2,0:T(8,128)(2,1)} fusion(bf16[128,8,128]{0,2,1:T(8,128)(2,1)S(1)} %bitcast.228, f32[8,128]{1,0:T(8,128)S(1)} %get-tuple-element.72, f32[8,128,128]{1,2,0:T(8,128)} %copy-done.10), kind=kOutput, calls=%fused_computation.55 | convolution fusion | flops 34079872 | bytes 1052672 | tf_op jit(solution)/shard_map/ghlm,glhe->gmhe/dot_general | solution.py:64
  115.6 2.8 %fusion.30 = bf16[1,128,8,128]{3,1,2,0:T(8,128)(2,1)} fusion(f32[8,128,128]{1,2,0:T(8,128)} %fusion.72, bf16[128,8,128]{2,1,0:T(8,128)(2,1)} %bitcast.236, f32[8,128,128]{1,2,0:T(8,128)} %get-tuple-element.73, f32[8,128]{1,0:T(8,128)S(1)} %get-tuple-element.72), kind=kOutput, calls=%fused_computation.53 | convolution fusion | flops 34604160 | bytes 1576960 | tf_op jit(solution)/shard_map/ghlm,gmhe->glhe/dot_general | solution.py:51
  118.4 2.7 %fusion.31 = bf16[1,128,8,128]{3,1,2,0:T(8,128)(2,1)} fusion(f32[8,128,128]{1,2,0:T(8,128)} %fusion.72, bf16[128,8,128]{2,1,0:T(8,128)(2,1)S(1)} %bitcast.234, f32[8,128,128]{1,2,0:T(8,128)} %get-tuple-element.73, f32[8,128]{1,0:T(8,128)S(1)} %get-tuple-element.72), kind=kOutput, calls=%fused_computation.54 | convolution fusion | flops 34604160 | bytes 1576960 | tf_op jit(solution)/shard_map/ghlm,glhe->gmhe/dot_general | solution.py:57
  124.5 2.0 %convert_add_fusion.2 = (f32[1,2,32,3072]{3,2,1,0:T(8,128)S(1)}, bf16[2,32,3072]{2,1,0:T(8,128)(2,1)}) fusion(f32[2,2,32,3072]{3,2,1,0:T(8,128)S(1)} %copy-done.3, s32[]{:T(128)S(6)} %select_n.284, bf16[2,2,32,3072]{3,2,1,0:T(8,128)(2,1)} %collective-permute-done.6, s32[]{:T(128)S(6)} %select_n.274), kind=kLoop, calls=%fused_computation.64 | loop fusion | flops 983040 | bytes 3538952 | tf_op jit(solution)/shard_map/add | solution.py:134
  130.6 4.3 %collective-permute-done.12 = bf16[2,32,1025]{2,1,0:T(8,128)(2,1)S(1)} collective-permute-done((bf16[2,32,1025]{2,1,0:T(8,128)(2,1)S(1)}, bf16[2,32,1025]{2,1,0:T(8,128)(2,1)S(1)}, u32[]{:S(2)}, u32[]{:S(2)}) %collective-permute-start.12) | collective-permute-done | bytes 131232 | tf_op jit(solution)/shard_map/ppermute | solution.py:153
  134.9 2.5 %collective-permute-start.13 = (bf16[32,1025]{1,0:T(8,128)(2,1)S(1)}, bf16[32,1025]{1,0:T(8,128)(2,1)S(1)}, u32[]{:S(2)}, u32[]{:S(2)}) collective-permute-start(bf16[32,1025]{1,0:T(8,128)(2,1)S(1)} %fusion.88), channel_id=1, source_target_pairs={{0,8},{1,9},{2,10},{3,11},{4,12},{5,13},{6,14},{7,15},{8,0},{9,1},... | collective-permute-start | bytes 196808 | tf_op jit(solution)/shard_map/ppermute | solution.py:153
  141.9 9.8 %collective-permute-done.8 = bf16[32,3072]{1,0:T(8,128)(2,1)S(1)} collective-permute-done((bf16[32,3072]{1,0:T(8,128)(2,1)S(1)}, bf16[32,3072]{1,0:T(8,128)(2,1)S(1)}, u32[]{:S(2)}, u32[]{:S(2)}) %collective-permute-start.8) | collective-permute-done | bytes 196640 | tf_op jit(solution)/shard_map/ppermute | solution.py:153
  159.2 1.8 %copy.145 = bf16[1,1,128,1024]{3,2,1,0:T(8,128)(2,1)} copy(bf16[1,1,128,1024]{2,3,1,0:T(8,128)(2,1)} %bitcast.237) | data formatting | bytes 524288
  161.4 1.8 %maximum_select_fusion = bf16[64,3072]{1,0:T(8,128)(2,1)} fusion(bf16[32,3072]{1,0:T(8,128)(2,1)} %fusion.63, bf16[32,3072]{1,0:T(8,128)(2,1)S(1)} %collective-permute-done.9, pred[]{:T(512)S(6)} %eq.45), kind=kLoop, calls=%fused_computation.94 | loop fusion | flops 1769472 | bytes 786433 | tf_op jit(solution)/shard_map/jit(_where)/select_n | solution.py:172
  (124 shorter events, 55.8 us)
Async XLA Ops:
  0.6 16.8 %copy-start = (bf16[1024,1024]{1,0:T(8,128)(2,1)S(1)}, bf16[1024,1024]{1,0:T(8,128)(2,1)}, u32[]{:S(2)}) copy-start(bf16[1024,1024]{1,0:T(8,128)(2,1)} %param.10) | copy-start | bytes 6291460
  0.6 12.5 %copy-start.11 = (bf16[1,1,128,1024]{3,2,1,0:T(8,128)(2,1)S(1)}, bf16[1,1,128,1024]{3,2,1,0:T(8,128)(2,1)}, u32[]{:S(2)}) copy-start(bf16[1,1,128,1024]{3,2,1,0:T(8,128)(2,1)} %param.7) | copy-start | bytes 786436
  4.8 9.5 %copy-start.12 = (bf16[1,1,128,1024]{3,2,1,0:T(8,128)(2,1)S(1)}, bf16[1,1,128,1024]{3,2,1,0:T(8,128)(2,1)}, u32[]{:S(2)}) copy-start(bf16[1,1,128,1024]{3,2,1,0:T(8,128)(2,1)} %param.9) | copy-start | bytes 786436
  5.7 18.4 %all-to-all-start.1 = ((bf16[16,2,4096]{2,1,0:T(2,128)(2,1)}), bf16[16,2,4096]{2,1,0:T(2,128)(2,1)S(1)}, u32[]{:S(2)}, u32[]{:S(2)}) async-start(bf16[16,2,4096]{2,1,0:T(2,128)(2,1)} %reshape.349), calls=%async_computation.1 | async-start | bytes 524288 | tf_op jit(solution)/shard_map/all_to_all | solution.py:211
  14.4 2.6 %copy-start.7 = (bf16[16,8,8,128]{3,2,1,0:T(8,128)(2,1)}, bf16[16,8,8,128]{3,2,1,0:T(8,128)(2,1)S(1)}, u32[]{:S(2)}) copy-start(bf16[16,8,8,128]{3,2,1,0:T(8,128)(2,1)S(1)} %copy.157) | copy-start | bytes 786436
  15.0 3.9 %copy-start.10 = (f32[8,128,128]{1,2,0:T(8,128)}, f32[8,128,128]{1,2,0:T(8,128)S(1)}, u32[]{:S(2)}) copy-start(f32[8,128,128]{1,2,0:T(8,128)S(1)} %fusion.21) | copy-start | bytes 1572868
  16.0 3.0 %copy-start.18 = (f32[1024]{0:T(1024)S(1)}, f32[1024]{0:T(1024)}, u32[]{:S(2)}) copy-start(f32[1024]{0:T(1024)} %param.11) | copy-start | bytes 12292
  17.0 13.1 %collective-permute-start.3 = (bf16[128,1024]{0,1:T(8,128)(2,1)}, bf16[128,1024]{0,1:T(8,128)(2,1)}, u32[]{:S(2)}, u32[]{:S(2)}) collective-permute-start(bf16[128,1024]{0,1:T(8,128)(2,1)} %bitcast.3), channel_id=1, source_target_pairs={{0,1},{1,0},{2,3},{3,2},{4,5},{5,4},{6,7},{7,6},{8,9},{9,8},{10,11... | collective-permute-start | bytes 786440 | tf_op jit(solution)/shard_map/ppermute | solution.py:260
  24.2 15.9 %all-to-all-start = ((bf16[16,2,4096]{2,1,0:T(2,128)(2,1)}), bf16[16,2,4096]{2,1,0:T(2,128)(2,1)}, u32[]{:S(2)}, u32[]{:S(2)}) async-start(bf16[16,2,4096]{2,1,0:T(2,128)(2,1)} %reshape.351), calls=%async_computation | async-start | bytes 524288 | tf_op jit(solution)/shard_map/all_to_all | solution.py:194
  58.9 14.4 %collective-permute-start = (bf16[128,1024]{0,1:T(8,128)(2,1)}, bf16[128,1024]{0,1:T(8,128)(2,1)}, u32[]{:S(2)}, u32[]{:S(2)}) collective-permute-start(bf16[128,1024]{0,1:T(8,128)(2,1)} %bitcast.6), channel_id=1, source_target_pairs={{0,1},{1,0},{2,3},{3,2},{4,5},{5,4},{6,7},{7,6},{8,9},{9,8},{10,11... | collective-permute-start | bytes 786440 | tf_op jit(solution)/shard_map/ppermute | solution.py:235
  62.6 13.9 %collective-permute-start.1 = (bf16[128,3072]{1,0:T(8,128)(2,1)S(1)}, bf16[128,3072]{1,0:T(8,128)(2,1)}, u32[]{:S(2)}, u32[]{:S(2)}) collective-permute-start(bf16[128,3072]{1,0:T(8,128)(2,1)S(1)} %reshape_reshape.7), channel_id=1, source_target_pairs={{0,1},{1,0},{2,3},{3,2},{4,5},{5,4},{6,7},{7,6},{8,9},{9,8},{10,11... | collective-permute-start | bytes 2359304 | tf_op jit(solution)/shard_map/ppermute | solution.py:235
  68.9 14.2 %all-to-all-start.2 = ((bf16[1,16,8,1024]{3,2,0,1:T(8,128)(2,1)}), bf16[1,16,8,1024]{3,2,0,1:T(8,128)(2,1)}, u32[]{:S(2)}, u32[]{:S(2)}) async-start(bf16[1,16,8,1024]{3,2,0,1:T(8,128)(2,1)} %fusion.28), calls=%async_computation.2 | async-start | bytes 524288 | tf_op jit(solution)/shard_map/all_to_all | solution.py:241
  78.7 2.7 %copy-start.1 = (f32[512,3072]{1,0:T(8,128)}, f32[512,3072]{1,0:T(8,128)S(1)}, u32[]{:S(2)}) copy-start(f32[512,3072]{1,0:T(8,128)S(1)} %fusion.5) | copy-start | bytes 18874372
  82.8 6.6 %copy-start.4 = (bf16[256,2,2,2,2,2,32]{0,6,3,1,2,4,5:T(8,128)(2,1)S(1)}, bf16[256,2,2,2,2,2,32]{0,6,3,1,2,4,5:T(8,128)(2,1)}, u32[]{:S(2)}) copy-start(bf16[256,2,2,2,2,2,32]{0,6,3,1,2,4,5:T(8,128)(2,1)} %get-tuple-element.78) | copy-start | bytes 1572868
  84.3 6.0 %collective-permute-start.5 = (f32[1024]{0:T(1024)S(1)}, f32[1024]{0:T(1024)S(1)}, u32[]{:S(2)}, u32[]{:S(2)}) collective-permute-start(f32[1024]{0:T(1024)S(1)} %get-tuple-element.56), channel_id=1, source_target_pairs={{0,1},{1,0},{2,3},{3,2},{4,5},{5,4},{6,7},{7,6},{8,9},{9,8},{10,11... | collective-permute-start | bytes 12296 | tf_op jit(solution)/shard_map/ppermute | solution.py:260
  84.4 21.9 %collective-permute-start.2 = (bf16[2,2,2,32,3072]{4,3,2,1,0:T(8,128)(2,1)}, bf16[2,2,2,32,3072]{4,3,2,1,0:T(8,128)(2,1)}, u32[]{:S(2)}, u32[]{:S(2)}) collective-permute-start(bf16[2,2,2,32,3072]{4,3,2,1,0:T(8,128)(2,1)} %fusion.4), channel_id=1, source_target_pairs={{0,2},{1,17},{2,0},{3,19},{4,6},{5,21},{6,4},{7,23},{8,10},{9,25},... | collective-permute-start | bytes 4718600 | tf_op jit(solution)/shard_map/ppermute | solution.py:153
  86.9 3.9 %collective-permute-start.4 = (bf16[128,1024]{1,0:T(8,128)(2,1)S(1)}, bf16[128,1024]{1,0:T(8,128)(2,1)S(1)}, u32[]{:S(2)}, u32[]{:S(2)}) collective-permute-start(bf16[128,1024]{1,0:T(8,128)(2,1)S(1)} %fusion.53), channel_id=1, source_target_pairs={{0,1},{1,0},{2,3},{3,2},{4,5},{5,4},{6,7},{7,6},{8,9},{9,8},{10,11... | collective-permute-start | bytes 786440 | tf_op jit(solution)/shard_map/ppermute | solution.py:260
  95.3 15.9 %all-to-all-start.3 = ((bf16[1,16,8,1024]{3,2,0,1:T(8,128)(2,1)}), bf16[1,16,8,1024]{3,2,0,1:T(8,128)(2,1)S(1)}, u32[]{:S(2)}, u32[]{:S(2)}) async-start(bf16[1,16,8,1024]{3,2,0,1:T(8,128)(2,1)} %bitcast.51), calls=%async_computation.3 | async-start | bytes 524288 | tf_op jit(solution)/shard_map/all_to_all | solution.py:277
  101.7 19.5 %collective-permute-start.10 = (bf16[2,2,2,32,1025]{4,3,2,1,0:T(8,128)(2,1)}, bf16[2,2,2,32,1025]{4,3,2,1,0:T(8,128)(2,1)}, u32[]{:S(2)}, u32[]{:S(2)}) collective-permute-start(bf16[2,2,2,32,1025]{4,3,2,1,0:T(8,128)(2,1)} %fusion.44), channel_id=1, source_target_pairs={{0,4},{1,5},{2,6},{3,7},{4,0},{5,1},{6,2},{7,3},{8,12},{9,13},{10,... | collective-permute-start | bytes 1574408 | tf_op jit(solution)/shard_map/ppermute | solution.py:153
  110.3 4.3 %copy-start.8 = (bf16[16,8,8,128]{3,2,1,0:T(8,128)(2,1)S(1)}, bf16[16,8,8,128]{3,2,1,0:T(8,128)(2,1)}, u32[]{:S(2)}) copy-start(bf16[16,8,8,128]{3,2,1,0:T(8,128)(2,1)} %copy-done.7) | copy-start | bytes 786436
  111.3 7.2 %copy-start.5 = (bf16[1,16,8,1024]{3,2,0,1:T(8,128)(2,1)}, bf16[1,16,8,1024]{3,2,0,1:T(8,128)(2,1)S(1)}, u32[]{:S(2)}) copy-start(bf16[1,16,8,1024]{3,2,0,1:T(8,128)(2,1)S(1)} %all-to-all-done.3) | copy-start | bytes 786436
  111.3 13.2 %collective-permute-start.6 = (bf16[2,2,32,3072]{3,2,1,0:T(8,128)(2,1)}, bf16[2,2,32,3072]{3,2,1,0:T(8,128)(2,1)}, u32[]{:S(2)}, u32[]{:S(2)}) collective-permute-start(bf16[2,2,32,3072]{3,2,1,0:T(8,128)(2,1)} %get-tuple-element.20), channel_id=1, source_target_pairs={{0,16},{1,5},{2,18},{3,7},{4,20},{5,1},{6,22},{7,3},{8,24},{9,13},... | collective-permute-start | bytes 2359304 | tf_op jit(solution)/shard_map/ppermute | solution.py:153
  114.6 3.8 %copy-start.14 = (bf16[16,8,8,128]{3,2,1,0:T(8,128)(2,1)S(1)}, bf16[16,8,8,128]{3,2,1,0:T(8,128)(2,1)}, u32[]{:S(2)}) copy-start(bf16[16,8,8,128]{3,2,1,0:T(8,128)(2,1)} %copy-done.13) | copy-start | bytes 786436
  121.1 3.4 %copy-start.3 = (f32[2,2,32,3072]{3,2,1,0:T(8,128)S(1)}, f32[2,2,32,3072]{3,2,1,0:T(8,128)}, u32[]{:S(2)}) copy-start(f32[2,2,32,3072]{3,2,1,0:T(8,128)} %get-tuple-element.58) | copy-start | bytes 4718596
  122.8 6.8 %collective-permute-start.11 = (bf16[2,2,32,1025]{3,2,1,0:T(8,128)(2,1)S(1)}, bf16[2,2,32,1025]{3,2,1,0:T(8,128)(2,1)S(1)}, u32[]{:S(2)}, u32[]{:S(2)}) collective-permute-start(bf16[2,2,32,1025]{3,2,1,0:T(8,128)(2,1)S(1)} %get-tuple-element.59), channel_id=1, source_target_pairs={{0,2},{1,17},{2,0},{3,19},{4,6},{5,21},{6,4},{7,23},{8,10},{9,25},... | collective-permute-start | bytes 787208 | tf_op jit(solution)/shard_map/ppermute | solution.py:153
  126.5 10.9 %collective-permute-start.7 = (bf16[2,32,3072]{2,1,0:T(8,128)(2,1)}, bf16[2,32,3072]{2,1,0:T(8,128)(2,1)}, u32[]{:S(2)}, u32[]{:S(2)}) collective-permute-start(bf16[2,32,3072]{2,1,0:T(8,128)(2,1)} %get-tuple-element.25), channel_id=1, source_target_pairs={{0,4},{1,3},{2,6},{3,1},{4,0},{5,7},{6,2},{7,5},{8,12},{9,11},{10,... | collective-permute-start | bytes 1179656 | tf_op jit(solution)/shard_map/ppermute | solution.py:153
  129.7 5.2 %collective-permute-start.12 = (bf16[2,32,1025]{2,1,0:T(8,128)(2,1)S(1)}, bf16[2,32,1025]{2,1,0:T(8,128)(2,1)S(1)}, u32[]{:S(2)}, u32[]{:S(2)}) collective-permute-start(bf16[2,32,1025]{2,1,0:T(8,128)(2,1)S(1)} %get-tuple-element.63), channel_id=1, source_target_pairs={{0,16},{1,3},{2,18},{3,1},{4,20},{5,7},{6,22},{7,5},{8,24},{9,11},... | collective-permute-start | bytes 393608 | tf_op jit(solution)/shard_map/ppermute | solution.py:153
  134.9 5.3 %collective-permute-start.13 = (bf16[32,1025]{1,0:T(8,128)(2,1)S(1)}, bf16[32,1025]{1,0:T(8,128)(2,1)S(1)}, u32[]{:S(2)}, u32[]{:S(2)}) collective-permute-start(bf16[32,1025]{1,0:T(8,128)(2,1)S(1)} %fusion.88), channel_id=1, source_target_pairs={{0,8},{1,9},{2,10},{3,11},{4,12},{5,13},{6,14},{7,15},{8,0},{9,1},... | collective-permute-start | bytes 196808 | tf_op jit(solution)/shard_map/ppermute | solution.py:153
  138.4 13.4 %collective-permute-start.8 = (bf16[32,3072]{1,0:T(8,128)(2,1)S(1)}, bf16[32,3072]{1,0:T(8,128)(2,1)S(1)}, u32[]{:S(2)}, u32[]{:S(2)}) collective-permute-start(bf16[32,3072]{1,0:T(8,128)(2,1)S(1)} %fusion.80), channel_id=1, source_target_pairs={{0,8},{1,9},{2,10},{3,11},{4,12},{5,13},{6,14},{7,15},{8,0},{9,1},... | collective-permute-start | bytes 589832 | tf_op jit(solution)/shard_map/ppermute | solution.py:153
  140.2 13.7 %collective-permute-start.14 = (bf16[32,1025]{1,0:T(8,128)(2,1)S(1)}, bf16[32,1025]{1,0:T(8,128)(2,1)S(1)}, u32[]{:S(2)}, u32[]{:S(2)}) collective-permute-start(bf16[32,1025]{1,0:T(8,128)(2,1)S(1)} %fusion.83), channel_id=1, source_target_pairs={{0,16},{16,0},{1,17},{17,1},{2,18},{18,2},{3,19},{19,3},{4,20},{20... | collective-permute-start | bytes 196808 | tf_op jit(solution)/shard_map/ppermute | solution.py:169
  153.4 9.8 %copy-start.6 = (bf16[1,16,8,1024]{3,2,0,1:T(8,128)(2,1)S(1)}, bf16[1,16,8,1024]{3,2,0,1:T(8,128)(2,1)}, u32[]{:S(2)}) copy-start(bf16[1,16,8,1024]{3,2,0,1:T(8,128)(2,1)} %copy-done.5) | copy-start | bytes 786436
  153.4 8.0 %collective-permute-start.9 = (bf16[32,3072]{1,0:T(8,128)(2,1)}, bf16[32,3072]{1,0:T(8,128)(2,1)S(1)}, u32[]{:S(2)}, u32[]{:S(2)}) collective-permute-start(bf16[32,3072]{1,0:T(8,128)(2,1)} %fusion.63), channel_id=1, source_target_pairs={{0,16},{16,0},{1,17},{17,1},{2,18},{18,2},{3,19},{19,3},{4,20},{20... | collective-permute-start | bytes 589832 | tf_op jit(solution)/shard_map/ppermute | solution.py:169
  (6 other events, 8.8 us)

commit v10 on v7

--- a/solution.py
+++ b/solution.py
@@ -1,6 +1,8 @@
 import jax
 import jax.numpy as jnp
 from jax import lax
+from jax.experimental import pallas as pl
+from jax.experimental.pallas import tpu as pltpu
 from jax.sharding import PartitionSpec as P
 
 HEAD_DIM = 128
@@ -73,6 +75,56 @@
         grad_value.astype(jnp.bfloat16),
     )
 
+
+def _times_kernel(x_ref, w_ref, o_ref):
+    o_ref[...] = jnp.dot(x_ref[...], w_ref[...], preferred_element_type=jnp.float32).astype(o_ref.dtype)
+
+
+def times_weight(x, w, tile=512):
+    rows, inner = x.shape
+    width = w.shape[1]
+    return pl.pallas_call(
+        _times_kernel,
+        grid=(width // tile,),
+        in_specs=[
+            pl.BlockSpec((rows, inner), lambda j: (0, 0)),
+            pl.BlockSpec((inner, tile), lambda j: (0, j)),
+        ],
+        out_specs=pl.BlockSpec((rows, tile), lambda j: (0, j)),
+        out_shape=jax.ShapeDtypeStruct((rows, width), jnp.bfloat16),
+    )(x, w)
+
+
+def _times_t_kernel(x_ref, w_ref, o_ref, acc_ref):
+    step = pl.program_id(0)
+
+    @pl.when(step == 0)
+    def _():
+        acc_ref[...] = jnp.zeros_like(acc_ref)
+
+    acc_ref[...] += lax.dot_general(
+        x_ref[...], w_ref[...], (((1,), (1,)), ((), ())), preferred_element_type=jnp.float32
+    )
+
+    @pl.when(step == pl.num_programs(0) - 1)
+    def _():
+        o_ref[...] = acc_ref[...].astype(o_ref.dtype)
+
+
+def times_weight_t(x, w, tile=512):
+    rows, inner = x.shape
+    width = w.shape[0]
+    return pl.pallas_call(
+        _times_t_kernel,
+        grid=(inner // tile,),
+        in_specs=[
+            pl.BlockSpec((rows, tile), lambda k: (0, k)),
+            pl.BlockSpec((width, tile), lambda k: (0, k)),
+        ],
+        out_specs=pl.BlockSpec((rows, width), lambda k: (0, 0)),
+        out_shape=jax.ShapeDtypeStruct((rows, width), jnp.bfloat16),
+        scratch_shapes=[pltpu.VMEM((rows, width), jnp.float32)],
+    )(x, w)
 
 def split_orders(seq_n, dp_n, z_first=False):
     bits = seq_n.bit_length() - 1
@@ -188,10 +240,8 @@
         concat_axis=1,
         tiled=True,
     )
-    joint_flat = jnp.dot(
-        normed_cols.reshape(-1, model_width), joint_weight, preferred_element_type=jnp.float32
-    )
-    joint_cols = joint_flat.astype(jnp.bfloat16).reshape(
+    joint_flat = times_weight(normed_cols.reshape(-1, model_width), joint_weight)
+    joint_cols = joint_flat.reshape(
         batches, normed_cols.shape[1], normed_cols.shape[2], 3 * feature
     )
     all_rows, col_share = (joint_cols.shape[1], joint_cols.shape[2])
@@ -206,9 +256,7 @@
     stacked = jnp.stack(grads_cols, axis=3).reshape(batches, all_rows, col_share, 3 * feature)
     used_normed = normed_cols.reshape(-1, model_width)
     used_grads = stacked.reshape(-1, 3 * feature)
-    grad_local = jnp.dot(used_grads, joint_weight.T, preferred_element_type=jnp.float32).astype(
-        jnp.bfloat16
-    )
+    grad_local = times_weight_t(used_grads, joint_weight)
     seq_n = lax.axis_size("seq")
     dp_n = lax.axis_size("dp")
     orders = split_orders(seq_n, dp_n)

time: 162 us -> 167 us (1.031)
  Pallas kernels: 0 us -> 12.9 us
  matrix products: 39.6 us -> 31.6 us
  local copies, waits for them, and re-layouts: 35.3 us -> 38.6 us
  waiting for transfers between devices: 26.8 us -> 24.4 us
  other arithmetic: 21.7 us -> 19.9 us
    pallas_call x0 -> x2, Pallas kernels: none -> 12.9 us  [the longest x1 6.71 us: times_weight_t(): pl.pallas_call(_times_t_kernel, grid=(inner // tile,), in_specs=[pl.Block...]
    dot_general x2 -> x0, matrix products: 9.57 us -> none  [the longest x1 5.68 us: on_device(): jnp.dot(used_grads, joint_weight.T, preferred_element_type=jnp.float32)]
    unnamed x54 -> x57, local copies, waits for them, and re-layouts: 20.7 us -> 22.8 us
    another operation x3 -> x2, local copies, waits for them, and re-layouts: 3.48 us -> 2.05 us
  transfers between devices with their start and end apart: 19 -> 19, of which waited for: 7 -> 7; matrix products, arithmetic and copies ran while one was open for 39% -> 44% of each run, Pallas kernels for 0% -> 8%
where the time goes in v10:
time: 167 us; the launch traced here: 165 us
  local copies, waits for them, and re-layouts  38.6 us (23%)
  starting transfers between devices  36.8 us (22%)
  matrix products  31.6 us (19%)
  waiting for transfers between devices  24.4 us (15%)
  other arithmetic  19.9 us (12%)
  Pallas kernels  12.9 us (8%)
    unnamed x57, local copies, waits for them, and re-layouts  22.8 us
    ppermute x8, waiting for transfers between devices, reduce_rows(): lax.ppermute(given, ('dp', 'seq'), perm).astype(jnp.float32)  15.5 us
    ppermute x8, starting transfers between devices, reduce_rows(): lax.ppermute(given, ('dp', 'seq'), perm).astype(jnp.float32)  12.8 us
    all_to_all x1, starting transfers between devices, on_device(): lax.all_to_all(upstream, 'seq', split_axis=2, concat_axis=1, tiled=True)  7.39 us
    add x6, other arithmetic, reduce_rows(): kept + lax.ppermute(given, ('dp', 'seq'), perm).astype(jnp.float32)  7.28 us
    pallas_call x1, Pallas kernels, times_weight_t(): pl.pallas_call(_times_t_kernel, grid=(inner // tile,), in_specs=[pl.Block...  6.71 us
    pallas_call x1, Pallas kernels, times_weight(): pl.pallas_call(_times_kernel, grid=(width // tile,), in_specs=[pl.BlockSp...  6.23 us
    all_to_all x1, starting transfers between devices, on_device(): lax.all_to_all(normed.reshape(batches, local_rows, columns, model_width),...  5.83 us
  transfers between devices with their start and end apart: 19, of which 7 were waited for; matrix products, arithmetic and copies ran while one was open for 44% of the time, Pallas kernels for 8%

profile of v10, /device:TPU:0, one launch (start us, length us, event | category | flops | bytes accessed | tf_op | source)
XLA Modules:
  0.0 165.5 jit_solution(301334265275921007)
XLA Ops:
  2.7 2.1 %reduce.20 = bf16[128,1024]{1,0:T(8,128)(2,1)S(1)} reduce(bf16[128,1,1,1024]{3,2,1,0:T(2,128)(2,1)S(1)} %bitcast.186, bf16[]{:T(256)} %broadcast.113), dimensions={1,2}, to_apply=%bitcast.175.reduce_sub_computation | reduce | bytes 524290
  5.7 7.4 %all-to-all-start.1 = ((bf16[16,2,4096]{2,1,0:T(2,128)(2,1)}), bf16[16,2,4096]{2,1,0:T(2,128)(2,1)S(1)}, u32[]{:S(2)}, u32[]{:S(2)}) async-start(bf16[16,2,4096]{2,1,0:T(2,128)(2,1)} %reshape.311), calls=%async_computation.1 | async-start | bytes 524288 | tf_op jit(solution)/shard_map/all_to_all | solution.py:251
  16.7 2.0 %convolution_convert_fusion.2 = bf16[8,128,128]{1,2,0:T(8,128)(2,1)} fusion(bf16[128,8,128]{2,1,0:T(8,128)(2,1)} %bitcast.199, f32[8,128]{1,0:T(8,128)S(1)} %get-tuple-element.59, f32[8,128,128]{1,2,0:T(8,128)S(1)} %fusion.20), kind=kOutput, calls=%fused_computation.36 | convolution fusion | flops 34079872 | bytes 1052672 | tf_op jit(solution)/shard_map/ghlm,gmhe->glhe/dot_general | solution.py:33
  21.2 2.9 %reduce.21 = bf16[128,1024]{1,0:T(8,128)(2,1)} reduce(bf16[128,1,1,1024]{3,2,1,0:T(2,128)(2,1)S(1)} %bitcast.187, bf16[]{:T(256)} %broadcast.113), dimensions={1,2}, to_apply=%bitcast.176.reduce_sub_computation | reduce | bytes 524290
  24.1 1.8 %reshape.313 = bf16[16,2,4096]{2,1,0:T(2,128)(2,1)} reshape(bf16[128,1024]{1,0:T(8,128)(2,1)} %reduce.21) | data formatting | bytes 524288
  25.9 5.8 %all-to-all-start = ((bf16[16,2,4096]{2,1,0:T(2,128)(2,1)}), bf16[16,2,4096]{2,1,0:T(2,128)(2,1)}, u32[]{:S(2)}, u32[]{:S(2)}) async-start(bf16[16,2,4096]{2,1,0:T(2,128)(2,1)} %reshape.313), calls=%async_computation | async-start | bytes 524288 | tf_op jit(solution)/shard_map/all_to_all | solution.py:236
  31.9 2.1 %pad_maximum_fusion.2 = (bf16[256,2,2,2,2,2,32]{0,6,5,4,3,2,1:T(8,128)(2,1)}, bf16[256,2,2,2,2,2,32]{0,6,3,1,4,2,5:T(8,128)(2,1)}) fusion(bf16[128,2,2,2,2,2,32]{0,6,5,4,3,2,1:T(8,128)(2,1)} %bitcast.46, bf16[128,2,2,2,2,2,32]{0,6,5,4,3,2,1:T(8,128)(2,1)} %bitcast.44), kind=kLoop, calls=%fused_computation.75 | loop fusion | flops 1048576 | bytes 1572864 | tf_op jit(solution)/shard_map/concatenate | solution.py:296
  36.6 5.3 %all-to-all-done = bf16[16,2,4096]{2,1,0:T(2,128)(2,1)} async-done(((bf16[16,2,4096]{2,1,0:T(2,128)(2,1)}), bf16[16,2,4096]{2,1,0:T(2,128)(2,1)}, u32[]{:S(2)}, u32[]{:S(2)}) %all-to-all-start) | async-done | bytes 262176 | tf_op jit(solution)/shard_map/all_to_all | solution.py:236
  41.8 2.2 %reshape.314 = bf16[128,1,1,1024]{3,2,1,0:T(2,128)(2,1)S(1)} reshape(bf16[16,2,4096]{2,1,0:T(2,128)(2,1)} %all-to-all-done) | data formatting | bytes 524288
  44.8 6.2 %shard_map.126 = bf16[128,3072]{1,0:T(8,128)(2,1)} custom-call(bf16[128,1024]{1,0:T(8,128)(2,1)} %bitcast.191, bf16[1024,3072]{1,0:T(8,128)(2,1)} %w_ref.3), custom_call_target="tpu_custom_call" | custom-call | tf_op jit(solution)/shard_map/pallas_call | solution.py:86
  51.0 2.0 %fusion.90 = (bf16[1,16,8,1,8,128]{5,2,4,3,1,0:T(8,128)(2,1)S(1)}, bf16[1,16,8,1,8,128]{5,2,4,3,1,0:T(8,128)(2,1)}, bf16[1,16,8,1,8,128]{5,2,4,3,1,0:T(8,128)(2,1)}) fusion(bf16[1,16,8,3,8,128]{5,2,4,3,1,0:T(8,128)(2,1)} %bitcast.183), kind=kLoop, calls=%fused_computation.144 | loop fusion | bytes 1572864 | tf_op jit(solution)/shard_map/slice | solution.py:249
  53.7 2.3 %convolution_bitcast_fusion = f32[8,8,16,16]{2,3,1,0:T(8,128)} fusion(bf16[1,16,8,1,8,128]{5,2,4,3,1,0:T(8,128)(2,1)S(1)} %get-tuple-element.52, bf16[16,8,8,128]{3,2,1,0:T(8,128)(2,1)} %copy.232), kind=kOutput, calls=%fused_computation.21 | convolution fusion | flops 4194304 | bytes 589824 | tf_op jit(solution)/shard_map/blche,bmche->bchlm/dot_general | solution.py:45
  55.9 2.6 %fusion.92 = (f32[8,8,16]{2,1,0:T(8,128)S(1)}, f32[8,8,16,16]{2,3,1,0:T(8,128)}) fusion(pred[16,16]{0,1:T(8,128)(4,1)S(1)} %iota_compare_fusion.1, bf16[1,16,8,1,8,128]{5,2,4,3,1,0:T(8,128)(2,1)} %get-tuple-element.54, bf16[1,16,8,1,8,128]{5,2,4,3,1,0:T(8,128)(2,1)} %get-tuple-element.53), kind=kOutput, calls=%fused_computation.146 | convolution fusion | flops 4259855 | bytes 594176 | tf_op jit(solution)/shard_map/sub | solution.py:30
  58.6 2.1 %fusion.29 = bf16[1,16,8,1,8,128]{5,1,4,2,3,0:T(8,128)(2,1)} fusion(bf16[16,8,8,128]{3,2,1,0:T(8,128)(2,1)} %copy.232, f32[8,8,16,16]{2,3,1,0:T(8,128)} %get-tuple-element.64, f32[8,8,16]{2,1,0:T(8,128)S(1)} %get-tuple-element.63), kind=kOutput, calls=%fused_computation.49 | convolution fusion | flops 4358144 | bytes 593920 | tf_op jit(solution)/shard_map/bchlm,blche->bmche/dot_general | solution.py:66
  60.7 2.9 %fusion.31 = bf16[1,16,8,1,8,128]{5,1,4,2,3,0:T(8,128)(2,1)} fusion(f32[8,8,16,16]{2,3,1,0:T(8,128)} %convolution_bitcast_fusion, bf16[1,16,8,1,8,128]{5,2,4,3,1,0:T(8,128)(2,1)} %get-tuple-element.53, f32[8,8,16,16]{2,3,1,0:T(8,128)} %get-tuple-element.64, f32[8,8,16]{2,1,0:T(8,128)S(1)} %get-tuple-element.63), kind=kOutput, calls=%fused_computation.51 | convolution fusion | flops 4441103 | bytes 659456 | tf_op jit(solution)/shard_map/bchlm,blche->bmche/dot_general | solution.py:59
  63.5 2.8 %fusion.28 = bf16[1,16,8,1,8,128]{5,1,4,2,3,0:T(8,128)(2,1)} fusion(f32[8,8,16,16]{2,3,1,0:T(8,128)} %convolution_bitcast_fusion, bf16[1,16,8,1,8,128]{5,2,4,3,1,0:T(8,128)(2,1)} %get-tuple-element.54, f32[8,8,16,16]{2,3,1,0:T(8,128)} %get-tuple-element.64, f32[8,8,16]{2,1,0:T(8,128)S(1)} %get-tuple-element.63), kind=kOutput, calls=%fused_computation.48 | convolution fusion | flops 4441103 | bytes 659456 | tf_op jit(solution)/shard_map/bchlm,bmche->blche/dot_general | solution.py:53
  70.9 6.7 %shard_map.127 = bf16[128,1024]{1,0:T(8,128)(2,1)} custom-call(bf16[128,3072]{1,0:T(8,128)(2,1)} %bitcast.25.x_ref, bf16[1024,3072]{1,0:T(8,128)(2,1)} %w_ref.3), custom_call_target="tpu_custom_call" | custom-call | tf_op jit(solution)/shard_map/pallas_call | solution.py:117
  77.7 3.7 %all-to-all-start.2 = ((bf16[1,16,8,1024]{3,2,0,1:T(8,128)(2,1)}), bf16[1,16,8,1024]{3,2,0,1:T(8,128)(2,1)S(1)}, u32[]{:S(2)}, u32[]{:S(2)}) async-start(bf16[1,16,8,1024]{3,2,0,1:T(8,128)(2,1)} %bitcast.192), calls=%async_computation.2 | async-start | bytes 524288 | tf_op jit(solution)/shard_map/all_to_all | solution.py:279
  81.3 2.2 %fusion.30 = bf16[1,16,8,8,128]{4,1,3,2,0:T(8,128)(2,1)} fusion(bf16[1,16,8,1,8,128]{5,2,4,3,1,0:T(8,128)(2,1)} %copy-done.17, f32[8,8,16,16]{2,3,1,0:T(8,128)} %get-tuple-element.64, f32[8,8,16]{2,1,0:T(8,128)S(1)} %get-tuple-element.63), kind=kOutput, calls=%fused_computation.50 | convolution fusion | flops 4358144 | bytes 593920 | tf_op jit(solution)/shard_map/bchlm,bmche->blche/dot_general | solution.py:33
  84.8 2.4 %fusion.5 = f32[512,3072]{1,0:T(8,128)S(1)} fusion(bf16[128,3072]{1,0:T(8,128)(2,1)} %collective-permute-done.1, bf16[128,3072]{1,0:T(8,128)(2,1)} %bitcast.25.x_ref, bf16[256,1024]{0,1:T(8,128)(2,1)S(1)} %bitcast.189, s32[]{:T(128)S(6)} %select_n.231), kind=kOutput, calls=%fused_computation.11 | convolution fusion | flops 808452096 | bytes 8126468 | tf_op jit(solution)/shard_map/dot_general | solution.py:274
  87.2 2.7 %copy-done.1 = f32[512,3072]{1,0:T(8,128)} copy-done((f32[512,3072]{1,0:T(8,128)}, f32[512,3072]{1,0:T(8,128)S(1)}, u32[]{:S(2)}) %copy-start.1) | copy-done | bytes 6291480
  102.4 2.6 %convolution_convert_fusion = bf16[8,128,128]{1,2,0:T(8,128)(2,1)} fusion(bf16[128,8,128]{0,2,1:T(8,128)(2,1)S(1)} %bitcast.198, f32[8,128,128]{1,2,0:T(8,128)} %fusion.64, f32[8,128,128]{1,2,0:T(8,128)} %get-tuple-element.60, f32[8,128]{1,0:T(8,128)S(1)} %get-tuple-element.59), kind=kOutput, calls=%fused_computation.34 | convolution fusion | flops 34604160 | bytes 1576960 | tf_op jit(solution)/shard_map/ghlm,gmhe->glhe/dot_general | solution.py:53
  105.0 2.6 %convolution_convert_fusion.5 = bf16[8,128,128]{1,2,0:T(8,128)(2,1)} fusion(bf16[128,8,128]{0,2,1:T(8,128)(2,1)S(1)} %bitcast.196, f32[8,128,128]{1,2,0:T(8,128)} %fusion.64, f32[8,128,128]{1,2,0:T(8,128)} %get-tuple-element.60, f32[8,128]{1,0:T(8,128)S(1)} %get-tuple-element.59), kind=kOutput, calls=%fused_computation.39 | convolution fusion | flops 34604160 | bytes 1576960 | tf_op jit(solution)/shard_map/ghlm,glhe->gmhe/dot_general | solution.py:59
  108.6 4.4 %all-to-all-start.3 = ((bf16[1,16,8,1024]{3,2,0,1:T(8,128)(2,1)}), bf16[1,16,8,1024]{3,2,0,1:T(8,128)(2,1)}, u32[]{:S(2)}, u32[]{:S(2)}) async-start(bf16[1,16,8,1024]{3,2,0,1:T(8,128)(2,1)} %bitcast.58), calls=%async_computation.3 | async-start | bytes 524288 | tf_op jit(solution)/shard_map/all_to_all | solution.py:305
  113.0 2.3 %collective-permute-done.10 = bf16[2,2,2,32,1025]{4,3,2,1,0:T(8,128)(2,1)} collective-permute-done((bf16[2,2,2,32,1025]{4,3,2,1,0:T(8,128)(2,1)}, bf16[2,2,2,32,1025]{4,3,2,1,0:T(8,128)(2,1)}, u32[]{:S(2)}, u32[]{:S(2)}) %collective-permute-start.10) | collective-permute-done | bytes 524832 | tf_op jit(solution)/shard_map/ppermute | solution.py:205
  118.9 2.8 %bitcast_add_fusion = f32[2,2,2,32,3072]{4,3,2,1,0:T(8,128)S(1)} fusion(bf16[2,2,2,32,3072]{4,3,2,1,0:T(8,128)(2,1)} %collective-permute-done.5, f32[2,2,2,2,32,3072]{5,4,3,2,1,0:T(8,128)} %bitcast.178, s32[]{:T(128)S(6)} %select_n.247), kind=kLoop, calls=%fused_computation.6 | loop fusion | flops 1572864 | bytes 7864324 | tf_op jit(solution)/shard_map/add | solution.py:205
  125.1 2.2 %convolution_convert_fusion.4 = bf16[8,128,128]{2,1,0:T(8,128)(2,1)} fusion(bf16[128,8,128]{0,2,1:T(8,128)(2,1)S(1)} %bitcast.202, f32[8,128]{1,0:T(8,128)S(1)} %get-tuple-element.59, f32[8,128,128]{1,2,0:T(8,128)} %copy-done.6), kind=kOutput, calls=%fused_computation.38 | convolution fusion | flops 34079872 | bytes 1052672 | tf_op jit(solution)/shard_map/ghlm,glhe->gmhe/dot_general | solution.py:66
  138.5 2.0 %collective-permute-start.7 = (bf16[2,32,3072]{2,1,0:T(8,128)(2,1)S(1)}, bf16[2,32,3072]{2,1,0:T(8,128)(2,1)S(1)}, u32[]{:S(2)}, u32[]{:S(2)}) collective-permute-start(bf16[2,32,3072]{2,1,0:T(8,128)(2,1)S(1)} %fusion.53), channel_id=1, source_target_pairs={{0,4},{1,3},{2,6},{3,1},{4,0},{5,7},{6,2},{7,5},{8,12},{9,11},{10,... | collective-permute-start | bytes 1179656 | tf_op jit(solution)/shard_map/ppermute | solution.py:205
  140.5 2.8 %collective-permute-start.13 = (bf16[32,1025]{1,0:T(8,128)(2,1)S(1)}, bf16[32,1025]{1,0:T(8,128)(2,1)S(1)}, u32[]{:S(2)}, u32[]{:S(2)}) collective-permute-start(bf16[32,1025]{1,0:T(8,128)(2,1)S(1)} %fusion.75), channel_id=1, source_target_pairs={{0,8},{1,9},{2,10},{3,11},{4,12},{5,13},{6,14},{7,15},{8,0},{9,1},... | collective-permute-start | bytes 196808 | tf_op jit(solution)/shard_map/ppermute | solution.py:205
  143.4 5.0 %collective-permute-done.7 = bf16[2,32,3072]{2,1,0:T(8,128)(2,1)S(1)} collective-permute-done((bf16[2,32,3072]{2,1,0:T(8,128)(2,1)S(1)}, bf16[2,32,3072]{2,1,0:T(8,128)(2,1)S(1)}, u32[]{:S(2)}, u32[]{:S(2)}) %collective-permute-start.7) | collective-permute-done | bytes 393248 | tf_op jit(solution)/shard_map/ppermute | solution.py:205
  150.5 6.7 %collective-permute-done.8 = bf16[32,3072]{1,0:T(8,128)(2,1)S(1)} collective-permute-done((bf16[32,3072]{1,0:T(8,128)(2,1)S(1)}, bf16[32,3072]{1,0:T(8,128)(2,1)S(1)}, u32[]{:S(2)}, u32[]{:S(2)}) %collective-permute-start.8) | collective-permute-done | bytes 196640 | tf_op jit(solution)/shard_map/ppermute | solution.py:205
  159.5 3.5 %collective-permute-done.9 = bf16[32,3072]{1,0:T(8,128)(2,1)S(1)} collective-permute-done((bf16[32,3072]{1,0:T(8,128)(2,1)S(1)}, bf16[32,3072]{1,0:T(8,128)(2,1)S(1)}, u32[]{:S(2)}, u32[]{:S(2)}) %collective-permute-start.9) | collective-permute-done | bytes 196640 | tf_op jit(solution)/shard_map/ppermute | solution.py:211
  (136 shorter events, 57.2 us)
Async XLA Ops:
  0.6 18.5 %copy-start = (bf16[1024,1024]{1,0:T(8,128)(2,1)S(1)}, bf16[1024,1024]{1,0:T(8,128)(2,1)}, u32[]{:S(2)}) copy-start(bf16[1024,1024]{1,0:T(8,128)(2,1)} %param.10) | copy-start | bytes 6291460
  0.6 12.5 %copy-start.18 = (bf16[1,1,128,1024]{3,2,1,0:T(8,128)(2,1)S(1)}, bf16[1,1,128,1024]{3,2,1,0:T(8,128)(2,1)}, u32[]{:S(2)}) copy-start(bf16[1,1,128,1024]{3,2,1,0:T(8,128)(2,1)} %param.7) | copy-start | bytes 786436
  4.8 9.7 %copy-start.19 = (bf16[1,1,128,1024]{3,2,1,0:T(8,128)(2,1)S(1)}, bf16[1,1,128,1024]{3,2,1,0:T(8,128)(2,1)}, u32[]{:S(2)}) copy-start(bf16[1,1,128,1024]{3,2,1,0:T(8,128)(2,1)} %param.9) | copy-start | bytes 786436
  5.7 20.2 %all-to-all-start.1 = ((bf16[16,2,4096]{2,1,0:T(2,128)(2,1)}), bf16[16,2,4096]{2,1,0:T(2,128)(2,1)S(1)}, u32[]{:S(2)}, u32[]{:S(2)}) async-start(bf16[16,2,4096]{2,1,0:T(2,128)(2,1)} %reshape.311), calls=%async_computation.1 | async-start | bytes 524288 | tf_op jit(solution)/shard_map/all_to_all | solution.py:251
  13.3 5.3 %copy-start.10 = (bf16[1,1,128,1024]{2,3,1,0:T(8,128)(2,1)}, bf16[1,1,128,1024]{2,3,1,0:T(8,128)(2,1)S(1)}, u32[]{:S(2)}) copy-start(bf16[1,1,128,1024]{2,3,1,0:T(8,128)(2,1)S(1)} %copy.199) | copy-start | bytes 786436
  14.6 4.1 %copy-start.12 = (bf16[1,1,128,1024]{2,3,1,0:T(8,128)(2,1)}, bf16[1,1,128,1024]{2,3,1,0:T(8,128)(2,1)S(1)}, u32[]{:S(2)}) copy-start(bf16[1,1,128,1024]{2,3,1,0:T(8,128)(2,1)S(1)} %copy.198) | copy-start | bytes 786436
  16.7 4.0 %copy-start.21 = (f32[1024]{0:T(1024)S(1)}, f32[1024]{0:T(1024)}, u32[]{:S(2)}) copy-start(f32[1024]{0:T(1024)} %param.11) | copy-start | bytes 12292
  18.7 13.2 %collective-permute-start.2 = (bf16[128,1024]{0,1:T(8,128)(2,1)}, bf16[128,1024]{0,1:T(8,128)(2,1)}, u32[]{:S(2)}, u32[]{:S(2)}) collective-permute-start(bf16[128,1024]{0,1:T(8,128)(2,1)} %bitcast.3), channel_id=1, source_target_pairs={{0,1},{1,0},{2,3},{3,2},{4,5},{5,4},{6,7},{7,6},{8,9},{9,8},{10,11... | collective-permute-start | bytes 786440 | tf_op jit(solution)/shard_map/ppermute | solution.py:294
  25.9 15.9 %all-to-all-start = ((bf16[16,2,4096]{2,1,0:T(2,128)(2,1)}), bf16[16,2,4096]{2,1,0:T(2,128)(2,1)}, u32[]{:S(2)}, u32[]{:S(2)}) async-start(bf16[16,2,4096]{2,1,0:T(2,128)(2,1)} %reshape.313), calls=%async_computation | async-start | bytes 524288 | tf_op jit(solution)/shard_map/all_to_all | solution.py:236
  44.1 39.4 %collective-permute-start = (bf16[128,1024]{1,0:T(8,128)(2,1)S(1)}, bf16[128,1024]{1,0:T(8,128)(2,1)}, u32[]{:S(2)}, u32[]{:S(2)}) collective-permute-start(bf16[128,1024]{1,0:T(8,128)(2,1)S(1)} %bitcast.190), channel_id=1, source_target_pairs={{0,1},{1,0},{2,3},{3,2},{4,5},{5,4},{6,7},{7,6},{8,9},{9,8},{10,11... | collective-permute-start | bytes 786440 | tf_op jit(solution)/shard_map/ppermute | solution.py:273
  69.0 15.8 %collective-permute-start.1 = (bf16[128,3072]{1,0:T(8,128)(2,1)}, bf16[128,3072]{1,0:T(8,128)(2,1)}, u32[]{:S(2)}, u32[]{:S(2)}) collective-permute-start(bf16[128,3072]{1,0:T(8,128)(2,1)} %bitcast.25.x_ref), channel_id=1, source_target_pairs={{0,1},{1,0},{2,3},{3,2},{4,5},{5,4},{6,7},{7,6},{8,9},{9,8},{10,11... | collective-permute-start | bytes 2359304 | tf_op jit(solution)/shard_map/ppermute | solution.py:273
  77.7 7.0 %copy-start.9 = (bf16[1,1,128,1024]{2,3,1,0:T(8,128)(2,1)S(1)}, bf16[1,1,128,1024]{2,3,1,0:T(8,128)(2,1)}, u32[]{:S(2)}) copy-start(bf16[1,1,128,1024]{2,3,1,0:T(8,128)(2,1)} %copy.152) | copy-start | bytes 786436
  77.7 13.7 %all-to-all-start.2 = ((bf16[1,16,8,1024]{3,2,0,1:T(8,128)(2,1)}), bf16[1,16,8,1024]{3,2,0,1:T(8,128)(2,1)S(1)}, u32[]{:S(2)}, u32[]{:S(2)}) async-start(bf16[1,16,8,1024]{3,2,0,1:T(8,128)(2,1)} %bitcast.192), calls=%async_computation.2 | async-start | bytes 524288 | tf_op jit(solution)/shard_map/all_to_all | solution.py:279
  91.5 4.3 %collective-permute-start.4 = (f32[1024]{0:T(1024)S(1)}, f32[1024]{0:T(1024)S(1)}, u32[]{:S(2)}, u32[]{:S(2)}) collective-permute-start(f32[1024]{0:T(1024)S(1)} %get-tuple-element.50), channel_id=1, source_target_pairs={{0,1},{1,0},{2,3},{3,2},{4,5},{5,4},{6,7},{7,6},{8,9},{9,8},{10,11... | collective-permute-start | bytes 12296 | tf_op jit(solution)/shard_map/ppermute | solution.py:294
  92.1 4.2 %copy-start.7 = (bf16[256,2,2,2,2,2,32]{0,6,5,4,3,2,1:T(8,128)(2,1)S(1)}, bf16[256,2,2,2,2,2,32]{0,6,5,4,3,2,1:T(8,128)(2,1)}, u32[]{:S(2)}) copy-start(bf16[256,2,2,2,2,2,32]{0,6,5,4,3,2,1:T(8,128)(2,1)} %copy.176) | copy-start | bytes 1572868
  92.1 4.1 %collective-permute-start.3 = (bf16[128,1024]{1,0:T(8,128)(2,1)S(1)}, bf16[128,1024]{1,0:T(8,128)(2,1)}, u32[]{:S(2)}, u32[]{:S(2)}) collective-permute-start(bf16[128,1024]{1,0:T(8,128)(2,1)S(1)} %fusion.45), channel_id=1, source_target_pairs={{0,1},{1,0},{2,3},{3,2},{4,5},{5,4},{6,7},{7,6},{8,9},{9,8},{10,11... | collective-permute-start | bytes 786440 | tf_op jit(solution)/shard_map/ppermute | solution.py:294
  94.0 24.8 %collective-permute-start.5 = (bf16[2,2,2,32,3072]{4,3,2,1,0:T(8,128)(2,1)}, bf16[2,2,2,32,3072]{4,3,2,1,0:T(8,128)(2,1)}, u32[]{:S(2)}, u32[]{:S(2)}) collective-permute-start(bf16[2,2,2,32,3072]{4,3,2,1,0:T(8,128)(2,1)} %fusion.4), channel_id=1, source_target_pairs={{0,2},{1,17},{2,0},{3,19},{4,6},{5,21},{6,4},{7,23},{8,10},{9,25},... | collective-permute-start | bytes 4718600 | tf_op jit(solution)/shard_map/ppermute | solution.py:205
  97.7 3.7 %copy-start.14 = (bf16[16,8,8,128]{3,2,1,0:T(8,128)(2,1)S(1)}, bf16[16,8,8,128]{3,2,1,0:T(8,128)(2,1)}, u32[]{:S(2)}) copy-start(bf16[16,8,8,128]{3,2,1,0:T(8,128)(2,1)} %copy.201) | copy-start | bytes 786436
  97.7 4.7 %copy-start.13 = (bf16[1,1,128,1024]{2,3,1,0:T(8,128)(2,1)S(1)}, bf16[1,1,128,1024]{2,3,1,0:T(8,128)(2,1)}, u32[]{:S(2)}) copy-start(bf16[1,1,128,1024]{2,3,1,0:T(8,128)(2,1)} %copy-done.12) | copy-start | bytes 786436
  99.9 5.1 %copy-start.11 = (bf16[1,1,128,1024]{2,3,1,0:T(8,128)(2,1)S(1)}, bf16[1,1,128,1024]{2,3,1,0:T(8,128)(2,1)}, u32[]{:S(2)}) copy-start(bf16[1,1,128,1024]{2,3,1,0:T(8,128)(2,1)} %copy-done.10) | copy-start | bytes 786436
  99.9 15.3 %collective-permute-start.10 = (bf16[2,2,2,32,1025]{4,3,2,1,0:T(8,128)(2,1)}, bf16[2,2,2,32,1025]{4,3,2,1,0:T(8,128)(2,1)}, u32[]{:S(2)}, u32[]{:S(2)}) collective-permute-start(bf16[2,2,2,32,1025]{4,3,2,1,0:T(8,128)(2,1)} %fusion.43), channel_id=1, source_target_pairs={{0,4},{1,5},{2,6},{3,7},{4,0},{5,1},{6,2},{7,3},{8,12},{9,13},{10,... | collective-permute-start | bytes 1574408 | tf_op jit(solution)/shard_map/ppermute | solution.py:205
  102.4 5.2 %copy-start.20 = (bf16[1,16,8,8,128]{4,1,3,2,0:T(8,128)(2,1)S(1)}, bf16[1,16,8,8,128]{4,1,3,2,0:T(8,128)(2,1)}, u32[]{:S(2)}) copy-start(bf16[1,16,8,8,128]{4,1,3,2,0:T(8,128)(2,1)} %fusion.30) | copy-start | bytes 786436
  108.6 24.2 %all-to-all-start.3 = ((bf16[1,16,8,1024]{3,2,0,1:T(8,128)(2,1)}), bf16[1,16,8,1024]{3,2,0,1:T(8,128)(2,1)}, u32[]{:S(2)}, u32[]{:S(2)}) async-start(bf16[1,16,8,1024]{3,2,0,1:T(8,128)(2,1)} %bitcast.58), calls=%async_computation.3 | async-start | bytes 524288 | tf_op jit(solution)/shard_map/all_to_all | solution.py:305
  117.5 7.6 %copy-start.16 = (bf16[128,1024]{0,1:T(8,128)(2,1)S(1)}, bf16[128,1024]{0,1:T(8,128)(2,1)}, u32[]{:S(2)}) copy-start(bf16[128,1024]{0,1:T(8,128)(2,1)} %copy.200) | copy-start | bytes 786436
  117.5 15.2 %collective-permute-start.11 = (bf16[2,2,32,1025]{3,2,1,0:T(8,128)(2,1)}, bf16[2,2,32,1025]{3,2,1,0:T(8,128)(2,1)}, u32[]{:S(2)}, u32[]{:S(2)}) collective-permute-start(bf16[2,2,32,1025]{3,2,1,0:T(8,128)(2,1)} %fusion.55), channel_id=1, source_target_pairs={{0,2},{1,17},{2,0},{3,19},{4,6},{5,21},{6,4},{7,23},{8,10},{9,25},... | collective-permute-start | bytes 787208 | tf_op jit(solution)/shard_map/ppermute | solution.py:205
  124.3 12.3 %collective-permute-start.6 = (bf16[2,2,32,3072]{3,2,1,0:T(8,128)(2,1)}, bf16[2,2,32,3072]{3,2,1,0:T(8,128)(2,1)}, u32[]{:S(2)}, u32[]{:S(2)}) collective-permute-start(bf16[2,2,32,3072]{3,2,1,0:T(8,128)(2,1)} %fusion.40), channel_id=1, source_target_pairs={{0,16},{1,5},{2,18},{3,7},{4,20},{5,1},{6,22},{7,3},{8,24},{9,13},... | collective-permute-start | bytes 2359304 | tf_op jit(solution)/shard_map/ppermute | solution.py:205
  133.8 6.7 %collective-permute-start.12 = (bf16[2,32,1025]{2,1,0:T(8,128)(2,1)S(1)}, bf16[2,32,1025]{2,1,0:T(8,128)(2,1)S(1)}, u32[]{:S(2)}, u32[]{:S(2)}) collective-permute-start(bf16[2,32,1025]{2,1,0:T(8,128)(2,1)S(1)} %fusion.69), channel_id=1, source_target_pairs={{0,16},{1,3},{2,18},{3,1},{4,20},{5,7},{6,22},{7,5},{8,24},{9,11},... | collective-permute-start | bytes 393608 | tf_op jit(solution)/shard_map/ppermute | solution.py:205
  138.5 9.8 %collective-permute-start.7 = (bf16[2,32,3072]{2,1,0:T(8,128)(2,1)S(1)}, bf16[2,32,3072]{2,1,0:T(8,128)(2,1)S(1)}, u32[]{:S(2)}, u32[]{:S(2)}) collective-permute-start(bf16[2,32,3072]{2,1,0:T(8,128)(2,1)S(1)} %fusion.53), channel_id=1, source_target_pairs={{0,4},{1,3},{2,6},{3,1},{4,0},{5,7},{6,2},{7,5},{8,12},{9,11},{10,... | collective-permute-start | bytes 1179656 | tf_op jit(solution)/shard_map/ppermute | solution.py:205
  140.5 9.3 %collective-permute-start.13 = (bf16[32,1025]{1,0:T(8,128)(2,1)S(1)}, bf16[32,1025]{1,0:T(8,128)(2,1)S(1)}, u32[]{:S(2)}, u32[]{:S(2)}) collective-permute-start(bf16[32,1025]{1,0:T(8,128)(2,1)S(1)} %fusion.75), channel_id=1, source_target_pairs={{0,8},{1,9},{2,10},{3,11},{4,12},{5,13},{6,14},{7,15},{8,0},{9,1},... | collective-permute-start | bytes 196808 | tf_op jit(solution)/shard_map/ppermute | solution.py:205
  148.5 8.7 %collective-permute-start.8 = (bf16[32,3072]{1,0:T(8,128)(2,1)S(1)}, bf16[32,3072]{1,0:T(8,128)(2,1)S(1)}, u32[]{:S(2)}, u32[]{:S(2)}) collective-permute-start(bf16[32,3072]{1,0:T(8,128)(2,1)S(1)} %fusion.68), channel_id=1, source_target_pairs={{0,8},{1,9},{2,10},{3,11},{4,12},{5,13},{6,14},{7,15},{8,0},{9,1},... | collective-permute-start | bytes 589832 | tf_op jit(solution)/shard_map/ppermute | solution.py:205
  149.9 8.3 %collective-permute-start.14 = (bf16[32,1025]{1,0:T(8,128)(2,1)S(1)}, bf16[32,1025]{1,0:T(8,128)(2,1)S(1)}, u32[]{:S(2)}, u32[]{:S(2)}) collective-permute-start(bf16[32,1025]{1,0:T(8,128)(2,1)S(1)} %fusion.70), channel_id=1, source_target_pairs={{0,16},{16,0},{1,17},{17,1},{2,18},{18,2},{3,19},{19,3},{4,20},{20... | collective-permute-start | bytes 196808 | tf_op jit(solution)/shard_map/ppermute | solution.py:211
  157.3 5.7 %collective-permute-start.9 = (bf16[32,3072]{1,0:T(8,128)(2,1)S(1)}, bf16[32,3072]{1,0:T(8,128)(2,1)S(1)}, u32[]{:S(2)}, u32[]{:S(2)}) collective-permute-start(bf16[32,3072]{1,0:T(8,128)(2,1)S(1)} %fusion.54), channel_id=1, source_target_pairs={{0,16},{16,0},{1,17},{17,1},{2,18},{18,2},{3,19},{19,3},{4,20},{20... | collective-permute-start | bytes 589832 | tf_op jit(solution)/shard_map/ppermute | solution.py:211
  (9 other events, 19.2 us)

commit v11 on v7

--- a/solution.py
+++ b/solution.py
@@ -222,7 +222,8 @@
         half = arranged.shape[1] // 2
         return lax.dynamic_slice_in_dim(arranged, core * half, half, axis=1)
 
-    normed_peer, grads_peer = lax.ppermute((used_normed, used_grads), "seq", pair)
+    normed_peer = lax.ppermute(used_normed, "seq", pair)
+    grads_peer = jnp.stack(lax.ppermute(grads_cols, "seq", pair), axis=3).reshape(-1, 3 * feature)
     joint_term = jnp.dot(
         my_half(jnp.concatenate([used_normed, normed_peer], axis=0)).T,
         jnp.concatenate([used_grads, grads_peer], axis=0),

time: 162 us -> 168 us (1.037)
  local copies, waits for them, and re-layouts: 35.3 us -> 39.4 us
    reshape x1 -> x2, local copies, waits for them, and re-layouts: 0.17 us -> 2.33 us  [the longest x1 2.16 us: on_device(): jnp.stack(lax.ppermute(grads_cols, 'seq', pair), axis=3)]
    unnamed x54 -> x52, local copies, waits for them, and re-layouts: 20.7 us -> 20.7 us
  transfers between devices with their start and end apart: 19 -> 21, of which waited for: 7 -> 6; matrix products, arithmetic and copies ran while one was open for 39% -> 41% of each run, Pallas kernels for 0% -> 0%
where the time goes in v11:
time: 168 us; the launch traced here: 167 us
  matrix products  39.6 us (24%)
  local copies, waits for them, and re-layouts  39.4 us (23%)
  starting transfers between devices  37.3 us (22%)
  waiting for transfers between devices  26.3 us (16%)
  other arithmetic  22.9 us (14%)
    unnamed x52, local copies, waits for them, and re-layouts  20.7 us
    ppermute x8, waiting for transfers between devices, reduce_rows(): lax.ppermute(given, ('dp', 'seq'), perm).astype(jnp.float32)  16.3 us
    ppermute x8, starting transfers between devices, reduce_rows(): lax.ppermute(given, ('dp', 'seq'), perm).astype(jnp.float32)  12.1 us
    all_to_all x1, starting transfers between devices, on_device(): lax.all_to_all(upstream, 'seq', split_axis=2, concat_axis=1, tiled=True)  7.39 us
    add x6, other arithmetic, reduce_rows(): kept + lax.ppermute(given, ('dp', 'seq'), perm).astype(jnp.float32)  7.28 us
    all_to_all x1, waiting for transfers between devices, on_device(): lax.all_to_all(normed.reshape(batches, local_rows, columns, model_width),...  6.19 us
    all_to_all x1, starting transfers between devices, on_device(): lax.all_to_all(normed.reshape(batches, local_rows, columns, model_width),...  5.86 us
    dot_general x1, matrix products, on_device(): jnp.dot(used_grads, joint_weight.T, preferred_element_type=jnp.float32)  5.69 us
  transfers between devices with their start and end apart: 21, of which 6 were waited for; matrix products, arithmetic and copies ran while one was open for 41% of the time, Pallas kernels for 0%

profile of v11, /device:TPU:0, one launch (start us, length us, event | category | flops | bytes accessed | tf_op | source)
XLA Modules:
  0.0 166.7 jit_solution(13463711789171166067)
XLA Ops:
  2.7 2.1 %reduce.20 = bf16[128,1024]{1,0:T(8,128)(2,1)S(1)} reduce(bf16[128,1,1,1024]{3,2,1,0:T(2,128)(2,1)S(1)} %bitcast.190, bf16[]{:T(256)} %broadcast.113), dimensions={1,2}, to_apply=%bitcast.182.reduce_sub_computation | reduce | bytes 524290
  5.7 7.4 %all-to-all-start.1 = ((bf16[16,2,4096]{2,1,0:T(2,128)(2,1)}), bf16[16,2,4096]{2,1,0:T(2,128)(2,1)S(1)}, u32[]{:S(2)}, u32[]{:S(2)}) async-start(bf16[16,2,4096]{2,1,0:T(2,128)(2,1)} %reshape.315), calls=%async_computation.1 | async-start | bytes 524288 | tf_op jit(solution)/shard_map/all_to_all | solution.py:201
  16.7 2.0 %convolution_convert_fusion.3 = bf16[8,128,128]{1,2,0:T(8,128)(2,1)} fusion(bf16[128,8,128]{2,1,0:T(8,128)(2,1)} %bitcast.199, f32[8,128]{1,0:T(8,128)S(1)} %get-tuple-element.52, f32[8,128,128]{1,2,0:T(8,128)S(1)} %fusion.20), kind=kOutput, calls=%fused_computation.37 | convolution fusion | flops 34079872 | bytes 1052672 | tf_op jit(solution)/shard_map/ghlm,gmhe->glhe/dot_general | solution.py:31
  21.2 2.9 %reduce.21 = bf16[128,1024]{1,0:T(8,128)(2,1)} reduce(bf16[128,1,1,1024]{3,2,1,0:T(2,128)(2,1)S(1)} %bitcast.191, bf16[]{:T(256)} %broadcast.113), dimensions={1,2}, to_apply=%bitcast.183.reduce_sub_computation | reduce | bytes 524290
  24.0 1.8 %reshape.317 = bf16[16,2,4096]{2,1,0:T(2,128)(2,1)} reshape(bf16[128,1024]{1,0:T(8,128)(2,1)} %reduce.21) | data formatting | bytes 524288
  25.9 5.9 %all-to-all-start = ((bf16[16,2,4096]{2,1,0:T(2,128)(2,1)}), bf16[16,2,4096]{2,1,0:T(2,128)(2,1)}, u32[]{:S(2)}, u32[]{:S(2)}) async-start(bf16[16,2,4096]{2,1,0:T(2,128)(2,1)} %reshape.317), calls=%async_computation | async-start | bytes 524288 | tf_op jit(solution)/shard_map/all_to_all | solution.py:184
  35.6 6.2 %all-to-all-done = bf16[16,2,4096]{2,1,0:T(2,128)(2,1)} async-done(((bf16[16,2,4096]{2,1,0:T(2,128)(2,1)}), bf16[16,2,4096]{2,1,0:T(2,128)(2,1)}, u32[]{:S(2)}, u32[]{:S(2)}) %all-to-all-start) | async-done | bytes 262176 | tf_op jit(solution)/shard_map/all_to_all | solution.py:184
  41.8 2.2 %reshape.318 = bf16[128,1,1,1024]{3,2,1,0:T(2,128)(2,1)S(1)} reshape(bf16[16,2,4096]{2,1,0:T(2,128)(2,1)} %all-to-all-done) | data formatting | bytes 524288
  45.1 3.9 %convolution_convert_fusion = bf16[128,3072]{1,0:T(8,128)(2,1)S(1)} fusion(bf16[1024,3072]{1,0:T(8,128)(2,1)} %param.12, bf16[1,1,128,1024]{2,3,1,0:T(8,128)(2,1)} %copy.114), kind=kOutput, calls=%fused_computation.4 | convolution fusion | flops 805699584 | bytes 7340032 | tf_op jit(solution)/shard_map/dot_general | solution.py:191
  51.0 2.5 %fusion.91 = (f32[8,8,16]{2,1,0:T(8,128)S(1)}, f32[8,8,16,16]{2,3,1,0:T(8,128)}) fusion(pred[16,16]{0,1:T(8,128)(4,1)S(1)} %iota_compare_fusion.1, bf16[1,16,8,1,8,128]{5,2,4,3,1,0:T(8,128)(2,1)S(1)} %get-tuple-element.47, bf16[1,16,8,1,8,128]{5,2,4,3,1,0:T(8,128)(2,1)} %get-tuple-element.46), kind=kOutput, calls=%fused_computation.147 | convolution fusion | flops 4259855 | bytes 594176 | tf_op jit(solution)/shard_map/sub | solution.py:28
  53.6 2.1 %convolution_convert_fusion.9 = bf16[8,8,16,128]{3,2,1,0:T(8,128)(2,1)} fusion(bf16[16,8,8,128]{3,2,1,0:T(8,128)(2,1)S(1)} %copy.193, f32[8,8,16,16]{2,3,1,0:T(8,128)} %get-tuple-element.57, f32[8,8,16]{2,1,0:T(8,128)S(1)} %get-tuple-element.56), kind=kOutput, calls=%fused_computation.43 | convolution fusion | flops 4358144 | bytes 593920 | tf_op jit(solution)/shard_map/bchlm,blche->bmche/dot_general | solution.py:64
  55.7 2.9 %convolution_convert_fusion.2 = bf16[8,8,128,16]{2,3,1,0:T(8,128)(2,1)} fusion(f32[8,8,16,16]{2,3,1,0:T(8,128)} %convolution_bitcast_fusion, bf16[1,16,8,1,8,128]{5,2,4,3,1,0:T(8,128)(2,1)} %get-tuple-element.46, f32[8,8,16,16]{2,3,1,0:T(8,128)} %get-tuple-element.57, f32[8,8,16]{2,1,0:T(8,128)S(1)} %get-tuple-element.56), kind=kOutput, calls=%fused_computation.36 | convolution fusion | flops 4441103 | bytes 659456 | tf_op jit(solution)/shard_map/bchlm,blche->bmche/dot_general | solution.py:57
  58.5 2.4 %convolution_convert_fusion.10 = bf16[8,8,128,16]{2,3,1,0:T(8,128)(2,1)} fusion(f32[8,8,16,16]{2,3,1,0:T(8,128)S(1)} %copy-done.14, bf16[1,16,8,1,8,128]{5,2,4,3,1,0:T(8,128)(2,1)} %copy-done.18, f32[8,8,16,16]{2,3,1,0:T(8,128)} %get-tuple-element.57, f32[8,8,16]{2,1,0:T(8,128)S(1)} %get-tuple-element.56), kind=kOutput, calls=%fused_computation.44 | convolution fusion | flops 4441103 | bytes 659456 | tf_op jit(solution)/shard_map/bchlm,bmche->blche/dot_general | solution.py:51
  65.7 5.7 %fusion.28 = bf16[1,16,8,1024]{3,2,0,1:T(8,128)(2,1)} fusion(bf16[128,3072]{1,0:T(8,128)(2,1)S(1)} %reshape_reshape.7, bf16[1024,3072]{1,0:T(8,128)(2,1)} %param.12), kind=kOutput, calls=%fused_computation.50 | convolution fusion | flops 805437440 | bytes 7340032 | tf_op jit(solution)/shard_map/dot_general | solution.py:209
  71.4 4.4 %all-to-all-start.2 = ((bf16[1,16,8,1024]{3,2,0,1:T(8,128)(2,1)}), bf16[1,16,8,1024]{3,2,0,1:T(8,128)(2,1)}, u32[]{:S(2)}, u32[]{:S(2)}) async-start(bf16[1,16,8,1024]{3,2,0,1:T(8,128)(2,1)} %fusion.28), calls=%async_computation.2 | async-start | bytes 524288 | tf_op jit(solution)/shard_map/all_to_all | solution.py:232
  75.8 2.1 %fusion.29 = bf16[1,16,8,8,128]{4,1,3,2,0:T(8,128)(2,1)} fusion(bf16[1,16,8,1,8,128]{5,2,4,3,1,0:T(8,128)(2,1)} %copy-done.13, f32[8,8,16,16]{2,3,1,0:T(8,128)} %get-tuple-element.57, f32[8,8,16]{2,1,0:T(8,128)S(1)} %get-tuple-element.56), kind=kOutput, calls=%fused_computation.51 | convolution fusion | flops 4358144 | bytes 593920 | tf_op jit(solution)/shard_map/bchlm,bmche->blche/dot_general | solution.py:31
  82.3 2.2 %reshape.296 = bf16[128,3072]{1,0:T(8,128)(2,1)} reshape(bf16[1,16,8,3,8,128]{5,4,3,2,1,0:T(8,128)(2,1)} %copy.126) | data formatting | bytes 1572864 | tf_op jit(solution)/shard_map/reshape | solution.py:226
  84.5 2.2 %fusion.5 = f32[512,3072]{1,0:T(8,128)S(1)} fusion(bf16[128,3072]{1,0:T(8,128)(2,1)} %reshape.296, bf16[128,3072]{1,0:T(8,128)(2,1)S(1)} %reshape_reshape.7, bf16[256,1024]{0,1:T(8,128)(2,1)} %bitcast.193, s32[]{:T(128)S(6)} %select_n.231), kind=kOutput, calls=%fused_computation.12 | convolution fusion | flops 808452096 | bytes 8126468 | tf_op jit(solution)/shard_map/dot_general | solution.py:227
  86.7 2.7 %copy-done.1 = f32[512,3072]{1,0:T(8,128)} copy-done((f32[512,3072]{1,0:T(8,128)}, f32[512,3072]{1,0:T(8,128)S(1)}, u32[]{:S(2)}) %copy-start.1) | copy-done | bytes 6291480
  103.5 2.6 %convolution_convert_fusion.1 = bf16[8,128,128]{1,2,0:T(8,128)(2,1)} fusion(bf16[128,8,128]{0,2,1:T(8,128)(2,1)S(1)} %bitcast.198, f32[8,128,128]{1,2,0:T(8,128)} %fusion.62, f32[8,128,128]{1,2,0:T(8,128)} %get-tuple-element.53, f32[8,128]{1,0:T(8,128)S(1)} %get-tuple-element.52), kind=kOutput, calls=%fused_computation.35 | convolution fusion | flops 34604160 | bytes 1576960 | tf_op jit(solution)/shard_map/ghlm,gmhe->glhe/dot_general | solution.py:51
  106.2 2.6 %convolution_convert_fusion.6 = bf16[8,128,128]{1,2,0:T(8,128)(2,1)} fusion(bf16[128,8,128]{0,2,1:T(8,128)(2,1)S(1)} %bitcast.196, f32[8,128,128]{1,2,0:T(8,128)} %fusion.62, f32[8,128,128]{1,2,0:T(8,128)} %get-tuple-element.53, f32[8,128]{1,0:T(8,128)S(1)} %get-tuple-element.52), kind=kOutput, calls=%fused_computation.40 | convolution fusion | flops 34604160 | bytes 1576960 | tf_op jit(solution)/shard_map/ghlm,glhe->gmhe/dot_general | solution.py:57
  109.7 4.2 %all-to-all-start.3 = ((bf16[1,16,8,1024]{3,2,0,1:T(8,128)(2,1)}), bf16[1,16,8,1024]{3,2,0,1:T(8,128)(2,1)}, u32[]{:S(2)}, u32[]{:S(2)}) async-start(bf16[1,16,8,1024]{3,2,0,1:T(8,128)(2,1)} %bitcast.65), calls=%async_computation.3 | async-start | bytes 524288 | tf_op jit(solution)/shard_map/all_to_all | solution.py:258
  113.9 2.4 %collective-permute-done.12 = bf16[2,2,2,32,1025]{4,3,2,1,0:T(8,128)(2,1)} collective-permute-done((bf16[2,2,2,32,1025]{4,3,2,1,0:T(8,128)(2,1)}, bf16[2,2,2,32,1025]{4,3,2,1,0:T(8,128)(2,1)}, u32[]{:S(2)}, u32[]{:S(2)}) %collective-permute-start.12) | collective-permute-done | bytes 524832 | tf_op jit(solution)/shard_map/ppermute | solution.py:153
  120.2 2.8 %bitcast_add_fusion = f32[2,2,2,32,3072]{4,3,2,1,0:T(8,128)S(1)} fusion(bf16[2,2,2,32,3072]{4,3,2,1,0:T(8,128)(2,1)} %collective-permute-done.7, f32[2,2,2,2,32,3072]{5,4,3,2,1,0:T(8,128)} %bitcast.185, s32[]{:T(128)S(6)} %select_n.247), kind=kLoop, calls=%fused_computation.7 | loop fusion | flops 1572864 | bytes 7864324 | tf_op jit(solution)/shard_map/add | solution.py:153
  126.2 2.2 %convolution_convert_fusion.5 = bf16[8,128,128]{2,1,0:T(8,128)(2,1)} fusion(bf16[128,8,128]{0,2,1:T(8,128)(2,1)S(1)} %bitcast.202, f32[8,128]{1,0:T(8,128)S(1)} %get-tuple-element.52, f32[8,128,128]{1,2,0:T(8,128)} %copy-done.4), kind=kOutput, calls=%fused_computation.39 | convolution fusion | flops 34079872 | bytes 1052672 | tf_op jit(solution)/shard_map/ghlm,glhe->gmhe/dot_general | solution.py:64
  128.5 1.8 %copy.147 = bf16[1,1,128,1024]{3,2,1,0:T(8,128)(2,1)} copy(bf16[1,1,128,1024]{2,3,1,0:T(8,128)(2,1)} %bitcast.205) | data formatting | bytes 524288
  132.1 1.8 %copy.148 = bf16[1,1,128,1024]{3,2,1,0:T(8,128)(2,1)} copy(bf16[1,1,128,1024]{2,3,1,0:T(8,128)(2,1)} %bitcast.206) | data formatting | bytes 524288
  138.0 1.8 %bitcast_add_fusion.1 = f32[2,2,32,3072]{3,2,1,0:T(8,128)S(1)} fusion(bf16[2,2,32,3072]{3,2,1,0:T(8,128)(2,1)} %collective-permute-done.8, f32[2,2,2,32,3072]{4,3,2,1,0:T(8,128)} %copy-done.3, s32[]{:T(128)S(6)} %select_n.249), kind=kLoop, calls=%fused_computation.16 | loop fusion | flops 786432 | bytes 3932164 | tf_op jit(solution)/shard_map/add | solution.py:153
  141.7 2.8 %collective-permute-start.15 = (bf16[32,1025]{1,0:T(8,128)(2,1)S(1)}, bf16[32,1025]{1,0:T(8,128)(2,1)S(1)}, u32[]{:S(2)}, u32[]{:S(2)}) collective-permute-start(bf16[32,1025]{1,0:T(8,128)(2,1)S(1)} %fusion.73), channel_id=1, source_target_pairs={{0,8},{1,9},{2,10},{3,11},{4,12},{5,13},{6,14},{7,15},{8,0},{9,1},... | collective-permute-start | bytes 196808 | tf_op jit(solution)/shard_map/ppermute | solution.py:153
  144.5 5.4 %collective-permute-done.9 = bf16[2,32,3072]{2,1,0:T(8,128)(2,1)S(1)} collective-permute-done((bf16[2,32,3072]{2,1,0:T(8,128)(2,1)S(1)}, bf16[2,32,3072]{2,1,0:T(8,128)(2,1)S(1)}, u32[]{:S(2)}, u32[]{:S(2)}) %collective-permute-start.9) | collective-permute-done | bytes 393248 | tf_op jit(solution)/shard_map/ppermute | solution.py:153
  151.5 6.9 %collective-permute-done.10 = bf16[32,3072]{1,0:T(8,128)(2,1)S(1)} collective-permute-done((bf16[32,3072]{1,0:T(8,128)(2,1)S(1)}, bf16[32,3072]{1,0:T(8,128)(2,1)S(1)}, u32[]{:S(2)}, u32[]{:S(2)}) %collective-permute-start.10) | collective-permute-done | bytes 196640 | tf_op jit(solution)/shard_map/ppermute | solution.py:153
  160.4 3.8 %collective-permute-done.11 = bf16[32,3072]{1,0:T(8,128)(2,1)S(1)} collective-permute-done((bf16[32,3072]{1,0:T(8,128)(2,1)S(1)}, bf16[32,3072]{1,0:T(8,128)(2,1)S(1)}, u32[]{:S(2)}, u32[]{:S(2)}) %collective-permute-start.11) | collective-permute-done | bytes 196640 | tf_op jit(solution)/shard_map/ppermute | solution.py:159
  (138 shorter events, 60.8 us)
Async XLA Ops:
  0.6 18.5 %copy-start = (bf16[1024,1024]{1,0:T(8,128)(2,1)S(1)}, bf16[1024,1024]{1,0:T(8,128)(2,1)}, u32[]{:S(2)}) copy-start(bf16[1024,1024]{1,0:T(8,128)(2,1)} %param.10) | copy-start | bytes 6291460
  0.6 12.5 %copy-start.15 = (bf16[1,1,128,1024]{3,2,1,0:T(8,128)(2,1)S(1)}, bf16[1,1,128,1024]{3,2,1,0:T(8,128)(2,1)}, u32[]{:S(2)}) copy-start(bf16[1,1,128,1024]{3,2,1,0:T(8,128)(2,1)} %param.7) | copy-start | bytes 786436
  4.8 9.7 %copy-start.16 = (bf16[1,1,128,1024]{3,2,1,0:T(8,128)(2,1)S(1)}, bf16[1,1,128,1024]{3,2,1,0:T(8,128)(2,1)}, u32[]{:S(2)}) copy-start(bf16[1,1,128,1024]{3,2,1,0:T(8,128)(2,1)} %param.9) | copy-start | bytes 786436
  5.7 20.1 %all-to-all-start.1 = ((bf16[16,2,4096]{2,1,0:T(2,128)(2,1)}), bf16[16,2,4096]{2,1,0:T(2,128)(2,1)S(1)}, u32[]{:S(2)}, u32[]{:S(2)}) async-start(bf16[16,2,4096]{2,1,0:T(2,128)(2,1)} %reshape.315), calls=%async_computation.1 | async-start | bytes 524288 | tf_op jit(solution)/shard_map/all_to_all | solution.py:201
  13.3 5.3 %copy-start.6 = (bf16[1,1,128,1024]{2,3,1,0:T(8,128)(2,1)}, bf16[1,1,128,1024]{2,3,1,0:T(8,128)(2,1)S(1)}, u32[]{:S(2)}) copy-start(bf16[1,1,128,1024]{2,3,1,0:T(8,128)(2,1)S(1)} %copy.161) | copy-start | bytes 786436
  14.6 4.1 %copy-start.8 = (bf16[1,1,128,1024]{2,3,1,0:T(8,128)(2,1)}, bf16[1,1,128,1024]{2,3,1,0:T(8,128)(2,1)S(1)}, u32[]{:S(2)}) copy-start(bf16[1,1,128,1024]{2,3,1,0:T(8,128)(2,1)S(1)} %copy.160) | copy-start | bytes 786436
  18.7 13.1 %collective-permute-start.4 = (bf16[128,1024]{0,1:T(8,128)(2,1)}, bf16[128,1024]{0,1:T(8,128)(2,1)}, u32[]{:S(2)}, u32[]{:S(2)}) collective-permute-start(bf16[128,1024]{0,1:T(8,128)(2,1)} %bitcast.3), channel_id=1, source_target_pairs={{0,1},{1,0},{2,3},{3,2},{4,5},{5,4},{6,7},{7,6},{8,9},{9,8},{10,11... | collective-permute-start | bytes 786440 | tf_op jit(solution)/shard_map/ppermute | solution.py:247
  25.9 16.0 %all-to-all-start = ((bf16[16,2,4096]{2,1,0:T(2,128)(2,1)}), bf16[16,2,4096]{2,1,0:T(2,128)(2,1)}, u32[]{:S(2)}, u32[]{:S(2)}) async-start(bf16[16,2,4096]{2,1,0:T(2,128)(2,1)} %reshape.317), calls=%async_computation | async-start | bytes 524288 | tf_op jit(solution)/shard_map/all_to_all | solution.py:184
  49.7 5.9 %copy-start.13 = (bf16[1,16,8,1,8,128]{5,2,4,3,1,0:T(8,128)(2,1)}, bf16[1,16,8,1,8,128]{5,2,4,3,1,0:T(8,128)(2,1)S(1)}, u32[]{:S(2)}) copy-start(bf16[1,16,8,1,8,128]{5,2,4,3,1,0:T(8,128)(2,1)S(1)} %get-tuple-element.45) | copy-start | bytes 786436
  61.0 17.0 %collective-permute-start = (bf16[128,1024]{0,1:T(8,128)(2,1)}, bf16[128,1024]{0,1:T(8,128)(2,1)}, u32[]{:S(2)}, u32[]{:S(2)}) collective-permute-start(bf16[128,1024]{0,1:T(8,128)(2,1)} %bitcast.6), channel_id=1, source_target_pairs={{0,1},{1,0},{2,3},{3,2},{4,5},{5,4},{6,7},{7,6},{8,9},{9,8},{10,11... | collective-permute-start | bytes 786440 | tf_op jit(solution)/shard_map/ppermute | solution.py:225
  61.0 19.0 %collective-permute-start.3 = (bf16[1,16,8,8,128]{4,1,3,2,0:T(8,128)(2,1)}, bf16[1,16,8,8,128]{4,1,3,2,0:T(8,128)(2,1)}, u32[]{:S(2)}, u32[]{:S(2)}) collective-permute-start(bf16[1,16,8,8,128]{4,1,3,2,0:T(8,128)(2,1)} %bitcast.24), channel_id=1, source_target_pairs={{0,1},{1,0},{2,3},{3,2},{4,5},{5,4},{6,7},{7,6},{8,9},{9,8},{10,11... | collective-permute-start | bytes 786440 | tf_op jit(solution)/shard_map/ppermute | solution.py:226
  61.5 18.5 %collective-permute-start.2 = (bf16[1,16,8,8,128]{4,1,3,2,0:T(8,128)(2,1)}, bf16[1,16,8,8,128]{4,1,3,2,0:T(8,128)(2,1)}, u32[]{:S(2)}, u32[]{:S(2)}) collective-permute-start(bf16[1,16,8,8,128]{4,1,3,2,0:T(8,128)(2,1)} %bitcast.20), channel_id=1, source_target_pairs={{0,1},{1,0},{2,3},{3,2},{4,5},{5,4},{6,7},{7,6},{8,9},{9,8},{10,11... | collective-permute-start | bytes 786440 | tf_op jit(solution)/shard_map/ppermute | solution.py:226
  61.5 18.5 %collective-permute-start.1 = (bf16[1,16,8,8,128]{4,1,3,2,0:T(8,128)(2,1)}, bf16[1,16,8,8,128]{4,1,3,2,0:T(8,128)(2,1)}, u32[]{:S(2)}, u32[]{:S(2)}) collective-permute-start(bf16[1,16,8,8,128]{4,1,3,2,0:T(8,128)(2,1)} %bitcast.17), channel_id=1, source_target_pairs={{0,1},{1,0},{2,3},{3,2},{4,5},{5,4},{6,7},{7,6},{8,9},{9,8},{10,11... | collective-permute-start | bytes 786440 | tf_op jit(solution)/shard_map/ppermute | solution.py:226
  71.4 19.4 %all-to-all-start.2 = ((bf16[1,16,8,1024]{3,2,0,1:T(8,128)(2,1)}), bf16[1,16,8,1024]{3,2,0,1:T(8,128)(2,1)}, u32[]{:S(2)}, u32[]{:S(2)}) async-start(bf16[1,16,8,1024]{3,2,0,1:T(8,128)(2,1)} %fusion.28), calls=%async_computation.2 | async-start | bytes 524288 | tf_op jit(solution)/shard_map/all_to_all | solution.py:232
  91.9 5.0 %collective-permute-start.6 = (f32[1024]{0:T(1024)S(1)}, f32[1024]{0:T(1024)S(1)}, u32[]{:S(2)}, u32[]{:S(2)}) collective-permute-start(f32[1024]{0:T(1024)S(1)} %get-tuple-element.43), channel_id=1, source_target_pairs={{0,1},{1,0},{2,3},{3,2},{4,5},{5,4},{6,7},{7,6},{8,9},{9,8},{10,11... | collective-permute-start | bytes 12296 | tf_op jit(solution)/shard_map/ppermute | solution.py:247
  93.1 4.3 %copy-start.5 = (bf16[256,2,2,2,2,2,32]{0,6,5,4,3,2,1:T(8,128)(2,1)S(1)}, bf16[256,2,2,2,2,2,32]{0,6,5,4,3,2,1:T(8,128)(2,1)}, u32[]{:S(2)}) copy-start(bf16[256,2,2,2,2,2,32]{0,6,5,4,3,2,1:T(8,128)(2,1)} %copy.139) | copy-start | bytes 1572868
  93.1 4.2 %collective-permute-start.5 = (bf16[128,1024]{1,0:T(8,128)(2,1)S(1)}, bf16[128,1024]{1,0:T(8,128)(2,1)}, u32[]{:S(2)}, u32[]{:S(2)}) collective-permute-start(bf16[128,1024]{1,0:T(8,128)(2,1)S(1)} %fusion.43), channel_id=1, source_target_pairs={{0,1},{1,0},{2,3},{3,2},{4,5},{5,4},{6,7},{7,6},{8,9},{9,8},{10,11... | collective-permute-start | bytes 786440 | tf_op jit(solution)/shard_map/ppermute | solution.py:247
  95.4 24.9 %collective-permute-start.7 = (bf16[2,2,2,32,3072]{4,3,2,1,0:T(8,128)(2,1)}, bf16[2,2,2,32,3072]{4,3,2,1,0:T(8,128)(2,1)}, u32[]{:S(2)}, u32[]{:S(2)}) collective-permute-start(bf16[2,2,2,32,3072]{4,3,2,1,0:T(8,128)(2,1)} %fusion.4), channel_id=1, source_target_pairs={{0,2},{1,17},{2,0},{3,19},{4,6},{5,21},{6,4},{7,23},{8,10},{9,25},... | collective-permute-start | bytes 4718600 | tf_op jit(solution)/shard_map/ppermute | solution.py:153
  98.8 4.7 %copy-start.9 = (bf16[1,1,128,1024]{2,3,1,0:T(8,128)(2,1)S(1)}, bf16[1,1,128,1024]{2,3,1,0:T(8,128)(2,1)}, u32[]{:S(2)}) copy-start(bf16[1,1,128,1024]{2,3,1,0:T(8,128)(2,1)} %copy-done.8) | copy-start | bytes 786436
  101.0 5.1 %copy-start.7 = (bf16[1,1,128,1024]{2,3,1,0:T(8,128)(2,1)S(1)}, bf16[1,1,128,1024]{2,3,1,0:T(8,128)(2,1)}, u32[]{:S(2)}) copy-start(bf16[1,1,128,1024]{2,3,1,0:T(8,128)(2,1)} %copy-done.6) | copy-start | bytes 786436
  101.0 15.2 %collective-permute-start.12 = (bf16[2,2,2,32,1025]{4,3,2,1,0:T(8,128)(2,1)}, bf16[2,2,2,32,1025]{4,3,2,1,0:T(8,128)(2,1)}, u32[]{:S(2)}, u32[]{:S(2)}) collective-permute-start(bf16[2,2,2,32,1025]{4,3,2,1,0:T(8,128)(2,1)} %fusion.41), channel_id=1, source_target_pairs={{0,4},{1,5},{2,6},{3,7},{4,0},{5,1},{6,2},{7,3},{8,12},{9,13},{10,... | collective-permute-start | bytes 1574408 | tf_op jit(solution)/shard_map/ppermute | solution.py:153
  103.5 5.2 %copy-start.17 = (bf16[1,16,8,8,128]{4,1,3,2,0:T(8,128)(2,1)S(1)}, bf16[1,16,8,8,128]{4,1,3,2,0:T(8,128)(2,1)}, u32[]{:S(2)}) copy-start(bf16[1,16,8,8,128]{4,1,3,2,0:T(8,128)(2,1)} %fusion.29) | copy-start | bytes 786436
  109.7 24.2 %all-to-all-start.3 = ((bf16[1,16,8,1024]{3,2,0,1:T(8,128)(2,1)}), bf16[1,16,8,1024]{3,2,0,1:T(8,128)(2,1)}, u32[]{:S(2)}, u32[]{:S(2)}) async-start(bf16[1,16,8,1024]{3,2,0,1:T(8,128)(2,1)} %bitcast.65), calls=%async_computation.3 | async-start | bytes 524288 | tf_op jit(solution)/shard_map/all_to_all | solution.py:258
  118.5 7.7 %copy-start.12 = (bf16[128,1024]{0,1:T(8,128)(2,1)S(1)}, bf16[128,1024]{0,1:T(8,128)(2,1)}, u32[]{:S(2)}) copy-start(bf16[128,1024]{0,1:T(8,128)(2,1)} %copy.162) | copy-start | bytes 786436
  118.5 15.3 %collective-permute-start.13 = (bf16[2,2,32,1025]{3,2,1,0:T(8,128)(2,1)}, bf16[2,2,32,1025]{3,2,1,0:T(8,128)(2,1)}, u32[]{:S(2)}, u32[]{:S(2)}) collective-permute-start(bf16[2,2,32,1025]{3,2,1,0:T(8,128)(2,1)} %fusion.53), channel_id=1, source_target_pairs={{0,2},{1,17},{2,0},{3,19},{4,6},{5,21},{6,4},{7,23},{8,10},{9,25},... | collective-permute-start | bytes 787208 | tf_op jit(solution)/shard_map/ppermute | solution.py:153
  125.7 12.3 %collective-permute-start.8 = (bf16[2,2,32,3072]{3,2,1,0:T(8,128)(2,1)}, bf16[2,2,32,3072]{3,2,1,0:T(8,128)(2,1)}, u32[]{:S(2)}, u32[]{:S(2)}) collective-permute-start(bf16[2,2,32,3072]{3,2,1,0:T(8,128)(2,1)} %fusion.38), channel_id=1, source_target_pairs={{0,16},{1,5},{2,18},{3,7},{4,20},{5,1},{6,22},{7,3},{8,24},{9,13},... | collective-permute-start | bytes 2359304 | tf_op jit(solution)/shard_map/ppermute | solution.py:153
  134.9 6.7 %collective-permute-start.14 = (bf16[2,32,1025]{2,1,0:T(8,128)(2,1)S(1)}, bf16[2,32,1025]{2,1,0:T(8,128)(2,1)S(1)}, u32[]{:S(2)}, u32[]{:S(2)}) collective-permute-start(bf16[2,32,1025]{2,1,0:T(8,128)(2,1)S(1)} %fusion.67), channel_id=1, source_target_pairs={{0,16},{1,3},{2,18},{3,1},{4,20},{5,7},{6,22},{7,5},{8,24},{9,11},... | collective-permute-start | bytes 393608 | tf_op jit(solution)/shard_map/ppermute | solution.py:153
  139.9 10.0 %collective-permute-start.9 = (bf16[2,32,3072]{2,1,0:T(8,128)(2,1)S(1)}, bf16[2,32,3072]{2,1,0:T(8,128)(2,1)S(1)}, u32[]{:S(2)}, u32[]{:S(2)}) collective-permute-start(bf16[2,32,3072]{2,1,0:T(8,128)(2,1)S(1)} %fusion.51), channel_id=1, source_target_pairs={{0,4},{1,3},{2,6},{3,1},{4,0},{5,7},{6,2},{7,5},{8,12},{9,11},{10,... | collective-permute-start | bytes 1179656 | tf_op jit(solution)/shard_map/ppermute | solution.py:153
  141.7 9.2 %collective-permute-start.15 = (bf16[32,1025]{1,0:T(8,128)(2,1)S(1)}, bf16[32,1025]{1,0:T(8,128)(2,1)S(1)}, u32[]{:S(2)}, u32[]{:S(2)}) collective-permute-start(bf16[32,1025]{1,0:T(8,128)(2,1)S(1)} %fusion.73), channel_id=1, source_target_pairs={{0,8},{1,9},{2,10},{3,11},{4,12},{5,13},{6,14},{7,15},{8,0},{9,1},... | collective-permute-start | bytes 196808 | tf_op jit(solution)/shard_map/ppermute | solution.py:153
  150.0 8.4 %collective-permute-start.10 = (bf16[32,3072]{1,0:T(8,128)(2,1)S(1)}, bf16[32,3072]{1,0:T(8,128)(2,1)S(1)}, u32[]{:S(2)}, u32[]{:S(2)}) collective-permute-start(bf16[32,3072]{1,0:T(8,128)(2,1)S(1)} %fusion.66), channel_id=1, source_target_pairs={{0,8},{1,9},{2,10},{3,11},{4,12},{5,13},{6,14},{7,15},{8,0},{9,1},... | collective-permute-start | bytes 589832 | tf_op jit(solution)/shard_map/ppermute | solution.py:153
  150.9 8.2 %collective-permute-start.16 = (bf16[32,1025]{1,0:T(8,128)(2,1)S(1)}, bf16[32,1025]{1,0:T(8,128)(2,1)S(1)}, u32[]{:S(2)}, u32[]{:S(2)}) collective-permute-start(bf16[32,1025]{1,0:T(8,128)(2,1)S(1)} %fusion.68), channel_id=1, source_target_pairs={{0,16},{16,0},{1,17},{17,1},{2,18},{18,2},{3,19},{19,3},{4,20},{20... | collective-permute-start | bytes 196808 | tf_op jit(solution)/shard_map/ppermute | solution.py:159
  158.5 5.7 %collective-permute-start.11 = (bf16[32,3072]{1,0:T(8,128)(2,1)S(1)}, bf16[32,3072]{1,0:T(8,128)(2,1)S(1)}, u32[]{:S(2)}, u32[]{:S(2)}) collective-permute-start(bf16[32,3072]{1,0:T(8,128)(2,1)S(1)} %fusion.52), channel_id=1, source_target_pairs={{0,16},{16,0},{1,17},{17,1},{2,18},{18,2},{3,19},{19,3},{4,20},{20... | collective-permute-start | bytes 589832 | tf_op jit(solution)/shard_map/ppermute | solution.py:159
  (9 other events, 25.4 us)

commit v12 on v7

--- a/solution.py
+++ b/solution.py
@@ -243,17 +243,12 @@
     grad_hidden = (
         inverse * scaled - hidden * inverse**3 * jnp.mean(scaled * hidden, axis=-1, keepdims=True)
     ).astype(jnp.bfloat16)
-    first_peer, hidden_peer, gain_peer = lax.ppermute((flat_first, grad_hidden, gain_term), "seq", pair)
-    out_term = jnp.dot(
-        my_half(jnp.concatenate([flat_first, first_peer], axis=0), out_orders).T,
-        jnp.concatenate([grad_hidden, hidden_peer], axis=0),
-        preferred_element_type=jnp.float32,
-    )
-    gain_term = my_half((gain_term + gain_peer)[None, :], out_orders)[0][:, None]
+    out_term = jnp.dot(flat_first.T, grad_hidden, preferred_element_type=jnp.float32)
     out_width = out_term.shape[1]
-    (out_sum,), out_cols = reduce_rows(
-        (jnp.concatenate([out_term, gain_term], axis=1),), (out_orders,), seq_n, dp_n, out_cols
-    )
+    out_terms = jnp.concatenate([out_term, gain_term[:, None]], axis=1).astype(jnp.bfloat16)
+    out_terms, out_cols = lax.optimization_barrier((out_terms, out_cols))
+    out_sum = lax.psum_scatter(out_terms, ("seq", "dp"), scatter_dimension=0, tiled=True)
+    out_sum = lax.all_gather(out_sum, "dp", axis=0, tiled=True)
     column_out = lax.all_to_all(
         out_cols.reshape(batches, all_rows, col_share, feature),
         "seq",

time: 162 us -> 250 us (1.54)
  waiting for transfers between devices: 26.8 us -> 107 us
  between operations: 1.16 us -> 14.6 us
  starting transfers between devices: 36.5 us -> 28.7 us
  blocking collectives: 0 us -> 5.23 us
    reduce_scatter x0 -> x1, waiting for transfers between devices: none -> 70 us  [on_device(): lax.psum_scatter(out_terms, ('seq', 'dp'), scatter_dimension=0, tiled=True)]
    ppermute x8 -> x4, waiting for transfers between devices: 16.5 us -> 27.4 us  [reduce_rows(): lax.ppermute(given, ('dp', 'seq'), perm).astype(jnp.float32)]
    ppermute x8 -> x4, starting transfers between devices: 11.7 us -> 6.08 us  [reduce_rows(): lax.ppermute(given, ('dp', 'seq'), perm).astype(jnp.float32)]
    all_gather x0 -> x1, blocking collectives: none -> 5.23 us  [on_device(): out_sum = lax.all_gather(out_sum, 'dp', axis=0, tiled=True)]
    ppermute x2 -> x1, waiting for transfers between devices: 3.84 us -> 0.01 us  [reduce_rows(): got = lax.ppermute(accs, 'dp', perm)]
    unnamed x54 -> x65, local copies, waits for them, and re-layouts: 20.7 us -> 22.7 us
    add x6 -> x3, other arithmetic: 7.28 us -> 6.03 us  [reduce_rows(): kept + lax.ppermute(given, ('dp', 'seq'), perm).astype(jnp.float32)]
  transfers between devices with their start and end apart: 19 -> 12, of which waited for: 7 -> 6; matrix products, arithmetic and copies ran while one was open for 39% -> 22% of each run, Pallas kernels for 0% -> 0%
where the time goes in v12:
time: 250 us; the launch traced here: 248 us
  waiting for transfers between devices  107 us (43%)
  matrix products  37.7 us (15%)
  local copies, waits for them, and re-layouts  35.4 us (14%)
  starting transfers between devices  28.7 us (11%)
  other arithmetic  19.5 us (8%)
  between operations  14.6 us (6%)
  blocking collectives  5.23 us (2%)
    reduce_scatter x1, waiting for transfers between devices, on_device(): lax.psum_scatter(out_terms, ('seq', 'dp'), scatter_dimension=0, tiled=True)  70 us
    ppermute x4, waiting for transfers between devices, reduce_rows(): lax.ppermute(given, ('dp', 'seq'), perm).astype(jnp.float32)  27.4 us
    unnamed x65, local copies, waits for them, and re-layouts  22.7 us
    all_to_all x1, waiting for transfers between devices, on_device(): lax.all_to_all(normed.reshape(batches, local_rows, columns, model_width),...  7.49 us
    all_to_all x1, starting transfers between devices, on_device(): lax.all_to_all(upstream, 'seq', split_axis=2, concat_axis=1, tiled=True)  7.39 us
    ppermute x4, starting transfers between devices, reduce_rows(): lax.ppermute(given, ('dp', 'seq'), perm).astype(jnp.float32)  6.08 us
    all_to_all x1, starting transfers between devices, on_device(): lax.all_to_all(normed.reshape(batches, local_rows, columns, model_width),...  6.07 us
    add x3, other arithmetic, reduce_rows(): kept + lax.ppermute(given, ('dp', 'seq'), perm).astype(jnp.float32)  6.03 us
  transfers between devices with their start and end apart: 12, of which 6 were waited for; matrix products, arithmetic and copies ran while one was open for 22% of the time, Pallas kernels for 0%

profile of v12, /device:TPU:0, one launch (start us, length us, event | category | flops | bytes accessed | tf_op | source)
XLA Modules:
  0.0 248.4 jit_solution(14356744977584507787)
XLA Ops:
  9.2 2.1 reduce.16
  12.2 7.4 %all-to-all-start.1 = ((bf16[16,2,4096]{2,1,0:T(2,128)(2,1)}), bf16[16,2,4096]{2,1,0:T(2,128)(2,1)S(1)}, u32[]{:S(2)}, u32[]{:S(2)}) async-start(bf16[16,2,4096]{2,1,0:T(2,128)(2,1)} %reshape.262), calls=%async_computation.1 | async-start | bytes 524288 | tf_op jit(solution)/shard_map/all_to_all | solution.py:201
  20.8 1.8 copy.145
  26.6 2.9 %reduce.17 = bf16[128,1024]{1,0:T(8,128)(2,1)} reduce(bf16[128,1,1,1024]{3,2,1,0:T(2,128)(2,1)S(1)} %bitcast.156, bf16[]{:T(256)} %broadcast.99), dimensions={1,2}, to_apply=%bitcast.148.reduce_sub_computation | reduce | bytes 524290
  29.4 1.8 reshape.264
  31.3 6.1 %all-to-all-start = ((bf16[16,2,4096]{2,1,0:T(2,128)(2,1)}), bf16[16,2,4096]{2,1,0:T(2,128)(2,1)}, u32[]{:S(2)}, u32[]{:S(2)}) async-start(bf16[16,2,4096]{2,1,0:T(2,128)(2,1)} %reshape.264), calls=%async_computation | async-start | bytes 524288 | tf_op jit(solution)/shard_map/all_to_all | solution.py:184
  39.9 7.5 %all-to-all-done = bf16[16,2,4096]{2,1,0:T(2,128)(2,1)} async-done(((bf16[16,2,4096]{2,1,0:T(2,128)(2,1)}), bf16[16,2,4096]{2,1,0:T(2,128)(2,1)}, u32[]{:S(2)}, u32[]{:S(2)}) %all-to-all-start) | async-done | bytes 262176 | tf_op jit(solution)/shard_map/all_to_all | solution.py:184
  47.4 2.2 reshape.265
  50.1 3.9 %convolution_convert_fusion = bf16[128,3072]{1,0:T(8,128)(2,1)S(1)} fusion(bf16[1024,3072]{1,0:T(8,128)(2,1)} %param.12, bf16[1,1,128,1024]{2,3,1,0:T(8,128)(2,1)S(1)} %copy.103), kind=kOutput, calls=%fused_computation.4 | convolution fusion | flops 805699584 | bytes 7340032 | tf_op jit(solution)/shard_map/dot_general | solution.py:191
  56.1 2.6 %fusion.75 = (f32[8,8,16]{2,1,0:T(8,128)S(1)}, f32[8,8,16,16]{2,3,1,0:T(8,128)}) fusion(pred[16,16]{0,1:T(8,128)(4,1)S(1)} %iota_compare_fusion.1, bf16[1,16,8,1,8,128]{5,2,4,3,1,0:T(8,128)(2,1)S(1)} %get-tuple-element.47, bf16[1,16,8,1,8,128]{5,2,4,3,1,0:T(8,128)(2,1)} %get-tuple-element.46), kind=kOutput, calls=%fused_computation.117 | convolution fusion | flops 4259855 | bytes 594176 | tf_op jit(solution)/shard_map/sub | solution.py:28
  58.6 2.1 fusion.24
  60.7 2.9 %fusion.27 = bf16[1,16,8,1,8,128]{5,1,4,2,3,0:T(8,128)(2,1)} fusion(f32[8,8,16,16]{2,3,1,0:T(8,128)} %convolution_bitcast_fusion, bf16[1,16,8,1,8,128]{5,2,4,3,1,0:T(8,128)(2,1)} %get-tuple-element.46, f32[8,8,16,16]{2,3,1,0:T(8,128)} %get-tuple-element.55, f32[8,8,16]{2,1,0:T(8,128)S(1)} %get-tuple-element.54), kind=kOutput, calls=%fused_computation.47 | convolution fusion | flops 4441103 | bytes 659456 | tf_op jit(solution)/shard_map/bchlm,blche->bmche/dot_general | solution.py:57
  63.6 2.5 fusion.23
  70.3 5.7 %fusion.25 = bf16[1,16,8,1024]{3,2,0,1:T(8,128)(2,1)} fusion(bf16[128,3072]{1,0:T(8,128)(2,1)S(1)} %reshape_reshape.7, bf16[1024,3072]{1,0:T(8,128)(2,1)} %param.12), kind=kOutput, calls=%fused_computation.45 | convolution fusion | flops 805437440 | bytes 7340032 | tf_op jit(solution)/shard_map/dot_general | solution.py:209
  76.0 4.4 %all-to-all-start.2 = ((bf16[1,16,8,1024]{3,2,0,1:T(8,128)(2,1)}), bf16[1,16,8,1024]{3,2,0,1:T(8,128)(2,1)}, u32[]{:S(2)}, u32[]{:S(2)}) async-start(bf16[1,16,8,1024]{3,2,0,1:T(8,128)(2,1)} %fusion.25), calls=%async_computation.2 | async-start | bytes 524288 | tf_op jit(solution)/shard_map/all_to_all | solution.py:231
  81.6 2.1 fusion.5
  83.8 2.6 %copy-done.1 = f32[512,3072]{1,0:T(8,128)} copy-done((f32[512,3072]{1,0:T(8,128)}, f32[512,3072]{1,0:T(8,128)S(1)}, u32[]{:S(2)}) %copy-start.1) | copy-done | bytes 6291480
  87.9 2.4 all-to-all-done.2
  92.4 18.5 %collective-permute-done.2 = bf16[2,2,2,32,3072]{4,3,2,1,0:T(8,128)(2,1)} collective-permute-done((bf16[2,2,2,32,3072]{4,3,2,1,0:T(8,128)(2,1)}, bf16[2,2,2,32,3072]{4,3,2,1,0:T(8,128)(2,1)}, u32[]{:S(2)}, u32[]{:S(2)}) %collective-permute-start.2) | collective-permute-done | bytes 1572896 | tf_op jit(solution)/shard_map/ppermute | solution.py:153
  111.0 2.8 %bitcast_add_fusion = f32[2,2,2,32,3072]{4,3,2,1,0:T(8,128)S(1)} fusion(bf16[2,2,2,32,3072]{4,3,2,1,0:T(8,128)(2,1)} %collective-permute-done.2, f32[2,2,2,2,32,3072]{5,4,3,2,1,0:T(8,128)} %bitcast.150, s32[]{:T(128)S(6)} %select_n.142), kind=kLoop, calls=%fused_computation.5 | loop fusion | flops 1572864 | bytes 7864324 | tf_op jit(solution)/shard_map/add | solution.py:153
  120.0 1.9 convolution_convert_fusion.1
  124.3 3.5 %all-to-all-start.3 = ((bf16[1,16,8,1024]{3,2,0,1:T(8,128)(2,1)}), bf16[1,16,8,1024]{3,2,0,1:T(8,128)(2,1)S(1)}, u32[]{:S(2)}, u32[]{:S(2)}) async-start(bf16[1,16,8,1024]{3,2,0,1:T(8,128)(2,1)} %bitcast.47), calls=%async_computation.3 | async-start | bytes 524288 | tf_op jit(solution)/shard_map/all_to_all | solution.py:252
  127.9 4.1 %copy.137 = bf16[1024,1025]{1,0:T(8,128)(2,1)} copy(bf16[1024,1025]{0,1:T(8,128)(2,1)} %pad_maximum_fusion) | data formatting | bytes 4198400
  132.1 1.9 bitcast_add_fusion.1
  135.9 1.8 collective-permute-start.4
  138.8 2.6 %convolution_convert_fusion.2 = bf16[8,128,128]{1,2,0:T(8,128)(2,1)} fusion(bf16[128,8,128]{0,2,1:T(8,128)(2,1)S(1)} %bitcast.165, f32[8,128,128]{1,2,0:T(8,128)} %fusion.53, f32[8,128,128]{1,2,0:T(8,128)} %get-tuple-element.51, f32[8,128]{1,0:T(8,128)S(1)} %get-tuple-element.50), kind=kOutput, calls=%fused_computation.33 | convolution fusion | flops 34604160 | bytes 1576960 | tf_op jit(solution)/shard_map/ghlm,gmhe->glhe/dot_general | solution.py:51
  141.4 2.6 %collective-permute-done.4 = bf16[2,32,3072]{2,1,0:T(8,128)(2,1)} collective-permute-done((bf16[2,32,3072]{2,1,0:T(8,128)(2,1)}, bf16[2,32,3072]{2,1,0:T(8,128)(2,1)}, u32[]{:S(2)}, u32[]{:S(2)}) %collective-permute-start.4) | collective-permute-done | bytes 393248 | tf_op jit(solution)/shard_map/ppermute | solution.py:153
  146.1 2.7 %collective-permute-start.5 = (bf16[32,3072]{1,0:T(8,128)(2,1)}, bf16[32,3072]{1,0:T(8,128)(2,1)}, u32[]{:S(2)}, u32[]{:S(2)}) collective-permute-start(bf16[32,3072]{1,0:T(8,128)(2,1)} %fusion.57), channel_id=1, source_target_pairs={{0,8},{1,9},{2,10},{3,11},{4,12},{5,13},{6,14},{7,15},{8,0},{9,1},... | collective-permute-start | bytes 589832 | tf_op jit(solution)/shard_map/ppermute | solution.py:153
  148.8 2.6 %convolution_convert_fusion.7 = bf16[8,128,128]{1,2,0:T(8,128)(2,1)} fusion(bf16[128,8,128]{0,2,1:T(8,128)(2,1)S(1)} %bitcast.163, f32[8,128,128]{1,2,0:T(8,128)} %fusion.53, f32[8,128,128]{1,2,0:T(8,128)} %get-tuple-element.51, f32[8,128]{1,0:T(8,128)S(1)} %get-tuple-element.50), kind=kOutput, calls=%fused_computation.38 | convolution fusion | flops 34604160 | bytes 1576960 | tf_op jit(solution)/shard_map/ghlm,glhe->gmhe/dot_general | solution.py:57
  151.4 6.3 %collective-permute-done.5 = bf16[32,3072]{1,0:T(8,128)(2,1)} collective-permute-done((bf16[32,3072]{1,0:T(8,128)(2,1)}, bf16[32,3072]{1,0:T(8,128)(2,1)}, u32[]{:S(2)}, u32[]{:S(2)}) %collective-permute-start.5) | collective-permute-done | bytes 196640 | tf_op jit(solution)/shard_map/ppermute | solution.py:153
  163.5 70.0 %reduce-scatter.4.cloned.1.call-done = bf16[32,1025]{1,0:T(8,128)(2,1)} async-done(((bf16[1024,1025]{1,0:T(8,128)(2,1)}), bf16[32,1025]{1,0:T(8,128)(2,1)}) %reduce-scatter.4.cloned.1.call-update) | async-done | bytes 65616 | tf_op jit(solution)/shard_map/reduce_scatter | solution.py:250
  233.5 5.2 %all_gather.3 = bf16[64,1025]{1,0:T(8,128)(2,1)S(1)} all-gather(bf16[32,1025]{1,0:T(8,128)(2,1)} %reduce-scatter.4.cloned.1.call-done), channel_id=1, replica_groups=mesh['dp'=2,'seq'=16] {'dp'}, dimensions={0}, use_global_device_ids=true | all-gather | bytes 196800 | tf_op jit(solution)/shard_map/all_gather | solution.py:251
  (114 shorter events, 44.3 us)
Async XLA Ops:
  7.2 18.2 %copy-start = (bf16[1024,1024]{1,0:T(8,128)(2,1)S(1)}, bf16[1024,1024]{1,0:T(8,128)(2,1)}, u32[]{:S(2)}) copy-start(bf16[1024,1024]{1,0:T(8,128)(2,1)} %param.10) | copy-start | bytes 6291460
  11.4 11.2 %copy-start.18 = (bf16[1,1,128,1024]{3,2,1,0:T(8,128)(2,1)S(1)}, bf16[1,1,128,1024]{3,2,1,0:T(8,128)(2,1)}, u32[]{:S(2)}) copy-start(bf16[1,1,128,1024]{3,2,1,0:T(8,128)(2,1)} %param.7) | copy-start | bytes 786436
  12.2 19.0 %all-to-all-start.1 = ((bf16[16,2,4096]{2,1,0:T(2,128)(2,1)}), bf16[16,2,4096]{2,1,0:T(2,128)(2,1)S(1)}, u32[]{:S(2)}, u32[]{:S(2)}) async-start(bf16[16,2,4096]{2,1,0:T(2,128)(2,1)} %reshape.262), calls=%async_computation.1 | async-start | bytes 524288 | tf_op jit(solution)/shard_map/all_to_all | solution.py:201
  20.8 4.6 %copy-start.10 = (bf16[1,1,128,1024]{2,3,1,0:T(8,128)(2,1)}, bf16[1,1,128,1024]{2,3,1,0:T(8,128)(2,1)S(1)}, u32[]{:S(2)}) copy-start(bf16[1,1,128,1024]{2,3,1,0:T(8,128)(2,1)S(1)} %copy.142) | copy-start | bytes 786436
  23.1 2.3 copy-start.5
  31.3 16.2 %all-to-all-start = ((bf16[16,2,4096]{2,1,0:T(2,128)(2,1)}), bf16[16,2,4096]{2,1,0:T(2,128)(2,1)}, u32[]{:S(2)}, u32[]{:S(2)}) async-start(bf16[16,2,4096]{2,1,0:T(2,128)(2,1)} %reshape.264), calls=%async_computation | async-start | bytes 524288 | tf_op jit(solution)/shard_map/all_to_all | solution.py:184
  50.0 3.9 %copy-start.4 = (bf16[1,1,128,1024]{2,3,1,0:T(8,128)(2,1)}, bf16[1,1,128,1024]{2,3,1,0:T(8,128)(2,1)S(1)}, u32[]{:S(2)}) copy-start(bf16[1,1,128,1024]{2,3,1,0:T(8,128)(2,1)S(1)} %copy.103) | copy-start | bytes 786436
  50.1 4.7 %copy-start.14 = (bf16[16,8,8,128]{3,2,1,0:T(8,128)(2,1)S(1)}, bf16[16,8,8,128]{3,2,1,0:T(8,128)(2,1)}, u32[]{:S(2)}) copy-start(bf16[16,8,8,128]{3,2,1,0:T(8,128)(2,1)} %copy.172) | copy-start | bytes 786436
  54.7 3.9 %copy-start.22 = (bf16[1,16,8,1,8,128]{5,2,4,3,1,0:T(8,128)(2,1)}, bf16[1,16,8,1,8,128]{5,2,4,3,1,0:T(8,128)(2,1)S(1)}, u32[]{:S(2)}) copy-start(bf16[1,16,8,1,8,128]{5,2,4,3,1,0:T(8,128)(2,1)S(1)} %get-tuple-element.47) | copy-start | bytes 786436
  54.7 6.0 %copy-start.15 = (bf16[1,16,8,1,8,128]{5,2,4,3,1,0:T(8,128)(2,1)}, bf16[1,16,8,1,8,128]{5,2,4,3,1,0:T(8,128)(2,1)S(1)}, u32[]{:S(2)}) copy-start(bf16[1,16,8,1,8,128]{5,2,4,3,1,0:T(8,128)(2,1)S(1)} %get-tuple-element.45) | copy-start | bytes 786436
  60.7 2.9 %copy-start.17 = (f32[8,8,16,16]{2,3,1,0:T(8,128)S(1)}, f32[8,8,16,16]{2,3,1,0:T(8,128)}, u32[]{:S(2)}) copy-start(f32[8,8,16,16]{2,3,1,0:T(8,128)} %convolution_bitcast_fusion) | copy-start | bytes 196612
  63.6 2.5 %copy-start.23 = (bf16[1,16,8,1,8,128]{5,1,4,2,3,0:T(8,128)(2,1)S(1)}, bf16[1,16,8,1,8,128]{5,1,4,2,3,0:T(8,128)(2,1)}, u32[]{:S(2)}) copy-start(bf16[1,16,8,1,8,128]{5,1,4,2,3,0:T(8,128)(2,1)} %fusion.24) | copy-start | bytes 786436
  69.7 11.9 %collective-permute-start.1 = (bf16[128,3072]{1,0:T(8,128)(2,1)S(1)}, bf16[128,3072]{1,0:T(8,128)(2,1)}, u32[]{:S(2)}, u32[]{:S(2)}) collective-permute-start(bf16[128,3072]{1,0:T(8,128)(2,1)S(1)} %reshape_reshape.7), channel_id=1, source_target_pairs={{0,1},{1,0},{2,3},{3,2},{4,5},{5,4},{6,7},{7,6},{8,9},{9,8},{10,11... | collective-permute-start | bytes 2359304 | tf_op jit(solution)/shard_map/ppermute | solution.py:225
  69.8 10.6 %collective-permute-start = (bf16[128,1024]{0,1:T(8,128)(2,1)}, bf16[128,1024]{0,1:T(8,128)(2,1)}, u32[]{:S(2)}, u32[]{:S(2)}) collective-permute-start(bf16[128,1024]{0,1:T(8,128)(2,1)} %bitcast.151), channel_id=1, source_target_pairs={{0,1},{1,0},{2,3},{3,2},{4,5},{5,4},{6,7},{7,6},{8,9},{9,8},{10,11... | collective-permute-start | bytes 786440 | tf_op jit(solution)/shard_map/ppermute | solution.py:225
  76.0 14.3 %all-to-all-start.2 = ((bf16[1,16,8,1024]{3,2,0,1:T(8,128)(2,1)}), bf16[1,16,8,1024]{3,2,0,1:T(8,128)(2,1)}, u32[]{:S(2)}, u32[]{:S(2)}) async-start(bf16[1,16,8,1024]{3,2,0,1:T(8,128)(2,1)} %fusion.25), calls=%async_computation.2 | async-start | bytes 524288 | tf_op jit(solution)/shard_map/all_to_all | solution.py:231
  83.8 2.7 %copy-start.1 = (f32[512,3072]{1,0:T(8,128)}, f32[512,3072]{1,0:T(8,128)S(1)}, u32[]{:S(2)}) copy-start(f32[512,3072]{1,0:T(8,128)S(1)} %fusion.5) | copy-start | bytes 18874372
  83.8 6.5 %copy-start.16 = (bf16[1,16,8,1,8,128]{5,2,4,3,1,0:T(8,128)(2,1)S(1)}, bf16[1,16,8,1,8,128]{5,2,4,3,1,0:T(8,128)(2,1)}, u32[]{:S(2)}) copy-start(bf16[1,16,8,1,8,128]{5,2,4,3,1,0:T(8,128)(2,1)} %copy-done.15) | copy-start | bytes 786436
  83.8 6.5 %copy-start.25 = (f32[8,8,16,16]{2,3,1,0:T(8,128)S(1)}, f32[8,8,16,16]{2,3,1,0:T(8,128)}, u32[]{:S(2)}) copy-start(f32[8,8,16,16]{2,3,1,0:T(8,128)} %get-tuple-element.55) | copy-start | bytes 196612
  90.2 20.7 %collective-permute-start.2 = (bf16[2,2,2,32,3072]{4,3,2,1,0:T(8,128)(2,1)}, bf16[2,2,2,32,3072]{4,3,2,1,0:T(8,128)(2,1)}, u32[]{:S(2)}, u32[]{:S(2)}) collective-permute-start(bf16[2,2,2,32,3072]{4,3,2,1,0:T(8,128)(2,1)} %fusion.4), channel_id=1, source_target_pairs={{0,2},{1,17},{2,0},{3,19},{4,6},{5,21},{6,4},{7,23},{8,10},{9,25},... | collective-permute-start | bytes 4718600 | tf_op jit(solution)/shard_map/ppermute | solution.py:153
  116.5 3.5 %copy-start.7 = (bf16[8,128,128]{1,2,0:T(8,128)(2,1)S(1)}, bf16[8,128,128]{1,2,0:T(8,128)(2,1)}, u32[]{:S(2)}) copy-start(bf16[8,128,128]{1,2,0:T(8,128)(2,1)} %copy-done.6) | copy-start | bytes 786436
  116.5 15.6 %collective-permute-start.3 = (bf16[2,2,32,3072]{3,2,1,0:T(8,128)(2,1)}, bf16[2,2,32,3072]{3,2,1,0:T(8,128)(2,1)}, u32[]{:S(2)}, u32[]{:S(2)}) collective-permute-start(bf16[2,2,32,3072]{3,2,1,0:T(8,128)(2,1)} %fusion.36), channel_id=1, source_target_pairs={{0,16},{1,5},{2,18},{3,7},{4,20},{5,1},{6,22},{7,3},{8,24},{9,13},... | collective-permute-start | bytes 2359304 | tf_op jit(solution)/shard_map/ppermute | solution.py:153
  120.0 17.8 %copy-start.13 = (bf16[128,1024]{0,1:T(8,128)(2,1)}, bf16[128,1024]{0,1:T(8,128)(2,1)S(1)}, u32[]{:S(2)}) copy-start(bf16[128,1024]{0,1:T(8,128)(2,1)S(1)} %copy.144) | copy-start | bytes 786436
  124.3 39.2 %all-to-all-start.3 = ((bf16[1,16,8,1024]{3,2,0,1:T(8,128)(2,1)}), bf16[1,16,8,1024]{3,2,0,1:T(8,128)(2,1)S(1)}, u32[]{:S(2)}, u32[]{:S(2)}) async-start(bf16[1,16,8,1024]{3,2,0,1:T(8,128)(2,1)} %bitcast.47), calls=%async_computation.3 | async-start | bytes 524288 | tf_op jit(solution)/shard_map/all_to_all | solution.py:252
  127.9 105.6 %reduce-scatter.4.cloned.1.call-start = ((), (), s32[]{:S(2)}) async-start(), calls=%async_computation.5 | async-start | bytes 2433024 | tf_op jit(solution)/shard_map/reduce_scatter | solution.py:250
  132.1 5.7 %copy-start.12 = (bf16[16,8,8,128]{3,2,1,0:T(8,128)(2,1)S(1)}, bf16[16,8,8,128]{3,2,1,0:T(8,128)(2,1)}, u32[]{:S(2)}) copy-start(bf16[16,8,8,128]{3,2,1,0:T(8,128)(2,1)} %copy.145) | copy-start | bytes 786436
  132.1 6.7 %copy-start.11 = (bf16[1,1,128,1024]{2,3,1,0:T(8,128)(2,1)S(1)}, bf16[1,1,128,1024]{2,3,1,0:T(8,128)(2,1)}, u32[]{:S(2)}) copy-start(bf16[1,1,128,1024]{2,3,1,0:T(8,128)(2,1)} %copy-done.10) | copy-start | bytes 786436
  135.9 8.1 %collective-permute-start.4 = (bf16[2,32,3072]{2,1,0:T(8,128)(2,1)}, bf16[2,32,3072]{2,1,0:T(8,128)(2,1)}, u32[]{:S(2)}, u32[]{:S(2)}) collective-permute-start(bf16[2,32,3072]{2,1,0:T(8,128)(2,1)} %fusion.44), channel_id=1, source_target_pairs={{0,4},{1,3},{2,6},{3,1},{4,0},{5,7},{6,2},{7,5},{8,12},{9,11},{10,... | collective-permute-start | bytes 1179656 | tf_op jit(solution)/shard_map/ppermute | solution.py:153
  138.8 10.0 %copy-start.9 = (bf16[1,1,128,1024]{2,3,1,0:T(8,128)(2,1)S(1)}, bf16[1,1,128,1024]{2,3,1,0:T(8,128)(2,1)}, u32[]{:S(2)}) copy-start(bf16[1,1,128,1024]{2,3,1,0:T(8,128)(2,1)} %copy-done.8) | copy-start | bytes 786436
  146.1 11.7 %collective-permute-start.5 = (bf16[32,3072]{1,0:T(8,128)(2,1)}, bf16[32,3072]{1,0:T(8,128)(2,1)}, u32[]{:S(2)}, u32[]{:S(2)}) collective-permute-start(bf16[32,3072]{1,0:T(8,128)(2,1)} %fusion.57), channel_id=1, source_target_pairs={{0,8},{1,9},{2,10},{3,11},{4,12},{5,13},{6,14},{7,15},{8,0},{9,1},... | collective-permute-start | bytes 589832 | tf_op jit(solution)/shard_map/ppermute | solution.py:153
  158.7 2.2 copy-start.20
  158.7 3.1 %copy-start.21 = (bf16[8,128,128]{1,2,0:T(8,128)(2,1)S(1)}, bf16[8,128,128]{1,2,0:T(8,128)(2,1)}, u32[]{:S(2)}) copy-start(bf16[8,128,128]{1,2,0:T(8,128)(2,1)} %convolution_convert_fusion.7) | copy-start | bytes 786436
  158.7 81.3 %collective-permute-start.6 = (bf16[32,3072]{1,0:T(8,128)(2,1)S(1)}, bf16[32,3072]{1,0:T(8,128)(2,1)S(1)}, u32[]{:S(2)}, u32[]{:S(2)}) collective-permute-start(bf16[32,3072]{1,0:T(8,128)(2,1)S(1)} %fusion.45), channel_id=1, source_target_pairs={{0,16},{16,0},{1,17},{17,1},{2,18},{18,2},{3,19},{19,3},{4,20},{20... | collective-permute-start | bytes 589832 | tf_op jit(solution)/shard_map/ppermute | solution.py:159
  (6 other events, 8.3 us)
Sparse Core Ops, SparseCore 0:
  134.0 99.4 reduce-scatter.3

commit v13 on v8

--- a/solution.py
+++ b/solution.py
@@ -250,6 +250,7 @@
     grad_hidden = (
         inverse * scaled - hidden * inverse**3 * jnp.mean(scaled * hidden, axis=-1, keepdims=True)
     ).astype(jnp.bfloat16)
+    out_cols, grad_hidden = lax.optimization_barrier((out_cols, grad_hidden))
     first_peer, hidden_peer, gain_peer = lax.ppermute((flat_first, grad_hidden, gain_term), "seq", pair)
     out_term = jnp.dot(
         my_half(jnp.concatenate([flat_first, first_peer], axis=0), out_orders).T,
@@ -258,15 +259,15 @@
     )
     gain_term = my_half((gain_term + gain_peer)[None, :], out_orders)[0][:, None]
     out_width = out_term.shape[1]
-    (out_sum,), out_cols = reduce_rows(
-        (jnp.concatenate([out_term, gain_term], axis=1),), (out_orders,), seq_n, dp_n, out_cols
-    )
     column_out = lax.all_to_all(
         out_cols.reshape(batches, all_rows, col_share, feature),
         "seq",
         split_axis=1,
         concat_axis=2,
         tiled=True,
+    )
+    (out_sum,), column_out = reduce_rows(
+        (jnp.concatenate([out_term, gain_term], axis=1),), (out_orders,), seq_n, dp_n, column_out
     )
     replicas = (joint_sum, out_sum[:, :out_width], out_sum[:, out_width].astype(jnp.float32))
     grad_first = jnp.dot(grad_hidden, out_weight.T, preferred_element_type=jnp.float32).astype(

time: 164 us -> 172 us (1.049)
  waiting for transfers between devices: 29.3 us -> 33.1 us
  local copies, waits for them, and re-layouts: 29.5 us -> 31.7 us
    all_to_all x1, waiting for transfers between devices: 0.01 us -> 8.39 us  [on_device(): lax.all_to_all(out_cols.reshape(batches, all_rows, col_share, feature), '...]
    ppermute x8, waiting for transfers between devices: 18.9 us -> 14.3 us  [reduce_rows(): lax.ppermute(given, ('dp', 'seq'), perm)]
    unnamed x46, local copies, waits for them, and re-layouts: 15.9 us -> 18.1 us
    convert_element_type x7, other arithmetic: 10.2 us -> 12 us  [reduce_rows(): givens.append(half(pending, 1 - keep_at).astype(jnp.bfloat16))]
  transfers between devices with their start and end apart: 19 -> 19, of which waited for: 6 -> 7; matrix products, arithmetic and copies ran while one was open for 40% -> 39% of each run, Pallas kernels for 0% -> 0%
where the time goes in v13:
time: 172 us; the launch traced here: 171 us
  matrix products  39.4 us (23%)
  starting transfers between devices  39 us (23%)
  waiting for transfers between devices  33.1 us (19%)
  local copies, waits for them, and re-layouts  31.7 us (18%)
  other arithmetic  26.3 us (15%)
    unnamed x46, local copies, waits for them, and re-layouts  18.1 us
    ppermute x8, waiting for transfers between devices, reduce_rows(): lax.ppermute(given, ('dp', 'seq'), perm)  14.3 us
    ppermute x8, starting transfers between devices, reduce_rows(): lax.ppermute(given, ('dp', 'seq'), perm)  13.5 us
    convert_element_type x7, other arithmetic, reduce_rows(): givens.append(half(pending, 1 - keep_at).astype(jnp.bfloat16))  12 us
    all_to_all x1, waiting for transfers between devices, on_device(): lax.all_to_all(out_cols.reshape(batches, all_rows, col_share, feature), '...  8.39 us
    all_to_all x1, starting transfers between devices, on_device(): lax.all_to_all(upstream, 'seq', split_axis=2, concat_axis=1, tiled=True)  7.39 us
    all_to_all x1, waiting for transfers between devices, on_device(): lax.all_to_all(normed.reshape(batches, local_rows, columns, model_width),...  6.19 us
    all_to_all x1, starting transfers between devices, on_device(): lax.all_to_all(normed.reshape(batches, local_rows, columns, model_width),...  5.88 us
  transfers between devices with their start and end apart: 19, of which 7 were waited for; matrix products, arithmetic and copies ran while one was open for 39% of the time, Pallas kernels for 0%

profile of v13, /device:TPU:0, one launch (start us, length us, event | category | flops | bytes accessed | tf_op | source)
XLA Modules:
  0.0 170.7 jit_solution(11016391465970487080)
XLA Ops:
  2.7 2.1 %reduce.21 = bf16[128,1024]{1,0:T(8,128)(2,1)S(1)} reduce(bf16[128,1,1,1024]{3,2,1,0:T(2,128)(2,1)S(1)} %bitcast.216, bf16[]{:T(256)} %broadcast.113), dimensions={1,2}, to_apply=%bitcast.208.reduce_sub_computation | reduce | bytes 524290
  5.7 7.4 %all-to-all-start.1 = ((bf16[16,2,4096]{2,1,0:T(2,128)(2,1)}), bf16[16,2,4096]{2,1,0:T(2,128)(2,1)S(1)}, u32[]{:S(2)}, u32[]{:S(2)}) async-start(bf16[16,2,4096]{2,1,0:T(2,128)(2,1)} %reshape.351), calls=%async_computation.1 | async-start | bytes 524288 | tf_op jit(solution)/shard_map/all_to_all | solution.py:208
  17.6 2.0 %convolution_convert_fusion.3 = bf16[8,128,128]{1,2,0:T(8,128)(2,1)} fusion(bf16[128,8,128]{2,1,0:T(8,128)(2,1)} %bitcast.227, f32[8,128]{1,0:T(8,128)S(1)} %get-tuple-element.64, f32[8,128,128]{1,2,0:T(8,128)S(1)} %fusion.21), kind=kOutput, calls=%fused_computation.39 | convolution fusion | flops 34079872 | bytes 1052672 | tf_op jit(solution)/shard_map/ghlm,gmhe->glhe/dot_general | solution.py:31
  22.1 2.9 %reduce.20 = bf16[128,1024]{1,0:T(8,128)(2,1)} reduce(bf16[128,1,1,1024]{3,2,1,0:T(2,128)(2,1)S(1)} %bitcast.217, bf16[]{:T(256)} %broadcast.113), dimensions={1,2}, to_apply=%bitcast.209.reduce_sub_computation | reduce | bytes 524290
  25.0 1.8 %reshape.349 = bf16[16,2,4096]{2,1,0:T(2,128)(2,1)} reshape(bf16[128,1024]{1,0:T(8,128)(2,1)} %reduce.20) | data formatting | bytes 524288
  26.8 5.9 %all-to-all-start = ((bf16[16,2,4096]{2,1,0:T(2,128)(2,1)}), bf16[16,2,4096]{2,1,0:T(2,128)(2,1)}, u32[]{:S(2)}, u32[]{:S(2)}) async-start(bf16[16,2,4096]{2,1,0:T(2,128)(2,1)} %reshape.349), calls=%async_computation | async-start | bytes 524288 | tf_op jit(solution)/shard_map/all_to_all | solution.py:191
  36.6 6.2 %all-to-all-done = bf16[16,2,4096]{2,1,0:T(2,128)(2,1)} async-done(((bf16[16,2,4096]{2,1,0:T(2,128)(2,1)}), bf16[16,2,4096]{2,1,0:T(2,128)(2,1)}, u32[]{:S(2)}, u32[]{:S(2)}) %all-to-all-start) | async-done | bytes 262176 | tf_op jit(solution)/shard_map/all_to_all | solution.py:191
  42.8 2.2 %reshape.350 = bf16[128,1,1,1024]{3,2,1,0:T(2,128)(2,1)S(1)} reshape(bf16[16,2,4096]{2,1,0:T(2,128)(2,1)} %all-to-all-done) | data formatting | bytes 524288
  46.0 3.9 %convolution_convert_fusion = bf16[128,3072]{1,0:T(8,128)(2,1)S(1)} fusion(bf16[1024,3072]{1,0:T(8,128)(2,1)} %param.12, bf16[1,1,128,1024]{2,3,1,0:T(8,128)(2,1)} %copy.112), kind=kOutput, calls=%fused_computation.7 | convolution fusion | flops 805699584 | bytes 7340032 | tf_op jit(solution)/shard_map/dot_general | solution.py:198
  52.0 2.5 %fusion.99 = (f32[8,8,16]{2,1,0:T(8,128)S(1)}, f32[8,8,16,16]{2,3,1,0:T(8,128)}) fusion(pred[16,16]{0,1:T(8,128)(4,1)S(1)} %iota_compare_fusion.1, bf16[1,16,8,1,8,128]{5,2,4,3,1,0:T(8,128)(2,1)S(1)} %get-tuple-element.58, bf16[1,16,8,1,8,128]{5,2,4,3,1,0:T(8,128)(2,1)} %get-tuple-element.57), kind=kOutput, calls=%fused_computation.155 | convolution fusion | flops 4259855 | bytes 594176 | tf_op jit(solution)/shard_map/sub | solution.py:28
  54.5 2.8 %fusion.27 = bf16[1,16,8,1,8,128]{5,1,4,2,3,0:T(8,128)(2,1)} fusion(f32[8,8,16,16]{2,3,1,0:T(8,128)} %convolution_bitcast_fusion, bf16[1,16,8,1,8,128]{5,2,4,3,1,0:T(8,128)(2,1)} %get-tuple-element.57, f32[8,8,16,16]{2,3,1,0:T(8,128)} %get-tuple-element.69, f32[8,8,16]{2,1,0:T(8,128)S(1)} %get-tuple-element.68), kind=kOutput, calls=%fused_computation.50 | convolution fusion | flops 4441103 | bytes 659456 | tf_op jit(solution)/shard_map/bchlm,bmche->blche/dot_general | solution.py:51
  57.3 2.8 %fusion.30 = bf16[1,16,8,1,8,128]{5,1,4,2,3,0:T(8,128)(2,1)} fusion(f32[8,8,16,16]{2,3,1,0:T(8,128)} %convolution_bitcast_fusion, bf16[1,16,8,1,8,128]{5,2,4,3,1,0:T(8,128)(2,1)S(1)} %get-tuple-element.58, f32[8,8,16,16]{2,3,1,0:T(8,128)} %get-tuple-element.69, f32[8,8,16]{2,1,0:T(8,128)S(1)} %get-tuple-element.68), kind=kOutput, calls=%fused_computation.53 | convolution fusion | flops 4441103 | bytes 659456 | tf_op jit(solution)/shard_map/bchlm,blche->bmche/dot_general | solution.py:57
  64.7 5.7 %fusion.29 = bf16[1,16,8,1024]{3,2,0,1:T(8,128)(2,1)} fusion(bf16[128,3072]{1,0:T(8,128)(2,1)S(1)} %reshape_reshape.7, bf16[1024,3072]{1,0:T(8,128)(2,1)} %param.12), kind=kOutput, calls=%fused_computation.52 | convolution fusion | flops 805437440 | bytes 7340032 | tf_op jit(solution)/shard_map/dot_general | solution.py:216
  70.4 4.2 %all-to-all-start.2 = ((bf16[1,16,8,1024]{3,2,0,1:T(8,128)(2,1)}), bf16[1,16,8,1024]{3,2,0,1:T(8,128)(2,1)}, u32[]{:S(2)}, u32[]{:S(2)}) async-start(bf16[1,16,8,1024]{3,2,0,1:T(8,128)(2,1)} %fusion.29), calls=%async_computation.2 | async-start | bytes 524288 | tf_op jit(solution)/shard_map/all_to_all | solution.py:238
  74.6 2.2 %fusion.26 = bf16[1,16,8,8,128]{4,1,3,2,0:T(8,128)(2,1)} fusion(bf16[1,16,8,1,8,128]{5,2,4,3,1,0:T(8,128)(2,1)} %copy-done.11, f32[8,8,16,16]{2,3,1,0:T(8,128)} %get-tuple-element.69, f32[8,8,16]{2,1,0:T(8,128)S(1)} %get-tuple-element.68), kind=kOutput, calls=%fused_computation.49 | convolution fusion | flops 4358144 | bytes 593920 | tf_op jit(solution)/shard_map/bchlm,bmche->blche/dot_general | solution.py:31
  78.0 2.1 %fusion.5 = f32[512,3072]{1,0:T(8,128)S(1)} fusion(bf16[128,3072]{1,0:T(8,128)(2,1)} %collective-permute-done.1, bf16[128,3072]{1,0:T(8,128)(2,1)S(1)} %reshape_reshape.7, bf16[256,1024]{0,1:T(8,128)(2,1)S(1)} %bitcast.219, s32[]{:T(128)S(6)} %select_n.260), kind=kOutput, calls=%fused_computation.13 | convolution fusion | flops 808452096 | bytes 8126468 | tf_op jit(solution)/shard_map/dot_general | solution.py:233
  80.1 2.7 %copy-done.1 = f32[512,3072]{1,0:T(8,128)} copy-done((f32[512,3072]{1,0:T(8,128)}, f32[512,3072]{1,0:T(8,128)S(1)}, u32[]{:S(2)}) %copy-start.1) | copy-done | bytes 6291480
  90.7 5.1 %all-to-all-start.3 = ((bf16[1,16,8,1024]{3,2,0,1:T(8,128)(2,1)}), bf16[1,16,8,1024]{3,2,0,1:T(8,128)(2,1)S(1)}, u32[]{:S(2)}, u32[]{:S(2)}) async-start(bf16[1,16,8,1024]{3,2,0,1:T(8,128)(2,1)} %bitcast.222), calls=%async_computation.3 | async-start | bytes 524288 | tf_op jit(solution)/shard_map/all_to_all | solution.py:262
  100.8 8.4 %all-to-all-done.3 = bf16[1,16,8,1024]{3,2,0,1:T(8,128)(2,1)S(1)} async-done(((bf16[1,16,8,1024]{3,2,0,1:T(8,128)(2,1)}), bf16[1,16,8,1024]{3,2,0,1:T(8,128)(2,1)S(1)}, u32[]{:S(2)}, u32[]{:S(2)}) %all-to-all-start.3) | async-done | bytes 262176 | tf_op jit(solution)/shard_map/all_to_all | solution.py:262
  111.6 4.2 %fusion.9 = (bf16[2,2,32,3072]{3,2,1,0:T(8,128)(2,1)}, f32[2,2,32,3072]{3,2,1,0:T(8,128)}) fusion(f32[2,2,2,2,32,3072]{5,4,3,2,1,0:T(8,128)} %bitcast.211, s32[]{:T(128)S(6)} %select_n.276, s32[]{:T(128)S(6)} %select_n.283, bf16[2,2,2,32,3072]{4,3,2,1,0:T(8,128)(2,1)} %collective-permute-done.5, s32[]{:T(128)S(6)} %select_n.282, s32[]{:T(128)S(6)} %select_n.278, ...), kind=kLoop, calls=%fused_computation.18 | loop fusion | flops 1966080 | bytes 7077908 | tf_op jit(solution)/shard_map/convert_element_type | solution.py:155
  117.3 8.3 %collective-permute-done.10 = bf16[2,2,2,32,1025]{4,3,2,1,0:T(8,128)(2,1)S(1)} collective-permute-done((bf16[2,2,2,32,1025]{4,3,2,1,0:T(8,128)(2,1)}, bf16[2,2,2,32,1025]{4,3,2,1,0:T(8,128)(2,1)S(1)}, u32[]{:S(2)}, u32[]{:S(2)}) %collective-permute-start.10) | collective-permute-done | bytes 524832 | tf_op jit(solution)/shard_map/ppermute | solution.py:159
  127.9 2.8 %convolution_convert_fusion.5 = bf16[8,128,128]{1,2,0:T(8,128)(2,1)} fusion(bf16[128,8,128]{0,2,1:T(8,128)(2,1)} %bitcast.226, f32[8,128,128]{1,2,0:T(8,128)} %fusion.69, f32[8,128,128]{1,2,0:T(8,128)} %get-tuple-element.65, f32[8,128]{1,0:T(8,128)S(1)} %get-tuple-element.64), kind=kOutput, calls=%fused_computation.41 | convolution fusion | flops 34604160 | bytes 1576960 | tf_op jit(solution)/shard_map/ghlm,glhe->gmhe/dot_general | solution.py:57
  130.7 1.8 %copy.144 = bf16[1,1,128,1024]{3,2,1,0:T(8,128)(2,1)} copy(bf16[1,1,128,1024]{2,3,1,0:T(8,128)(2,1)} %bitcast.234) | data formatting | bytes 524288
  132.5 2.6 %convolution_convert_fusion.1 = bf16[8,128,128]{1,2,0:T(8,128)(2,1)} fusion(bf16[128,8,128]{0,2,1:T(8,128)(2,1)S(1)} %bitcast.224, f32[8,128,128]{1,2,0:T(8,128)} %fusion.69, f32[8,128,128]{1,2,0:T(8,128)} %get-tuple-element.65, f32[8,128]{1,0:T(8,128)S(1)} %get-tuple-element.64), kind=kOutput, calls=%fused_computation.37 | convolution fusion | flops 34604160 | bytes 1576960 | tf_op jit(solution)/shard_map/ghlm,gmhe->glhe/dot_general | solution.py:51
  140.1 2.5 %fusion.58 = (bf16[2,32,3072]{2,1,0:T(8,128)(2,1)}, f32[1,2,32,3072]{3,2,1,0:T(8,128)S(1)}) fusion(f32[2,2,32,3072]{3,2,1,0:T(8,128)} %get-tuple-element.50, s32[]{:T(128)S(6)} %select_n.287, bf16[2,2,32,3072]{3,2,1,0:T(8,128)(2,1)} %collective-permute-done.6, s32[]{:T(128)S(6)} %select_n.281), kind=kLoop, calls=%fused_computation.90 | loop fusion | flops 983040 | bytes 3538952 | tf_op jit(solution)/shard_map/convert_element_type | solution.py:155
  144.1 2.3 %convolution_convert_fusion.4 = bf16[8,128,128]{2,1,0:T(8,128)(2,1)} fusion(bf16[128,8,128]{0,2,1:T(8,128)(2,1)} %bitcast.229, f32[8,128]{1,0:T(8,128)S(1)} %get-tuple-element.64, f32[8,128,128]{1,2,0:T(8,128)} %copy-done.4), kind=kOutput, calls=%fused_computation.40 | convolution fusion | flops 34079872 | bytes 1052672 | tf_op jit(solution)/shard_map/ghlm,glhe->gmhe/dot_general | solution.py:64
  146.4 1.8 %copy.145 = bf16[1,1,128,1024]{3,2,1,0:T(8,128)(2,1)} copy(bf16[1,1,128,1024]{2,3,1,0:T(8,128)(2,1)} %bitcast.233) | data formatting | bytes 524288
  149.1 2.5 %collective-permute-start.13 = (bf16[32,1025]{1,0:T(8,128)(2,1)S(1)}, bf16[32,1025]{1,0:T(8,128)(2,1)S(1)}, u32[]{:S(2)}, u32[]{:S(2)}) collective-permute-start(bf16[32,1025]{1,0:T(8,128)(2,1)S(1)} %fusion.81), channel_id=1, source_target_pairs={{0,8},{1,9},{2,10},{3,11},{4,12},{5,13},{6,14},{7,15},{8,0},{9,1},... | collective-permute-start | bytes 196808 | tf_op jit(solution)/shard_map/ppermute | solution.py:159
  152.6 2.4 %collective-permute-start.8 = (bf16[32,3072]{1,0:T(8,128)(2,1)S(1)}, bf16[32,3072]{1,0:T(8,128)(2,1)S(1)}, u32[]{:S(2)}, u32[]{:S(2)}) collective-permute-start(bf16[32,3072]{1,0:T(8,128)(2,1)S(1)} %fusion.73), channel_id=1, source_target_pairs={{0,8},{1,9},{2,10},{3,11},{4,12},{5,13},{6,14},{7,15},{8,0},{9,1},... | collective-permute-start | bytes 589832 | tf_op jit(solution)/shard_map/ppermute | solution.py:159
  154.9 3.0 %collective-permute-done.13 = bf16[32,1025]{1,0:T(8,128)(2,1)S(1)} collective-permute-done((bf16[32,1025]{1,0:T(8,128)(2,1)S(1)}, bf16[32,1025]{1,0:T(8,128)(2,1)S(1)}, u32[]{:S(2)}, u32[]{:S(2)}) %collective-permute-start.13) | collective-permute-done | bytes 65632 | tf_op jit(solution)/shard_map/ppermute | solution.py:159
  159.5 2.9 %collective-permute-done.8 = bf16[32,3072]{1,0:T(8,128)(2,1)S(1)} collective-permute-done((bf16[32,3072]{1,0:T(8,128)(2,1)S(1)}, bf16[32,3072]{1,0:T(8,128)(2,1)S(1)}, u32[]{:S(2)}, u32[]{:S(2)}) %collective-permute-start.8) | collective-permute-done | bytes 196640 | tf_op jit(solution)/shard_map/ppermute | solution.py:159
  165.3 3.8 %collective-permute-done.9 = bf16[32,3072]{1,0:T(8,128)(2,1)S(1)} collective-permute-done((bf16[32,3072]{1,0:T(8,128)(2,1)S(1)}, bf16[32,3072]{1,0:T(8,128)(2,1)S(1)}, u32[]{:S(2)}, u32[]{:S(2)}) %collective-permute-start.9) | collective-permute-done | bytes 196640 | tf_op jit(solution)/shard_map/ppermute | solution.py:166
  (119 shorter events, 55.9 us)
Async XLA Ops:
  0.6 19.4 %copy-start = (bf16[1024,1024]{1,0:T(8,128)(2,1)S(1)}, bf16[1024,1024]{1,0:T(8,128)(2,1)}, u32[]{:S(2)}) copy-start(bf16[1024,1024]{1,0:T(8,128)(2,1)} %param.10) | copy-start | bytes 6291460
  4.8 10.7 %copy-start.12 = (bf16[1,1,128,1024]{3,2,1,0:T(8,128)(2,1)S(1)}, bf16[1,1,128,1024]{3,2,1,0:T(8,128)(2,1)}, u32[]{:S(2)}) copy-start(bf16[1,1,128,1024]{3,2,1,0:T(8,128)(2,1)} %param.9) | copy-start | bytes 786436
  5.7 21.1 %all-to-all-start.1 = ((bf16[16,2,4096]{2,1,0:T(2,128)(2,1)}), bf16[16,2,4096]{2,1,0:T(2,128)(2,1)S(1)}, u32[]{:S(2)}, u32[]{:S(2)}) async-start(bf16[16,2,4096]{2,1,0:T(2,128)(2,1)} %reshape.351), calls=%async_computation.1 | async-start | bytes 524288 | tf_op jit(solution)/shard_map/all_to_all | solution.py:208
  14.2 5.3 %copy-start.8 = (bf16[1,1,128,1024]{2,3,1,0:T(8,128)(2,1)}, bf16[1,1,128,1024]{2,3,1,0:T(8,128)(2,1)S(1)}, u32[]{:S(2)}) copy-start(bf16[1,1,128,1024]{2,3,1,0:T(8,128)(2,1)S(1)} %copy.158) | copy-start | bytes 786436
  15.5 4.1 %copy-start.6 = (bf16[1,1,128,1024]{2,3,1,0:T(8,128)(2,1)}, bf16[1,1,128,1024]{2,3,1,0:T(8,128)(2,1)S(1)}, u32[]{:S(2)}) copy-start(bf16[1,1,128,1024]{2,3,1,0:T(8,128)(2,1)S(1)} %copy.157) | copy-start | bytes 786436
  16.6 3.5 %copy-start.4 = (f32[8,128,128]{1,2,0:T(8,128)}, f32[8,128,128]{1,2,0:T(8,128)S(1)}, u32[]{:S(2)}) copy-start(f32[8,128,128]{1,2,0:T(8,128)S(1)} %fusion.21) | copy-start | bytes 1572868
  19.6 13.1 %collective-permute-start.2 = (bf16[128,1024]{0,1:T(8,128)(2,1)}, bf16[128,1024]{0,1:T(8,128)(2,1)}, u32[]{:S(2)}, u32[]{:S(2)}) collective-permute-start(bf16[128,1024]{0,1:T(8,128)(2,1)} %bitcast.3), channel_id=1, source_target_pairs={{0,1},{1,0},{2,3},{3,2},{4,5},{5,4},{6,7},{7,6},{8,9},{9,8},{10,11... | collective-permute-start | bytes 786440 | tf_op jit(solution)/shard_map/ppermute | solution.py:254
  26.8 16.0 %all-to-all-start = ((bf16[16,2,4096]{2,1,0:T(2,128)(2,1)}), bf16[16,2,4096]{2,1,0:T(2,128)(2,1)}, u32[]{:S(2)}, u32[]{:S(2)}) async-start(bf16[16,2,4096]{2,1,0:T(2,128)(2,1)} %reshape.349), calls=%async_computation | async-start | bytes 524288 | tf_op jit(solution)/shard_map/all_to_all | solution.py:191
  50.6 6.7 %copy-start.11 = (bf16[1,16,8,1,8,128]{5,2,4,3,1,0:T(8,128)(2,1)}, bf16[1,16,8,1,8,128]{5,2,4,3,1,0:T(8,128)(2,1)S(1)}, u32[]{:S(2)}) copy-start(bf16[1,16,8,1,8,128]{5,2,4,3,1,0:T(8,128)(2,1)S(1)} %get-tuple-element.59) | copy-start | bytes 786436
  61.5 15.3 %collective-permute-start = (bf16[128,1024]{0,1:T(8,128)(2,1)}, bf16[128,1024]{0,1:T(8,128)(2,1)}, u32[]{:S(2)}, u32[]{:S(2)}) collective-permute-start(bf16[128,1024]{0,1:T(8,128)(2,1)} %bitcast.5), channel_id=1, source_target_pairs={{0,1},{1,0},{2,3},{3,2},{4,5},{5,4},{6,7},{7,6},{8,9},{9,8},{10,11... | collective-permute-start | bytes 786440 | tf_op jit(solution)/shard_map/ppermute | solution.py:232
  64.2 13.8 %collective-permute-start.1 = (bf16[128,3072]{1,0:T(8,128)(2,1)S(1)}, bf16[128,3072]{1,0:T(8,128)(2,1)}, u32[]{:S(2)}, u32[]{:S(2)}) collective-permute-start(bf16[128,3072]{1,0:T(8,128)(2,1)S(1)} %reshape_reshape.7), channel_id=1, source_target_pairs={{0,1},{1,0},{2,3},{3,2},{4,5},{5,4},{6,7},{7,6},{8,9},{9,8},{10,11... | collective-permute-start | bytes 2359304 | tf_op jit(solution)/shard_map/ppermute | solution.py:232
  70.4 14.2 %all-to-all-start.2 = ((bf16[1,16,8,1024]{3,2,0,1:T(8,128)(2,1)}), bf16[1,16,8,1024]{3,2,0,1:T(8,128)(2,1)}, u32[]{:S(2)}, u32[]{:S(2)}) async-start(bf16[1,16,8,1024]{3,2,0,1:T(8,128)(2,1)} %fusion.29), calls=%async_computation.2 | async-start | bytes 524288 | tf_op jit(solution)/shard_map/all_to_all | solution.py:238
  80.1 2.7 %copy-start.1 = (f32[512,3072]{1,0:T(8,128)}, f32[512,3072]{1,0:T(8,128)S(1)}, u32[]{:S(2)}) copy-start(f32[512,3072]{1,0:T(8,128)S(1)} %fusion.5) | copy-start | bytes 18874372
  84.7 5.1 %copy-start.13 = (bf16[1,16,8,8,128]{4,1,3,2,0:T(8,128)(2,1)S(1)}, bf16[1,16,8,8,128]{4,1,3,2,0:T(8,128)(2,1)}, u32[]{:S(2)}) copy-start(bf16[1,16,8,8,128]{4,1,3,2,0:T(8,128)(2,1)} %fusion.26) | copy-start | bytes 786436
  85.9 25.7 %collective-permute-start.5 = (bf16[2,2,2,32,3072]{4,3,2,1,0:T(8,128)(2,1)}, bf16[2,2,2,32,3072]{4,3,2,1,0:T(8,128)(2,1)}, u32[]{:S(2)}, u32[]{:S(2)}) collective-permute-start(bf16[2,2,2,32,3072]{4,3,2,1,0:T(8,128)(2,1)} %fusion.4), channel_id=1, source_target_pairs={{0,2},{1,17},{2,0},{3,19},{4,6},{5,21},{6,4},{7,23},{8,10},{9,25},... | collective-permute-start | bytes 4718600 | tf_op jit(solution)/shard_map/ppermute | solution.py:159
  88.3 8.8 %copy-start.5 = (bf16[256,2,2,2,2,2,32]{0,6,5,4,3,2,1:T(8,128)(2,1)S(1)}, bf16[256,2,2,2,2,2,32]{0,6,5,4,3,2,1:T(8,128)(2,1)}, u32[]{:S(2)}) copy-start(bf16[256,2,2,2,2,2,32]{0,6,5,4,3,2,1:T(8,128)(2,1)} %copy.137) | copy-start | bytes 1572868
  88.4 8.3 %collective-permute-start.4 = (f32[1024]{0:T(1024)S(1)}, f32[1024]{0:T(1024)S(1)}, u32[]{:S(2)}, u32[]{:S(2)}) collective-permute-start(f32[1024]{0:T(1024)S(1)} %get-tuple-element.47), channel_id=1, source_target_pairs={{0,1},{1,0},{2,3},{3,2},{4,5},{5,4},{6,7},{7,6},{8,9},{9,8},{10,11... | collective-permute-start | bytes 12296 | tf_op jit(solution)/shard_map/ppermute | solution.py:254
  88.4 8.7 %collective-permute-start.3 = (bf16[128,1024]{1,0:T(8,128)(2,1)S(1)}, bf16[128,1024]{1,0:T(8,128)(2,1)}, u32[]{:S(2)}, u32[]{:S(2)}) collective-permute-start(bf16[128,1024]{1,0:T(8,128)(2,1)S(1)} %fusion.50), channel_id=1, source_target_pairs={{0,1},{1,0},{2,3},{3,2},{4,5},{5,4},{6,7},{7,6},{8,9},{9,8},{10,11... | collective-permute-start | bytes 786440 | tf_op jit(solution)/shard_map/ppermute | solution.py:254
  90.7 18.5 %all-to-all-start.3 = ((bf16[1,16,8,1024]{3,2,0,1:T(8,128)(2,1)}), bf16[1,16,8,1024]{3,2,0,1:T(8,128)(2,1)S(1)}, u32[]{:S(2)}, u32[]{:S(2)}) async-start(bf16[1,16,8,1024]{3,2,0,1:T(8,128)(2,1)} %bitcast.222), calls=%async_computation.3 | async-start | bytes 524288 | tf_op jit(solution)/shard_map/all_to_all | solution.py:262
  98.5 12.0 %copy-start.9 = (bf16[16,8,8,128]{3,2,1,0:T(8,128)(2,1)S(1)}, bf16[16,8,8,128]{3,2,1,0:T(8,128)(2,1)}, u32[]{:S(2)}) copy-start(bf16[16,8,8,128]{3,2,1,0:T(8,128)(2,1)} %copy.160) | copy-start | bytes 786436
  98.6 12.0 %copy-start.10 = (bf16[128,1024]{0,1:T(8,128)(2,1)S(1)}, bf16[128,1024]{0,1:T(8,128)(2,1)}, u32[]{:S(2)}) copy-start(bf16[128,1024]{0,1:T(8,128)(2,1)} %copy.159) | copy-start | bytes 786436
  109.2 16.4 %collective-permute-start.10 = (bf16[2,2,2,32,1025]{4,3,2,1,0:T(8,128)(2,1)}, bf16[2,2,2,32,1025]{4,3,2,1,0:T(8,128)(2,1)S(1)}, u32[]{:S(2)}, u32[]{:S(2)}) collective-permute-start(bf16[2,2,2,32,1025]{4,3,2,1,0:T(8,128)(2,1)} %fusion.41), channel_id=1, source_target_pairs={{0,4},{1,5},{2,6},{3,7},{4,0},{5,1},{6,2},{7,3},{8,12},{9,13},{10,... | collective-permute-start | bytes 1574408 | tf_op jit(solution)/shard_map/ppermute | solution.py:159
  111.5 14.0 %copy-start.3 = (f32[512,1024]{1,0:T(8,128)S(1)}, f32[512,1024]{1,0:T(8,128)}, u32[]{:S(2)}) copy-start(f32[512,1024]{1,0:T(8,128)} %copy-done.2) | copy-start | bytes 6291460
  115.8 24.3 %collective-permute-start.6 = (bf16[2,2,32,3072]{3,2,1,0:T(8,128)(2,1)}, bf16[2,2,32,3072]{3,2,1,0:T(8,128)(2,1)}, u32[]{:S(2)}, u32[]{:S(2)}) collective-permute-start(bf16[2,2,32,3072]{3,2,1,0:T(8,128)(2,1)} %get-tuple-element.49), channel_id=1, source_target_pairs={{0,16},{1,5},{2,18},{3,7},{4,20},{5,1},{6,22},{7,3},{8,24},{9,13},... | collective-permute-start | bytes 2359304 | tf_op jit(solution)/shard_map/ppermute | solution.py:159
  126.4 6.1 %copy-start.7 = (bf16[1,1,128,1024]{2,3,1,0:T(8,128)(2,1)S(1)}, bf16[1,1,128,1024]{2,3,1,0:T(8,128)(2,1)}, u32[]{:S(2)}) copy-start(bf16[1,1,128,1024]{2,3,1,0:T(8,128)(2,1)} %copy-done.6) | copy-start | bytes 786436
  126.4 10.5 %collective-permute-start.11 = (bf16[2,2,32,1025]{3,2,1,0:T(8,128)(2,1)}, bf16[2,2,32,1025]{3,2,1,0:T(8,128)(2,1)}, u32[]{:S(2)}, u32[]{:S(2)}) collective-permute-start(bf16[2,2,32,1025]{3,2,1,0:T(8,128)(2,1)} %get-tuple-element.51), channel_id=1, source_target_pairs={{0,2},{1,17},{2,0},{3,19},{4,6},{5,21},{6,4},{7,23},{8,10},{9,25},... | collective-permute-start | bytes 787208 | tf_op jit(solution)/shard_map/ppermute | solution.py:159
  138.6 9.6 %collective-permute-start.12 = (bf16[2,32,1025]{2,1,0:T(8,128)(2,1)}, bf16[2,32,1025]{2,1,0:T(8,128)(2,1)}, u32[]{:S(2)}, u32[]{:S(2)}) collective-permute-start(bf16[2,32,1025]{2,1,0:T(8,128)(2,1)} %get-tuple-element.55), channel_id=1, source_target_pairs={{0,16},{1,3},{2,18},{3,1},{4,20},{5,7},{6,22},{7,5},{8,24},{9,11},... | collective-permute-start | bytes 393608 | tf_op jit(solution)/shard_map/ppermute | solution.py:159
  142.6 9.0 %collective-permute-start.7 = (bf16[2,32,3072]{2,1,0:T(8,128)(2,1)}, bf16[2,32,3072]{2,1,0:T(8,128)(2,1)}, u32[]{:S(2)}, u32[]{:S(2)}) collective-permute-start(bf16[2,32,3072]{2,1,0:T(8,128)(2,1)} %get-tuple-element.53), channel_id=1, source_target_pairs={{0,4},{1,3},{2,6},{3,1},{4,0},{5,7},{6,2},{7,5},{8,12},{9,11},{10,... | collective-permute-start | bytes 1179656 | tf_op jit(solution)/shard_map/ppermute | solution.py:159
  149.1 8.8 %collective-permute-start.13 = (bf16[32,1025]{1,0:T(8,128)(2,1)S(1)}, bf16[32,1025]{1,0:T(8,128)(2,1)S(1)}, u32[]{:S(2)}, u32[]{:S(2)}) collective-permute-start(bf16[32,1025]{1,0:T(8,128)(2,1)S(1)} %fusion.81), channel_id=1, source_target_pairs={{0,8},{1,9},{2,10},{3,11},{4,12},{5,13},{6,14},{7,15},{8,0},{9,1},... | collective-permute-start | bytes 196808 | tf_op jit(solution)/shard_map/ppermute | solution.py:159
  152.6 9.9 %collective-permute-start.8 = (bf16[32,3072]{1,0:T(8,128)(2,1)S(1)}, bf16[32,3072]{1,0:T(8,128)(2,1)S(1)}, u32[]{:S(2)}, u32[]{:S(2)}) collective-permute-start(bf16[32,3072]{1,0:T(8,128)(2,1)S(1)} %fusion.73), channel_id=1, source_target_pairs={{0,8},{1,9},{2,10},{3,11},{4,12},{5,13},{6,14},{7,15},{8,0},{9,1},... | collective-permute-start | bytes 589832 | tf_op jit(solution)/shard_map/ppermute | solution.py:159
  158.9 5.2 %collective-permute-start.14 = (bf16[32,1025]{1,0:T(8,128)(2,1)S(1)}, bf16[32,1025]{1,0:T(8,128)(2,1)S(1)}, u32[]{:S(2)}, u32[]{:S(2)}) collective-permute-start(bf16[32,1025]{1,0:T(8,128)(2,1)S(1)} %fusion.76), channel_id=1, source_target_pairs={{0,16},{16,0},{1,17},{17,1},{2,18},{18,2},{3,19},{19,3},{4,20},{20... | collective-permute-start | bytes 196808 | tf_op jit(solution)/shard_map/ppermute | solution.py:166
  163.4 5.7 %collective-permute-start.9 = (bf16[32,3072]{1,0:T(8,128)(2,1)S(1)}, bf16[32,3072]{1,0:T(8,128)(2,1)S(1)}, u32[]{:S(2)}, u32[]{:S(2)}) collective-permute-start(bf16[32,3072]{1,0:T(8,128)(2,1)S(1)} %fusion.60), channel_id=1, source_target_pairs={{0,16},{16,0},{1,17},{17,1},{2,18},{18,2},{3,19},{19,3},{4,20},{20... | collective-permute-start | bytes 589832 | tf_op jit(solution)/shard_map/ppermute | solution.py:166
  (4 other events, 6.4 us)

commit v14 on v7

--- a/solution.py
+++ b/solution.py
@@ -73,6 +73,18 @@
         grad_value.astype(jnp.bfloat16),
     )
 
+
+def to_cols(rows_block):
+    b, one, c, f = rows_block.shape
+    n = lax.axis_size("seq")
+    grouped = rows_block.reshape(b, n, c // n, f)
+    return lax.all_to_all(grouped, "seq", split_axis=1, concat_axis=1, tiled=True)
+
+
+def to_rows(cols_block):
+    b, n, share, f = cols_block.shape
+    gathered = lax.all_to_all(cols_block, "seq", split_axis=1, concat_axis=1, tiled=True)
+    return gathered.reshape(b, 1, n * share, f)
 
 def split_orders(seq_n, dp_n, z_first=False):
     bits = seq_n.bit_length() - 1
@@ -181,13 +193,7 @@
     hidden = jnp.dot(flat_first, out_weight, preferred_element_type=jnp.float32)
     inverse = lax.rsqrt(jnp.mean(hidden * hidden, axis=-1, keepdims=True) + epsilon)
     normed = (hidden * inverse * norm_gain).astype(jnp.bfloat16)
-    normed_cols = lax.all_to_all(
-        normed.reshape(batches, local_rows, columns, model_width),
-        "seq",
-        split_axis=2,
-        concat_axis=1,
-        tiled=True,
-    )
+    normed_cols = to_cols(normed.reshape(batches, local_rows, columns, model_width))
     joint_flat = jnp.dot(
         normed_cols.reshape(-1, model_width), joint_weight, preferred_element_type=jnp.float32
     )
@@ -198,7 +204,7 @@
     pieces = joint_cols.reshape(batches, all_rows, col_share, 3, head_count, HEAD_DIM)
     query_cols, key_cols, value_cols = (pieces[:, :, :, 0], pieces[:, :, :, 1], pieces[:, :, :, 2])
     out_cols, probs_cols = attend(query_cols, key_cols, value_cols, "blche", "bchlm")
-    upstream_cols = lax.all_to_all(upstream, "seq", split_axis=2, concat_axis=1, tiled=True)
+    upstream_cols = to_cols(upstream)
     upstream_cols = upstream_cols.reshape(batches, all_rows, col_share, head_count, HEAD_DIM)
     grads_cols = attend_back(
         query_cols, key_cols, value_cols, probs_cols, upstream_cols, "blche", "bchlm"
@@ -228,13 +234,7 @@
         jnp.concatenate([used_grads, grads_peer], axis=0),
         preferred_element_type=jnp.float32,
     )
-    grad_normed = lax.all_to_all(
-        grad_local.reshape(batches, all_rows, col_share, model_width),
-        "seq",
-        split_axis=1,
-        concat_axis=2,
-        tiled=True,
-    )
+    grad_normed = to_rows(grad_local.reshape(batches, all_rows, col_share, model_width))
     grad_normed = grad_normed.reshape(-1, model_width)
     (joint_sum,), grad_normed = reduce_rows((joint_term,), (orders,), seq_n, dp_n, grad_normed)
     grad_float = grad_normed.astype(jnp.float32)
@@ -254,13 +254,7 @@
     (out_sum,), out_cols = reduce_rows(
         (jnp.concatenate([out_term, gain_term], axis=1),), (out_orders,), seq_n, dp_n, out_cols
     )
-    column_out = lax.all_to_all(
-        out_cols.reshape(batches, all_rows, col_share, feature),
-        "seq",
-        split_axis=1,
-        concat_axis=2,
-        tiled=True,
-    )
+    column_out = to_rows(out_cols.reshape(batches, all_rows, col_share, feature))
     replicas = (joint_sum, out_sum[:, :out_width], out_sum[:, out_width].astype(jnp.float32))
     grad_first = jnp.dot(grad_hidden, out_weight.T, preferred_element_type=jnp.float32).astype(
         jnp.bfloat16

time: 162 us -> 185 us (1.14)
  local copies, waits for them, and re-layouts: 35.3 us -> 55.8 us
  other arithmetic: 21.7 us -> 30.4 us
  waiting for transfers between devices: 26.8 us -> 18.9 us
  starting transfers between devices: 36.5 us -> 39.7 us
  matrix products: 39.6 us -> 37 us
    concatenate x0 -> x4, local copies, waits for them, and re-layouts: none -> 14.9 us  [the longest x2 7.79 us: on_device(): jnp.concatenate([flat_first, first_peer], axis=0)]
    select_n x4, local copies, waits for them, and re-layouts: 0.98 us -> 11.4 us  [by_split_order(): return jnp.where(core_odd, arrange(odd), arrange(even))]
    select_n x3, other arithmetic: 0.11 us -> 9.47 us  [by_split_order(): return jnp.where(core_odd, arrange(odd), arrange(even))]
    all_to_all x4, waiting for transfers between devices: 6.41 us -> 0.01 us  [the longest x2 0.01 us: to_rows(): lax.all_to_all(cols_block, 'seq', split_axis=1, concat_axis=1, tiled=True)]
    unnamed x2 -> x0, other arithmetic: 5 us -> none
    unnamed x54 -> x44, local copies, waits for them, and re-layouts: 20.7 us -> 15.9 us
    concatenate x1, other arithmetic: 1.11 us -> 4.78 us  [on_device(): jnp.concatenate([used_normed, normed_peer], axis=0)]
    all_to_all x2 -> x0, local copies, waits for them, and re-layouts: 2.54 us -> none  [the longest x1 1.48 us: on_device(): lax.all_to_all(upstream, 'seq', split_axis=2, concat_axis=1, tiled=True)]
  transfers between devices with their start and end apart: 19 -> 19, of which waited for: 7 -> 5; matrix products, arithmetic and copies ran while one was open for 39% -> 53% of each run, Pallas kernels for 0% -> 0%
where the time goes in v14:
time: 185 us; the launch traced here: 183 us
  local copies, waits for them, and re-layouts  55.8 us (30%)
  starting transfers between devices  39.7 us (21%)
  matrix products  37 us (20%)
  other arithmetic  30.4 us (16%)
  waiting for transfers between devices  18.9 us (10%)
    unnamed x44, local copies, waits for them, and re-layouts  15.9 us
    ppermute x8, waiting for transfers between devices, reduce_rows(): lax.ppermute(given, ('dp', 'seq'), perm).astype(jnp.float32)  15.4 us
    all_to_all x2, starting transfers between devices, to_cols(): lax.all_to_all(grouped, 'seq', split_axis=1, concat_axis=1, tiled=True)  13.3 us
    ppermute x8, starting transfers between devices, reduce_rows(): lax.ppermute(given, ('dp', 'seq'), perm).astype(jnp.float32)  13 us
    select_n x4, local copies, waits for them, and re-layouts, by_split_order(): return jnp.where(core_odd, arrange(odd), arrange(even))  11.4 us
    all_to_all x2, starting transfers between devices, to_rows(): lax.all_to_all(cols_block, 'seq', split_axis=1, concat_axis=1, tiled=True)  10.2 us
    select_n x3, other arithmetic, by_split_order(): return jnp.where(core_odd, arrange(odd), arrange(even))  9.47 us
    concatenate x2, local copies, waits for them, and re-layouts, on_device(): jnp.concatenate([flat_first, first_peer], axis=0)  7.79 us
  transfers between devices with their start and end apart: 19, of which 5 were waited for; matrix products, arithmetic and copies ran while one was open for 53% of the time, Pallas kernels for 0%

profile of v14, /device:TPU:0, one launch (start us, length us, event | category | flops | bytes accessed | tf_op | source)
XLA Modules:
  0.0 183.0 jit_solution(1637880204096731204)
XLA Ops:
  0.6 7.5 %all-to-all-start.1 = ((bf16[1,16,8,1024]{3,2,0,1:T(8,128)(2,1)}), bf16[1,16,8,1024]{3,2,0,1:T(8,128)(2,1)S(1)}, u32[]{:S(2)}, u32[]{:S(2)}) async-start(bf16[1,16,8,1024]{3,2,0,1:T(8,128)(2,1)} %bitcast.202), calls=%async_computation.1 | async-start | bytes 524288 | tf_op jit(solution)/shard_map/all_to_all | solution.py:81
  18.9 3.9 %copy.167 = bf16[256,2,2,2,2,2,32]{6,3,4,2,5,1,0:T(2,128)(2,1)} copy(bf16[256,2,2,2,2,2,32]{0,6,5,4,3,2,1:T(8,128)(2,1)S(1)} %pad_maximum_fusion.2) | data formatting | bytes 1048576 | tf_op jit(solution)/shard_map/concatenate | solution.py:248
  22.8 3.9 %copy.166 = bf16[256,2,2,2,2,2,32]{6,5,4,2,3,1,0:T(2,128)(2,1)} copy(bf16[256,2,2,2,2,2,32]{0,6,5,4,3,2,1:T(8,128)(2,1)S(1)} %pad_maximum_fusion.2) | data formatting | bytes 1048576 | tf_op jit(solution)/shard_map/concatenate | solution.py:248
  26.7 5.8 %all-to-all-start = ((bf16[1,16,8,1024]{3,2,0,1:T(8,128)(2,1)}), bf16[1,16,8,1024]{3,2,0,1:T(8,128)(2,1)}, u32[]{:S(2)}, u32[]{:S(2)}) async-start(bf16[1,16,8,1024]{3,2,0,1:T(8,128)(2,1)} %fusion.57), calls=%async_computation | async-start | bytes 524288 | tf_op jit(solution)/shard_map/all_to_all | solution.py:81
  32.5 5.7 %broadcast_select_fusion = bf16[256,2,2,2,2,2,32]{6,3,1,2,4,5,0:T(2,128)(2,1)} fusion(pred[]{:T(512)S(6)} %eq.44, bf16[256,2,2,2,2,2,32]{6,3,4,2,5,1,0:T(2,128)(2,1)} %copy.167, bf16[256,2,2,2,2,2,32]{6,5,4,2,3,1,0:T(2,128)(2,1)} %copy.166), kind=kLoop, calls=%fused_computation.4 | loop fusion | flops 262144 | bytes 1572865 | tf_op jit(solution)/shard_map/jit(_where)/select_n | solution.py:124
  38.2 5.7 %copy.168 = bf16[256,2,2,2,2,2,32]{0,6,5,4,3,2,1:T(8,128)(2,1)} copy(bf16[256,2,2,2,2,2,32]{6,3,1,2,4,5,0:T(2,128)(2,1)} %broadcast_select_fusion) | data formatting | bytes 1048576 | tf_op jit(solution)/shard_map/jit(_where)/select_n | solution.py:124
  43.9 3.9 %convolution_convert_fusion = bf16[128,3072]{1,0:T(8,128)(2,1)S(1)} fusion(bf16[1024,3072]{1,0:T(8,128)(2,1)} %param.12, bf16[1,16,8,1024]{3,2,0,1:T(8,128)(2,1)} %all-to-all-done), kind=kOutput, calls=%fused_computation.6 | convolution fusion | flops 805699584 | bytes 7340032 | tf_op jit(solution)/shard_map/dot_general | solution.py:197
  49.9 2.6 %fusion.93 = (f32[8,8,16]{2,1,0:T(8,128)S(1)}, f32[8,8,16,16]{2,3,1,0:T(8,128)}) fusion(pred[16,16]{0,1:T(8,128)(4,1)S(1)} %iota_compare_fusion.1, bf16[1,16,8,1,8,128]{5,2,4,3,1,0:T(8,128)(2,1)} %get-tuple-element.54, bf16[1,16,8,1,8,128]{5,2,4,3,1,0:T(8,128)(2,1)} %get-tuple-element.53), kind=kOutput, calls=%fused_computation.148 | convolution fusion | flops 4259855 | bytes 594176 | tf_op jit(solution)/shard_map/sub | solution.py:28
  52.5 2.1 %fusion.29 = bf16[1,16,8,1,8,128]{5,1,4,2,3,0:T(8,128)(2,1)} fusion(bf16[16,8,8,128]{3,2,1,0:T(8,128)(2,1)S(1)} %copy.216, f32[8,8,16,16]{2,3,1,0:T(8,128)} %get-tuple-element.62, f32[8,8,16]{2,1,0:T(8,128)S(1)} %get-tuple-element.61), kind=kOutput, calls=%fused_computation.54 | convolution fusion | flops 4358144 | bytes 593920 | tf_op jit(solution)/shard_map/bchlm,blche->bmche/dot_general | solution.py:64
  54.6 2.5 %fusion.32 = bf16[1,16,8,1,8,128]{5,1,4,2,3,0:T(8,128)(2,1)} fusion(f32[8,8,16,16]{2,3,1,0:T(8,128)S(1)} %convolution_bitcast_fusion, bf16[1,16,8,1,8,128]{5,2,4,3,1,0:T(8,128)(2,1)} %get-tuple-element.53, f32[8,8,16,16]{2,3,1,0:T(8,128)} %get-tuple-element.62, f32[8,8,16]{2,1,0:T(8,128)S(1)} %get-tuple-element.61), kind=kOutput, calls=%fused_computation.57 | convolution fusion | flops 4441103 | bytes 659456 | tf_op jit(solution)/shard_map/bchlm,blche->bmche/dot_general | solution.py:57
  57.1 2.4 %fusion.28 = bf16[1,16,8,1,8,128]{5,1,4,2,3,0:T(8,128)(2,1)} fusion(f32[8,8,16,16]{2,3,1,0:T(8,128)S(1)} %convolution_bitcast_fusion, bf16[1,16,8,1,8,128]{5,2,4,3,1,0:T(8,128)(2,1)S(1)} %copy-done.17, f32[8,8,16,16]{2,3,1,0:T(8,128)} %get-tuple-element.62, f32[8,8,16]{2,1,0:T(8,128)S(1)} %get-tuple-element.61), kind=kOutput, calls=%fused_computation.53 | convolution fusion | flops 4441103 | bytes 659456 | tf_op jit(solution)/shard_map/bchlm,bmche->blche/dot_general | solution.py:51
  63.5 5.7 %fusion.30 = bf16[1,16,8,1024]{3,2,0,1:T(8,128)(2,1)} fusion(bf16[128,3072]{1,0:T(8,128)(2,1)S(1)} %reshape_reshape.14, bf16[1024,3072]{1,0:T(8,128)(2,1)} %param.12), kind=kOutput, calls=%fused_computation.55 | convolution fusion | flops 805437440 | bytes 7340032 | tf_op jit(solution)/shard_map/dot_general | solution.py:215
  69.4 6.0 %all-to-all-start.2 = ((bf16[1,16,8,1024]{3,2,0,1:T(8,128)(2,1)}), bf16[1,16,8,1024]{3,2,0,1:T(8,128)(2,1)}, u32[]{:S(2)}, u32[]{:S(2)}) async-start(bf16[1,16,8,1024]{3,2,0,1:T(8,128)(2,1)} %fusion.30), calls=%async_computation.2 | async-start | bytes 524288 | tf_op jit(solution)/shard_map/all_to_all | solution.py:86
  75.4 3.7 %concatenate.42 = bf16[128,2,2,2,2,2,32]{6,5,4,3,2,1,0:T(2,128)(2,1)} reshape(bf16[1,16,8,1024]{3,2,0,1:T(8,128)(2,1)} %all-to-all-done) | data formatting | bytes 524288 | tf_op jit(solution)/shard_map/concatenate | solution.py:233
  79.1 2.2 %fusion.31 = bf16[1,16,8,8,128]{4,1,3,2,0:T(8,128)(2,1)} fusion(bf16[1,16,8,1,8,128]{5,2,4,3,1,0:T(8,128)(2,1)} %copy-done.14, f32[8,8,16,16]{2,3,1,0:T(8,128)} %get-tuple-element.62, f32[8,8,16]{2,1,0:T(8,128)S(1)} %get-tuple-element.61), kind=kOutput, calls=%fused_computation.56 | convolution fusion | flops 4358144 | bytes 593920 | tf_op jit(solution)/shard_map/bchlm,bmche->blche/dot_general | solution.py:31
  83.0 3.5 %copy.147 = bf16[128,2,2,2,2,2,32]{6,5,4,3,2,1,0:T(2,128)(2,1)} copy(bf16[128,2,2,2,2,2,32]{0,6,5,4,3,2,1:T(8,128)(2,1)} %bitcast.188) | data formatting | bytes 524288 | tf_op jit(solution)/shard_map/concatenate | solution.py:233
  86.5 4.8 %pad_maximum_fusion = bf16[256,2,2,2,2,2,32]{6,5,4,3,2,1,0:T(2,128)(2,1)S(1)} fusion(bf16[128,2,2,2,2,2,32]{6,5,4,3,2,1,0:T(2,128)(2,1)} %copy.147, bf16[128,2,2,2,2,2,32]{6,5,4,3,2,1,0:T(2,128)(2,1)} %concatenate.42), kind=kLoop, calls=%fused_computation.13 | loop fusion | flops 262144 | bytes 1048576 | tf_op jit(solution)/shard_map/concatenate | solution.py:233
  91.3 3.8 %broadcast_select_fusion.1 = bf16[256,2,2,2,2,2,32]{6,3,1,2,4,5,0:T(2,128)(2,1)} fusion(pred[]{:T(512)S(6)} %eq.44, bf16[256,2,2,2,2,2,32]{6,5,4,3,2,1,0:T(2,128)(2,1)S(1)} %pad_maximum_fusion), kind=kLoop, calls=%fused_computation.5 | loop fusion | flops 262144 | bytes 1048577 | tf_op jit(solution)/shard_map/jit(_where)/select_n | solution.py:124
  95.0 5.7 %copy.149 = bf16[256,2,2,2,2,2,32]{0,6,5,4,3,2,1:T(8,128)(2,1)} copy(bf16[256,2,2,2,2,2,32]{6,3,1,2,4,5,0:T(2,128)(2,1)} %broadcast_select_fusion.1) | data formatting | bytes 1048576 | tf_op jit(solution)/shard_map/jit(_where)/select_n | solution.py:124
  100.7 2.2 %fusion.5 = f32[512,3072]{1,0:T(8,128)S(1)} fusion(bf16[128,3072]{1,0:T(8,128)(2,1)} %collective-permute-done.1, bf16[128,3072]{1,0:T(8,128)(2,1)S(1)} %reshape_reshape.14, bf16[256,1024]{0,1:T(8,128)(2,1)} %bitcast.187, s32[]{:T(128)S(6)} %select_n.231), kind=kOutput, calls=%fused_computation.15 | convolution fusion | flops 808452096 | bytes 8126468 | tf_op jit(solution)/shard_map/dot_general | solution.py:232
  102.9 2.6 %copy-done.1 = f32[512,3072]{1,0:T(8,128)} copy-done((f32[512,3072]{1,0:T(8,128)}, f32[512,3072]{1,0:T(8,128)S(1)}, u32[]{:S(2)}) %copy-start.1) | copy-done | bytes 6291480
  120.1 2.7 %convolution_convert_fusion.1 = bf16[8,128,128]{1,2,0:T(8,128)(2,1)} fusion(bf16[128,8,128]{0,2,1:T(8,128)(2,1)S(1)} %bitcast.196, f32[8,128,128]{1,2,0:T(8,128)} %fusion.65, f32[8,128,128]{1,2,0:T(8,128)} %get-tuple-element.58, f32[8,128]{1,0:T(8,128)S(1)} %get-tuple-element.57), kind=kOutput, calls=%fused_computation.38 | convolution fusion | flops 34604160 | bytes 1576960 | tf_op jit(solution)/shard_map/ghlm,gmhe->glhe/dot_general | solution.py:51
  122.8 2.7 %convolution_convert_fusion.6 = bf16[8,128,128]{1,2,0:T(8,128)(2,1)} fusion(bf16[128,8,128]{0,2,1:T(8,128)(2,1)S(1)} %bitcast.194, f32[8,128,128]{1,2,0:T(8,128)} %fusion.65, f32[8,128,128]{1,2,0:T(8,128)} %get-tuple-element.58, f32[8,128]{1,0:T(8,128)S(1)} %get-tuple-element.57), kind=kOutput, calls=%fused_computation.43 | convolution fusion | flops 34604160 | bytes 1576960 | tf_op jit(solution)/shard_map/ghlm,glhe->gmhe/dot_general | solution.py:57
  126.3 4.2 %all-to-all-start.3 = ((bf16[1,16,8,1024]{3,2,0,1:T(8,128)(2,1)}), bf16[1,16,8,1024]{3,2,0,1:T(8,128)(2,1)}, u32[]{:S(2)}, u32[]{:S(2)}) async-start(bf16[1,16,8,1024]{3,2,0,1:T(8,128)(2,1)} %bitcast.57), calls=%async_computation.3 | async-start | bytes 524288 | tf_op jit(solution)/shard_map/all_to_all | solution.py:86
  130.5 2.3 %collective-permute-done.10 = bf16[2,2,2,32,1025]{4,3,2,1,0:T(8,128)(2,1)} collective-permute-done((bf16[2,2,2,32,1025]{4,3,2,1,0:T(8,128)(2,1)}, bf16[2,2,2,32,1025]{4,3,2,1,0:T(8,128)(2,1)}, u32[]{:S(2)}, u32[]{:S(2)}) %collective-permute-start.10) | collective-permute-done | bytes 524832 | tf_op jit(solution)/shard_map/ppermute | solution.py:165
  136.3 2.8 %bitcast_add_fusion = f32[2,2,2,32,3072]{4,3,2,1,0:T(8,128)S(1)} fusion(bf16[2,2,2,32,3072]{4,3,2,1,0:T(8,128)(2,1)} %collective-permute-done.5, f32[2,2,2,2,32,3072]{5,4,3,2,1,0:T(8,128)} %bitcast.182, s32[]{:T(128)S(6)} %select_n.247), kind=kLoop, calls=%fused_computation.9 | loop fusion | flops 1572864 | bytes 7864324 | tf_op jit(solution)/shard_map/add | solution.py:165
  142.8 2.3 %convolution_convert_fusion.5 = bf16[8,128,128]{2,1,0:T(8,128)(2,1)} fusion(bf16[128,8,128]{0,2,1:T(8,128)(2,1)S(1)} %bitcast.200, f32[8,128]{1,0:T(8,128)S(1)} %get-tuple-element.57, f32[8,128,128]{1,2,0:T(8,128)} %copy-done.4), kind=kOutput, calls=%fused_computation.42 | convolution fusion | flops 34079872 | bytes 1052672 | tf_op jit(solution)/shard_map/ghlm,glhe->gmhe/dot_general | solution.py:64
  156.0 2.1 %collective-permute-start.7 = (bf16[2,32,3072]{2,1,0:T(8,128)(2,1)S(1)}, bf16[2,32,3072]{2,1,0:T(8,128)(2,1)S(1)}, u32[]{:S(2)}, u32[]{:S(2)}) collective-permute-start(bf16[2,32,3072]{2,1,0:T(8,128)(2,1)S(1)} %fusion.54), channel_id=1, source_target_pairs={{0,4},{1,3},{2,6},{3,1},{4,0},{5,7},{6,2},{7,5},{8,12},{9,11},{10,... | collective-permute-start | bytes 1179656 | tf_op jit(solution)/shard_map/ppermute | solution.py:165
  158.2 2.8 %collective-permute-start.13 = (bf16[32,1025]{1,0:T(8,128)(2,1)S(1)}, bf16[32,1025]{1,0:T(8,128)(2,1)S(1)}, u32[]{:S(2)}, u32[]{:S(2)}) collective-permute-start(bf16[32,1025]{1,0:T(8,128)(2,1)S(1)} %fusion.76), channel_id=1, source_target_pairs={{0,8},{1,9},{2,10},{3,11},{4,12},{5,13},{6,14},{7,15},{8,0},{9,1},... | collective-permute-start | bytes 196808 | tf_op jit(solution)/shard_map/ppermute | solution.py:165
  161.0 4.9 %collective-permute-done.7 = bf16[2,32,3072]{2,1,0:T(8,128)(2,1)S(1)} collective-permute-done((bf16[2,32,3072]{2,1,0:T(8,128)(2,1)S(1)}, bf16[2,32,3072]{2,1,0:T(8,128)(2,1)S(1)}, u32[]{:S(2)}, u32[]{:S(2)}) %collective-permute-start.7) | collective-permute-done | bytes 393248 | tf_op jit(solution)/shard_map/ppermute | solution.py:165
  168.1 6.7 %collective-permute-done.8 = bf16[32,3072]{1,0:T(8,128)(2,1)S(1)} collective-permute-done((bf16[32,3072]{1,0:T(8,128)(2,1)S(1)}, bf16[32,3072]{1,0:T(8,128)(2,1)S(1)}, u32[]{:S(2)}, u32[]{:S(2)}) %collective-permute-start.8) | collective-permute-done | bytes 196640 | tf_op jit(solution)/shard_map/ppermute | solution.py:165
  177.1 3.5 %collective-permute-done.9 = bf16[32,3072]{1,0:T(8,128)(2,1)S(1)} collective-permute-done((bf16[32,3072]{1,0:T(8,128)(2,1)S(1)}, bf16[32,3072]{1,0:T(8,128)(2,1)S(1)}, u32[]{:S(2)}, u32[]{:S(2)}) %collective-permute-start.9) | collective-permute-done | bytes 196640 | tf_op jit(solution)/shard_map/ppermute | solution.py:171
  (123 shorter events, 58.9 us)
Async XLA Ops:
  0.6 14.9 %copy-start = (bf16[1024,1024]{1,0:T(8,128)(2,1)S(1)}, bf16[1024,1024]{1,0:T(8,128)(2,1)}, u32[]{:S(2)}) copy-start(bf16[1024,1024]{1,0:T(8,128)(2,1)} %param.10) | copy-start | bytes 6291460
  0.6 26.0 %all-to-all-start.1 = ((bf16[1,16,8,1024]{3,2,0,1:T(8,128)(2,1)}), bf16[1,16,8,1024]{3,2,0,1:T(8,128)(2,1)S(1)}, u32[]{:S(2)}, u32[]{:S(2)}) async-start(bf16[1,16,8,1024]{3,2,0,1:T(8,128)(2,1)} %bitcast.202), calls=%async_computation.1 | async-start | bytes 524288 | tf_op jit(solution)/shard_map/all_to_all | solution.py:81
  9.3 4.4 %copy-start.7 = (bf16[1,1,128,1024]{2,3,1,0:T(8,128)(2,1)}, bf16[1,1,128,1024]{2,3,1,0:T(8,128)(2,1)S(1)}, u32[]{:S(2)}) copy-start(bf16[1,1,128,1024]{2,3,1,0:T(8,128)(2,1)S(1)} %copy.188) | copy-start | bytes 786436
  10.6 4.4 %copy-start.9 = (bf16[1,1,128,1024]{2,3,1,0:T(8,128)(2,1)}, bf16[1,1,128,1024]{2,3,1,0:T(8,128)(2,1)S(1)}, u32[]{:S(2)}) copy-start(bf16[1,1,128,1024]{2,3,1,0:T(8,128)(2,1)S(1)} %copy.187) | copy-start | bytes 786436
  12.7 2.4 %copy-start.4 = (f32[8,128,128]{1,2,0:T(8,128)}, f32[8,128,128]{1,2,0:T(8,128)S(1)}, u32[]{:S(2)}) copy-start(f32[8,128,128]{1,2,0:T(8,128)S(1)} %fusion.20) | copy-start | bytes 1572868
  15.0 2.0 %collective-permute-start.2 = (bf16[128,1024]{0,1:T(8,128)(2,1)S(1)}, bf16[128,1024]{0,1:T(8,128)(2,1)S(1)}, u32[]{:S(2)}, u32[]{:S(2)}) collective-permute-start(bf16[128,1024]{0,1:T(8,128)(2,1)S(1)} %bitcast.190), channel_id=1, source_target_pairs={{0,1},{1,0},{2,3},{3,2},{4,5},{5,4},{6,7},{7,6},{8,9},{9,8},{10,11... | collective-permute-start | bytes 786440 | tf_op jit(solution)/shard_map/ppermute | solution.py:246
  26.7 17.2 %all-to-all-start = ((bf16[1,16,8,1024]{3,2,0,1:T(8,128)(2,1)}), bf16[1,16,8,1024]{3,2,0,1:T(8,128)(2,1)}, u32[]{:S(2)}, u32[]{:S(2)}) async-start(bf16[1,16,8,1024]{3,2,0,1:T(8,128)(2,1)} %fusion.57), calls=%async_computation | async-start | bytes 524288 | tf_op jit(solution)/shard_map/all_to_all | solution.py:81
  54.6 2.5 %copy-start.17 = (bf16[1,16,8,1,8,128]{5,2,4,3,1,0:T(8,128)(2,1)S(1)}, bf16[1,16,8,1,8,128]{5,2,4,3,1,0:T(8,128)(2,1)}, u32[]{:S(2)}) copy-start(bf16[1,16,8,1,8,128]{5,2,4,3,1,0:T(8,128)(2,1)} %get-tuple-element.54) | copy-start | bytes 786436
  59.5 21.8 %collective-permute-start = (bf16[128,1024]{1,0:T(8,128)(2,1)}, bf16[128,1024]{1,0:T(8,128)(2,1)}, u32[]{:S(2)}, u32[]{:S(2)}) collective-permute-start(bf16[128,1024]{1,0:T(8,128)(2,1)} %bitcast.6), channel_id=1, source_target_pairs={{0,1},{1,0},{2,3},{3,2},{4,5},{5,4},{6,7},{7,6},{8,9},{9,8},{10,11... | collective-permute-start | bytes 786440 | tf_op jit(solution)/shard_map/ppermute | solution.py:231
  69.2 31.5 %collective-permute-start.1 = (bf16[128,3072]{1,0:T(8,128)(2,1)S(1)}, bf16[128,3072]{1,0:T(8,128)(2,1)}, u32[]{:S(2)}, u32[]{:S(2)}) collective-permute-start(bf16[128,3072]{1,0:T(8,128)(2,1)S(1)} %reshape_reshape.14), channel_id=1, source_target_pairs={{0,1},{1,0},{2,3},{3,2},{4,5},{5,4},{6,7},{7,6},{8,9},{9,8},{10,11... | collective-permute-start | bytes 2359304 | tf_op jit(solution)/shard_map/ppermute | solution.py:231
  69.4 37.6 %all-to-all-start.2 = ((bf16[1,16,8,1024]{3,2,0,1:T(8,128)(2,1)}), bf16[1,16,8,1024]{3,2,0,1:T(8,128)(2,1)}, u32[]{:S(2)}, u32[]{:S(2)}) async-start(bf16[1,16,8,1024]{3,2,0,1:T(8,128)(2,1)} %fusion.30), calls=%async_computation.2 | async-start | bytes 524288 | tf_op jit(solution)/shard_map/all_to_all | solution.py:86
  102.9 2.6 %copy-start.1 = (f32[512,3072]{1,0:T(8,128)}, f32[512,3072]{1,0:T(8,128)S(1)}, u32[]{:S(2)}) copy-start(f32[512,3072]{1,0:T(8,128)S(1)} %fusion.5) | copy-start | bytes 18874372
  108.2 5.3 %collective-permute-start.4 = (f32[1024]{0:T(1024)S(1)}, f32[1024]{0:T(1024)S(1)}, u32[]{:S(2)}, u32[]{:S(2)}) collective-permute-start(f32[1024]{0:T(1024)S(1)} %get-tuple-element.50), channel_id=1, source_target_pairs={{0,1},{1,0},{2,3},{3,2},{4,5},{5,4},{6,7},{7,6},{8,9},{9,8},{10,11... | collective-permute-start | bytes 12296 | tf_op jit(solution)/shard_map/ppermute | solution.py:246
  109.7 4.3 %copy-start.5 = (bf16[256,2,2,2,2,2,32]{0,6,5,4,3,2,1:T(8,128)(2,1)S(1)}, bf16[256,2,2,2,2,2,32]{0,6,5,4,3,2,1:T(8,128)(2,1)}, u32[]{:S(2)}) copy-start(bf16[256,2,2,2,2,2,32]{0,6,5,4,3,2,1:T(8,128)(2,1)} %copy.168) | copy-start | bytes 1572868
  109.7 4.2 %collective-permute-start.3 = (bf16[128,1024]{1,0:T(8,128)(2,1)S(1)}, bf16[128,1024]{1,0:T(8,128)(2,1)}, u32[]{:S(2)}, u32[]{:S(2)}) collective-permute-start(bf16[128,1024]{1,0:T(8,128)(2,1)S(1)} %fusion.46), channel_id=1, source_target_pairs={{0,1},{1,0},{2,3},{3,2},{4,5},{5,4},{6,7},{7,6},{8,9},{9,8},{10,11... | collective-permute-start | bytes 786440 | tf_op jit(solution)/shard_map/ppermute | solution.py:246
  111.6 24.7 %collective-permute-start.5 = (bf16[2,2,2,32,3072]{4,3,2,1,0:T(8,128)(2,1)}, bf16[2,2,2,32,3072]{4,3,2,1,0:T(8,128)(2,1)}, u32[]{:S(2)}, u32[]{:S(2)}) collective-permute-start(bf16[2,2,2,32,3072]{4,3,2,1,0:T(8,128)(2,1)} %fusion.4), channel_id=1, source_target_pairs={{0,2},{1,17},{2,0},{3,19},{4,6},{5,21},{6,4},{7,23},{8,10},{9,25},... | collective-permute-start | bytes 4718600 | tf_op jit(solution)/shard_map/ppermute | solution.py:165
  115.3 3.7 %copy-start.11 = (bf16[16,8,8,128]{3,2,1,0:T(8,128)(2,1)S(1)}, bf16[16,8,8,128]{3,2,1,0:T(8,128)(2,1)}, u32[]{:S(2)}) copy-start(bf16[16,8,8,128]{3,2,1,0:T(8,128)(2,1)} %copy.190) | copy-start | bytes 786436
  115.4 3.7 %copy-start.12 = (bf16[128,1024]{0,1:T(8,128)(2,1)S(1)}, bf16[128,1024]{0,1:T(8,128)(2,1)}, u32[]{:S(2)}) copy-start(bf16[128,1024]{0,1:T(8,128)(2,1)} %copy.189) | copy-start | bytes 786436
  115.4 4.7 %copy-start.10 = (bf16[1,1,128,1024]{2,3,1,0:T(8,128)(2,1)S(1)}, bf16[1,1,128,1024]{2,3,1,0:T(8,128)(2,1)}, u32[]{:S(2)}) copy-start(bf16[1,1,128,1024]{2,3,1,0:T(8,128)(2,1)} %copy-done.9) | copy-start | bytes 786436
  117.6 5.2 %copy-start.8 = (bf16[1,1,128,1024]{2,3,1,0:T(8,128)(2,1)S(1)}, bf16[1,1,128,1024]{2,3,1,0:T(8,128)(2,1)}, u32[]{:S(2)}) copy-start(bf16[1,1,128,1024]{2,3,1,0:T(8,128)(2,1)} %copy-done.7) | copy-start | bytes 786436
  117.6 15.2 %collective-permute-start.10 = (bf16[2,2,2,32,1025]{4,3,2,1,0:T(8,128)(2,1)}, bf16[2,2,2,32,1025]{4,3,2,1,0:T(8,128)(2,1)}, u32[]{:S(2)}, u32[]{:S(2)}) collective-permute-start(bf16[2,2,2,32,1025]{4,3,2,1,0:T(8,128)(2,1)} %fusion.44), channel_id=1, source_target_pairs={{0,4},{1,5},{2,6},{3,7},{4,0},{5,1},{6,2},{7,3},{8,12},{9,13},{10,... | collective-permute-start | bytes 1574408 | tf_op jit(solution)/shard_map/ppermute | solution.py:165
  120.1 5.4 %copy-start.15 = (bf16[1,16,8,8,128]{4,1,3,2,0:T(8,128)(2,1)S(1)}, bf16[1,16,8,8,128]{4,1,3,2,0:T(8,128)(2,1)}, u32[]{:S(2)}) copy-start(bf16[1,16,8,8,128]{4,1,3,2,0:T(8,128)(2,1)} %fusion.31) | copy-start | bytes 786436
  126.3 24.1 %all-to-all-start.3 = ((bf16[1,16,8,1024]{3,2,0,1:T(8,128)(2,1)}), bf16[1,16,8,1024]{3,2,0,1:T(8,128)(2,1)}, u32[]{:S(2)}, u32[]{:S(2)}) async-start(bf16[1,16,8,1024]{3,2,0,1:T(8,128)(2,1)} %bitcast.57), calls=%async_computation.3 | async-start | bytes 524288 | tf_op jit(solution)/shard_map/all_to_all | solution.py:86
  135.1 7.7 %copy-start.13 = (bf16[128,1024]{0,1:T(8,128)(2,1)S(1)}, bf16[128,1024]{0,1:T(8,128)(2,1)}, u32[]{:S(2)}) copy-start(bf16[128,1024]{0,1:T(8,128)(2,1)} %copy.189) | copy-start | bytes 786436
  135.1 15.3 %collective-permute-start.11 = (bf16[2,2,32,1025]{3,2,1,0:T(8,128)(2,1)}, bf16[2,2,32,1025]{3,2,1,0:T(8,128)(2,1)}, u32[]{:S(2)}, u32[]{:S(2)}) collective-permute-start(bf16[2,2,32,1025]{3,2,1,0:T(8,128)(2,1)} %fusion.56), channel_id=1, source_target_pairs={{0,2},{1,17},{2,0},{3,19},{4,6},{5,21},{6,4},{7,23},{8,10},{9,25},... | collective-permute-start | bytes 787208 | tf_op jit(solution)/shard_map/ppermute | solution.py:165
  141.8 12.3 %collective-permute-start.6 = (bf16[2,2,32,3072]{3,2,1,0:T(8,128)(2,1)}, bf16[2,2,32,3072]{3,2,1,0:T(8,128)(2,1)}, u32[]{:S(2)}, u32[]{:S(2)}) collective-permute-start(bf16[2,2,32,3072]{3,2,1,0:T(8,128)(2,1)} %fusion.41), channel_id=1, source_target_pairs={{0,16},{1,5},{2,18},{3,7},{4,20},{5,1},{6,22},{7,3},{8,24},{9,13},... | collective-permute-start | bytes 2359304 | tf_op jit(solution)/shard_map/ppermute | solution.py:165
  151.5 6.6 %collective-permute-start.12 = (bf16[2,32,1025]{2,1,0:T(8,128)(2,1)S(1)}, bf16[2,32,1025]{2,1,0:T(8,128)(2,1)S(1)}, u32[]{:S(2)}, u32[]{:S(2)}) collective-permute-start(bf16[2,32,1025]{2,1,0:T(8,128)(2,1)S(1)} %fusion.70), channel_id=1, source_target_pairs={{0,16},{1,3},{2,18},{3,1},{4,20},{5,7},{6,22},{7,5},{8,24},{9,11},... | collective-permute-start | bytes 393608 | tf_op jit(solution)/shard_map/ppermute | solution.py:165
  156.0 9.9 %collective-permute-start.7 = (bf16[2,32,3072]{2,1,0:T(8,128)(2,1)S(1)}, bf16[2,32,3072]{2,1,0:T(8,128)(2,1)S(1)}, u32[]{:S(2)}, u32[]{:S(2)}) collective-permute-start(bf16[2,32,3072]{2,1,0:T(8,128)(2,1)S(1)} %fusion.54), channel_id=1, source_target_pairs={{0,4},{1,3},{2,6},{3,1},{4,0},{5,7},{6,2},{7,5},{8,12},{9,11},{10,... | collective-permute-start | bytes 1179656 | tf_op jit(solution)/shard_map/ppermute | solution.py:165
  158.2 9.2 %collective-permute-start.13 = (bf16[32,1025]{1,0:T(8,128)(2,1)S(1)}, bf16[32,1025]{1,0:T(8,128)(2,1)S(1)}, u32[]{:S(2)}, u32[]{:S(2)}) collective-permute-start(bf16[32,1025]{1,0:T(8,128)(2,1)S(1)} %fusion.76), channel_id=1, source_target_pairs={{0,8},{1,9},{2,10},{3,11},{4,12},{5,13},{6,14},{7,15},{8,0},{9,1},... | collective-permute-start | bytes 196808 | tf_op jit(solution)/shard_map/ppermute | solution.py:165
  166.0 8.7 %collective-permute-start.8 = (bf16[32,3072]{1,0:T(8,128)(2,1)S(1)}, bf16[32,3072]{1,0:T(8,128)(2,1)S(1)}, u32[]{:S(2)}, u32[]{:S(2)}) collective-permute-start(bf16[32,3072]{1,0:T(8,128)(2,1)S(1)} %fusion.69), channel_id=1, source_target_pairs={{0,8},{1,9},{2,10},{3,11},{4,12},{5,13},{6,14},{7,15},{8,0},{9,1},... | collective-permute-start | bytes 589832 | tf_op jit(solution)/shard_map/ppermute | solution.py:165
  167.4 8.3 %collective-permute-start.14 = (bf16[32,1025]{1,0:T(8,128)(2,1)S(1)}, bf16[32,1025]{1,0:T(8,128)(2,1)S(1)}, u32[]{:S(2)}, u32[]{:S(2)}) collective-permute-start(bf16[32,1025]{1,0:T(8,128)(2,1)S(1)} %fusion.71), channel_id=1, source_target_pairs={{0,16},{16,0},{1,17},{17,1},{2,18},{18,2},{3,19},{19,3},{4,20},{20... | collective-permute-start | bytes 196808 | tf_op jit(solution)/shard_map/ppermute | solution.py:171
  174.8 5.7 %collective-permute-start.9 = (bf16[32,3072]{1,0:T(8,128)(2,1)S(1)}, bf16[32,3072]{1,0:T(8,128)(2,1)S(1)}, u32[]{:S(2)}, u32[]{:S(2)}) collective-permute-start(bf16[32,3072]{1,0:T(8,128)(2,1)S(1)} %fusion.55), channel_id=1, source_target_pairs={{0,16},{16,0},{1,17},{17,1},{2,18},{18,2},{3,19},{19,3},{4,20},{20... | collective-permute-start | bytes 589832 | tf_op jit(solution)/shard_map/ppermute | solution.py:171
  (6 other events, 7.7 us)

commit v15 on v7

--- a/solution.py
+++ b/solution.py
@@ -228,6 +228,7 @@
         jnp.concatenate([used_grads, grads_peer], axis=0),
         preferred_element_type=jnp.float32,
     )
+    (joint_sum,), grad_local = reduce_rows((joint_term,), (orders,), seq_n, dp_n, grad_local)
     grad_normed = lax.all_to_all(
         grad_local.reshape(batches, all_rows, col_share, model_width),
         "seq",
@@ -236,7 +237,6 @@
         tiled=True,
     )
     grad_normed = grad_normed.reshape(-1, model_width)
-    (joint_sum,), grad_normed = reduce_rows((joint_term,), (orders,), seq_n, dp_n, grad_normed)
     grad_float = grad_normed.astype(jnp.float32)
     gain_term = jnp.sum(grad_float * hidden * inverse, axis=0)
     scaled = norm_gain * grad_float

time: 162 us -> 162 us (level)
  waiting for transfers between devices: 26.8 us -> 39 us
  starting transfers between devices: 36.5 us -> 29.8 us
  matrix products: 39.6 us -> 35.8 us
  other arithmetic: 21.7 us -> 19.8 us
    ppermute x8, starting transfers between devices: 11.7 us -> 4.43 us  [reduce_rows(): lax.ppermute(given, ('dp', 'seq'), perm).astype(jnp.float32)]
    ppermute x8, waiting for transfers between devices: 16.5 us -> 22.8 us  [reduce_rows(): lax.ppermute(given, ('dp', 'seq'), perm).astype(jnp.float32)]
    all_to_all x1, waiting for transfers between devices: 0.21 us -> 5.07 us  [on_device(): lax.all_to_all(grad_local.reshape(batches, all_rows, col_share, model_wid...]
    dot_general x2, matrix products: 4.13 us -> 2.32 us  [attend(): jnp.einsum(scores_form + ',' + keyed + '->' + layout, rounded, values, pr...]
    all_to_all x1, waiting for transfers between devices: 6.19 us -> 7.86 us  [on_device(): lax.all_to_all(normed.reshape(batches, local_rows, columns, model_width),...]
    unnamed x54 -> x62, local copies, waits for them, and re-layouts: 20.7 us -> 20.8 us
  transfers between devices with their start and end apart: 19 -> 19, of which waited for: 7 -> 8; matrix products, arithmetic and copies ran while one was open for 39% -> 48% of each run, Pallas kernels for 0% -> 0%
where the time goes in v15:
time: 162 us; the launch traced here: 161 us
  waiting for transfers between devices  39 us (24%)
  matrix products  35.8 us (22%)
  local copies, waits for them, and re-layouts  35.4 us (22%)
  starting transfers between devices  29.8 us (18%)
  other arithmetic  19.8 us (12%)
    ppermute x8, waiting for transfers between devices, reduce_rows(): lax.ppermute(given, ('dp', 'seq'), perm).astype(jnp.float32)  22.8 us
    unnamed x62, local copies, waits for them, and re-layouts  20.8 us
    all_to_all x1, waiting for transfers between devices, on_device(): lax.all_to_all(normed.reshape(batches, local_rows, columns, model_width),...  7.86 us
    all_to_all x1, starting transfers between devices, on_device(): lax.all_to_all(upstream, 'seq', split_axis=2, concat_axis=1, tiled=True)  7.39 us
    add x6, other arithmetic, reduce_rows(): kept + lax.ppermute(given, ('dp', 'seq'), perm).astype(jnp.float32)  7.33 us
    all_to_all x1, starting transfers between devices, on_device(): lax.all_to_all(normed.reshape(batches, local_rows, columns, model_width),...  6.07 us
    dot_general x1, matrix products, on_device(): jnp.dot(used_grads, joint_weight.T, preferred_element_type=jnp.float32)  5.68 us
    dot_general x2, matrix products, attend_back(): jnp.einsum(scores_form + ',' + layout + '->' + keyed, grad_score, queries...  5.56 us
  transfers between devices with their start and end apart: 19, of which 8 were waited for; matrix products, arithmetic and copies ran while one was open for 48% of the time, Pallas kernels for 0%

profile of v15, /device:TPU:0, one launch (start us, length us, event | category | flops | bytes accessed | tf_op | source)
XLA Modules:
  0.0 161.0 jit_solution(17588507842408140048)
XLA Ops:
  2.7 2.1 %reduce.20 = bf16[128,1024]{1,0:T(8,128)(2,1)S(1)} reduce(bf16[128,1,1,1024]{3,2,1,0:T(2,128)(2,1)S(1)} %bitcast.191, bf16[]{:T(256)} %broadcast.113), dimensions={1,2}, to_apply=%bitcast.183.reduce_sub_computation | reduce | bytes 524290
  5.7 7.4 %all-to-all-start.1 = ((bf16[16,2,4096]{2,1,0:T(2,128)(2,1)}), bf16[16,2,4096]{2,1,0:T(2,128)(2,1)S(1)}, u32[]{:S(2)}, u32[]{:S(2)}) async-start(bf16[16,2,4096]{2,1,0:T(2,128)(2,1)} %reshape.311), calls=%async_computation.1 | async-start | bytes 524288 | tf_op jit(solution)/shard_map/all_to_all | solution.py:201
  19.2 2.9 %reduce.21 = bf16[128,1024]{1,0:T(8,128)(2,1)} reduce(bf16[128,1,1,1024]{3,2,1,0:T(2,128)(2,1)S(1)} %bitcast.192, bf16[]{:T(256)} %broadcast.113), dimensions={1,2}, to_apply=%bitcast.184.reduce_sub_computation | reduce | bytes 524290
  22.1 1.8 %reshape.313 = bf16[16,2,4096]{2,1,0:T(2,128)(2,1)} reshape(bf16[128,1024]{1,0:T(8,128)(2,1)} %reduce.21) | data formatting | bytes 524288
  23.9 6.1 %all-to-all-start = ((bf16[16,2,4096]{2,1,0:T(2,128)(2,1)}), bf16[16,2,4096]{2,1,0:T(2,128)(2,1)}, u32[]{:S(2)}, u32[]{:S(2)}) async-start(bf16[16,2,4096]{2,1,0:T(2,128)(2,1)} %reshape.313), calls=%async_computation | async-start | bytes 524288 | tf_op jit(solution)/shard_map/all_to_all | solution.py:184
  32.2 7.9 %all-to-all-done = bf16[16,2,4096]{2,1,0:T(2,128)(2,1)} async-done(((bf16[16,2,4096]{2,1,0:T(2,128)(2,1)}), bf16[16,2,4096]{2,1,0:T(2,128)(2,1)}, u32[]{:S(2)}, u32[]{:S(2)}) %all-to-all-start) | async-done | bytes 262176 | tf_op jit(solution)/shard_map/all_to_all | solution.py:184
  40.1 2.2 %reshape.314 = bf16[128,1,1,1024]{3,2,1,0:T(2,128)(2,1)S(1)} reshape(bf16[16,2,4096]{2,1,0:T(2,128)(2,1)} %all-to-all-done) | data formatting | bytes 524288
  43.3 3.9 %convolution_convert_fusion = bf16[128,3072]{1,0:T(8,128)(2,1)S(1)} fusion(bf16[1024,3072]{1,0:T(8,128)(2,1)} %param.12, bf16[1,1,128,1024]{2,3,1,0:T(8,128)(2,1)} %copy.112), kind=kOutput, calls=%fused_computation.4 | convolution fusion | flops 805699584 | bytes 7340032 | tf_op jit(solution)/shard_map/dot_general | solution.py:191
  49.3 2.5 %fusion.93 = (f32[8,8,16]{2,1,0:T(8,128)S(1)}, f32[8,8,16,16]{2,3,1,0:T(8,128)}) fusion(pred[16,16]{0,1:T(8,128)(4,1)S(1)} %iota_compare_fusion.1, bf16[1,16,8,1,8,128]{5,2,4,3,1,0:T(8,128)(2,1)S(1)} %get-tuple-element.47, bf16[1,16,8,1,8,128]{5,2,4,3,1,0:T(8,128)(2,1)} %get-tuple-element.46), kind=kOutput, calls=%fused_computation.148 | convolution fusion | flops 4259855 | bytes 594176 | tf_op jit(solution)/shard_map/sub | solution.py:28
  51.8 2.1 %fusion.29 = bf16[1,16,8,1,8,128]{5,1,4,2,3,0:T(8,128)(2,1)} fusion(bf16[16,8,8,128]{3,2,1,0:T(8,128)(2,1)S(1)} %copy.190, f32[8,8,16,16]{2,3,1,0:T(8,128)} %get-tuple-element.57, f32[8,8,16]{2,1,0:T(8,128)S(1)} %get-tuple-element.56), kind=kOutput, calls=%fused_computation.51 | convolution fusion | flops 4358144 | bytes 593920 | tf_op jit(solution)/shard_map/bchlm,blche->bmche/dot_general | solution.py:64
  53.9 2.9 %fusion.31 = bf16[1,16,8,1,8,128]{5,1,4,2,3,0:T(8,128)(2,1)} fusion(f32[8,8,16,16]{2,3,1,0:T(8,128)} %convolution_bitcast_fusion, bf16[1,16,8,1,8,128]{5,2,4,3,1,0:T(8,128)(2,1)} %get-tuple-element.46, f32[8,8,16,16]{2,3,1,0:T(8,128)} %get-tuple-element.57, f32[8,8,16]{2,1,0:T(8,128)S(1)} %get-tuple-element.56), kind=kOutput, calls=%fused_computation.53 | convolution fusion | flops 4441103 | bytes 659456 | tf_op jit(solution)/shard_map/bchlm,blche->bmche/dot_general | solution.py:57
  56.9 2.5 %fusion.28 = bf16[1,16,8,1,8,128]{5,1,4,2,3,0:T(8,128)(2,1)} fusion(f32[8,8,16,16]{2,3,1,0:T(8,128)S(1)} %copy-done.17, bf16[1,16,8,1,8,128]{5,2,4,3,1,0:T(8,128)(2,1)} %copy-done.21, f32[8,8,16,16]{2,3,1,0:T(8,128)} %get-tuple-element.57, f32[8,8,16]{2,1,0:T(8,128)S(1)} %get-tuple-element.56), kind=kOutput, calls=%fused_computation.50 | convolution fusion | flops 4441103 | bytes 659456 | tf_op jit(solution)/shard_map/bchlm,bmche->blche/dot_general | solution.py:51
  63.6 5.7 %convolution_convert_fusion.8 = bf16[128,1024]{1,0:T(8,128)(2,1)} fusion(bf16[128,3072]{1,0:T(8,128)(2,1)S(1)} %reshape_reshape.7, bf16[1024,3072]{1,0:T(8,128)(2,1)} %param.12), kind=kOutput, calls=%fused_computation.42 | convolution fusion | flops 805437440 | bytes 7340032 | tf_op jit(solution)/shard_map/dot_general | solution.py:209
  71.5 2.6 %copy-done.1 = f32[512,3072]{1,0:T(8,128)} copy-done((f32[512,3072]{1,0:T(8,128)}, f32[512,3072]{1,0:T(8,128)S(1)}, u32[]{:S(2)}) %copy-start.1) | copy-done | bytes 6291480
  75.6 3.8 %all-to-all-start.2 = ((bf16[1,16,8,1024]{3,2,0,1:T(8,128)(2,1)}), bf16[1,16,8,1024]{3,2,0,1:T(8,128)(2,1)S(1)}, u32[]{:S(2)}, u32[]{:S(2)}) async-start(bf16[1,16,8,1024]{3,2,0,1:T(8,128)(2,1)} %bitcast.29), calls=%async_computation.2 | async-start | bytes 524288 | tf_op jit(solution)/shard_map/all_to_all | solution.py:232
  82.5 1.6 collective-permute-start.5
  84.0 5.1 %all-to-all-done.2 = bf16[1,16,8,1024]{3,2,0,1:T(8,128)(2,1)S(1)} async-done(((bf16[1,16,8,1024]{3,2,0,1:T(8,128)(2,1)}), bf16[1,16,8,1024]{3,2,0,1:T(8,128)(2,1)S(1)}, u32[]{:S(2)}, u32[]{:S(2)}) %all-to-all-start.2) | async-done | bytes 262176 | tf_op jit(solution)/shard_map/all_to_all | solution.py:232
  97.2 2.6 %convolution_convert_fusion.1 = bf16[8,128,128]{1,2,0:T(8,128)(2,1)} fusion(bf16[128,8,128]{0,2,1:T(8,128)(2,1)S(1)} %bitcast.202, f32[8,128,128]{1,2,0:T(8,128)} %fusion.64, f32[8,128,128]{1,2,0:T(8,128)} %get-tuple-element.53, f32[8,128]{1,0:T(8,128)S(1)} %get-tuple-element.52), kind=kOutput, calls=%fused_computation.35 | convolution fusion | flops 34604160 | bytes 1576960 | tf_op jit(solution)/shard_map/ghlm,gmhe->glhe/dot_general | solution.py:51
  99.9 2.6 %convolution_convert_fusion.6 = bf16[8,128,128]{1,2,0:T(8,128)(2,1)} fusion(bf16[128,8,128]{0,2,1:T(8,128)(2,1)S(1)} %bitcast.200, f32[8,128,128]{1,2,0:T(8,128)} %fusion.64, f32[8,128,128]{1,2,0:T(8,128)} %get-tuple-element.53, f32[8,128]{1,0:T(8,128)S(1)} %get-tuple-element.52), kind=kOutput, calls=%fused_computation.40 | convolution fusion | flops 34604160 | bytes 1576960 | tf_op jit(solution)/shard_map/ghlm,glhe->gmhe/dot_general | solution.py:57
  103.4 4.2 %all-to-all-start.3 = ((bf16[1,16,8,1024]{3,2,0,1:T(8,128)(2,1)}), bf16[1,16,8,1024]{3,2,0,1:T(8,128)(2,1)}, u32[]{:S(2)}, u32[]{:S(2)}) async-start(bf16[1,16,8,1024]{3,2,0,1:T(8,128)(2,1)} %bitcast.59), calls=%async_computation.3 | async-start | bytes 524288 | tf_op jit(solution)/shard_map/all_to_all | solution.py:257
  107.6 5.8 %collective-permute-done.10 = bf16[2,2,2,32,1025]{4,3,2,1,0:T(8,128)(2,1)} collective-permute-done((bf16[2,2,2,32,1025]{4,3,2,1,0:T(8,128)(2,1)}, bf16[2,2,2,32,1025]{4,3,2,1,0:T(8,128)(2,1)}, u32[]{:S(2)}, u32[]{:S(2)}) %collective-permute-start.10) | collective-permute-done | bytes 524832 | tf_op jit(solution)/shard_map/ppermute | solution.py:153
  115.7 2.9 %bitcast_add_fusion = f32[2,2,2,32,3072]{4,3,2,1,0:T(8,128)S(1)} fusion(bf16[2,2,2,32,3072]{4,3,2,1,0:T(8,128)(2,1)} %collective-permute-done.5, f32[2,2,2,2,32,3072]{5,4,3,2,1,0:T(8,128)} %bitcast.186, s32[]{:T(128)S(6)} %select_n.247), kind=kLoop, calls=%fused_computation.7 | loop fusion | flops 1572864 | bytes 7864324 | tf_op jit(solution)/shard_map/add | solution.py:153
  118.6 1.6 %copy-done.3 = f32[2,2,2,32,3072]{4,3,2,1,0:T(8,128)} copy-done((f32[2,2,2,32,3072]{4,3,2,1,0:T(8,128)}, f32[2,2,2,32,3072]{4,3,2,1,0:T(8,128)S(1)}, u32[]{:S(2)}) %copy-start.3) | copy-done | bytes 3145752
  122.7 2.2 %convolution_convert_fusion.5 = bf16[8,128,128]{2,1,0:T(8,128)(2,1)} fusion(bf16[128,8,128]{0,2,1:T(8,128)(2,1)S(1)} %bitcast.206, f32[8,128]{1,0:T(8,128)S(1)} %get-tuple-element.52, f32[8,128,128]{1,2,0:T(8,128)} %copy-done.4), kind=kOutput, calls=%fused_computation.39 | convolution fusion | flops 34079872 | bytes 1052672 | tf_op jit(solution)/shard_map/ghlm,glhe->gmhe/dot_general | solution.py:64
  124.9 1.8 %copy.144 = bf16[1,1,128,1024]{3,2,1,0:T(8,128)(2,1)} copy(bf16[1,1,128,1024]{2,3,1,0:T(8,128)(2,1)} %bitcast.209) | data formatting | bytes 524288
  126.7 1.8 %copy.143 = bf16[1,1,128,1024]{3,2,1,0:T(8,128)(2,1)} copy(bf16[1,1,128,1024]{2,3,1,0:T(8,128)(2,1)} %bitcast.208) | data formatting | bytes 524288
  128.5 1.8 %copy.145 = bf16[1,1,128,1024]{3,2,1,0:T(8,128)(2,1)} copy(bf16[1,1,128,1024]{2,3,1,0:T(8,128)(2,1)} %bitcast.210) | data formatting | bytes 524288
  133.5 1.8 %bitcast_add_fusion.1 = f32[2,2,32,3072]{3,2,1,0:T(8,128)S(1)} fusion(bf16[2,2,32,3072]{3,2,1,0:T(8,128)(2,1)} %collective-permute-done.6, f32[2,2,2,32,3072]{4,3,2,1,0:T(8,128)} %copy-done.3, s32[]{:T(128)S(6)} %select_n.249), kind=kLoop, calls=%fused_computation.16 | loop fusion | flops 786432 | bytes 3932164 | tf_op jit(solution)/shard_map/add | solution.py:153
  136.7 8.1 %collective-permute-done.7 = bf16[2,32,3072]{2,1,0:T(8,128)(2,1)S(1)} collective-permute-done((bf16[2,32,3072]{2,1,0:T(8,128)(2,1)S(1)}, bf16[2,32,3072]{2,1,0:T(8,128)(2,1)S(1)}, u32[]{:S(2)}, u32[]{:S(2)}) %collective-permute-start.7) | collective-permute-done | bytes 393248 | tf_op jit(solution)/shard_map/ppermute | solution.py:153
  146.2 6.5 %collective-permute-done.8 = bf16[32,3072]{1,0:T(8,128)(2,1)S(1)} collective-permute-done((bf16[32,3072]{1,0:T(8,128)(2,1)S(1)}, bf16[32,3072]{1,0:T(8,128)(2,1)S(1)}, u32[]{:S(2)}, u32[]{:S(2)}) %collective-permute-start.8) | collective-permute-done | bytes 196640 | tf_op jit(solution)/shard_map/ppermute | solution.py:153
  155.3 3.2 %collective-permute-done.9 = bf16[32,3072]{1,0:T(8,128)(2,1)S(1)} collective-permute-done((bf16[32,3072]{1,0:T(8,128)(2,1)S(1)}, bf16[32,3072]{1,0:T(8,128)(2,1)S(1)}, u32[]{:S(2)}, u32[]{:S(2)}) %collective-permute-start.9) | collective-permute-done | bytes 196640 | tf_op jit(solution)/shard_map/ppermute | solution.py:159
  159.3 1.7 %copy.194 = bf16[1,1,128,1024]{3,2,1,0:T(8,128)(2,1)} copy(bf16[1,1,128,1024]{3,2,1,0:T(8,128)(2,1)} %bitcast.60) | data formatting | bytes 524288
  (141 shorter events, 48.2 us)
Async XLA Ops:
  0.6 17.4 %copy-start = (bf16[1024,1024]{1,0:T(8,128)(2,1)S(1)}, bf16[1024,1024]{1,0:T(8,128)(2,1)}, u32[]{:S(2)}) copy-start(bf16[1024,1024]{1,0:T(8,128)(2,1)} %param.10) | copy-start | bytes 6291460
  0.6 12.5 %copy-start.18 = (bf16[1,1,128,1024]{3,2,1,0:T(8,128)(2,1)S(1)}, bf16[1,1,128,1024]{3,2,1,0:T(8,128)(2,1)}, u32[]{:S(2)}) copy-start(bf16[1,1,128,1024]{3,2,1,0:T(8,128)(2,1)} %param.7) | copy-start | bytes 786436
  4.8 9.7 %copy-start.19 = (bf16[1,1,128,1024]{3,2,1,0:T(8,128)(2,1)S(1)}, bf16[1,1,128,1024]{3,2,1,0:T(8,128)(2,1)}, u32[]{:S(2)}) copy-start(bf16[1,1,128,1024]{3,2,1,0:T(8,128)(2,1)} %param.9) | copy-start | bytes 786436
  5.7 18.2 %all-to-all-start.1 = ((bf16[16,2,4096]{2,1,0:T(2,128)(2,1)}), bf16[16,2,4096]{2,1,0:T(2,128)(2,1)S(1)}, u32[]{:S(2)}, u32[]{:S(2)}) async-start(bf16[16,2,4096]{2,1,0:T(2,128)(2,1)} %reshape.311), calls=%async_computation.1 | async-start | bytes 524288 | tf_op jit(solution)/shard_map/all_to_all | solution.py:201
  13.3 3.4 %copy-start.8 = (bf16[1,1,128,1024]{2,3,1,0:T(8,128)(2,1)}, bf16[1,1,128,1024]{2,3,1,0:T(8,128)(2,1)S(1)}, u32[]{:S(2)}) copy-start(bf16[1,1,128,1024]{2,3,1,0:T(8,128)(2,1)S(1)} %copy.158) | copy-start | bytes 786436
  14.6 3.4 %copy-start.10 = (bf16[1,1,128,1024]{2,3,1,0:T(8,128)(2,1)}, bf16[1,1,128,1024]{2,3,1,0:T(8,128)(2,1)S(1)}, u32[]{:S(2)}) copy-start(bf16[1,1,128,1024]{2,3,1,0:T(8,128)(2,1)S(1)} %copy.157) | copy-start | bytes 786436
  23.9 16.2 %all-to-all-start = ((bf16[16,2,4096]{2,1,0:T(2,128)(2,1)}), bf16[16,2,4096]{2,1,0:T(2,128)(2,1)}, u32[]{:S(2)}, u32[]{:S(2)}) async-start(bf16[16,2,4096]{2,1,0:T(2,128)(2,1)} %reshape.313), calls=%async_computation | async-start | bytes 524288 | tf_op jit(solution)/shard_map/all_to_all | solution.py:184
  30.0 49.3 %collective-permute-start.2 = (bf16[128,1024]{0,1:T(8,128)(2,1)}, bf16[128,1024]{0,1:T(8,128)(2,1)}, u32[]{:S(2)}, u32[]{:S(2)}) collective-permute-start(bf16[128,1024]{0,1:T(8,128)(2,1)} %bitcast.197), channel_id=1, source_target_pairs={{0,1},{1,0},{2,3},{3,2},{4,5},{5,4},{6,7},{7,6},{8,9},{9,8},{10,11... | collective-permute-start | bytes 786440 | tf_op jit(solution)/shard_map/ppermute | solution.py:246
  48.0 3.9 %copy-start.21 = (bf16[1,16,8,1,8,128]{5,2,4,3,1,0:T(8,128)(2,1)}, bf16[1,16,8,1,8,128]{5,2,4,3,1,0:T(8,128)(2,1)S(1)}, u32[]{:S(2)}) copy-start(bf16[1,16,8,1,8,128]{5,2,4,3,1,0:T(8,128)(2,1)S(1)} %get-tuple-element.47) | copy-start | bytes 786436
  48.0 6.0 %copy-start.15 = (bf16[1,16,8,1,8,128]{5,2,4,3,1,0:T(8,128)(2,1)}, bf16[1,16,8,1,8,128]{5,2,4,3,1,0:T(8,128)(2,1)S(1)}, u32[]{:S(2)}) copy-start(bf16[1,16,8,1,8,128]{5,2,4,3,1,0:T(8,128)(2,1)S(1)} %get-tuple-element.45) | copy-start | bytes 786436
  53.9 3.0 %copy-start.17 = (f32[8,8,16,16]{2,3,1,0:T(8,128)S(1)}, f32[8,8,16,16]{2,3,1,0:T(8,128)}, u32[]{:S(2)}) copy-start(f32[8,8,16,16]{2,3,1,0:T(8,128)} %convolution_bitcast_fusion) | copy-start | bytes 196612
  59.3 9.9 %collective-permute-start = (bf16[128,1024]{0,1:T(8,128)(2,1)}, bf16[128,1024]{0,1:T(8,128)(2,1)}, u32[]{:S(2)}, u32[]{:S(2)}) collective-permute-start(bf16[128,1024]{0,1:T(8,128)(2,1)} %bitcast.6), channel_id=1, source_target_pairs={{0,1},{1,0},{2,3},{3,2},{4,5},{5,4},{6,7},{7,6},{8,9},{9,8},{10,11... | collective-permute-start | bytes 786440 | tf_op jit(solution)/shard_map/ppermute | solution.py:225
  63.0 7.5 %collective-permute-start.1 = (bf16[128,3072]{1,0:T(8,128)(2,1)S(1)}, bf16[128,3072]{1,0:T(8,128)(2,1)S(1)}, u32[]{:S(2)}, u32[]{:S(2)}) collective-permute-start(bf16[128,3072]{1,0:T(8,128)(2,1)S(1)} %reshape_reshape.7), channel_id=1, source_target_pairs={{0,1},{1,0},{2,3},{3,2},{4,5},{5,4},{6,7},{7,6},{8,9},{9,8},{10,11... | collective-permute-start | bytes 2359304 | tf_op jit(solution)/shard_map/ppermute | solution.py:225
  71.5 7.9 %copy-start.7 = (bf16[8,128,128]{1,2,0:T(8,128)(2,1)S(1)}, bf16[8,128,128]{1,2,0:T(8,128)(2,1)}, u32[]{:S(2)}) copy-start(bf16[8,128,128]{1,2,0:T(8,128)(2,1)} %copy-done.6) | copy-start | bytes 786436
  75.6 13.6 %all-to-all-start.2 = ((bf16[1,16,8,1024]{3,2,0,1:T(8,128)(2,1)}), bf16[1,16,8,1024]{3,2,0,1:T(8,128)(2,1)S(1)}, u32[]{:S(2)}, u32[]{:S(2)}) async-start(bf16[1,16,8,1024]{3,2,0,1:T(8,128)(2,1)} %bitcast.29), calls=%async_computation.2 | async-start | bytes 524288 | tf_op jit(solution)/shard_map/all_to_all | solution.py:232
  82.5 33.2 %collective-permute-start.5 = (bf16[2,2,2,32,3072]{4,3,2,1,0:T(8,128)(2,1)}, bf16[2,2,2,32,3072]{4,3,2,1,0:T(8,128)(2,1)}, u32[]{:S(2)}, u32[]{:S(2)}) collective-permute-start(bf16[2,2,2,32,3072]{4,3,2,1,0:T(8,128)(2,1)} %fusion.4), channel_id=1, source_target_pairs={{0,2},{1,17},{2,0},{3,19},{4,6},{5,21},{6,4},{7,23},{8,10},{9,25},... | collective-permute-start | bytes 4718600 | tf_op jit(solution)/shard_map/ppermute | solution.py:153
  89.3 2.5 %collective-permute-start.4 = (f32[1024]{0:T(1024)S(1)}, f32[1024]{0:T(1024)S(1)}, u32[]{:S(2)}, u32[]{:S(2)}) collective-permute-start(f32[1024]{0:T(1024)S(1)} %get-tuple-element.43), channel_id=1, source_target_pairs={{0,1},{1,0},{2,3},{3,2},{4,5},{5,4},{6,7},{7,6},{8,9},{9,8},{10,11... | collective-permute-start | bytes 12296 | tf_op jit(solution)/shard_map/ppermute | solution.py:246
  89.6 2.7 %collective-permute-start.3 = (bf16[128,1024]{1,0:T(8,128)(2,1)S(1)}, bf16[128,1024]{1,0:T(8,128)(2,1)}, u32[]{:S(2)}, u32[]{:S(2)}) collective-permute-start(bf16[128,1024]{1,0:T(8,128)(2,1)S(1)} %fusion.45), channel_id=1, source_target_pairs={{0,1},{1,0},{2,3},{3,2},{4,5},{5,4},{6,7},{7,6},{8,9},{9,8},{10,11... | collective-permute-start | bytes 786440 | tf_op jit(solution)/shard_map/ppermute | solution.py:246
  93.7 3.5 %copy-start.11 = (bf16[1,1,128,1024]{2,3,1,0:T(8,128)(2,1)S(1)}, bf16[1,1,128,1024]{2,3,1,0:T(8,128)(2,1)}, u32[]{:S(2)}) copy-start(bf16[1,1,128,1024]{2,3,1,0:T(8,128)(2,1)} %copy-done.10) | copy-start | bytes 786436
  95.9 3.9 %copy-start.9 = (bf16[1,1,128,1024]{2,3,1,0:T(8,128)(2,1)S(1)}, bf16[1,1,128,1024]{2,3,1,0:T(8,128)(2,1)}, u32[]{:S(2)}) copy-start(bf16[1,1,128,1024]{2,3,1,0:T(8,128)(2,1)} %copy-done.8) | copy-start | bytes 786436
  95.9 17.4 %collective-permute-start.10 = (bf16[2,2,2,32,1025]{4,3,2,1,0:T(8,128)(2,1)}, bf16[2,2,2,32,1025]{4,3,2,1,0:T(8,128)(2,1)}, u32[]{:S(2)}, u32[]{:S(2)}) collective-permute-start(bf16[2,2,2,32,1025]{4,3,2,1,0:T(8,128)(2,1)} %fusion.43), channel_id=1, source_target_pairs={{0,4},{1,5},{2,6},{3,7},{4,0},{5,1},{6,2},{7,3},{8,12},{9,13},{10,... | collective-permute-start | bytes 1574408 | tf_op jit(solution)/shard_map/ppermute | solution.py:153
  97.2 5.2 %copy-start.20 = (bf16[1,16,8,8,128]{4,1,3,2,0:T(8,128)(2,1)S(1)}, bf16[1,16,8,8,128]{4,1,3,2,0:T(8,128)(2,1)}, u32[]{:S(2)}) copy-start(bf16[1,16,8,8,128]{4,1,3,2,0:T(8,128)(2,1)} %fusion.30) | copy-start | bytes 786436
  103.4 26.9 %all-to-all-start.3 = ((bf16[1,16,8,1024]{3,2,0,1:T(8,128)(2,1)}), bf16[1,16,8,1024]{3,2,0,1:T(8,128)(2,1)}, u32[]{:S(2)}, u32[]{:S(2)}) async-start(bf16[1,16,8,1024]{3,2,0,1:T(8,128)(2,1)} %bitcast.59), calls=%async_computation.3 | async-start | bytes 524288 | tf_op jit(solution)/shard_map/all_to_all | solution.py:257
  115.7 7.0 %copy-start.14 = (bf16[128,1024]{0,1:T(8,128)(2,1)S(1)}, bf16[128,1024]{0,1:T(8,128)(2,1)}, u32[]{:S(2)}) copy-start(bf16[128,1024]{0,1:T(8,128)(2,1)} %copy.159) | copy-start | bytes 786436
  115.7 14.7 %collective-permute-start.11 = (bf16[2,2,32,1025]{3,2,1,0:T(8,128)(2,1)}, bf16[2,2,32,1025]{3,2,1,0:T(8,128)(2,1)}, u32[]{:S(2)}, u32[]{:S(2)}) collective-permute-start(bf16[2,2,32,1025]{3,2,1,0:T(8,128)(2,1)} %fusion.55), channel_id=1, source_target_pairs={{0,2},{1,17},{2,0},{3,19},{4,6},{5,21},{6,4},{7,23},{8,10},{9,25},... | collective-permute-start | bytes 787208 | tf_op jit(solution)/shard_map/ppermute | solution.py:153
  121.2 12.3 %collective-permute-start.6 = (bf16[2,2,32,3072]{3,2,1,0:T(8,128)(2,1)}, bf16[2,2,32,3072]{3,2,1,0:T(8,128)(2,1)}, u32[]{:S(2)}, u32[]{:S(2)}) collective-permute-start(bf16[2,2,32,3072]{3,2,1,0:T(8,128)(2,1)} %fusion.40), channel_id=1, source_target_pairs={{0,16},{1,5},{2,18},{3,7},{4,20},{5,1},{6,22},{7,3},{8,24},{9,13},... | collective-permute-start | bytes 2359304 | tf_op jit(solution)/shard_map/ppermute | solution.py:153
  131.4 5.2 %collective-permute-start.12 = (bf16[2,32,1025]{2,1,0:T(8,128)(2,1)S(1)}, bf16[2,32,1025]{2,1,0:T(8,128)(2,1)S(1)}, u32[]{:S(2)}, u32[]{:S(2)}) collective-permute-start(bf16[2,32,1025]{2,1,0:T(8,128)(2,1)S(1)} %fusion.69), channel_id=1, source_target_pairs={{0,16},{1,3},{2,18},{3,1},{4,20},{5,7},{6,22},{7,5},{8,24},{9,11},... | collective-permute-start | bytes 393608 | tf_op jit(solution)/shard_map/ppermute | solution.py:153
  135.4 9.5 %collective-permute-start.7 = (bf16[2,32,3072]{2,1,0:T(8,128)(2,1)S(1)}, bf16[2,32,3072]{2,1,0:T(8,128)(2,1)S(1)}, u32[]{:S(2)}, u32[]{:S(2)}) collective-permute-start(bf16[2,32,3072]{2,1,0:T(8,128)(2,1)S(1)} %fusion.53), channel_id=1, source_target_pairs={{0,4},{1,3},{2,6},{3,1},{4,0},{5,7},{6,2},{7,5},{8,12},{9,11},{10,... | collective-permute-start | bytes 1179656 | tf_op jit(solution)/shard_map/ppermute | solution.py:153
  136.6 8.4 %collective-permute-start.13 = (bf16[32,1025]{1,0:T(8,128)(2,1)S(1)}, bf16[32,1025]{1,0:T(8,128)(2,1)S(1)}, u32[]{:S(2)}, u32[]{:S(2)}) collective-permute-start(bf16[32,1025]{1,0:T(8,128)(2,1)S(1)} %fusion.75), channel_id=1, source_target_pairs={{0,8},{1,9},{2,10},{3,11},{4,12},{5,13},{6,14},{7,15},{8,0},{9,1},... | collective-permute-start | bytes 196808 | tf_op jit(solution)/shard_map/ppermute | solution.py:153
  145.0 7.8 %collective-permute-start.8 = (bf16[32,3072]{1,0:T(8,128)(2,1)S(1)}, bf16[32,3072]{1,0:T(8,128)(2,1)S(1)}, u32[]{:S(2)}, u32[]{:S(2)}) collective-permute-start(bf16[32,3072]{1,0:T(8,128)(2,1)S(1)} %fusion.68), channel_id=1, source_target_pairs={{0,8},{1,9},{2,10},{3,11},{4,12},{5,13},{6,14},{7,15},{8,0},{9,1},... | collective-permute-start | bytes 589832 | tf_op jit(solution)/shard_map/ppermute | solution.py:153
  145.1 8.9 %collective-permute-start.14 = (bf16[32,1025]{1,0:T(8,128)(2,1)S(1)}, bf16[32,1025]{1,0:T(8,128)(2,1)S(1)}, u32[]{:S(2)}, u32[]{:S(2)}) collective-permute-start(bf16[32,1025]{1,0:T(8,128)(2,1)S(1)} %fusion.70), channel_id=1, source_target_pairs={{0,16},{16,0},{1,17},{17,1},{2,18},{18,2},{3,19},{19,3},{4,20},{20... | collective-permute-start | bytes 196808 | tf_op jit(solution)/shard_map/ppermute | solution.py:159
  152.8 5.7 %collective-permute-start.9 = (bf16[32,3072]{1,0:T(8,128)(2,1)S(1)}, bf16[32,3072]{1,0:T(8,128)(2,1)S(1)}, u32[]{:S(2)}, u32[]{:S(2)}) collective-permute-start(bf16[32,3072]{1,0:T(8,128)(2,1)S(1)} %fusion.54), channel_id=1, source_target_pairs={{0,16},{16,0},{1,17},{17,1},{2,18},{18,2},{3,19},{19,3},{4,20},{20... | collective-permute-start | bytes 589832 | tf_op jit(solution)/shard_map/ppermute | solution.py:159
  (12 other events, 25.1 us)

commit v16 on v7

--- a/solution.py
+++ b/solution.py
@@ -159,7 +159,7 @@
         got = lax.ppermute(accs, "dp", perm)
         upper = (dp_at // (1 << step)) % 2 == 1
         accs = tuple(
-            jnp.where(upper, jnp.concatenate([g, acc], axis=0), jnp.concatenate([acc, g], axis=0))
+            jnp.concatenate([jnp.where(upper, g, acc), jnp.where(upper, acc, g)], axis=0)
             for acc, g in zip(accs, got)
         )
     return accs, tie

time: 162 us -> 162 us (level)
  no operation moved by 1% of the time
where the time goes in v16:
time: 162 us; the launch traced here: 161 us
  matrix products  39.6 us (24%)
  starting transfers between devices  36.5 us (23%)
  local copies, waits for them, and re-layouts  34.6 us (21%)
  waiting for transfers between devices  26.8 us (17%)
  other arithmetic  22.3 us (14%)
    unnamed x54, local copies, waits for them, and re-layouts  20.7 us
    ppermute x8, waiting for transfers between devices, reduce_rows(): lax.ppermute(given, ('dp', 'seq'), perm).astype(jnp.float32)  16.5 us
    ppermute x8, starting transfers between devices, reduce_rows(): lax.ppermute(given, ('dp', 'seq'), perm).astype(jnp.float32)  11.7 us
    all_to_all x1, starting transfers between devices, on_device(): lax.all_to_all(upstream, 'seq', split_axis=2, concat_axis=1, tiled=True)  7.39 us
    add x6, other arithmetic, reduce_rows(): kept + lax.ppermute(given, ('dp', 'seq'), perm).astype(jnp.float32)  7.28 us
    all_to_all x1, waiting for transfers between devices, on_device(): lax.all_to_all(normed.reshape(batches, local_rows, columns, model_width),...  6.19 us
    all_to_all x1, starting transfers between devices, on_device(): lax.all_to_all(normed.reshape(batches, local_rows, columns, model_width),...  5.86 us
    dot_general x1, matrix products, on_device(): jnp.dot(used_grads, joint_weight.T, preferred_element_type=jnp.float32)  5.68 us
  transfers between devices with their start and end apart: 19, of which 7 were waited for; matrix products, arithmetic and copies ran while one was open for 39% of the time, Pallas kernels for 0%

profile of v16, /device:TPU:0, one launch (start us, length us, event | category | flops | bytes accessed | tf_op | source)
XLA Modules:
  0.0 160.9 jit_solution(12563320903553420453)
XLA Ops:
  2.7 2.1 %reduce.20 = bf16[128,1024]{1,0:T(8,128)(2,1)S(1)} reduce(bf16[128,1,1,1024]{3,2,1,0:T(2,128)(2,1)S(1)} %bitcast.188, bf16[]{:T(256)} %broadcast.113), dimensions={1,2}, to_apply=%bitcast.180.reduce_sub_computation | reduce | bytes 524290
  5.7 7.4 %all-to-all-start.1 = ((bf16[16,2,4096]{2,1,0:T(2,128)(2,1)}), bf16[16,2,4096]{2,1,0:T(2,128)(2,1)S(1)}, u32[]{:S(2)}, u32[]{:S(2)}) async-start(bf16[16,2,4096]{2,1,0:T(2,128)(2,1)} %reshape.311), calls=%async_computation.1 | async-start | bytes 524288 | tf_op jit(solution)/shard_map/all_to_all | solution.py:201
  16.7 2.0 %convolution_convert_fusion.3 = bf16[8,128,128]{1,2,0:T(8,128)(2,1)} fusion(bf16[128,8,128]{2,1,0:T(8,128)(2,1)} %bitcast.197, f32[8,128]{1,0:T(8,128)S(1)} %get-tuple-element.56, f32[8,128,128]{1,2,0:T(8,128)S(1)} %fusion.20), kind=kOutput, calls=%fused_computation.37 | convolution fusion | flops 34079872 | bytes 1052672 | tf_op jit(solution)/shard_map/ghlm,gmhe->glhe/dot_general | solution.py:31
  21.2 2.9 %reduce.21 = bf16[128,1024]{1,0:T(8,128)(2,1)} reduce(bf16[128,1,1,1024]{3,2,1,0:T(2,128)(2,1)S(1)} %bitcast.189, bf16[]{:T(256)} %broadcast.113), dimensions={1,2}, to_apply=%bitcast.181.reduce_sub_computation | reduce | bytes 524290
  24.0 1.8 %reshape.313 = bf16[16,2,4096]{2,1,0:T(2,128)(2,1)} reshape(bf16[128,1024]{1,0:T(8,128)(2,1)} %reduce.21) | data formatting | bytes 524288
  25.9 5.9 %all-to-all-start = ((bf16[16,2,4096]{2,1,0:T(2,128)(2,1)}), bf16[16,2,4096]{2,1,0:T(2,128)(2,1)}, u32[]{:S(2)}, u32[]{:S(2)}) async-start(bf16[16,2,4096]{2,1,0:T(2,128)(2,1)} %reshape.313), calls=%async_computation | async-start | bytes 524288 | tf_op jit(solution)/shard_map/all_to_all | solution.py:184
  35.6 6.2 %all-to-all-done = bf16[16,2,4096]{2,1,0:T(2,128)(2,1)} async-done(((bf16[16,2,4096]{2,1,0:T(2,128)(2,1)}), bf16[16,2,4096]{2,1,0:T(2,128)(2,1)}, u32[]{:S(2)}, u32[]{:S(2)}) %all-to-all-start) | async-done | bytes 262176 | tf_op jit(solution)/shard_map/all_to_all | solution.py:184
  41.8 2.2 %reshape.314 = bf16[128,1,1,1024]{3,2,1,0:T(2,128)(2,1)S(1)} reshape(bf16[16,2,4096]{2,1,0:T(2,128)(2,1)} %all-to-all-done) | data formatting | bytes 524288
  45.1 3.9 %convolution_convert_fusion = bf16[128,3072]{1,0:T(8,128)(2,1)S(1)} fusion(bf16[1024,3072]{1,0:T(8,128)(2,1)} %param.12, bf16[1,1,128,1024]{2,3,1,0:T(8,128)(2,1)} %copy.112), kind=kOutput, calls=%fused_computation.4 | convolution fusion | flops 805699584 | bytes 7340032 | tf_op jit(solution)/shard_map/dot_general | solution.py:191
  51.0 2.5 %fusion.95 = (f32[8,8,16]{2,1,0:T(8,128)S(1)}, f32[8,8,16,16]{2,3,1,0:T(8,128)}) fusion(pred[16,16]{0,1:T(8,128)(4,1)S(1)} %iota_compare_fusion.1, bf16[1,16,8,1,8,128]{5,2,4,3,1,0:T(8,128)(2,1)S(1)} %get-tuple-element.47, bf16[1,16,8,1,8,128]{5,2,4,3,1,0:T(8,128)(2,1)} %get-tuple-element.46), kind=kOutput, calls=%fused_computation.156 | convolution fusion | flops 4259855 | bytes 594176 | tf_op jit(solution)/shard_map/sub | solution.py:28
  53.6 2.1 %fusion.29 = bf16[1,16,8,1,8,128]{5,1,4,2,3,0:T(8,128)(2,1)} fusion(bf16[16,8,8,128]{3,2,1,0:T(8,128)(2,1)S(1)} %copy.190, f32[8,8,16,16]{2,3,1,0:T(8,128)} %get-tuple-element.61, f32[8,8,16]{2,1,0:T(8,128)S(1)} %get-tuple-element.60), kind=kOutput, calls=%fused_computation.51 | convolution fusion | flops 4358144 | bytes 593920 | tf_op jit(solution)/shard_map/bchlm,blche->bmche/dot_general | solution.py:64
  55.7 2.9 %fusion.32 = bf16[1,16,8,1,8,128]{5,1,4,2,3,0:T(8,128)(2,1)} fusion(f32[8,8,16,16]{2,3,1,0:T(8,128)} %convolution_bitcast_fusion, bf16[1,16,8,1,8,128]{5,2,4,3,1,0:T(8,128)(2,1)} %get-tuple-element.46, f32[8,8,16,16]{2,3,1,0:T(8,128)} %get-tuple-element.61, f32[8,8,16]{2,1,0:T(8,128)S(1)} %get-tuple-element.60), kind=kOutput, calls=%fused_computation.54 | convolution fusion | flops 4441103 | bytes 659456 | tf_op jit(solution)/shard_map/bchlm,blche->bmche/dot_general | solution.py:57
  58.5 2.5 %fusion.28 = bf16[1,16,8,1,8,128]{5,1,4,2,3,0:T(8,128)(2,1)} fusion(f32[8,8,16,16]{2,3,1,0:T(8,128)S(1)} %copy-done.14, bf16[1,16,8,1,8,128]{5,2,4,3,1,0:T(8,128)(2,1)} %copy-done.18, f32[8,8,16,16]{2,3,1,0:T(8,128)} %get-tuple-element.61, f32[8,8,16]{2,1,0:T(8,128)S(1)} %get-tuple-element.60), kind=kOutput, calls=%fused_computation.50 | convolution fusion | flops 4441103 | bytes 659456 | tf_op jit(solution)/shard_map/bchlm,bmche->blche/dot_general | solution.py:51
  65.2 5.7 %fusion.30 = bf16[1,16,8,1024]{3,2,0,1:T(8,128)(2,1)} fusion(bf16[128,3072]{1,0:T(8,128)(2,1)S(1)} %reshape_reshape.7, bf16[1024,3072]{1,0:T(8,128)(2,1)} %param.12), kind=kOutput, calls=%fused_computation.52 | convolution fusion | flops 805437440 | bytes 7340032 | tf_op jit(solution)/shard_map/dot_general | solution.py:209
  70.9 4.4 %all-to-all-start.2 = ((bf16[1,16,8,1024]{3,2,0,1:T(8,128)(2,1)}), bf16[1,16,8,1024]{3,2,0,1:T(8,128)(2,1)}, u32[]{:S(2)}, u32[]{:S(2)}) async-start(bf16[1,16,8,1024]{3,2,0,1:T(8,128)(2,1)} %fusion.30), calls=%async_computation.2 | async-start | bytes 524288 | tf_op jit(solution)/shard_map/all_to_all | solution.py:231
  75.3 2.2 %fusion.31 = bf16[1,16,8,8,128]{4,1,3,2,0:T(8,128)(2,1)} fusion(bf16[1,16,8,1,8,128]{5,2,4,3,1,0:T(8,128)(2,1)} %copy-done.13, f32[8,8,16,16]{2,3,1,0:T(8,128)} %get-tuple-element.61, f32[8,8,16]{2,1,0:T(8,128)S(1)} %get-tuple-element.60), kind=kOutput, calls=%fused_computation.53 | convolution fusion | flops 4358144 | bytes 593920 | tf_op jit(solution)/shard_map/bchlm,bmche->blche/dot_general | solution.py:31
  78.7 2.1 %fusion.5 = f32[512,3072]{1,0:T(8,128)S(1)} fusion(bf16[128,3072]{1,0:T(8,128)(2,1)} %collective-permute-done.1, bf16[128,3072]{1,0:T(8,128)(2,1)S(1)} %reshape_reshape.7, bf16[256,1024]{0,1:T(8,128)(2,1)S(1)} %bitcast.191, s32[]{:T(128)S(6)} %select_n.239), kind=kOutput, calls=%fused_computation.12 | convolution fusion | flops 808452096 | bytes 8126468 | tf_op jit(solution)/shard_map/dot_general | solution.py:226
  80.9 2.7 %copy-done.1 = f32[512,3072]{1,0:T(8,128)} copy-done((f32[512,3072]{1,0:T(8,128)}, f32[512,3072]{1,0:T(8,128)S(1)}, u32[]{:S(2)}) %copy-start.1) | copy-done | bytes 6291480
  97.7 2.6 %convolution_convert_fusion.1 = bf16[8,128,128]{1,2,0:T(8,128)(2,1)} fusion(bf16[128,8,128]{0,2,1:T(8,128)(2,1)S(1)} %bitcast.196, f32[8,128,128]{1,2,0:T(8,128)} %fusion.65, f32[8,128,128]{1,2,0:T(8,128)} %get-tuple-element.57, f32[8,128]{1,0:T(8,128)S(1)} %get-tuple-element.56), kind=kOutput, calls=%fused_computation.35 | convolution fusion | flops 34604160 | bytes 1576960 | tf_op jit(solution)/shard_map/ghlm,gmhe->glhe/dot_general | solution.py:51
  100.3 2.6 %convolution_convert_fusion.6 = bf16[8,128,128]{1,2,0:T(8,128)(2,1)} fusion(bf16[128,8,128]{0,2,1:T(8,128)(2,1)S(1)} %bitcast.194, f32[8,128,128]{1,2,0:T(8,128)} %fusion.65, f32[8,128,128]{1,2,0:T(8,128)} %get-tuple-element.57, f32[8,128]{1,0:T(8,128)S(1)} %get-tuple-element.56), kind=kOutput, calls=%fused_computation.40 | convolution fusion | flops 34604160 | bytes 1576960 | tf_op jit(solution)/shard_map/ghlm,glhe->gmhe/dot_general | solution.py:57
  103.8 4.2 %all-to-all-start.3 = ((bf16[1,16,8,1024]{3,2,0,1:T(8,128)(2,1)}), bf16[1,16,8,1024]{3,2,0,1:T(8,128)(2,1)}, u32[]{:S(2)}, u32[]{:S(2)}) async-start(bf16[1,16,8,1024]{3,2,0,1:T(8,128)(2,1)} %bitcast.58), calls=%async_computation.3 | async-start | bytes 524288 | tf_op jit(solution)/shard_map/all_to_all | solution.py:257
  108.0 2.6 %collective-permute-done.10 = bf16[2,2,2,32,1025]{4,3,2,1,0:T(8,128)(2,1)} collective-permute-done((bf16[2,2,2,32,1025]{4,3,2,1,0:T(8,128)(2,1)}, bf16[2,2,2,32,1025]{4,3,2,1,0:T(8,128)(2,1)}, u32[]{:S(2)}, u32[]{:S(2)}) %collective-permute-start.10) | collective-permute-done | bytes 524832 | tf_op jit(solution)/shard_map/ppermute | solution.py:153
  114.4 2.8 %bitcast_add_fusion = f32[2,2,2,32,3072]{4,3,2,1,0:T(8,128)S(1)} fusion(bf16[2,2,2,32,3072]{4,3,2,1,0:T(8,128)(2,1)} %collective-permute-done.5, f32[2,2,2,2,32,3072]{5,4,3,2,1,0:T(8,128)} %bitcast.183, s32[]{:T(128)S(6)} %select_n.255), kind=kLoop, calls=%fused_computation.7 | loop fusion | flops 1572864 | bytes 7864324 | tf_op jit(solution)/shard_map/add | solution.py:153
  120.4 2.2 %convolution_convert_fusion.5 = bf16[8,128,128]{2,1,0:T(8,128)(2,1)} fusion(bf16[128,8,128]{0,2,1:T(8,128)(2,1)S(1)} %bitcast.200, f32[8,128]{1,0:T(8,128)S(1)} %get-tuple-element.56, f32[8,128,128]{1,2,0:T(8,128)} %copy-done.4), kind=kOutput, calls=%fused_computation.39 | convolution fusion | flops 34079872 | bytes 1052672 | tf_op jit(solution)/shard_map/ghlm,glhe->gmhe/dot_general | solution.py:64
  122.7 1.8 %copy.144 = bf16[1,1,128,1024]{3,2,1,0:T(8,128)(2,1)} copy(bf16[1,1,128,1024]{2,3,1,0:T(8,128)(2,1)} %bitcast.203) | data formatting | bytes 524288
  124.4 1.8 %copy.143 = bf16[1,1,128,1024]{3,2,1,0:T(8,128)(2,1)} copy(bf16[1,1,128,1024]{2,3,1,0:T(8,128)(2,1)} %bitcast.202) | data formatting | bytes 524288
  126.2 1.8 %copy.145 = bf16[1,1,128,1024]{3,2,1,0:T(8,128)(2,1)} copy(bf16[1,1,128,1024]{2,3,1,0:T(8,128)(2,1)} %bitcast.204) | data formatting | bytes 524288
  132.2 1.8 %bitcast_add_fusion.1 = f32[2,2,32,3072]{3,2,1,0:T(8,128)S(1)} fusion(bf16[2,2,32,3072]{3,2,1,0:T(8,128)(2,1)} %collective-permute-done.6, f32[2,2,2,32,3072]{4,3,2,1,0:T(8,128)} %copy-done.3, s32[]{:T(128)S(6)} %select_n.257), kind=kLoop, calls=%fused_computation.16 | loop fusion | flops 786432 | bytes 3932164 | tf_op jit(solution)/shard_map/add | solution.py:153
  135.8 2.8 %collective-permute-start.13 = (bf16[32,1025]{1,0:T(8,128)(2,1)S(1)}, bf16[32,1025]{1,0:T(8,128)(2,1)S(1)}, u32[]{:S(2)}, u32[]{:S(2)}) collective-permute-start(bf16[32,1025]{1,0:T(8,128)(2,1)S(1)} %fusion.77), channel_id=1, source_target_pairs={{0,8},{1,9},{2,10},{3,11},{4,12},{5,13},{6,14},{7,15},{8,0},{9,1},... | collective-permute-start | bytes 196808 | tf_op jit(solution)/shard_map/ppermute | solution.py:153
  138.7 5.4 %collective-permute-done.7 = bf16[2,32,3072]{2,1,0:T(8,128)(2,1)S(1)} collective-permute-done((bf16[2,32,3072]{2,1,0:T(8,128)(2,1)S(1)}, bf16[2,32,3072]{2,1,0:T(8,128)(2,1)S(1)}, u32[]{:S(2)}, u32[]{:S(2)}) %collective-permute-start.7) | collective-permute-done | bytes 393248 | tf_op jit(solution)/shard_map/ppermute | solution.py:153
  145.7 6.9 %collective-permute-done.8 = bf16[32,3072]{1,0:T(8,128)(2,1)S(1)} collective-permute-done((bf16[32,3072]{1,0:T(8,128)(2,1)S(1)}, bf16[32,3072]{1,0:T(8,128)(2,1)S(1)}, u32[]{:S(2)}, u32[]{:S(2)}) %collective-permute-start.8) | collective-permute-done | bytes 196640 | tf_op jit(solution)/shard_map/ppermute | solution.py:153
  154.6 3.8 %collective-permute-done.9 = bf16[32,3072]{1,0:T(8,128)(2,1)S(1)} collective-permute-done((bf16[32,3072]{1,0:T(8,128)(2,1)S(1)}, bf16[32,3072]{1,0:T(8,128)(2,1)S(1)}, u32[]{:S(2)}, u32[]{:S(2)}) %collective-permute-start.9) | collective-permute-done | bytes 196640 | tf_op jit(solution)/shard_map/ppermute | solution.py:159
  (134 shorter events, 55.2 us)
Async XLA Ops:
  0.6 18.5 %copy-start = (bf16[1024,1024]{1,0:T(8,128)(2,1)S(1)}, bf16[1024,1024]{1,0:T(8,128)(2,1)}, u32[]{:S(2)}) copy-start(bf16[1024,1024]{1,0:T(8,128)(2,1)} %param.10) | copy-start | bytes 6291460
  0.6 12.5 %copy-start.15 = (bf16[1,1,128,1024]{3,2,1,0:T(8,128)(2,1)S(1)}, bf16[1,1,128,1024]{3,2,1,0:T(8,128)(2,1)}, u32[]{:S(2)}) copy-start(bf16[1,1,128,1024]{3,2,1,0:T(8,128)(2,1)} %param.7) | copy-start | bytes 786436
  4.8 9.7 %copy-start.16 = (bf16[1,1,128,1024]{3,2,1,0:T(8,128)(2,1)S(1)}, bf16[1,1,128,1024]{3,2,1,0:T(8,128)(2,1)}, u32[]{:S(2)}) copy-start(bf16[1,1,128,1024]{3,2,1,0:T(8,128)(2,1)} %param.9) | copy-start | bytes 786436
  5.7 20.1 %all-to-all-start.1 = ((bf16[16,2,4096]{2,1,0:T(2,128)(2,1)}), bf16[16,2,4096]{2,1,0:T(2,128)(2,1)S(1)}, u32[]{:S(2)}, u32[]{:S(2)}) async-start(bf16[16,2,4096]{2,1,0:T(2,128)(2,1)} %reshape.311), calls=%async_computation.1 | async-start | bytes 524288 | tf_op jit(solution)/shard_map/all_to_all | solution.py:201
  13.3 5.3 %copy-start.6 = (bf16[1,1,128,1024]{2,3,1,0:T(8,128)(2,1)}, bf16[1,1,128,1024]{2,3,1,0:T(8,128)(2,1)S(1)}, u32[]{:S(2)}) copy-start(bf16[1,1,128,1024]{2,3,1,0:T(8,128)(2,1)S(1)} %copy.158) | copy-start | bytes 786436
  14.6 4.1 %copy-start.8 = (bf16[1,1,128,1024]{2,3,1,0:T(8,128)(2,1)}, bf16[1,1,128,1024]{2,3,1,0:T(8,128)(2,1)S(1)}, u32[]{:S(2)}) copy-start(bf16[1,1,128,1024]{2,3,1,0:T(8,128)(2,1)S(1)} %copy.157) | copy-start | bytes 786436
  18.7 13.1 %collective-permute-start.2 = (bf16[128,1024]{0,1:T(8,128)(2,1)}, bf16[128,1024]{0,1:T(8,128)(2,1)}, u32[]{:S(2)}, u32[]{:S(2)}) collective-permute-start(bf16[128,1024]{0,1:T(8,128)(2,1)} %bitcast.3), channel_id=1, source_target_pairs={{0,1},{1,0},{2,3},{3,2},{4,5},{5,4},{6,7},{7,6},{8,9},{9,8},{10,11... | collective-permute-start | bytes 786440 | tf_op jit(solution)/shard_map/ppermute | solution.py:246
  25.9 16.0 %all-to-all-start = ((bf16[16,2,4096]{2,1,0:T(2,128)(2,1)}), bf16[16,2,4096]{2,1,0:T(2,128)(2,1)}, u32[]{:S(2)}, u32[]{:S(2)}) async-start(bf16[16,2,4096]{2,1,0:T(2,128)(2,1)} %reshape.313), calls=%async_computation | async-start | bytes 524288 | tf_op jit(solution)/shard_map/all_to_all | solution.py:184
  49.7 3.9 %copy-start.18 = (bf16[1,16,8,1,8,128]{5,2,4,3,1,0:T(8,128)(2,1)}, bf16[1,16,8,1,8,128]{5,2,4,3,1,0:T(8,128)(2,1)S(1)}, u32[]{:S(2)}) copy-start(bf16[1,16,8,1,8,128]{5,2,4,3,1,0:T(8,128)(2,1)S(1)} %get-tuple-element.47) | copy-start | bytes 786436
  49.7 5.9 %copy-start.13 = (bf16[1,16,8,1,8,128]{5,2,4,3,1,0:T(8,128)(2,1)}, bf16[1,16,8,1,8,128]{5,2,4,3,1,0:T(8,128)(2,1)S(1)}, u32[]{:S(2)}) copy-start(bf16[1,16,8,1,8,128]{5,2,4,3,1,0:T(8,128)(2,1)S(1)} %get-tuple-element.45) | copy-start | bytes 786436
  61.0 16.5 %collective-permute-start = (bf16[128,1024]{0,1:T(8,128)(2,1)}, bf16[128,1024]{0,1:T(8,128)(2,1)}, u32[]{:S(2)}, u32[]{:S(2)}) collective-permute-start(bf16[128,1024]{0,1:T(8,128)(2,1)} %bitcast.6), channel_id=1, source_target_pairs={{0,1},{1,0},{2,3},{3,2},{4,5},{5,4},{6,7},{7,6},{8,9},{9,8},{10,11... | collective-permute-start | bytes 786440 | tf_op jit(solution)/shard_map/ppermute | solution.py:225
  64.7 14.0 %collective-permute-start.1 = (bf16[128,3072]{1,0:T(8,128)(2,1)S(1)}, bf16[128,3072]{1,0:T(8,128)(2,1)}, u32[]{:S(2)}, u32[]{:S(2)}) collective-permute-start(bf16[128,3072]{1,0:T(8,128)(2,1)S(1)} %reshape_reshape.7), channel_id=1, source_target_pairs={{0,1},{1,0},{2,3},{3,2},{4,5},{5,4},{6,7},{7,6},{8,9},{9,8},{10,11... | collective-permute-start | bytes 2359304 | tf_op jit(solution)/shard_map/ppermute | solution.py:225
  70.9 14.3 %all-to-all-start.2 = ((bf16[1,16,8,1024]{3,2,0,1:T(8,128)(2,1)}), bf16[1,16,8,1024]{3,2,0,1:T(8,128)(2,1)}, u32[]{:S(2)}, u32[]{:S(2)}) async-start(bf16[1,16,8,1024]{3,2,0,1:T(8,128)(2,1)} %fusion.30), calls=%async_computation.2 | async-start | bytes 524288 | tf_op jit(solution)/shard_map/all_to_all | solution.py:231
  86.3 4.8 %collective-permute-start.4 = (f32[1024]{0:T(1024)S(1)}, f32[1024]{0:T(1024)S(1)}, u32[]{:S(2)}, u32[]{:S(2)}) collective-permute-start(f32[1024]{0:T(1024)S(1)} %get-tuple-element.43), channel_id=1, source_target_pairs={{0,1},{1,0},{2,3},{3,2},{4,5},{5,4},{6,7},{7,6},{8,9},{9,8},{10,11... | collective-permute-start | bytes 12296 | tf_op jit(solution)/shard_map/ppermute | solution.py:246
  87.5 4.0 %copy-start.5 = (bf16[256,2,2,2,2,2,32]{0,6,5,4,3,2,1:T(8,128)(2,1)S(1)}, bf16[256,2,2,2,2,2,32]{0,6,5,4,3,2,1:T(8,128)(2,1)}, u32[]{:S(2)}) copy-start(bf16[256,2,2,2,2,2,32]{0,6,5,4,3,2,1:T(8,128)(2,1)} %copy.136) | copy-start | bytes 1572868
  87.5 4.0 %collective-permute-start.3 = (bf16[128,1024]{1,0:T(8,128)(2,1)S(1)}, bf16[128,1024]{1,0:T(8,128)(2,1)}, u32[]{:S(2)}, u32[]{:S(2)}) collective-permute-start(bf16[128,1024]{1,0:T(8,128)(2,1)S(1)} %fusion.46), channel_id=1, source_target_pairs={{0,1},{1,0},{2,3},{3,2},{4,5},{5,4},{6,7},{7,6},{8,9},{9,8},{10,11... | collective-permute-start | bytes 786440 | tf_op jit(solution)/shard_map/ppermute | solution.py:246
  89.7 24.6 %collective-permute-start.5 = (bf16[2,2,2,32,3072]{4,3,2,1,0:T(8,128)(2,1)}, bf16[2,2,2,32,3072]{4,3,2,1,0:T(8,128)(2,1)}, u32[]{:S(2)}, u32[]{:S(2)}) collective-permute-start(bf16[2,2,2,32,3072]{4,3,2,1,0:T(8,128)(2,1)} %fusion.4), channel_id=1, source_target_pairs={{0,2},{1,17},{2,0},{3,19},{4,6},{5,21},{6,4},{7,23},{8,10},{9,25},... | collective-permute-start | bytes 4718600 | tf_op jit(solution)/shard_map/ppermute | solution.py:153
  93.0 3.7 %copy-start.10 = (bf16[16,8,8,128]{3,2,1,0:T(8,128)(2,1)S(1)}, bf16[16,8,8,128]{3,2,1,0:T(8,128)(2,1)}, u32[]{:S(2)}) copy-start(bf16[16,8,8,128]{3,2,1,0:T(8,128)(2,1)} %copy.160) | copy-start | bytes 786436
  93.0 4.7 %copy-start.9 = (bf16[1,1,128,1024]{2,3,1,0:T(8,128)(2,1)S(1)}, bf16[1,1,128,1024]{2,3,1,0:T(8,128)(2,1)}, u32[]{:S(2)}) copy-start(bf16[1,1,128,1024]{2,3,1,0:T(8,128)(2,1)} %copy-done.8) | copy-start | bytes 786436
  95.2 5.1 %copy-start.7 = (bf16[1,1,128,1024]{2,3,1,0:T(8,128)(2,1)S(1)}, bf16[1,1,128,1024]{2,3,1,0:T(8,128)(2,1)}, u32[]{:S(2)}) copy-start(bf16[1,1,128,1024]{2,3,1,0:T(8,128)(2,1)} %copy-done.6) | copy-start | bytes 786436
  95.2 15.5 %collective-permute-start.10 = (bf16[2,2,2,32,1025]{4,3,2,1,0:T(8,128)(2,1)}, bf16[2,2,2,32,1025]{4,3,2,1,0:T(8,128)(2,1)}, u32[]{:S(2)}, u32[]{:S(2)}) collective-permute-start(bf16[2,2,2,32,1025]{4,3,2,1,0:T(8,128)(2,1)} %fusion.44), channel_id=1, source_target_pairs={{0,4},{1,5},{2,6},{3,7},{4,0},{5,1},{6,2},{7,3},{8,12},{9,13},{10,... | collective-permute-start | bytes 1574408 | tf_op jit(solution)/shard_map/ppermute | solution.py:153
  97.7 5.2 %copy-start.17 = (bf16[1,16,8,8,128]{4,1,3,2,0:T(8,128)(2,1)S(1)}, bf16[1,16,8,8,128]{4,1,3,2,0:T(8,128)(2,1)}, u32[]{:S(2)}) copy-start(bf16[1,16,8,8,128]{4,1,3,2,0:T(8,128)(2,1)} %fusion.31) | copy-start | bytes 786436
  103.8 24.2 %all-to-all-start.3 = ((bf16[1,16,8,1024]{3,2,0,1:T(8,128)(2,1)}), bf16[1,16,8,1024]{3,2,0,1:T(8,128)(2,1)}, u32[]{:S(2)}, u32[]{:S(2)}) async-start(bf16[1,16,8,1024]{3,2,0,1:T(8,128)(2,1)} %bitcast.58), calls=%async_computation.3 | async-start | bytes 524288 | tf_op jit(solution)/shard_map/all_to_all | solution.py:257
  112.9 7.5 %copy-start.12 = (bf16[128,1024]{0,1:T(8,128)(2,1)S(1)}, bf16[128,1024]{0,1:T(8,128)(2,1)}, u32[]{:S(2)}) copy-start(bf16[128,1024]{0,1:T(8,128)(2,1)} %copy.159) | copy-start | bytes 786436
  112.9 15.1 %collective-permute-start.11 = (bf16[2,2,32,1025]{3,2,1,0:T(8,128)(2,1)}, bf16[2,2,32,1025]{3,2,1,0:T(8,128)(2,1)}, u32[]{:S(2)}, u32[]{:S(2)}) collective-permute-start(bf16[2,2,32,1025]{3,2,1,0:T(8,128)(2,1)} %fusion.56), channel_id=1, source_target_pairs={{0,2},{1,17},{2,0},{3,19},{4,6},{5,21},{6,4},{7,23},{8,10},{9,25},... | collective-permute-start | bytes 787208 | tf_op jit(solution)/shard_map/ppermute | solution.py:153
  119.9 12.3 %collective-permute-start.6 = (bf16[2,2,32,3072]{3,2,1,0:T(8,128)(2,1)}, bf16[2,2,32,3072]{3,2,1,0:T(8,128)(2,1)}, u32[]{:S(2)}, u32[]{:S(2)}) collective-permute-start(bf16[2,2,32,3072]{3,2,1,0:T(8,128)(2,1)} %fusion.41), channel_id=1, source_target_pairs={{0,16},{1,5},{2,18},{3,7},{4,20},{5,1},{6,22},{7,3},{8,24},{9,13},... | collective-permute-start | bytes 2359304 | tf_op jit(solution)/shard_map/ppermute | solution.py:153
  129.1 6.7 %collective-permute-start.12 = (bf16[2,32,1025]{2,1,0:T(8,128)(2,1)S(1)}, bf16[2,32,1025]{2,1,0:T(8,128)(2,1)S(1)}, u32[]{:S(2)}, u32[]{:S(2)}) collective-permute-start(bf16[2,32,1025]{2,1,0:T(8,128)(2,1)S(1)} %fusion.70), channel_id=1, source_target_pairs={{0,16},{1,3},{2,18},{3,1},{4,20},{5,7},{6,22},{7,5},{8,24},{9,11},... | collective-permute-start | bytes 393608 | tf_op jit(solution)/shard_map/ppermute | solution.py:153
  134.1 10.0 %collective-permute-start.7 = (bf16[2,32,3072]{2,1,0:T(8,128)(2,1)S(1)}, bf16[2,32,3072]{2,1,0:T(8,128)(2,1)S(1)}, u32[]{:S(2)}, u32[]{:S(2)}) collective-permute-start(bf16[2,32,3072]{2,1,0:T(8,128)(2,1)S(1)} %fusion.54), channel_id=1, source_target_pairs={{0,4},{1,3},{2,6},{3,1},{4,0},{5,7},{6,2},{7,5},{8,12},{9,11},{10,... | collective-permute-start | bytes 1179656 | tf_op jit(solution)/shard_map/ppermute | solution.py:153
  135.8 9.2 %collective-permute-start.13 = (bf16[32,1025]{1,0:T(8,128)(2,1)S(1)}, bf16[32,1025]{1,0:T(8,128)(2,1)S(1)}, u32[]{:S(2)}, u32[]{:S(2)}) collective-permute-start(bf16[32,1025]{1,0:T(8,128)(2,1)S(1)} %fusion.77), channel_id=1, source_target_pairs={{0,8},{1,9},{2,10},{3,11},{4,12},{5,13},{6,14},{7,15},{8,0},{9,1},... | collective-permute-start | bytes 196808 | tf_op jit(solution)/shard_map/ppermute | solution.py:153
  144.2 8.4 %collective-permute-start.8 = (bf16[32,3072]{1,0:T(8,128)(2,1)S(1)}, bf16[32,3072]{1,0:T(8,128)(2,1)S(1)}, u32[]{:S(2)}, u32[]{:S(2)}) collective-permute-start(bf16[32,3072]{1,0:T(8,128)(2,1)S(1)} %fusion.69), channel_id=1, source_target_pairs={{0,8},{1,9},{2,10},{3,11},{4,12},{5,13},{6,14},{7,15},{8,0},{9,1},... | collective-permute-start | bytes 589832 | tf_op jit(solution)/shard_map/ppermute | solution.py:153
  145.0 8.2 %collective-permute-start.14 = (bf16[32,1025]{1,0:T(8,128)(2,1)S(1)}, bf16[32,1025]{1,0:T(8,128)(2,1)S(1)}, u32[]{:S(2)}, u32[]{:S(2)}) collective-permute-start(bf16[32,1025]{1,0:T(8,128)(2,1)S(1)} %fusion.71), channel_id=1, source_target_pairs={{0,16},{16,0},{1,17},{17,1},{2,18},{18,2},{3,19},{19,3},{4,20},{20... | collective-permute-start | bytes 196808 | tf_op jit(solution)/shard_map/ppermute | solution.py:159
  152.7 5.7 %collective-permute-start.9 = (bf16[32,3072]{1,0:T(8,128)(2,1)S(1)}, bf16[32,3072]{1,0:T(8,128)(2,1)S(1)}, u32[]{:S(2)}, u32[]{:S(2)}) collective-permute-start(bf16[32,3072]{1,0:T(8,128)(2,1)S(1)} %fusion.55), channel_id=1, source_target_pairs={{0,16},{16,0},{1,17},{17,1},{2,18},{18,2},{3,19},{19,3},{4,20},{20... | collective-permute-start | bytes 589832 | tf_op jit(solution)/shard_map/ppermute | solution.py:159
  (8 other events, 20.2 us)

commit v17 on v7

--- a/solution.py
+++ b/solution.py
@@ -212,7 +212,7 @@
     seq_n = lax.axis_size("seq")
     dp_n = lax.axis_size("dp")
     orders = split_orders(seq_n, dp_n)
-    out_orders = split_orders(seq_n, dp_n, z_first=True)
+    out_orders = orders
     core_odd = lax.axis_index("seq") % 2 == 1
     pair = [(member, member ^ 1) for member in range(seq_n)]
     core = lax.axis_index("seq") % 2

time: 162 us -> 164 us (1.012)
  waiting for transfers between devices: 26.8 us -> 32.8 us
  matrix products: 39.6 us -> 35.9 us
    ppermute x8, waiting for transfers between devices: 16.5 us -> 23.7 us  [reduce_rows(): lax.ppermute(given, ('dp', 'seq'), perm).astype(jnp.float32)]
    all_to_all x1, waiting for transfers between devices: 6.19 us -> 3.39 us  [on_device(): lax.all_to_all(normed.reshape(batches, local_rows, columns, model_width),...]
    all_to_all x1, starting transfers between devices: 5.86 us -> 3.99 us  [on_device(): lax.all_to_all(normed.reshape(batches, local_rows, columns, model_width),...]
    all_to_all x1, waiting for transfers between devices: 0.01 us -> 1.78 us  [on_device(): lax.all_to_all(upstream, 'seq', split_axis=2, concat_axis=1, tiled=True)]
    dot_general x2, matrix products: 4.13 us -> 2.47 us  [attend(): jnp.einsum(scores_form + ',' + keyed + '->' + layout, rounded, values, pr...]
    unnamed x54 -> x56, local copies, waits for them, and re-layouts: 20.7 us -> 21.4 us
  transfers between devices with their start and end apart: 19 -> 19, of which waited for: 7 -> 8; matrix products, arithmetic and copies ran while one was open for 39% -> 38% of each run, Pallas kernels for 0% -> 0%
where the time goes in v17:
time: 164 us; the launch traced here: 163 us
  starting transfers between devices  36.2 us (22%)
  matrix products  35.9 us (22%)
  local copies, waits for them, and re-layouts  35 us (21%)
  waiting for transfers between devices  32.8 us (20%)
  other arithmetic  21.7 us (13%)
    ppermute x8, waiting for transfers between devices, reduce_rows(): lax.ppermute(given, ('dp', 'seq'), perm).astype(jnp.float32)  23.7 us
    unnamed x56, local copies, waits for them, and re-layouts  21.4 us
    ppermute x8, starting transfers between devices, reduce_rows(): lax.ppermute(given, ('dp', 'seq'), perm).astype(jnp.float32)  11.9 us
    all_to_all x1, starting transfers between devices, on_device(): lax.all_to_all(upstream, 'seq', split_axis=2, concat_axis=1, tiled=True)  7.44 us
    add x6, other arithmetic, reduce_rows(): kept + lax.ppermute(given, ('dp', 'seq'), perm).astype(jnp.float32)  7.28 us
    dot_general x1, matrix products, on_device(): jnp.dot(used_grads, joint_weight.T, preferred_element_type=jnp.float32)  5.69 us
    all_to_all x1, starting transfers between devices, on_device(): lax.all_to_all(out_cols.reshape(batches, all_rows, col_share, feature), '...  5.53 us
    dot_general x2, matrix products, attend_back(): jnp.einsum(scores_form + ',' + layout + '->' + keyed, grad_score, queries...  5.13 us
  transfers between devices with their start and end apart: 19, of which 8 were waited for; matrix products, arithmetic and copies ran while one was open for 38% of the time, Pallas kernels for 0%

profile of v17, /device:TPU:0, one launch (start us, length us, event | category | flops | bytes accessed | tf_op | source)
XLA Modules:
  0.0 162.8 jit_solution(8538867055275249553)
XLA Ops:
  2.7 2.1 %reduce.20 = bf16[128,1024]{1,0:T(8,128)(2,1)S(1)} reduce(bf16[128,1,1,1024]{3,2,1,0:T(2,128)(2,1)S(1)} %bitcast.191, bf16[]{:T(256)} %broadcast.113), dimensions={1,2}, to_apply=%bitcast.180.reduce_sub_computation | reduce | bytes 524290
  5.7 7.4 %all-to-all-start.1 = ((bf16[16,2,4096]{2,1,0:T(2,128)(2,1)}), bf16[16,2,4096]{2,1,0:T(2,128)(2,1)}, u32[]{:S(2)}, u32[]{:S(2)}) async-start(bf16[16,2,4096]{2,1,0:T(2,128)(2,1)} %reshape.311), calls=%async_computation.1 | async-start | bytes 524288 | tf_op jit(solution)/shard_map/all_to_all | solution.py:201
  16.8 2.9 %reduce.21 = bf16[128,1024]{1,0:T(8,128)(2,1)} reduce(bf16[128,1,1,1024]{3,2,1,0:T(2,128)(2,1)S(1)} %bitcast.192, bf16[]{:T(256)} %broadcast.113), dimensions={1,2}, to_apply=%bitcast.181.reduce_sub_computation | reduce | bytes 524290
  19.7 1.8 %reshape.313 = bf16[16,2,4096]{2,1,0:T(2,128)(2,1)} reshape(bf16[128,1024]{1,0:T(8,128)(2,1)} %reduce.21) | data formatting | bytes 524288
  23.3 4.0 %all-to-all-start = ((bf16[16,2,4096]{2,1,0:T(2,128)(2,1)}), bf16[16,2,4096]{2,1,0:T(2,128)(2,1)S(1)}, u32[]{:S(2)}, u32[]{:S(2)}) async-start(bf16[16,2,4096]{2,1,0:T(2,128)(2,1)} %reshape.313), calls=%async_computation | async-start | bytes 524288 | tf_op jit(solution)/shard_map/all_to_all | solution.py:184
  29.5 2.2 %reshape.312 = bf16[128,1,1,1024]{3,2,1,0:T(2,128)(2,1)S(1)} reshape(bf16[16,2,4096]{2,1,0:T(2,128)(2,1)} %all-to-all-done.1) | data formatting | bytes 524288
  33.9 3.4 %all-to-all-done = bf16[16,2,4096]{2,1,0:T(2,128)(2,1)S(1)} async-done(((bf16[16,2,4096]{2,1,0:T(2,128)(2,1)}), bf16[16,2,4096]{2,1,0:T(2,128)(2,1)S(1)}, u32[]{:S(2)}, u32[]{:S(2)}) %all-to-all-start) | async-done | bytes 262176 | tf_op jit(solution)/shard_map/all_to_all | solution.py:184
  38.6 3.9 %convolution_convert_fusion = bf16[128,3072]{1,0:T(8,128)(2,1)S(1)} fusion(bf16[1024,3072]{1,0:T(8,128)(2,1)} %param.12, bf16[1,1,128,1024]{2,3,1,0:T(8,128)(2,1)} %copy.109), kind=kOutput, calls=%fused_computation.4 | convolution fusion | flops 805699584 | bytes 7340032 | tf_op jit(solution)/shard_map/dot_general | solution.py:191
  44.7 2.6 %fusion.94 = (f32[8,8,16]{2,1,0:T(8,128)S(1)}, f32[8,8,16,16]{2,3,1,0:T(8,128)}) fusion(pred[16,16]{0,1:T(8,128)(4,1)S(1)} %iota_compare_fusion.1, bf16[1,16,8,1,8,128]{5,2,4,3,1,0:T(8,128)(2,1)} %get-tuple-element.47, bf16[1,16,8,1,8,128]{5,2,4,3,1,0:T(8,128)(2,1)} %get-tuple-element.46), kind=kOutput, calls=%fused_computation.149 | convolution fusion | flops 4259855 | bytes 594176 | tf_op jit(solution)/shard_map/sub | solution.py:28
  47.3 2.1 %fusion.29 = bf16[1,16,8,1,8,128]{5,1,4,2,3,0:T(8,128)(2,1)} fusion(bf16[16,8,8,128]{3,2,1,0:T(8,128)(2,1)S(1)} %copy-done.14, f32[8,8,16,16]{2,3,1,0:T(8,128)} %get-tuple-element.55, f32[8,8,16]{2,1,0:T(8,128)S(1)} %get-tuple-element.54), kind=kOutput, calls=%fused_computation.51 | convolution fusion | flops 4358144 | bytes 593920 | tf_op jit(solution)/shard_map/bchlm,blche->bmche/dot_general | solution.py:64
  49.4 2.5 %fusion.32 = bf16[1,16,8,1,8,128]{5,1,4,2,3,0:T(8,128)(2,1)} fusion(f32[8,8,16,16]{2,3,1,0:T(8,128)S(1)} %convolution_bitcast_fusion, bf16[1,16,8,1,8,128]{5,2,4,3,1,0:T(8,128)(2,1)} %get-tuple-element.46, f32[8,8,16,16]{2,3,1,0:T(8,128)} %get-tuple-element.55, f32[8,8,16]{2,1,0:T(8,128)S(1)} %get-tuple-element.54), kind=kOutput, calls=%fused_computation.54 | convolution fusion | flops 4441103 | bytes 659456 | tf_op jit(solution)/shard_map/bchlm,blche->bmche/dot_general | solution.py:57
  51.9 2.4 %fusion.28 = bf16[1,16,8,1,8,128]{5,1,4,2,3,0:T(8,128)(2,1)} fusion(f32[8,8,16,16]{2,3,1,0:T(8,128)S(1)} %convolution_bitcast_fusion, bf16[1,16,8,1,8,128]{5,2,4,3,1,0:T(8,128)(2,1)S(1)} %copy-done.20, f32[8,8,16,16]{2,3,1,0:T(8,128)} %get-tuple-element.55, f32[8,8,16]{2,1,0:T(8,128)S(1)} %get-tuple-element.54), kind=kOutput, calls=%fused_computation.50 | convolution fusion | flops 4441103 | bytes 659456 | tf_op jit(solution)/shard_map/bchlm,bmche->blche/dot_general | solution.py:51
  58.5 5.7 %fusion.30 = bf16[1,16,8,1024]{3,2,0,1:T(8,128)(2,1)} fusion(bf16[128,3072]{1,0:T(8,128)(2,1)S(1)} %reshape_reshape.7, bf16[1024,3072]{1,0:T(8,128)(2,1)} %param.12), kind=kOutput, calls=%fused_computation.52 | convolution fusion | flops 805437440 | bytes 7340032 | tf_op jit(solution)/shard_map/dot_general | solution.py:209
  64.2 4.4 %all-to-all-start.2 = ((bf16[1,16,8,1024]{3,2,0,1:T(8,128)(2,1)}), bf16[1,16,8,1024]{3,2,0,1:T(8,128)(2,1)}, u32[]{:S(2)}, u32[]{:S(2)}) async-start(bf16[1,16,8,1024]{3,2,0,1:T(8,128)(2,1)} %fusion.30), calls=%async_computation.2 | async-start | bytes 524288 | tf_op jit(solution)/shard_map/all_to_all | solution.py:231
  68.6 2.2 %fusion.31 = bf16[1,16,8,8,128]{4,1,3,2,0:T(8,128)(2,1)} fusion(bf16[1,16,8,1,8,128]{5,2,4,3,1,0:T(8,128)(2,1)} %copy-done.15, f32[8,8,16,16]{2,3,1,0:T(8,128)} %get-tuple-element.55, f32[8,8,16]{2,1,0:T(8,128)S(1)} %get-tuple-element.54), kind=kOutput, calls=%fused_computation.53 | convolution fusion | flops 4358144 | bytes 593920 | tf_op jit(solution)/shard_map/bchlm,bmche->blche/dot_general | solution.py:31
  72.0 2.1 %fusion.5 = f32[512,3072]{1,0:T(8,128)S(1)} fusion(bf16[128,3072]{1,0:T(8,128)(2,1)} %collective-permute-done.1, bf16[128,3072]{1,0:T(8,128)(2,1)S(1)} %reshape_reshape.7, bf16[256,1024]{0,1:T(8,128)(2,1)S(1)} %bitcast.194, s32[]{:T(128)S(6)} %select_n.221), kind=kOutput, calls=%fused_computation.12 | convolution fusion | flops 808452096 | bytes 8126468 | tf_op jit(solution)/shard_map/dot_general | solution.py:226
  74.2 2.7 %copy-done.1 = f32[512,3072]{1,0:T(8,128)} copy-done((f32[512,3072]{1,0:T(8,128)}, f32[512,3072]{1,0:T(8,128)S(1)}, u32[]{:S(2)}) %copy-start.1) | copy-done | bytes 6291480
  90.2 2.6 %convolution_convert_fusion.1 = bf16[8,128,128]{1,2,0:T(8,128)(2,1)} fusion(bf16[128,8,128]{0,2,1:T(8,128)(2,1)S(1)} %bitcast.199, f32[8,128,128]{1,2,0:T(8,128)} %fusion.66, f32[8,128,128]{1,2,0:T(8,128)} %get-tuple-element.51, f32[8,128]{1,0:T(8,128)S(1)} %get-tuple-element.50), kind=kOutput, calls=%fused_computation.35 | convolution fusion | flops 34604160 | bytes 1576960 | tf_op jit(solution)/shard_map/ghlm,gmhe->glhe/dot_general | solution.py:51
  92.9 2.6 %convolution_convert_fusion.6 = bf16[8,128,128]{1,2,0:T(8,128)(2,1)} fusion(bf16[128,8,128]{0,2,1:T(8,128)(2,1)S(1)} %bitcast.197, f32[8,128,128]{1,2,0:T(8,128)} %fusion.66, f32[8,128,128]{1,2,0:T(8,128)} %get-tuple-element.51, f32[8,128]{1,0:T(8,128)S(1)} %get-tuple-element.50), kind=kOutput, calls=%fused_computation.40 | convolution fusion | flops 34604160 | bytes 1576960 | tf_op jit(solution)/shard_map/ghlm,glhe->gmhe/dot_general | solution.py:57
  96.4 5.5 %all-to-all-start.3 = ((bf16[1,16,8,1024]{3,2,0,1:T(8,128)(2,1)}), bf16[1,16,8,1024]{3,2,0,1:T(8,128)(2,1)}, u32[]{:S(2)}, u32[]{:S(2)}) async-start(bf16[1,16,8,1024]{3,2,0,1:T(8,128)(2,1)} %bitcast.56), calls=%async_computation.3 | async-start | bytes 524288 | tf_op jit(solution)/shard_map/all_to_all | solution.py:257
  101.9 10.7 %collective-permute-done.10 = bf16[2,2,2,32,1025]{4,3,2,1,0:T(8,128)(2,1)} collective-permute-done((bf16[2,2,2,32,1025]{4,3,2,1,0:T(8,128)(2,1)}, bf16[2,2,2,32,1025]{4,3,2,1,0:T(8,128)(2,1)}, u32[]{:S(2)}, u32[]{:S(2)}) %collective-permute-start.10) | collective-permute-done | bytes 524832 | tf_op jit(solution)/shard_map/ppermute | solution.py:153
  116.3 2.8 %bitcast_add_fusion = f32[2,2,2,32,3072]{4,3,2,1,0:T(8,128)S(1)} fusion(bf16[2,2,2,32,3072]{4,3,2,1,0:T(8,128)(2,1)} %collective-permute-done.5, f32[2,2,2,2,32,3072]{5,4,3,2,1,0:T(8,128)} %bitcast.183, s32[]{:T(128)S(6)} %select_n.234), kind=kLoop, calls=%fused_computation.7 | loop fusion | flops 1572864 | bytes 7864324 | tf_op jit(solution)/shard_map/add | solution.py:153
  122.4 2.2 %convolution_convert_fusion.5 = bf16[8,128,128]{2,1,0:T(8,128)(2,1)} fusion(bf16[128,8,128]{0,2,1:T(8,128)(2,1)S(1)} %bitcast.203, f32[8,128]{1,0:T(8,128)S(1)} %get-tuple-element.50, f32[8,128,128]{1,2,0:T(8,128)} %copy-done.4), kind=kOutput, calls=%fused_computation.39 | convolution fusion | flops 34079872 | bytes 1052672 | tf_op jit(solution)/shard_map/ghlm,glhe->gmhe/dot_general | solution.py:64
  124.6 1.8 %copy.139 = bf16[1,1,128,1024]{3,2,1,0:T(8,128)(2,1)} copy(bf16[1,1,128,1024]{2,3,1,0:T(8,128)(2,1)} %bitcast.206) | data formatting | bytes 524288
  126.4 1.8 %copy.138 = bf16[1,1,128,1024]{3,2,1,0:T(8,128)(2,1)} copy(bf16[1,1,128,1024]{2,3,1,0:T(8,128)(2,1)} %bitcast.205) | data formatting | bytes 524288
  128.2 1.8 %copy.140 = bf16[1,1,128,1024]{3,2,1,0:T(8,128)(2,1)} copy(bf16[1,1,128,1024]{2,3,1,0:T(8,128)(2,1)} %bitcast.207) | data formatting | bytes 524288
  134.1 1.8 %bitcast_add_fusion.1 = f32[2,2,32,3072]{3,2,1,0:T(8,128)S(1)} fusion(bf16[2,2,32,3072]{3,2,1,0:T(8,128)(2,1)} %collective-permute-done.6, f32[2,2,2,32,3072]{4,3,2,1,0:T(8,128)} %copy-done.3, s32[]{:T(128)S(6)} %select_n.238), kind=kLoop, calls=%fused_computation.16 | loop fusion | flops 786432 | bytes 3932164 | tf_op jit(solution)/shard_map/add | solution.py:153
  137.5 2.5 %collective-permute-start.13 = (bf16[32,1025]{1,0:T(8,128)(2,1)S(1)}, bf16[32,1025]{1,0:T(8,128)(2,1)S(1)}, u32[]{:S(2)}, u32[]{:S(2)}) collective-permute-start(bf16[32,1025]{1,0:T(8,128)(2,1)S(1)} %fusion.77), channel_id=1, source_target_pairs={{0,8},{1,9},{2,10},{3,11},{4,12},{5,13},{6,14},{7,15},{8,0},{9,1},... | collective-permute-start | bytes 196808 | tf_op jit(solution)/shard_map/ppermute | solution.py:153
  139.9 5.8 %collective-permute-done.7 = bf16[2,32,3072]{2,1,0:T(8,128)(2,1)S(1)} collective-permute-done((bf16[2,32,3072]{2,1,0:T(8,128)(2,1)S(1)}, bf16[2,32,3072]{2,1,0:T(8,128)(2,1)S(1)}, u32[]{:S(2)}, u32[]{:S(2)}) %collective-permute-start.7) | collective-permute-done | bytes 393248 | tf_op jit(solution)/shard_map/ppermute | solution.py:153
  145.8 2.6 %collective-permute-start.8 = (bf16[32,3072]{1,0:T(8,128)(2,1)S(1)}, bf16[32,3072]{1,0:T(8,128)(2,1)S(1)}, u32[]{:S(2)}, u32[]{:S(2)}) collective-permute-start(bf16[32,3072]{1,0:T(8,128)(2,1)S(1)} %fusion.70), channel_id=1, source_target_pairs={{0,8},{1,9},{2,10},{3,11},{4,12},{5,13},{6,14},{7,15},{8,0},{9,1},... | collective-permute-start | bytes 589832 | tf_op jit(solution)/shard_map/ppermute | solution.py:153
  149.0 5.5 %collective-permute-done.8 = bf16[32,3072]{1,0:T(8,128)(2,1)S(1)} collective-permute-done((bf16[32,3072]{1,0:T(8,128)(2,1)S(1)}, bf16[32,3072]{1,0:T(8,128)(2,1)S(1)}, u32[]{:S(2)}, u32[]{:S(2)}) %collective-permute-start.8) | collective-permute-done | bytes 196640 | tf_op jit(solution)/shard_map/ppermute | solution.py:153
  156.6 3.7 %collective-permute-done.9 = bf16[32,3072]{1,0:T(8,128)(2,1)S(1)} collective-permute-done((bf16[32,3072]{1,0:T(8,128)(2,1)S(1)}, bf16[32,3072]{1,0:T(8,128)(2,1)S(1)}, u32[]{:S(2)}, u32[]{:S(2)}) %collective-permute-start.9) | collective-permute-done | bytes 196640 | tf_op jit(solution)/shard_map/ppermute | solution.py:159
  (134 shorter events, 53.4 us)
Async XLA Ops:
  0.6 15.1 %copy-start = (bf16[1024,1024]{1,0:T(8,128)(2,1)S(1)}, bf16[1024,1024]{1,0:T(8,128)(2,1)}, u32[]{:S(2)}) copy-start(bf16[1024,1024]{1,0:T(8,128)(2,1)} %param.10) | copy-start | bytes 6291460
  0.6 12.6 %copy-start.16 = (bf16[1,1,128,1024]{3,2,1,0:T(8,128)(2,1)S(1)}, bf16[1,1,128,1024]{3,2,1,0:T(8,128)(2,1)}, u32[]{:S(2)}) copy-start(bf16[1,1,128,1024]{3,2,1,0:T(8,128)(2,1)} %param.7) | copy-start | bytes 786436
  0.7 12.7 %copy-start.17 = (bf16[1,1,128,1024]{3,2,1,0:T(8,128)(2,1)S(1)}, bf16[1,1,128,1024]{3,2,1,0:T(8,128)(2,1)}, u32[]{:S(2)}) copy-start(bf16[1,1,128,1024]{3,2,1,0:T(8,128)(2,1)} %param.8) | copy-start | bytes 786436
  4.8 8.7 %copy-start.18 = (bf16[1,1,128,1024]{3,2,1,0:T(8,128)(2,1)S(1)}, bf16[1,1,128,1024]{3,2,1,0:T(8,128)(2,1)}, u32[]{:S(2)}) copy-start(bf16[1,1,128,1024]{3,2,1,0:T(8,128)(2,1)} %param.9) | copy-start | bytes 786436
  5.7 17.5 %all-to-all-start.1 = ((bf16[16,2,4096]{2,1,0:T(2,128)(2,1)}), bf16[16,2,4096]{2,1,0:T(2,128)(2,1)}, u32[]{:S(2)}, u32[]{:S(2)}) async-start(bf16[16,2,4096]{2,1,0:T(2,128)(2,1)} %reshape.311), calls=%async_computation.1 | async-start | bytes 524288 | tf_op jit(solution)/shard_map/all_to_all | solution.py:201
  15.3 12.1 %collective-permute-start.2 = (bf16[128,1024]{0,1:T(8,128)(2,1)S(1)}, bf16[128,1024]{0,1:T(8,128)(2,1)}, u32[]{:S(2)}, u32[]{:S(2)}) collective-permute-start(bf16[128,1024]{0,1:T(8,128)(2,1)S(1)} %bitcast.187), channel_id=1, source_target_pairs={{0,1},{1,0},{2,3},{3,2},{4,5},{5,4},{6,7},{7,6},{8,9},{9,8},{10,11... | collective-permute-start | bytes 786440 | tf_op jit(solution)/shard_map/ppermute | solution.py:246
  23.3 14.0 %all-to-all-start = ((bf16[16,2,4096]{2,1,0:T(2,128)(2,1)}), bf16[16,2,4096]{2,1,0:T(2,128)(2,1)S(1)}, u32[]{:S(2)}, u32[]{:S(2)}) async-start(bf16[16,2,4096]{2,1,0:T(2,128)(2,1)} %reshape.313), calls=%async_computation | async-start | bytes 524288 | tf_op jit(solution)/shard_map/all_to_all | solution.py:184
  38.6 5.5 %copy-start.14 = (bf16[16,8,8,128]{3,2,1,0:T(8,128)(2,1)S(1)}, bf16[16,8,8,128]{3,2,1,0:T(8,128)(2,1)}, u32[]{:S(2)}) copy-start(bf16[16,8,8,128]{3,2,1,0:T(8,128)(2,1)} %copy.182) | copy-start | bytes 786436
  54.2 16.6 %collective-permute-start = (bf16[128,1024]{0,1:T(8,128)(2,1)}, bf16[128,1024]{0,1:T(8,128)(2,1)}, u32[]{:S(2)}, u32[]{:S(2)}) collective-permute-start(bf16[128,1024]{0,1:T(8,128)(2,1)} %bitcast.6), channel_id=1, source_target_pairs={{0,1},{1,0},{2,3},{3,2},{4,5},{5,4},{6,7},{7,6},{8,9},{9,8},{10,11... | collective-permute-start | bytes 786440 | tf_op jit(solution)/shard_map/ppermute | solution.py:225
  58.0 14.1 %collective-permute-start.1 = (bf16[128,3072]{1,0:T(8,128)(2,1)S(1)}, bf16[128,3072]{1,0:T(8,128)(2,1)}, u32[]{:S(2)}, u32[]{:S(2)}) collective-permute-start(bf16[128,3072]{1,0:T(8,128)(2,1)S(1)} %reshape_reshape.7), channel_id=1, source_target_pairs={{0,1},{1,0},{2,3},{3,2},{4,5},{5,4},{6,7},{7,6},{8,9},{9,8},{10,11... | collective-permute-start | bytes 2359304 | tf_op jit(solution)/shard_map/ppermute | solution.py:225
  64.2 14.3 %all-to-all-start.2 = ((bf16[1,16,8,1024]{3,2,0,1:T(8,128)(2,1)}), bf16[1,16,8,1024]{3,2,0,1:T(8,128)(2,1)}, u32[]{:S(2)}, u32[]{:S(2)}) async-start(bf16[1,16,8,1024]{3,2,0,1:T(8,128)(2,1)} %fusion.30), calls=%async_computation.2 | async-start | bytes 524288 | tf_op jit(solution)/shard_map/all_to_all | solution.py:231
  74.2 2.7 %copy-start.1 = (f32[512,3072]{1,0:T(8,128)}, f32[512,3072]{1,0:T(8,128)S(1)}, u32[]{:S(2)}) copy-start(f32[512,3072]{1,0:T(8,128)S(1)} %fusion.5) | copy-start | bytes 18874372
  79.6 4.8 %collective-permute-start.4 = (f32[1024]{0:T(1024)S(1)}, f32[1024]{0:T(1024)S(1)}, u32[]{:S(2)}, u32[]{:S(2)}) collective-permute-start(f32[1024]{0:T(1024)S(1)} %get-tuple-element.43), channel_id=1, source_target_pairs={{0,1},{1,0},{2,3},{3,2},{4,5},{5,4},{6,7},{7,6},{8,9},{9,8},{10,11... | collective-permute-start | bytes 12296 | tf_op jit(solution)/shard_map/ppermute | solution.py:246
  80.8 4.0 %copy-start.5 = (bf16[256,2,2,2,2,2,32]{0,6,5,4,3,2,1:T(8,128)(2,1)S(1)}, bf16[256,2,2,2,2,2,32]{0,6,5,4,3,2,1:T(8,128)(2,1)}, u32[]{:S(2)}) copy-start(bf16[256,2,2,2,2,2,32]{0,6,5,4,3,2,1:T(8,128)(2,1)} %copy.131) | copy-start | bytes 1572868
  80.8 4.0 %collective-permute-start.3 = (bf16[128,1024]{1,0:T(8,128)(2,1)S(1)}, bf16[128,1024]{1,0:T(8,128)(2,1)}, u32[]{:S(2)}, u32[]{:S(2)}) collective-permute-start(bf16[128,1024]{1,0:T(8,128)(2,1)S(1)} %fusion.46), channel_id=1, source_target_pairs={{0,1},{1,0},{2,3},{3,2},{4,5},{5,4},{6,7},{7,6},{8,9},{9,8},{10,11... | collective-permute-start | bytes 786440 | tf_op jit(solution)/shard_map/ppermute | solution.py:246
  83.1 33.3 %collective-permute-start.5 = (bf16[2,2,2,32,3072]{4,3,2,1,0:T(8,128)(2,1)}, bf16[2,2,2,32,3072]{4,3,2,1,0:T(8,128)(2,1)}, u32[]{:S(2)}, u32[]{:S(2)}) collective-permute-start(bf16[2,2,2,32,3072]{4,3,2,1,0:T(8,128)(2,1)} %fusion.4), channel_id=1, source_target_pairs={{0,2},{1,17},{2,0},{3,19},{4,6},{5,21},{6,4},{7,23},{8,10},{9,25},... | collective-permute-start | bytes 4718600 | tf_op jit(solution)/shard_map/ppermute | solution.py:153
  86.3 2.9 %copy-start.11 = (bf16[16,8,8,128]{3,2,1,0:T(8,128)(2,1)S(1)}, bf16[16,8,8,128]{3,2,1,0:T(8,128)(2,1)}, u32[]{:S(2)}) copy-start(bf16[16,8,8,128]{3,2,1,0:T(8,128)(2,1)} %copy-done.10) | copy-start | bytes 786436
  86.3 2.9 %copy-start.12 = (bf16[128,1024]{0,1:T(8,128)(2,1)S(1)}, bf16[128,1024]{0,1:T(8,128)(2,1)}, u32[]{:S(2)}) copy-start(bf16[128,1024]{0,1:T(8,128)(2,1)} %copy.152) | copy-start | bytes 786436
  86.3 3.9 %copy-start.9 = (bf16[1,1,128,1024]{2,3,1,0:T(8,128)(2,1)S(1)}, bf16[1,1,128,1024]{2,3,1,0:T(8,128)(2,1)}, u32[]{:S(2)}) copy-start(bf16[1,1,128,1024]{2,3,1,0:T(8,128)(2,1)} %copy-done.8) | copy-start | bytes 786436
  88.5 4.3 %copy-start.7 = (bf16[1,1,128,1024]{2,3,1,0:T(8,128)(2,1)S(1)}, bf16[1,1,128,1024]{2,3,1,0:T(8,128)(2,1)}, u32[]{:S(2)}) copy-start(bf16[1,1,128,1024]{2,3,1,0:T(8,128)(2,1)} %copy-done.6) | copy-start | bytes 786436
  88.5 24.1 %collective-permute-start.10 = (bf16[2,2,2,32,1025]{4,3,2,1,0:T(8,128)(2,1)}, bf16[2,2,2,32,1025]{4,3,2,1,0:T(8,128)(2,1)}, u32[]{:S(2)}, u32[]{:S(2)}) collective-permute-start(bf16[2,2,2,32,1025]{4,3,2,1,0:T(8,128)(2,1)} %fusion.44), channel_id=1, source_target_pairs={{0,2},{1,17},{2,0},{3,19},{4,6},{5,21},{6,4},{7,23},{8,10},{9,25},... | collective-permute-start | bytes 1574408 | tf_op jit(solution)/shard_map/ppermute | solution.py:153
  90.2 5.2 %copy-start.19 = (bf16[1,16,8,8,128]{4,1,3,2,0:T(8,128)(2,1)S(1)}, bf16[1,16,8,8,128]{4,1,3,2,0:T(8,128)(2,1)}, u32[]{:S(2)}) copy-start(bf16[1,16,8,8,128]{4,1,3,2,0:T(8,128)(2,1)} %fusion.31) | copy-start | bytes 786436
  96.4 33.6 %all-to-all-start.3 = ((bf16[1,16,8,1024]{3,2,0,1:T(8,128)(2,1)}), bf16[1,16,8,1024]{3,2,0,1:T(8,128)(2,1)}, u32[]{:S(2)}, u32[]{:S(2)}) async-start(bf16[1,16,8,1024]{3,2,0,1:T(8,128)(2,1)} %bitcast.56), calls=%async_computation.3 | async-start | bytes 524288 | tf_op jit(solution)/shard_map/all_to_all | solution.py:257
  114.8 7.5 %copy-start.13 = (bf16[128,1024]{0,1:T(8,128)(2,1)S(1)}, bf16[128,1024]{0,1:T(8,128)(2,1)}, u32[]{:S(2)}) copy-start(bf16[128,1024]{0,1:T(8,128)(2,1)} %copy.152) | copy-start | bytes 786436
  114.9 15.1 %collective-permute-start.11 = (bf16[2,2,32,1025]{3,2,1,0:T(8,128)(2,1)}, bf16[2,2,32,1025]{3,2,1,0:T(8,128)(2,1)}, u32[]{:S(2)}, u32[]{:S(2)}) collective-permute-start(bf16[2,2,32,1025]{3,2,1,0:T(8,128)(2,1)} %fusion.57), channel_id=1, source_target_pairs={{0,16},{1,5},{2,18},{3,7},{4,20},{5,1},{6,22},{7,3},{8,24},{9,13},... | collective-permute-start | bytes 787208 | tf_op jit(solution)/shard_map/ppermute | solution.py:153
  121.8 12.3 %collective-permute-start.6 = (bf16[2,2,32,3072]{3,2,1,0:T(8,128)(2,1)}, bf16[2,2,32,3072]{3,2,1,0:T(8,128)(2,1)}, u32[]{:S(2)}, u32[]{:S(2)}) collective-permute-start(bf16[2,2,32,3072]{3,2,1,0:T(8,128)(2,1)} %fusion.41), channel_id=1, source_target_pairs={{0,16},{1,5},{2,18},{3,7},{4,20},{5,1},{6,22},{7,3},{8,24},{9,13},... | collective-permute-start | bytes 2359304 | tf_op jit(solution)/shard_map/ppermute | solution.py:153
  131.0 6.4 %collective-permute-start.12 = (bf16[2,32,1025]{2,1,0:T(8,128)(2,1)S(1)}, bf16[2,32,1025]{2,1,0:T(8,128)(2,1)S(1)}, u32[]{:S(2)}, u32[]{:S(2)}) collective-permute-start(bf16[2,32,1025]{2,1,0:T(8,128)(2,1)S(1)} %fusion.71), channel_id=1, source_target_pairs={{0,4},{1,3},{2,6},{3,1},{4,0},{5,7},{6,2},{7,5},{8,12},{9,11},{10,... | collective-permute-start | bytes 393608 | tf_op jit(solution)/shard_map/ppermute | solution.py:153
  136.0 9.7 %collective-permute-start.7 = (bf16[2,32,3072]{2,1,0:T(8,128)(2,1)S(1)}, bf16[2,32,3072]{2,1,0:T(8,128)(2,1)S(1)}, u32[]{:S(2)}, u32[]{:S(2)}) collective-permute-start(bf16[2,32,3072]{2,1,0:T(8,128)(2,1)S(1)} %fusion.54), channel_id=1, source_target_pairs={{0,4},{1,3},{2,6},{3,1},{4,0},{5,7},{6,2},{7,5},{8,12},{9,11},{10,... | collective-permute-start | bytes 1179656 | tf_op jit(solution)/shard_map/ppermute | solution.py:153
  137.5 10.9 %collective-permute-start.13 = (bf16[32,1025]{1,0:T(8,128)(2,1)S(1)}, bf16[32,1025]{1,0:T(8,128)(2,1)S(1)}, u32[]{:S(2)}, u32[]{:S(2)}) collective-permute-start(bf16[32,1025]{1,0:T(8,128)(2,1)S(1)} %fusion.77), channel_id=1, source_target_pairs={{0,8},{1,9},{2,10},{3,11},{4,12},{5,13},{6,14},{7,15},{8,0},{9,1},... | collective-permute-start | bytes 196808 | tf_op jit(solution)/shard_map/ppermute | solution.py:153
  145.8 8.7 %collective-permute-start.8 = (bf16[32,3072]{1,0:T(8,128)(2,1)S(1)}, bf16[32,3072]{1,0:T(8,128)(2,1)S(1)}, u32[]{:S(2)}, u32[]{:S(2)}) collective-permute-start(bf16[32,3072]{1,0:T(8,128)(2,1)S(1)} %fusion.70), channel_id=1, source_target_pairs={{0,8},{1,9},{2,10},{3,11},{4,12},{5,13},{6,14},{7,15},{8,0},{9,1},... | collective-permute-start | bytes 589832 | tf_op jit(solution)/shard_map/ppermute | solution.py:153
  148.4 6.9 %collective-permute-start.14 = (bf16[32,1025]{1,0:T(8,128)(2,1)S(1)}, bf16[32,1025]{1,0:T(8,128)(2,1)S(1)}, u32[]{:S(2)}, u32[]{:S(2)}) collective-permute-start(bf16[32,1025]{1,0:T(8,128)(2,1)S(1)} %fusion.72), channel_id=1, source_target_pairs={{0,16},{16,0},{1,17},{17,1},{2,18},{18,2},{3,19},{19,3},{4,20},{20... | collective-permute-start | bytes 196808 | tf_op jit(solution)/shard_map/ppermute | solution.py:159
  154.6 5.7 %collective-permute-start.9 = (bf16[32,3072]{1,0:T(8,128)(2,1)S(1)}, bf16[32,3072]{1,0:T(8,128)(2,1)S(1)}, u32[]{:S(2)}, u32[]{:S(2)}) collective-permute-start(bf16[32,3072]{1,0:T(8,128)(2,1)S(1)} %fusion.55), channel_id=1, source_target_pairs={{0,16},{16,0},{1,17},{17,1},{2,18},{18,2},{3,19},{19,3},{4,20},{20... | collective-permute-start | bytes 589832 | tf_op jit(solution)/shard_map/ppermute | solution.py:159
  (9 other events, 13.8 us)
